TPU v7x, 32 devices: a whole 2x2x4 slice. The times are simulated.
32 devices in a mesh: gx: 4 (over x, core), gy: 8 (over z, y).
Axes of the slice: x: 2, y: 2, z: 4, core: 2. Of those that a mesh axis runs over, the one named last changes fastest.
Arguments:
- c_upper: bfloat16 [4, 8, 96, 96], P('gx', 'gy'), may hold values from -60 to 60
- edge_upper: bfloat16 [4, 8, 96, 1536], P('gx', 'gy'), may hold values from -60 to 60
- edge_left: bfloat16 [4, 8, 96, 1536], P('gx', 'gy'), may hold values from -60 to 60
- c_lower: bfloat16 [4, 8, 96, 96], P('gx', 'gy'), may hold values from -60 to 60
- edge_lower: bfloat16 [4, 8, 96, 1536], P('gx', 'gy'), may hold values from -60 to 60
- site_ket: bfloat16 [4, 8, 2, 256], P('gx', 'gy'), may hold values from -6 to 6
- time_gate: float32 [2, 2], replicated, may hold values from -3 to 3
- quench_sites: int32 [4], replicated, may hold values from 0 to 31
Outputs:
- new_c_upper: bfloat16 [4, 8, 96, 96], P('gx', 'gy')
- new_edge_left: bfloat16 [4, 8, 96, 1536], P('gx', 'gy')
- new_c_lower: bfloat16 [4, 8, 96, 96], P('gx', 'gy')
All inputs are finite; a program needn't handle non-finite values.
Results may differ from a plain program's by a relative error of at most 0.03.
Values may be sent and summed in bfloat16 or wider, within the bound.
No kernel may reach another device: no remote copies, remote signals or barrier semaphores. Data moves between devices by JAX's collectives and lax.ppermute only.
A program may use at most 64 MiB of HBM per device.

v0:
```python
import math

import jax
import jax.numpy as jnp
from jax import lax
from jax.experimental import pallas as pl
from jax.experimental.pallas import tpu as pltpu
from jax.sharding import PartitionSpec as P

NS_ITERS = 6
STEPS = 2
LANES = 128


def passed_along(shard, axis, by):
    peers = lax.axis_size(axis)
    return lax.ppermute(shard, axis, [(i, (i + by) % peers) for i in range(peers)])


def split_bf16(x):
    hi = x.astype(jnp.bfloat16)
    return hi, (x - hi.astype(jnp.float32)).astype(jnp.bfloat16)


def dot3(a, b, dims):
    ah, al = split_bf16(a)
    bh, bl = split_bf16(b)
    out = lambda p, q: lax.dot_general(p, q, (dims, ((), ())), preferred_element_type=jnp.float32)
    return out(ah, bh) + (out(ah, bl) + out(al, bh))


def polar_kernel(y_ref, o_ref):
    count = y_ref.shape[0]
    ys = []
    for b in range(count):
        y = y_ref[b]
        ys.append(y / jnp.sqrt(jnp.sum(y * y) + 1e-06))
    for sweep in range(NS_ITERS):
        grams = [dot3(y, y, ((1,), (1,))) for y in ys]
        ys = [1.5 * y - 0.5 * dot3(g, y, ((1,), (0,))) for g, y in zip(grams, ys)]
    for b in range(count):
        o_ref[b] = ys[b]


def polar_factor_t(stack):
    return pl.pallas_call(
        polar_kernel,
        out_shape=jax.ShapeDtypeStruct(stack.shape, jnp.float32),
        compiler_params=pltpu.CompilerParams(vmem_limit_bytes=32 * 1024 * 1024),
    )(stack)


def shifted(tree, dx, dy):
    nx = lax.axis_size("gx")
    ny = lax.axis_size("gy")
    pairs = []
    for x in range(nx):
        for y in range(ny):
            pairs.append((x * ny + y, ((x + dx) % nx) * ny + (y + dy) % ny))
    return lax.ppermute(tree, ("gx", "gy"), pairs)


def unit_scaled(tensor):
    return tensor / jnp.sqrt(jnp.mean(tensor * tensor) + 1e-06)


def edge_kernel(wd_ref, pm_ref, t_ref, qt_ref, o_ref, f_ref, g_ref):
    n = qt_ref.shape[0]
    dd = o_ref.shape[0]

    wd = wd_ref[...]
    for d in range(dd):
        part = jnp.dot(wd, pm_ref[:, d * LANES:(d + 1) * LANES], preferred_element_type=jnp.float32)
        f_ref[:, d] = part.astype(jnp.bfloat16).reshape(n, dd, LANES)
    t = t_ref[...]

    def mid_body(h, carry):
        x = jnp.concatenate([f_ref[h * 2 + k].reshape(dd * dd, LANES) for k in range(2)], axis=1)
        g = jnp.dot(t, x, preferred_element_type=jnp.float32).astype(jnp.bfloat16)
        for k in range(2):
            at = pl.multiple_of((h * 2 + k) * dd, dd)
            for r in range(dd):
                g_ref[pl.ds(at, dd), r * LANES:(r + 1) * LANES] = g[r * dd:(r + 1) * dd, k * LANES:(k + 1) * LANES]
        return carry

    lax.fori_loop(0, n // 2, mid_body, 0)
    qt = qt_ref[...]
    for r in range(dd):
        o_ref[r] = jnp.dot(qt, g_ref[:, r * LANES:(r + 1) * LANES], preferred_element_type=jnp.float32)


def edge_contract(west, low_t, up_t, site):
    n = west.shape[0]
    dd = west.shape[1] // n
    wd = west.reshape(n * dd, n)
    pm = jnp.transpose(low_t.reshape(n, n, dd), (1, 2, 0))
    pm = jnp.pad(pm, ((0, 0), (0, 0), (0, LANES - n))).reshape(n, dd * LANES)
    qt = up_t
    out = pl.pallas_call(
        edge_kernel,
        out_shape=jax.ShapeDtypeStruct((dd, n, LANES), jnp.float32),
        scratch_shapes=[
            pltpu.VMEM((n, dd, dd, LANES), jnp.bfloat16),
            pltpu.VMEM((n * dd, dd * LANES), jnp.bfloat16),
        ],
        compiler_params=pltpu.CompilerParams(vmem_limit_bytes=48 * 1024 * 1024),
    )(wd, pm, site, qt)
    return jnp.transpose(out[:, :, :n], (1, 0, 2)).reshape(n, dd * n)


def one_hot(rows, cols, row_key, col_key):
    r = lax.broadcasted_iota(jnp.int32, (rows, cols), 0)
    c = lax.broadcasted_iota(jnp.int32, (rows, cols), 1)
    return (row_key(r) == col_key(c)).astype(jnp.float32)


def double_layer(ket, bra):
    q = ket.shape[1]
    dd = q * q
    size = dd * dd
    ket_m = jnp.transpose(ket.astype(jnp.float32), (0, 3, 2, 4, 1)).reshape(ket.shape[0], dd, dd)
    bra_m = jnp.transpose(bra.astype(jnp.float32), (0, 3, 2, 4, 1)).reshape(bra.shape[0], dd, dd)
    k_row = one_hot(size, dd, lambda r: (r // (q * dd)) * q + (r // q) % q, lambda c: c)
    b_row = one_hot(size, dd, lambda r: ((r // dd) % q) * q + r % q, lambda c: c)
    k_col = one_hot(dd, size, lambda r: r, lambda c: (c // (q * dd)) * q + (c // q) % q)
    b_col = one_hot(dd, size, lambda r: r, lambda c: ((c // dd) % q) * q + c % q)
    hi = lax.Precision.HIGHEST
    ket_wide = jnp.einsum("ra,sab,bc->src", k_row, ket_m, k_col, precision=hi)
    bra_wide = jnp.einsum("ra,sab,bc->src", b_row, bra_m, b_col, precision=hi)
    return jnp.sum(ket_wide * bra_wide, axis=0).astype(jnp.bfloat16)


def per_device(
    c_upper, edge_upper, edge_left, c_lower, edge_lower, site_ket, time_gate, quench_sites
):
    env_width = c_upper.shape[-1]
    double_bond = edge_upper.shape[-1] // env_width
    bond_dim = math.isqrt(double_bond)
    phys_dim = site_ket.shape[2]
    ket_sites = site_ket[0, 0].reshape(phys_dim, bond_dim, bond_dim, bond_dim, bond_dim)
    gram = jnp.dot(time_gate.T, time_gate, precision=lax.Precision.HIGHEST)
    gated = jnp.einsum(
        "st,tabcd->sabcd", gram, ket_sites.astype(jnp.float32), precision=lax.Precision.HIGHEST
    )
    own_index = lax.axis_index("gx") * lax.axis_size("gy") + lax.axis_index("gy")
    chosen = jnp.any(quench_sites == own_index)
    bra = jnp.where(chosen, gated, ket_sites.astype(jnp.float32)).astype(jnp.bfloat16)
    site = double_layer(ket_sites, bra)
    north_edge = edge_upper[0, 0]
    south_edge = edge_lower[0, 0]
    corner_up = c_upper[0, 0]
    west_edge = edge_left[0, 0]
    corner_low = c_lower[0, 0]
    up_corner_nb, north_nb = shifted((corner_up, north_edge), 0, -1)
    low_corner_nb, south_nb = shifted((corner_low, south_edge), 0, 1)
    n = env_width
    for step in range(STEPS):
        def half(corner, edge):
            return jnp.dot(corner, edge, preferred_element_type=jnp.float32).reshape(n * double_bond, n)

        upper = half(corner_up, north_edge)
        lower = half(corner_low, south_edge)
        upper_nb = half(up_corner_nb, north_nb)
        lower_nb = half(low_corner_nb, south_nb)
        projs = polar_factor_t(jnp.swapaxes(jnp.stack([lower + upper_nb, lower_nb + upper]), 1, 2))
        below_t = projs[0]
        above_t = projs[1]
        new_up = jnp.dot(above_t, upper, precision=lax.Precision.HIGHEST)
        new_low = jnp.dot(below_t, lower, precision=lax.Precision.HIGHEST)
        new_up = unit_scaled(new_up).astype(jnp.bfloat16)
        new_low = unit_scaled(new_low).astype(jnp.bfloat16)
        if step + 1 < STEPS:
            up_corner_nb = shifted(new_up, 1, -1)
            low_corner_nb = shifted(new_low, 1, 1)
        edge_new = edge_contract(west_edge, below_t.astype(jnp.bfloat16), above_t.astype(jnp.bfloat16), site)
        edge_new = unit_scaled(edge_new).astype(jnp.bfloat16)
        corner_up, west_edge, corner_low = shifted((new_up, edge_new, new_low), 1, 0)
    return (corner_up[None, None], west_edge[None, None], corner_low[None, None])


def solution(mesh):
    return jax.shard_map(
        per_device,
        mesh=mesh,
        in_specs=(
            P("gx", "gy", None, None),
            P("gx", "gy", None, None),
            P("gx", "gy", None, None),
            P("gx", "gy", None, None),
            P("gx", "gy", None, None),
            P("gx", "gy", None, None),
            P(),
            P(),
        ),
        out_specs=(P("gx", "gy", None, None), P("gx", "gy", None, None), P("gx", "gy", None, None)),
        check_vma=False,
    )
```

profile of v0, /device:TPU:0, one launch (start us, length us, event | category | flops | bytes accessed | tf_op | source)
XLA Modules:
  0.0 97.7 jit_solution(10171308670139806347)
XLA Ops:
  0.7 6.1 %collective-permute-start.1 = (bf16[96,1536]{1,0:T(8,128)(2,1)}, bf16[96,1536]{1,0:T(8,128)(2,1)S(1)}, u32[]{:S(2)}, u32[]{:S(2)}) collective-permute-start(bf16[96,1536]{1,0:T(8,128)(2,1)} %bitcast.117), channel_id=1, source_target_pairs={{0,7},{1,0},{2,1},{3,2},{4,3},{5,4},{6,5},{7,6},{8,15},{9,8},{10,9... | collective-permute-start | bytes 884744 | tf_op jit(solution)/shard_map/ppermute | solution.py:60
  6.7 0.5 collective-permute-start
  7.2 1.5 %collective-permute-start.3 = (bf16[96,1536]{1,0:T(8,128)(2,1)}, bf16[96,1536]{1,0:T(8,128)(2,1)}, u32[]{:S(2)}, u32[]{:S(2)}) collective-permute-start(bf16[96,1536]{1,0:T(8,128)(2,1)} %bitcast.116), channel_id=1, source_target_pairs={{0,1},{1,2},{2,3},{3,4},{4,5},{5,6},{6,7},{7,0},{8,9},{9,10},{10,1... | collective-permute-start | bytes 884744 | tf_op jit(solution)/shard_map/ppermute | solution.py:60
  8.8 1.2 %fusion.91 = f32[96,1536]{1,0:T(8,128)S(1)} fusion(bf16[1,1,96,1536]{3,2,1,0:T(8,128)(2,1)} %param.12, bf16[1,1,96,96]{3,2,1,0:T(8,128)(2,1)} %param.11), kind=kOutput, calls=%fused_computation.149 | convolution fusion | flops 28311552 | bytes 903168 | tf_op jit(solution)/shard_map/dot_general | solution.py:159
  10.0 1.2 %fusion.86 = f32[96,1536]{1,0:T(8,128)S(1)} fusion(bf16[1,1,96,1536]{3,2,1,0:T(8,128)(2,1)} %param.9, bf16[1,1,96,96]{3,2,1,0:T(8,128)(2,1)} %param.8), kind=kOutput, calls=%fused_computation.144 | convolution fusion | flops 28311552 | bytes 903168 | tf_op jit(solution)/shard_map/dot_general | solution.py:159
  11.3 0.1 reshape_squeeze.7
  11.5 0.3 copy.18
  11.9 0.4 convolution_bitcast_fusion
  12.3 0.4 fusion.54
  12.7 0.2 convolution_bitcast_fusion.1
  12.9 0.6 compare_reduce_fusion
  13.6 0.9 fusion.2
  14.5 0.3 copy.21
  14.9 0.4 fusion.22
  15.3 0.4 fusion.t_ref
  15.7 0.3 reshape.123
  16.0 1.2 %reshape.124 = f32[1536,96]{1,0:T(8,128)} reshape(f32[96,1536]{1,0:T(8,128)S(1)} %fusion.86) | data formatting | bytes 1179648 | tf_op jit(solution)/shard_map/reshape | solution.py:159
  17.2 0.3 reshape_squeeze.6.wd_ref
  17.5 0.7 copy-done.6
  18.2 1.1 %convolution_add_fusion.3 = f32[96,1536]{1,0:T(8,128)} fusion(f32[96,1536]{1,0:T(8,128)S(1)} %fusion.91, bf16[96,96]{1,0:T(8,128)(2,1)S(1)} %collective-permute-done, bf16[96,1536]{1,0:T(8,128)(2,1)S(1)} %collective-permute-done.1), kind=kOutput, calls=%fused_computation.3 | convolution fusion | flops 28459008 | bytes 1492992 | tf_op jit(solution)/shard_map/dot_general | solution.py:159
  19.3 1.3 %add.132 = f32[1,1536,96]{2,1,0:T(8,128)S(1)} reshape(f32[96,1536]{1,0:T(8,128)} %convolution_add_fusion.3) | data formatting | bytes 1179648 | tf_op jit(solution)/shard_map/add | solution.py:165
  20.6 1.1 %copy.13 = f32[1,1536,96]{1,2,0:T(8,128)} copy(f32[1,1536,96]{2,1,0:T(8,128)S(1)} %add.132) | data formatting | bytes 1179648 | tf_op jit(solution)/shard_map/add | solution.py:165
  21.7 1.2 %convolution_add_fusion.2 = f32[96,1536]{1,0:T(8,128)S(1)} fusion(f32[96,1536]{1,0:T(8,128)S(1)} %fusion.86, bf16[96,96]{1,0:T(8,128)(2,1)S(1)} %collective-permute-done.2, bf16[96,1536]{1,0:T(8,128)(2,1)} %collective-permute-done.3), kind=kOutput, calls=%fused_computation.2 | convolution fusion | flops 28459008 | bytes 1492992 | tf_op jit(solution)/shard_map/dot_general | solution.py:159
  22.9 0.3 add.134
  23.2 0.3 copy.14
  23.5 0.5 copy-done.3
  24.1 6.8 %shard_map.103 = f32[2,96,1536]{2,1,0:T(8,128)S(1)} custom-call(f32[2,96,1536]{2,1,0:T(8,128)S(1)} %maximum_bitcast_fusion.y_ref), custom_call_target="tpu_custom_call" | custom-call | tf_op jit(solution)/shard_map/pallas_call | solution.py:46
  30.9 1.3 %multiply_reduce_fusion.4 = (f32[]{:T(128)}, f32[96,96]{1,0:T(8,128)S(1)}) fusion(f32[1536,96]{1,0:T(8,128)S(1)} %copy-done.2, f32[2,96,1536]{2,1,0:T(8,128)S(1)} %shard_map.103), kind=kOutput, calls=%fused_computation.78 | convolution fusion | flops 169887744 | bytes 1413124 | tf_op jit(solution)/shard_map/dot_general | solution.py:168
  33.0 3.0 %collective-permute-start.5 = (bf16[96,96]{1,0:T(8,128)(2,1)S(1)}, bf16[96,96]{1,0:T(8,128)(2,1)S(1)}, u32[]{:S(2)}, u32[]{:S(2)}) collective-permute-start(bf16[96,96]{1,0:T(8,128)(2,1)S(1)} %divide_convert_fusion.4), channel_id=1, source_target_pairs={{0,15},{1,8},{2,9},{3,10},{4,11},{5,12},{6,13},{7,14},{8,23},{9,16... | collective-permute-start | bytes 55304 | tf_op jit(solution)/shard_map/ppermute | solution.py:60
  36.0 2.7 %collective-permute-start.7 = (bf16[96,96]{1,0:T(8,128)(2,1)S(1)}, bf16[96,96]{1,0:T(8,128)(2,1)S(1)}, u32[]{:S(2)}, u32[]{:S(2)}) collective-permute-start(bf16[96,96]{1,0:T(8,128)(2,1)S(1)} %divide_convert_fusion.4), channel_id=1, source_target_pairs={{0,8},{1,9},{2,10},{3,11},{4,12},{5,13},{6,14},{7,15},{8,16},{9,17... | collective-permute-start | bytes 55304 | tf_op jit(solution)/shard_map/ppermute | solution.py:60
  38.7 1.3 %multiply_reduce_fusion.5 = (f32[]{:T(128)}, f32[96,96]{1,0:T(8,128)S(1)}) fusion(f32[1536,96]{1,0:T(8,128)S(1)} %reshape.123, f32[2,96,1536]{2,1,0:T(8,128)S(1)} %shard_map.103), kind=kOutput, calls=%fused_computation.80 | convolution fusion | flops 169887744 | bytes 1413124 | tf_op jit(solution)/shard_map/dot_general | solution.py:169
  40.8 0.2 collective-permute-start.6
  41.1 0.2 copy.17
  41.6 13.2 %shard_map.105 = f32[16,96,128]{2,1,0:T(8,128)S(1)} custom-call(bf16[1536,96]{1,0:T(8,128)(2,1)S(1)} %reshape_squeeze.6.wd_ref, bf16[96,2048]{1,0:T(8,128)(2,1)S(1)} %bitcast.111, bf16[256,256]{1,0:T(8,128)(2,1)S(1)} %fusion.t_ref, bf16[96,1536]{1,0:T(8,128)(2,1)S(1)} %get-tuple-element.5.qt_ref), custom_call_target="tpu_custom_call" | custom-call | tf_op jit(solution)/shard_map/pallas_call | solution.py:99
  54.8 0.8 multiply_reduce_fusion.1
  56.4 0.2 copy.22
  56.5 1.1 %convert_element_type.80 = bf16[96,1536]{1,0:T(8,128)(2,1)} reshape(bf16[96,16,96]{2,1,0:T(8,128)(2,1)S(1)} %copy.22) | data formatting | bytes 589824 | tf_op jit(solution)/shard_map/convert_element_type | solution.py:176
  57.7 0.4 collective-permute-start.9
  58.1 0.2 fusion.89
  58.3 0.2 convolution_add_fusion.1
  58.6 0.2 fusion.84
  58.9 0.3 reshape.131
  59.1 0.3 add.138
  59.4 0.3 copy.15
  59.6 1.2 %reshape.125 = f32[1536,96]{1,0:T(8,128)} reshape(f32[96,1536]{1,0:T(8,128)S(1)} %fusion.84) | data formatting | bytes 1179648 | tf_op jit(solution)/shard_map/reshape | solution.py:159
  60.8 1.2 %convolution_add_fusion = f32[96,1536]{1,0:T(8,128)S(1)} fusion(f32[96,1536]{1,0:T(8,128)S(1)} %fusion.84, bf16[96,96]{1,0:T(8,128)(2,1)S(1)} %collective-permute-done.6, bf16[96,1536]{1,0:T(8,128)(2,1)} %collective-permute-done.3), kind=kOutput, calls=%fused_computation | convolution fusion | flops 28459008 | bytes 1492992 | tf_op jit(solution)/shard_map/dot_general | solution.py:159
  62.0 0.3 add.140
  62.2 0.3 copy.16
  62.6 6.8 %shard_map.104 = f32[2,96,1536]{2,1,0:T(8,128)S(1)} custom-call(f32[2,96,1536]{2,1,0:T(8,128)S(1)} %maximum_bitcast_fusion.1.y_ref), custom_call_target="tpu_custom_call" | custom-call | tf_op jit(solution)/shard_map/pallas_call | solution.py:46
  69.4 1.3 %multiply_reduce_fusion.2 = (f32[]{:T(128)}, f32[96,96]{1,0:T(8,128)S(1)}) fusion(f32[1536,96]{1,0:T(8,128)S(1)} %reshape.131, f32[2,96,1536]{2,1,0:T(8,128)S(1)} %shard_map.104), kind=kOutput, calls=%fused_computation.74 | convolution fusion | flops 169887744 | bytes 1413124 | tf_op jit(solution)/shard_map/dot_general | solution.py:169
  71.5 0.7 collective-permute-start.11
  72.2 0.2 copy.23
  72.7 1.3 %reshape.129.wd_ref = bf16[1536,96]{1,0:T(8,128)(2,1)S(1)} reshape(bf16[96,1536]{1,0:T(8,128)(2,1)} %collective-permute-done.9) | data formatting | bytes 589824 | tf_op jit(solution)/shard_map/reshape | solution.py:95
  74.0 13.2 %shard_map.106 = f32[16,96,128]{2,1,0:T(8,128)S(1)} custom-call(bf16[1536,96]{1,0:T(8,128)(2,1)S(1)} %reshape.129.wd_ref, bf16[96,2048]{1,0:T(8,128)(2,1)S(1)} %bitcast.110, bf16[256,256]{1,0:T(8,128)(2,1)S(1)} %fusion.t_ref, bf16[96,1536]{1,0:T(8,128)(2,1)S(1)} %get-tuple-element.3.qt_ref), custom_call_target="tpu_custom_call" | custom-call | tf_op jit(solution)/shard_map/pallas_call | solution.py:99
  87.2 0.8 multiply_reduce_fusion
  88.8 0.2 copy.24
  88.9 0.4 convert_element_type.86
  89.3 0.9 collective-permute-start.10
  90.3 1.3 %multiply_reduce_fusion.3 = (f32[]{:T(128)}, f32[96,96]{1,0:T(8,128)S(1)}) fusion(f32[1536,96]{1,0:T(8,128)S(1)} %copy-done.1, f32[2,96,1536]{2,1,0:T(8,128)S(1)} %shard_map.104), kind=kOutput, calls=%fused_computation.76 | convolution fusion | flops 169887744 | bytes 1413124 | tf_op jit(solution)/shard_map/dot_general | solution.py:168
  92.3 0.6 collective-permute-start.8
  92.9 2.9 %collective-permute-done.8 = bf16[96,96]{1,0:T(8,128)(2,1)S(1)} collective-permute-done((bf16[96,96]{1,0:T(8,128)(2,1)S(1)}, bf16[96,96]{1,0:T(8,128)(2,1)S(1)}, u32[]{:S(2)}, u32[]{:S(2)}) %collective-permute-start.8) | collective-permute-done | bytes 18464 | tf_op jit(solution)/shard_map/ppermute | solution.py:60
  95.8 0.6 copy.37
  96.4 0.7 copy.38
  97.1 0.6 copy.39
  (55 shorter events, 1.3 us)
Async XLA Ops:
  0.6 12.1 %copy-start = (f32[2,2]{1,0:T(2,128)S(1)}, f32[2,2]{1,0:T(2,128)}, u32[]{:S(2)}) copy-start(f32[2,2]{1,0:T(2,128)} %param.14) | copy-start | bytes 52
  0.6 10.7 %copy-start.9 = (bf16[1,1,2,256]{3,2,1,0:T(2,128)(2,1)S(1)}, bf16[1,1,2,256]{3,2,1,0:T(2,128)(2,1)}, u32[]{:S(2)}) copy-start(bf16[1,1,2,256]{3,2,1,0:T(2,128)(2,1)} %param.13) | copy-start | bytes 3076
  0.7 16.8 %collective-permute-start.1 = (bf16[96,1536]{1,0:T(8,128)(2,1)}, bf16[96,1536]{1,0:T(8,128)(2,1)S(1)}, u32[]{:S(2)}, u32[]{:S(2)}) collective-permute-start(bf16[96,1536]{1,0:T(8,128)(2,1)} %bitcast.117), channel_id=1, source_target_pairs={{0,7},{1,0},{2,1},{3,2},{4,3},{5,4},{6,5},{7,6},{8,15},{9,8},{10,9... | collective-permute-start | bytes 884744 | tf_op jit(solution)/shard_map/ppermute | solution.py:60
  6.7 10.7 %collective-permute-start = (bf16[96,96]{1,0:T(8,128)(2,1)}, bf16[96,96]{1,0:T(8,128)(2,1)S(1)}, u32[]{:S(2)}, u32[]{:S(2)}) collective-permute-start(bf16[96,96]{1,0:T(8,128)(2,1)} %bitcast.122), channel_id=1, source_target_pairs={{0,7},{1,0},{2,1},{3,2},{4,3},{5,4},{6,5},{7,6},{8,15},{9,8},{10,9... | collective-permute-start | bytes 55304 | tf_op jit(solution)/shard_map/ppermute | solution.py:60
  7.2 14.5 %collective-permute-start.3 = (bf16[96,1536]{1,0:T(8,128)(2,1)}, bf16[96,1536]{1,0:T(8,128)(2,1)}, u32[]{:S(2)}, u32[]{:S(2)}) collective-permute-start(bf16[96,1536]{1,0:T(8,128)(2,1)} %bitcast.116), channel_id=1, source_target_pairs={{0,1},{1,2},{2,3},{3,4},{4,5},{5,6},{6,7},{7,0},{8,9},{9,10},{10,1... | collective-permute-start | bytes 884744 | tf_op jit(solution)/shard_map/ppermute | solution.py:60
  8.8 13.0 %collective-permute-start.2 = (bf16[96,96]{1,0:T(8,128)(2,1)}, bf16[96,96]{1,0:T(8,128)(2,1)S(1)}, u32[]{:S(2)}, u32[]{:S(2)}) collective-permute-start(bf16[96,96]{1,0:T(8,128)(2,1)} %bitcast.123), channel_id=1, source_target_pairs={{0,1},{1,2},{2,3},{3,4},{4,5},{5,6},{6,7},{7,0},{8,9},{9,10},{10,1... | collective-permute-start | bytes 55304 | tf_op jit(solution)/shard_map/ppermute | solution.py:60
  10.0 2.9 %copy-start.10 = (s32[4]{0:T(128)S(1)}, s32[4]{0:T(128)}, u32[]{:S(2)}) copy-start(s32[4]{0:T(128)} %param.15) | copy-start | bytes 52
  15.7 1.4 %copy-start.8 = (bf16[1,1,96,1536]{3,2,1,0:T(8,128)(2,1)S(1)}, bf16[1,1,96,1536]{3,2,1,0:T(8,128)(2,1)}, u32[]{:S(2)}) copy-start(bf16[1,1,96,1536]{3,2,1,0:T(8,128)(2,1)} %param.10) | copy-start | bytes 884740
  17.5 0.7 copy-start.6
  22.9 1.1 %copy-start.3 = (f32[1,1536,96]{1,2,0:T(8,128)S(1)}, f32[1,1536,96]{1,2,0:T(8,128)}, u32[]{:S(2)}) copy-start(f32[1,1536,96]{1,2,0:T(8,128)} %copy.13) | copy-start | bytes 1769476
  24.1 6.9 %copy-start.2 = (f32[1536,96]{1,0:T(8,128)S(1)}, f32[1536,96]{1,0:T(8,128)}, u32[]{:S(2)}) copy-start(f32[1536,96]{1,0:T(8,128)} %reshape.124) | copy-start | bytes 1769476
  33.0 25.3 %collective-permute-start.5 = (bf16[96,96]{1,0:T(8,128)(2,1)S(1)}, bf16[96,96]{1,0:T(8,128)(2,1)S(1)}, u32[]{:S(2)}, u32[]{:S(2)}) collective-permute-start(bf16[96,96]{1,0:T(8,128)(2,1)S(1)} %divide_convert_fusion.4), channel_id=1, source_target_pairs={{0,15},{1,8},{2,9},{3,10},{4,11},{5,12},{6,13},{7,14},{8,23},{9,16... | collective-permute-start | bytes 55304 | tf_op jit(solution)/shard_map/ppermute | solution.py:60
  36.0 22.6 %collective-permute-start.7 = (bf16[96,96]{1,0:T(8,128)(2,1)S(1)}, bf16[96,96]{1,0:T(8,128)(2,1)S(1)}, u32[]{:S(2)}, u32[]{:S(2)}) collective-permute-start(bf16[96,96]{1,0:T(8,128)(2,1)S(1)} %divide_convert_fusion.4), channel_id=1, source_target_pairs={{0,8},{1,9},{2,10},{3,11},{4,12},{5,13},{6,14},{7,15},{8,16},{9,17... | collective-permute-start | bytes 55304 | tf_op jit(solution)/shard_map/ppermute | solution.py:60
  40.8 17.3 %collective-permute-start.4 = (bf16[96,96]{1,0:T(8,128)(2,1)S(1)}, bf16[96,96]{1,0:T(8,128)(2,1)S(1)}, u32[]{:S(2)}, u32[]{:S(2)}) collective-permute-start(bf16[96,96]{1,0:T(8,128)(2,1)S(1)} %divide_convert_fusion.5), channel_id=1, source_target_pairs={{0,8},{1,9},{2,10},{3,11},{4,12},{5,13},{6,14},{7,15},{8,16},{9,17... | collective-permute-start | bytes 55304 | tf_op jit(solution)/shard_map/ppermute | solution.py:60
  40.8 20.0 %collective-permute-start.6 = (bf16[96,96]{1,0:T(8,128)(2,1)S(1)}, bf16[96,96]{1,0:T(8,128)(2,1)S(1)}, u32[]{:S(2)}, u32[]{:S(2)}) collective-permute-start(bf16[96,96]{1,0:T(8,128)(2,1)S(1)} %divide_convert_fusion.5), channel_id=1, source_target_pairs={{0,9},{1,10},{2,11},{3,12},{4,13},{5,14},{6,15},{7,8},{8,17},{9,18... | collective-permute-start | bytes 55304 | tf_op jit(solution)/shard_map/ppermute | solution.py:60
  56.3 1.8 %copy-start.4 = (bf16[1,1,96,1536]{3,2,1,0:T(8,128)(2,1)S(1)}, bf16[1,1,96,1536]{3,2,1,0:T(8,128)(2,1)}, u32[]{:S(2)}) copy-start(bf16[1,1,96,1536]{3,2,1,0:T(8,128)(2,1)} %param.12) | copy-start | bytes 884740
  56.4 2.0 %copy-start.7 = (bf16[96,1536]{1,0:T(8,128)(2,1)S(1)}, bf16[96,1536]{1,0:T(8,128)(2,1)}, u32[]{:S(2)}) copy-start(bf16[96,1536]{1,0:T(8,128)(2,1)} %copy-done.6) | copy-start | bytes 884740
  57.7 1.0 copy-start.5
  57.7 15.0 %collective-permute-start.9 = (bf16[96,1536]{1,0:T(8,128)(2,1)}, bf16[96,1536]{1,0:T(8,128)(2,1)}, u32[]{:S(2)}, u32[]{:S(2)}) collective-permute-start(bf16[96,1536]{1,0:T(8,128)(2,1)} %convert_element_type.80), channel_id=1, source_target_pairs={{0,8},{1,9},{2,10},{3,11},{4,12},{5,13},{6,14},{7,15},{8,16},{9,17... | collective-permute-start | bytes 884744 | tf_op jit(solution)/shard_map/ppermute | solution.py:60
  71.5 21.5 %collective-permute-start.11 = (bf16[96,96]{1,0:T(8,128)(2,1)S(1)}, bf16[96,96]{1,0:T(8,128)(2,1)S(1)}, u32[]{:S(2)}, u32[]{:S(2)}) collective-permute-start(bf16[96,96]{1,0:T(8,128)(2,1)S(1)} %divide_convert_fusion.2), channel_id=1, source_target_pairs={{0,8},{1,9},{2,10},{3,11},{4,12},{5,13},{6,14},{7,15},{8,16},{9,17... | collective-permute-start | bytes 55304 | tf_op jit(solution)/shard_map/ppermute | solution.py:60
  88.7 1.6 %copy-start.1 = (f32[1536,96]{1,0:T(8,128)S(1)}, f32[1536,96]{1,0:T(8,128)}, u32[]{:S(2)}) copy-start(f32[1536,96]{1,0:T(8,128)} %reshape.125) | copy-start | bytes 1769476
  89.3 6.5 %collective-permute-start.10 = (bf16[96,1536]{1,0:T(8,128)(2,1)S(1)}, bf16[96,1536]{1,0:T(8,128)(2,1)S(1)}, u32[]{:S(2)}, u32[]{:S(2)}) collective-permute-start(bf16[96,1536]{1,0:T(8,128)(2,1)S(1)} %convert_element_type.86), channel_id=1, source_target_pairs={{0,8},{1,9},{2,10},{3,11},{4,12},{5,13},{6,14},{7,15},{8,16},{9,17... | collective-permute-start | bytes 884744 | tf_op jit(solution)/shard_map/ppermute | solution.py:60
  92.3 3.5 %collective-permute-start.8 = (bf16[96,96]{1,0:T(8,128)(2,1)S(1)}, bf16[96,96]{1,0:T(8,128)(2,1)S(1)}, u32[]{:S(2)}, u32[]{:S(2)}) collective-permute-start(bf16[96,96]{1,0:T(8,128)(2,1)S(1)} %divide_convert_fusion.3), channel_id=1, source_target_pairs={{0,8},{1,9},{2,10},{3,11},{4,12},{5,13},{6,14},{7,15},{8,16},{9,17... | collective-permute-start | bytes 55304 | tf_op jit(solution)/shard_map/ppermute | solution.py:60
where the time goes:
time: 98.2 us; the launch traced here: 97.7 us
  Pallas kernels  40.1 us (41%)
  starting transfers between devices  16.8 us (17%)
  local copies, waits for them, and re-layouts  15.4 us (16%)
  matrix products  14.6 us (15%)
  between operations  5.37 us (5%)
  waiting for transfers between devices  2.89 us (3%)
  other arithmetic  2.61 us (3%)
    pallas_call x2, Pallas kernels, edge_contract(): pl.pallas_call(edge_kernel, out_shape=jax.ShapeDtypeStruct((dd, n, LANES)...  26.4 us
    ppermute x12, starting transfers between devices, shifted(): return lax.ppermute(tree, ('gx', 'gy'), pairs)  16.8 us
    pallas_call x2, Pallas kernels, polar_factor_t(): pl.pallas_call(polar_kernel, out_shape=jax.ShapeDtypeStruct(stack.shape,...  13.7 us
    dot_general x8, matrix products, half(): jnp.dot(corner, edge, preferred_element_type=jnp.float32)  6.5 us
    unnamed x27, local copies, waits for them, and re-layouts  3.5 us
    add x4, local copies, waits for them, and re-layouts, per_device(): lower + upper_nb  2.93 us
    ppermute x12, waiting for transfers between devices, shifted(): return lax.ppermute(tree, ('gx', 'gy'), pairs)  2.89 us
    reshape x4, local copies, waits for them, and re-layouts, half(): jnp.dot(corner, edge, preferred_element_type=jnp.float32)  2.82 us
  transfers between devices with their start and end apart: 12, of which 1 were waited for; matrix products, arithmetic and copies ran while one was open for 27% of the time, Pallas kernels for 34%

commit v1 on v0

--- a/solution.py
+++ b/solution.py
@@ -67,26 +67,31 @@
 def edge_kernel(wd_ref, pm_ref, t_ref, qt_ref, o_ref, f_ref, g_ref):
     n = qt_ref.shape[0]
     dd = o_ref.shape[0]
-
+    group = 4
     wd = wd_ref[...]
-    for d in range(dd):
-        part = jnp.dot(wd, pm_ref[:, d * LANES:(d + 1) * LANES], preferred_element_type=jnp.float32)
-        f_ref[:, d] = part.astype(jnp.bfloat16).reshape(n, dd, LANES)
+    for d0 in range(0, dd, group):
+        part = jnp.dot(wd, pm_ref[:, d0 * LANES:(d0 + group) * LANES], preferred_element_type=jnp.float32)
+        part = part.astype(jnp.bfloat16)
+        for k in range(group):
+            f_ref[:, d0 + k] = part[:, k * LANES:(k + 1) * LANES].reshape(n, dd, LANES)
     t = t_ref[...]
+    per = math.gcd(n, 24)
 
     def mid_body(h, carry):
-        x = jnp.concatenate([f_ref[h * 2 + k].reshape(dd * dd, LANES) for k in range(2)], axis=1)
+        x = jnp.concatenate([f_ref[h * per + k].reshape(dd * dd, LANES) for k in range(per)], axis=1)
         g = jnp.dot(t, x, preferred_element_type=jnp.float32).astype(jnp.bfloat16)
-        for k in range(2):
-            at = pl.multiple_of((h * 2 + k) * dd, dd)
+        for k in range(per):
+            at = pl.multiple_of((h * per + k) * dd, dd)
             for r in range(dd):
                 g_ref[pl.ds(at, dd), r * LANES:(r + 1) * LANES] = g[r * dd:(r + 1) * dd, k * LANES:(k + 1) * LANES]
         return carry
 
-    lax.fori_loop(0, n // 2, mid_body, 0)
+    lax.fori_loop(0, n // per, mid_body, 0)
     qt = qt_ref[...]
-    for r in range(dd):
-        o_ref[r] = jnp.dot(qt, g_ref[:, r * LANES:(r + 1) * LANES], preferred_element_type=jnp.float32)
+    for r0 in range(0, dd, group):
+        part = jnp.dot(qt, g_ref[:, r0 * LANES:(r0 + group) * LANES], preferred_element_type=jnp.float32)
+        for k in range(group):
+            o_ref[r0 + k] = part[:, k * LANES:(k + 1) * LANES]
 
 
 def edge_contract(west, low_t, up_t, site):

time: 98.2 us -> 82.8 us (0.84)
  Pallas kernels: 40.1 us -> 24.6 us
    pallas_call x2, Pallas kernels: 26.4 us -> 10.9 us  [edge_contract(): pl.pallas_call(edge_kernel, out_shape=jax.ShapeDtypeStruct((dd, n, LANES)...]
  transfers between devices with their start and end apart: 12 -> 12, of which waited for: 1 -> 1; matrix products, arithmetic and copies ran while one was open for 27% -> 32% of each run, Pallas kernels for 34% -> 22%
where the time goes in v1:
time: 82.8 us; the launch traced here: 82.3 us
  Pallas kernels  24.6 us (30%)
  starting transfers between devices  17 us (21%)
  local copies, waits for them, and re-layouts  15.4 us (19%)
  matrix products  14.6 us (18%)
  between operations  5.36 us (6%)
  waiting for transfers between devices  2.81 us (3%)
  other arithmetic  2.63 us (3%)
    ppermute x12, starting transfers between devices, shifted(): return lax.ppermute(tree, ('gx', 'gy'), pairs)  17 us
    pallas_call x2, Pallas kernels, polar_factor_t(): pl.pallas_call(polar_kernel, out_shape=jax.ShapeDtypeStruct(stack.shape,...  13.7 us
    pallas_call x2, Pallas kernels, edge_contract(): pl.pallas_call(edge_kernel, out_shape=jax.ShapeDtypeStruct((dd, n, LANES)...  10.9 us
    dot_general x8, matrix products, half(): jnp.dot(corner, edge, preferred_element_type=jnp.float32)  6.5 us
    unnamed x27, local copies, waits for them, and re-layouts  3.5 us
    add x4, local copies, waits for them, and re-layouts, per_device(): lower + upper_nb  2.93 us
    reshape x4, local copies, waits for them, and re-layouts, half(): jnp.dot(corner, edge, preferred_element_type=jnp.float32)  2.82 us
    ppermute x12, waiting for transfers between devices, shifted(): return lax.ppermute(tree, ('gx', 'gy'), pairs)  2.81 us
  transfers between devices with their start and end apart: 12, of which 1 were waited for; matrix products, arithmetic and copies ran while one was open for 32% of the time, Pallas kernels for 22%

profile of v1, /device:TPU:0, one launch (start us, length us, event | category | flops | bytes accessed | tf_op | source)
XLA Modules:
  0.0 82.3 jit_solution(6080333659914194933)
XLA Ops:
  0.7 6.1 %collective-permute-start.1 = (bf16[96,1536]{1,0:T(8,128)(2,1)}, bf16[96,1536]{1,0:T(8,128)(2,1)S(1)}, u32[]{:S(2)}, u32[]{:S(2)}) collective-permute-start(bf16[96,1536]{1,0:T(8,128)(2,1)} %bitcast.117), channel_id=1, source_target_pairs={{0,7},{1,0},{2,1},{3,2},{4,3},{5,4},{6,5},{7,6},{8,15},{9,8},{10,9... | collective-permute-start | bytes 884744 | tf_op jit(solution)/shard_map/ppermute | solution.py:60
  6.7 0.5 collective-permute-start
  7.2 1.5 %collective-permute-start.3 = (bf16[96,1536]{1,0:T(8,128)(2,1)}, bf16[96,1536]{1,0:T(8,128)(2,1)}, u32[]{:S(2)}, u32[]{:S(2)}) collective-permute-start(bf16[96,1536]{1,0:T(8,128)(2,1)} %bitcast.116), channel_id=1, source_target_pairs={{0,1},{1,2},{2,3},{3,4},{4,5},{5,6},{6,7},{7,0},{8,9},{9,10},{10,1... | collective-permute-start | bytes 884744 | tf_op jit(solution)/shard_map/ppermute | solution.py:60
  8.8 1.2 %fusion.91 = f32[96,1536]{1,0:T(8,128)S(1)} fusion(bf16[1,1,96,1536]{3,2,1,0:T(8,128)(2,1)} %param.12, bf16[1,1,96,96]{3,2,1,0:T(8,128)(2,1)} %param.11), kind=kOutput, calls=%fused_computation.149 | convolution fusion | flops 28311552 | bytes 903168 | tf_op jit(solution)/shard_map/dot_general | solution.py:164
  10.0 1.2 %fusion.86 = f32[96,1536]{1,0:T(8,128)S(1)} fusion(bf16[1,1,96,1536]{3,2,1,0:T(8,128)(2,1)} %param.9, bf16[1,1,96,96]{3,2,1,0:T(8,128)(2,1)} %param.8), kind=kOutput, calls=%fused_computation.144 | convolution fusion | flops 28311552 | bytes 903168 | tf_op jit(solution)/shard_map/dot_general | solution.py:164
  11.3 0.1 reshape_squeeze.7
  11.5 0.3 copy.18
  11.9 0.4 convolution_bitcast_fusion
  12.3 0.4 fusion.54
  12.7 0.2 convolution_bitcast_fusion.1
  12.9 0.6 compare_reduce_fusion
  13.6 0.9 %fusion.2 = bf16[2,4,4,4,4]{3,0,1,2,4:T(2,128)(2,1)S(1)} fusion(f32[2,2,1,1,1]{1,0,4,3,2:T(2,128)S(1)} %convolution_bitcast_fusion.1, pred[]{:T(512)} %compare_reduce_fusion, bf16[2,4,4,4,4]{4,3,2,1,0:T(4,128)(2,1)S(1)} %reshape_squeeze.7), kind=kOutput, calls=%fused_computation.10 | convolution fusion | flops 13824 | bytes 2065 | tf_op jit(solution)/shard_map/st,tabcd->sabcd/dot_general | solution.py:147
  14.5 0.3 copy.21
  14.9 0.4 fusion.22
  15.3 0.4 fusion.t_ref
  15.7 0.3 reshape.123
  16.0 1.2 %reshape.124 = f32[1536,96]{1,0:T(8,128)} reshape(f32[96,1536]{1,0:T(8,128)S(1)} %fusion.86) | data formatting | bytes 1179648 | tf_op jit(solution)/shard_map/reshape | solution.py:164
  17.2 0.3 reshape_squeeze.6.wd_ref
  17.5 0.7 copy-done.6
  18.2 1.1 %convolution_add_fusion.3 = f32[96,1536]{1,0:T(8,128)} fusion(f32[96,1536]{1,0:T(8,128)S(1)} %fusion.91, bf16[96,96]{1,0:T(8,128)(2,1)S(1)} %collective-permute-done, bf16[96,1536]{1,0:T(8,128)(2,1)S(1)} %collective-permute-done.1), kind=kOutput, calls=%fused_computation.3 | convolution fusion | flops 28459008 | bytes 1492992 | tf_op jit(solution)/shard_map/dot_general | solution.py:164
  19.3 1.3 %add.132 = f32[1,1536,96]{2,1,0:T(8,128)S(1)} reshape(f32[96,1536]{1,0:T(8,128)} %convolution_add_fusion.3) | data formatting | bytes 1179648 | tf_op jit(solution)/shard_map/add | solution.py:170
  20.6 1.1 %copy.13 = f32[1,1536,96]{1,2,0:T(8,128)} copy(f32[1,1536,96]{2,1,0:T(8,128)S(1)} %add.132) | data formatting | bytes 1179648 | tf_op jit(solution)/shard_map/add | solution.py:170
  21.7 1.2 %convolution_add_fusion.2 = f32[96,1536]{1,0:T(8,128)S(1)} fusion(f32[96,1536]{1,0:T(8,128)S(1)} %fusion.86, bf16[96,96]{1,0:T(8,128)(2,1)S(1)} %collective-permute-done.2, bf16[96,1536]{1,0:T(8,128)(2,1)} %collective-permute-done.3), kind=kOutput, calls=%fused_computation.2 | convolution fusion | flops 28459008 | bytes 1492992 | tf_op jit(solution)/shard_map/dot_general | solution.py:164
  22.9 0.3 add.134
  23.2 0.3 copy.14
  23.5 0.5 copy-done.3
  24.1 6.8 %shard_map.103 = f32[2,96,1536]{2,1,0:T(8,128)S(1)} custom-call(f32[2,96,1536]{2,1,0:T(8,128)S(1)} %maximum_bitcast_fusion.y_ref), custom_call_target="tpu_custom_call" | custom-call | tf_op jit(solution)/shard_map/pallas_call | solution.py:46
  30.9 1.3 %multiply_reduce_fusion.4 = (f32[]{:T(128)}, f32[96,96]{1,0:T(8,128)S(1)}) fusion(f32[1536,96]{1,0:T(8,128)S(1)} %copy-done.2, f32[2,96,1536]{2,1,0:T(8,128)S(1)} %shard_map.103), kind=kOutput, calls=%fused_computation.78 | convolution fusion | flops 169887744 | bytes 1413124 | tf_op jit(solution)/shard_map/dot_general | solution.py:173
  33.0 3.0 %collective-permute-start.5 = (bf16[96,96]{1,0:T(8,128)(2,1)S(1)}, bf16[96,96]{1,0:T(8,128)(2,1)S(1)}, u32[]{:S(2)}, u32[]{:S(2)}) collective-permute-start(bf16[96,96]{1,0:T(8,128)(2,1)S(1)} %divide_convert_fusion.4), channel_id=1, source_target_pairs={{0,15},{1,8},{2,9},{3,10},{4,11},{5,12},{6,13},{7,14},{8,23},{9,16... | collective-permute-start | bytes 55304 | tf_op jit(solution)/shard_map/ppermute | solution.py:60
  36.0 2.7 %collective-permute-start.7 = (bf16[96,96]{1,0:T(8,128)(2,1)S(1)}, bf16[96,96]{1,0:T(8,128)(2,1)S(1)}, u32[]{:S(2)}, u32[]{:S(2)}) collective-permute-start(bf16[96,96]{1,0:T(8,128)(2,1)S(1)} %divide_convert_fusion.4), channel_id=1, source_target_pairs={{0,8},{1,9},{2,10},{3,11},{4,12},{5,13},{6,14},{7,15},{8,16},{9,17... | collective-permute-start | bytes 55304 | tf_op jit(solution)/shard_map/ppermute | solution.py:60
  38.7 1.3 %multiply_reduce_fusion.5 = (f32[]{:T(128)}, f32[96,96]{1,0:T(8,128)S(1)}) fusion(f32[1536,96]{1,0:T(8,128)S(1)} %reshape.123, f32[2,96,1536]{2,1,0:T(8,128)S(1)} %shard_map.103), kind=kOutput, calls=%fused_computation.80 | convolution fusion | flops 169887744 | bytes 1413124 | tf_op jit(solution)/shard_map/dot_general | solution.py:174
  40.8 0.2 collective-permute-start.6
  41.1 0.2 copy.17
  41.6 5.5 %shard_map.105 = f32[16,96,128]{2,1,0:T(8,128)S(1)} custom-call(bf16[1536,96]{1,0:T(8,128)(2,1)S(1)} %reshape_squeeze.6.wd_ref, bf16[96,2048]{1,0:T(8,128)(2,1)S(1)} %bitcast.111, bf16[256,256]{1,0:T(8,128)(2,1)S(1)} %fusion.t_ref, bf16[96,1536]{1,0:T(8,128)(2,1)S(1)} %get-tuple-element.5.qt_ref), custom_call_target="tpu_custom_call" | custom-call | tf_op jit(solution)/shard_map/pallas_call | solution.py:104
  47.0 0.8 multiply_reduce_fusion.1
  48.6 0.2 copy.22
  48.8 1.1 %convert_element_type.80 = bf16[96,1536]{1,0:T(8,128)(2,1)} reshape(bf16[96,16,96]{2,1,0:T(8,128)(2,1)S(1)} %copy.22) | data formatting | bytes 589824 | tf_op jit(solution)/shard_map/convert_element_type | solution.py:181
  49.9 0.4 collective-permute-start.9
  50.4 0.2 fusion.89
  50.6 0.2 convolution_add_fusion.1
  50.9 0.2 fusion.84
  51.1 0.3 reshape.131
  51.4 0.3 add.138
  51.6 0.3 copy.15
  51.9 1.2 %reshape.125 = f32[1536,96]{1,0:T(8,128)} reshape(f32[96,1536]{1,0:T(8,128)S(1)} %fusion.84) | data formatting | bytes 1179648 | tf_op jit(solution)/shard_map/reshape | solution.py:164
  53.1 1.2 %convolution_add_fusion = f32[96,1536]{1,0:T(8,128)S(1)} fusion(f32[96,1536]{1,0:T(8,128)S(1)} %fusion.84, bf16[96,96]{1,0:T(8,128)(2,1)S(1)} %collective-permute-done.6, bf16[96,1536]{1,0:T(8,128)(2,1)} %collective-permute-done.3), kind=kOutput, calls=%fused_computation | convolution fusion | flops 28459008 | bytes 1492992 | tf_op jit(solution)/shard_map/dot_general | solution.py:164
  54.3 0.3 add.140
  54.5 0.3 copy.16
  54.9 6.9 %shard_map.104 = f32[2,96,1536]{2,1,0:T(8,128)S(1)} custom-call(f32[2,96,1536]{2,1,0:T(8,128)S(1)} %maximum_bitcast_fusion.1.y_ref), custom_call_target="tpu_custom_call" | custom-call | tf_op jit(solution)/shard_map/pallas_call | solution.py:46
  61.7 1.3 %multiply_reduce_fusion.2 = (f32[]{:T(128)}, f32[96,96]{1,0:T(8,128)S(1)}) fusion(f32[1536,96]{1,0:T(8,128)S(1)} %reshape.131, f32[2,96,1536]{2,1,0:T(8,128)S(1)} %shard_map.104), kind=kOutput, calls=%fused_computation.74 | convolution fusion | flops 169887744 | bytes 1413124 | tf_op jit(solution)/shard_map/dot_general | solution.py:174
  63.8 0.7 collective-permute-start.11
  64.5 0.2 copy.23
  64.9 1.3 %reshape.129.wd_ref = bf16[1536,96]{1,0:T(8,128)(2,1)S(1)} reshape(bf16[96,1536]{1,0:T(8,128)(2,1)} %collective-permute-done.9) | data formatting | bytes 589824 | tf_op jit(solution)/shard_map/reshape | solution.py:100
  66.2 5.5 %shard_map.106 = f32[16,96,128]{2,1,0:T(8,128)S(1)} custom-call(bf16[1536,96]{1,0:T(8,128)(2,1)S(1)} %reshape.129.wd_ref, bf16[96,2048]{1,0:T(8,128)(2,1)S(1)} %bitcast.110, bf16[256,256]{1,0:T(8,128)(2,1)S(1)} %fusion.t_ref, bf16[96,1536]{1,0:T(8,128)(2,1)S(1)} %get-tuple-element.3.qt_ref), custom_call_target="tpu_custom_call" | custom-call | tf_op jit(solution)/shard_map/pallas_call | solution.py:104
  71.7 0.8 multiply_reduce_fusion
  73.3 0.2 copy.24
  73.5 0.4 convert_element_type.86
  73.9 1.2 %collective-permute-start.10 = (bf16[96,1536]{1,0:T(8,128)(2,1)S(1)}, bf16[96,1536]{1,0:T(8,128)(2,1)S(1)}, u32[]{:S(2)}, u32[]{:S(2)}) collective-permute-start(bf16[96,1536]{1,0:T(8,128)(2,1)S(1)} %convert_element_type.86), channel_id=1, source_target_pairs={{0,8},{1,9},{2,10},{3,11},{4,12},{5,13},{6,14},{7,15},{8,16},{9,17... | collective-permute-start | bytes 884744 | tf_op jit(solution)/shard_map/ppermute | solution.py:60
  75.1 1.3 %multiply_reduce_fusion.3 = (f32[]{:T(128)}, f32[96,96]{1,0:T(8,128)S(1)}) fusion(f32[1536,96]{1,0:T(8,128)S(1)} %copy-done.1, f32[2,96,1536]{2,1,0:T(8,128)S(1)} %shard_map.104), kind=kOutput, calls=%fused_computation.76 | convolution fusion | flops 169887744 | bytes 1413124 | tf_op jit(solution)/shard_map/dot_general | solution.py:173
  77.1 0.5 collective-permute-start.8
  77.6 2.8 %collective-permute-done.8 = bf16[96,96]{1,0:T(8,128)(2,1)S(1)} collective-permute-done((bf16[96,96]{1,0:T(8,128)(2,1)S(1)}, bf16[96,96]{1,0:T(8,128)(2,1)S(1)}, u32[]{:S(2)}, u32[]{:S(2)}) %collective-permute-start.8) | collective-permute-done | bytes 18464 | tf_op jit(solution)/shard_map/ppermute | solution.py:60
  80.4 0.6 copy.37
  81.0 0.7 copy.38
  81.7 0.6 copy.39
  (55 shorter events, 1.3 us)
Async XLA Ops:
  0.6 12.1 %copy-start = (f32[2,2]{1,0:T(2,128)S(1)}, f32[2,2]{1,0:T(2,128)}, u32[]{:S(2)}) copy-start(f32[2,2]{1,0:T(2,128)} %param.14) | copy-start | bytes 52
  0.6 10.7 %copy-start.9 = (bf16[1,1,2,256]{3,2,1,0:T(2,128)(2,1)S(1)}, bf16[1,1,2,256]{3,2,1,0:T(2,128)(2,1)}, u32[]{:S(2)}) copy-start(bf16[1,1,2,256]{3,2,1,0:T(2,128)(2,1)} %param.13) | copy-start | bytes 3076
  0.7 16.8 %collective-permute-start.1 = (bf16[96,1536]{1,0:T(8,128)(2,1)}, bf16[96,1536]{1,0:T(8,128)(2,1)S(1)}, u32[]{:S(2)}, u32[]{:S(2)}) collective-permute-start(bf16[96,1536]{1,0:T(8,128)(2,1)} %bitcast.117), channel_id=1, source_target_pairs={{0,7},{1,0},{2,1},{3,2},{4,3},{5,4},{6,5},{7,6},{8,15},{9,8},{10,9... | collective-permute-start | bytes 884744 | tf_op jit(solution)/shard_map/ppermute | solution.py:60
  6.7 10.7 %collective-permute-start = (bf16[96,96]{1,0:T(8,128)(2,1)}, bf16[96,96]{1,0:T(8,128)(2,1)S(1)}, u32[]{:S(2)}, u32[]{:S(2)}) collective-permute-start(bf16[96,96]{1,0:T(8,128)(2,1)} %bitcast.122), channel_id=1, source_target_pairs={{0,7},{1,0},{2,1},{3,2},{4,3},{5,4},{6,5},{7,6},{8,15},{9,8},{10,9... | collective-permute-start | bytes 55304 | tf_op jit(solution)/shard_map/ppermute | solution.py:60
  7.2 14.5 %collective-permute-start.3 = (bf16[96,1536]{1,0:T(8,128)(2,1)}, bf16[96,1536]{1,0:T(8,128)(2,1)}, u32[]{:S(2)}, u32[]{:S(2)}) collective-permute-start(bf16[96,1536]{1,0:T(8,128)(2,1)} %bitcast.116), channel_id=1, source_target_pairs={{0,1},{1,2},{2,3},{3,4},{4,5},{5,6},{6,7},{7,0},{8,9},{9,10},{10,1... | collective-permute-start | bytes 884744 | tf_op jit(solution)/shard_map/ppermute | solution.py:60
  8.8 13.0 %collective-permute-start.2 = (bf16[96,96]{1,0:T(8,128)(2,1)}, bf16[96,96]{1,0:T(8,128)(2,1)S(1)}, u32[]{:S(2)}, u32[]{:S(2)}) collective-permute-start(bf16[96,96]{1,0:T(8,128)(2,1)} %bitcast.123), channel_id=1, source_target_pairs={{0,1},{1,2},{2,3},{3,4},{4,5},{5,6},{6,7},{7,0},{8,9},{9,10},{10,1... | collective-permute-start | bytes 55304 | tf_op jit(solution)/shard_map/ppermute | solution.py:60
  10.0 2.9 %copy-start.10 = (s32[4]{0:T(128)S(1)}, s32[4]{0:T(128)}, u32[]{:S(2)}) copy-start(s32[4]{0:T(128)} %param.15) | copy-start | bytes 52
  15.7 1.4 %copy-start.8 = (bf16[1,1,96,1536]{3,2,1,0:T(8,128)(2,1)S(1)}, bf16[1,1,96,1536]{3,2,1,0:T(8,128)(2,1)}, u32[]{:S(2)}) copy-start(bf16[1,1,96,1536]{3,2,1,0:T(8,128)(2,1)} %param.10) | copy-start | bytes 884740
  17.5 0.7 copy-start.6
  22.9 1.1 %copy-start.3 = (f32[1,1536,96]{1,2,0:T(8,128)S(1)}, f32[1,1536,96]{1,2,0:T(8,128)}, u32[]{:S(2)}) copy-start(f32[1,1536,96]{1,2,0:T(8,128)} %copy.13) | copy-start | bytes 1769476
  24.1 6.9 %copy-start.2 = (f32[1536,96]{1,0:T(8,128)S(1)}, f32[1536,96]{1,0:T(8,128)}, u32[]{:S(2)}) copy-start(f32[1536,96]{1,0:T(8,128)} %reshape.124) | copy-start | bytes 1769476
  33.0 17.6 %collective-permute-start.5 = (bf16[96,96]{1,0:T(8,128)(2,1)S(1)}, bf16[96,96]{1,0:T(8,128)(2,1)S(1)}, u32[]{:S(2)}, u32[]{:S(2)}) collective-permute-start(bf16[96,96]{1,0:T(8,128)(2,1)S(1)} %divide_convert_fusion.4), channel_id=1, source_target_pairs={{0,15},{1,8},{2,9},{3,10},{4,11},{5,12},{6,13},{7,14},{8,23},{9,16... | collective-permute-start | bytes 55304 | tf_op jit(solution)/shard_map/ppermute | solution.py:60
  36.0 14.8 %collective-permute-start.7 = (bf16[96,96]{1,0:T(8,128)(2,1)S(1)}, bf16[96,96]{1,0:T(8,128)(2,1)S(1)}, u32[]{:S(2)}, u32[]{:S(2)}) collective-permute-start(bf16[96,96]{1,0:T(8,128)(2,1)S(1)} %divide_convert_fusion.4), channel_id=1, source_target_pairs={{0,8},{1,9},{2,10},{3,11},{4,12},{5,13},{6,14},{7,15},{8,16},{9,17... | collective-permute-start | bytes 55304 | tf_op jit(solution)/shard_map/ppermute | solution.py:60
  40.8 9.6 %collective-permute-start.4 = (bf16[96,96]{1,0:T(8,128)(2,1)S(1)}, bf16[96,96]{1,0:T(8,128)(2,1)S(1)}, u32[]{:S(2)}, u32[]{:S(2)}) collective-permute-start(bf16[96,96]{1,0:T(8,128)(2,1)S(1)} %divide_convert_fusion.5), channel_id=1, source_target_pairs={{0,8},{1,9},{2,10},{3,11},{4,12},{5,13},{6,14},{7,15},{8,16},{9,17... | collective-permute-start | bytes 55304 | tf_op jit(solution)/shard_map/ppermute | solution.py:60
  40.8 12.2 %collective-permute-start.6 = (bf16[96,96]{1,0:T(8,128)(2,1)S(1)}, bf16[96,96]{1,0:T(8,128)(2,1)S(1)}, u32[]{:S(2)}, u32[]{:S(2)}) collective-permute-start(bf16[96,96]{1,0:T(8,128)(2,1)S(1)} %divide_convert_fusion.5), channel_id=1, source_target_pairs={{0,9},{1,10},{2,11},{3,12},{4,13},{5,14},{6,15},{7,8},{8,17},{9,18... | collective-permute-start | bytes 55304 | tf_op jit(solution)/shard_map/ppermute | solution.py:60
  48.5 1.8 %copy-start.4 = (bf16[1,1,96,1536]{3,2,1,0:T(8,128)(2,1)S(1)}, bf16[1,1,96,1536]{3,2,1,0:T(8,128)(2,1)}, u32[]{:S(2)}) copy-start(bf16[1,1,96,1536]{3,2,1,0:T(8,128)(2,1)} %param.12) | copy-start | bytes 884740
  48.6 2.0 %copy-start.7 = (bf16[96,1536]{1,0:T(8,128)(2,1)S(1)}, bf16[96,1536]{1,0:T(8,128)(2,1)}, u32[]{:S(2)}) copy-start(bf16[96,1536]{1,0:T(8,128)(2,1)} %copy-done.6) | copy-start | bytes 884740
  49.9 1.0 %copy-start.5 = (bf16[1,1,96,1536]{3,2,1,0:T(8,128)(2,1)S(1)}, bf16[1,1,96,1536]{3,2,1,0:T(8,128)(2,1)}, u32[]{:S(2)}) copy-start(bf16[1,1,96,1536]{3,2,1,0:T(8,128)(2,1)} %param.9) | copy-start | bytes 884740
  49.9 15.0 %collective-permute-start.9 = (bf16[96,1536]{1,0:T(8,128)(2,1)}, bf16[96,1536]{1,0:T(8,128)(2,1)}, u32[]{:S(2)}, u32[]{:S(2)}) collective-permute-start(bf16[96,1536]{1,0:T(8,128)(2,1)} %convert_element_type.80), channel_id=1, source_target_pairs={{0,8},{1,9},{2,10},{3,11},{4,12},{5,13},{6,14},{7,15},{8,16},{9,17... | collective-permute-start | bytes 884744 | tf_op jit(solution)/shard_map/ppermute | solution.py:60
  63.8 13.9 %collective-permute-start.11 = (bf16[96,96]{1,0:T(8,128)(2,1)S(1)}, bf16[96,96]{1,0:T(8,128)(2,1)S(1)}, u32[]{:S(2)}, u32[]{:S(2)}) collective-permute-start(bf16[96,96]{1,0:T(8,128)(2,1)S(1)} %divide_convert_fusion.2), channel_id=1, source_target_pairs={{0,8},{1,9},{2,10},{3,11},{4,12},{5,13},{6,14},{7,15},{8,16},{9,17... | collective-permute-start | bytes 55304 | tf_op jit(solution)/shard_map/ppermute | solution.py:60
  73.2 1.8 %copy-start.1 = (f32[1536,96]{1,0:T(8,128)S(1)}, f32[1536,96]{1,0:T(8,128)}, u32[]{:S(2)}) copy-start(f32[1536,96]{1,0:T(8,128)} %reshape.125) | copy-start | bytes 1769476
  73.9 6.5 %collective-permute-start.10 = (bf16[96,1536]{1,0:T(8,128)(2,1)S(1)}, bf16[96,1536]{1,0:T(8,128)(2,1)S(1)}, u32[]{:S(2)}, u32[]{:S(2)}) collective-permute-start(bf16[96,1536]{1,0:T(8,128)(2,1)S(1)} %convert_element_type.86), channel_id=1, source_target_pairs={{0,8},{1,9},{2,10},{3,11},{4,12},{5,13},{6,14},{7,15},{8,16},{9,17... | collective-permute-start | bytes 884744 | tf_op jit(solution)/shard_map/ppermute | solution.py:60
  77.1 3.3 %collective-permute-start.8 = (bf16[96,96]{1,0:T(8,128)(2,1)S(1)}, bf16[96,96]{1,0:T(8,128)(2,1)S(1)}, u32[]{:S(2)}, u32[]{:S(2)}) collective-permute-start(bf16[96,96]{1,0:T(8,128)(2,1)S(1)} %divide_convert_fusion.3), channel_id=1, source_target_pairs={{0,8},{1,9},{2,10},{3,11},{4,12},{5,13},{6,14},{7,15},{8,16},{9,17... | collective-permute-start | bytes 55304 | tf_op jit(solution)/shard_map/ppermute | solution.py:60

commit v2 on v1

--- a/solution.py
+++ b/solution.py
@@ -29,7 +29,7 @@
     return out(ah, bh) + (out(ah, bl) + out(al, bh))
 
 
-def polar_kernel(y_ref, o_ref):
+def polar_kernel(y_ref, h_ref, p_ref, c_ref):
     count = y_ref.shape[0]
     ys = []
     for b in range(count):
@@ -39,15 +39,21 @@
         grams = [dot3(y, y, ((1,), (1,))) for y in ys]
         ys = [1.5 * y - 0.5 * dot3(g, y, ((1,), (0,))) for g, y in zip(grams, ys)]
     for b in range(count):
-        o_ref[b] = ys[b]
-
-
-def polar_factor_t(stack):
+        p_ref[b] = ys[b].astype(p_ref.dtype)
+        corner = dot3(ys[b], h_ref[b], ((1,), (0,)))
+        c_ref[b] = (corner / jnp.sqrt(jnp.mean(corner * corner) + 1e-06)).astype(c_ref.dtype)
+
+
+def polar_factor_t(stack, halves):
+    count, n, _ = stack.shape
     return pl.pallas_call(
         polar_kernel,
-        out_shape=jax.ShapeDtypeStruct(stack.shape, jnp.float32),
+        out_shape=(
+            jax.ShapeDtypeStruct(stack.shape, jnp.bfloat16),
+            jax.ShapeDtypeStruct((count, n, n), jnp.bfloat16),
+        ),
         compiler_params=pltpu.CompilerParams(vmem_limit_bytes=32 * 1024 * 1024),
-    )(stack)
+    )(stack, halves)
 
 
 def shifted(tree, dx, dy):
@@ -167,17 +173,17 @@
         lower = half(corner_low, south_edge)
         upper_nb = half(up_corner_nb, north_nb)
         lower_nb = half(low_corner_nb, south_nb)
-        projs = polar_factor_t(jnp.swapaxes(jnp.stack([lower + upper_nb, lower_nb + upper]), 1, 2))
+        projs, corners = polar_factor_t(
+            jnp.swapaxes(jnp.stack([lower + upper_nb, lower_nb + upper]), 1, 2), jnp.stack([lower, upper])
+        )
         below_t = projs[0]
         above_t = projs[1]
-        new_up = jnp.dot(above_t, upper, precision=lax.Precision.HIGHEST)
-        new_low = jnp.dot(below_t, lower, precision=lax.Precision.HIGHEST)
-        new_up = unit_scaled(new_up).astype(jnp.bfloat16)
-        new_low = unit_scaled(new_low).astype(jnp.bfloat16)
+        new_low = corners[0]
+        new_up = corners[1]
         if step + 1 < STEPS:
             up_corner_nb = shifted(new_up, 1, -1)
             low_corner_nb = shifted(new_low, 1, 1)
-        edge_new = edge_contract(west_edge, below_t.astype(jnp.bfloat16), above_t.astype(jnp.bfloat16), site)
+        edge_new = edge_contract(west_edge, below_t, above_t, site)
         edge_new = unit_scaled(edge_new).astype(jnp.bfloat16)
         corner_up, west_edge, corner_low = shifted((new_up, edge_new, new_low), 1, 0)
     return (corner_up[None, None], west_edge[None, None], corner_low[None, None])

time: 82.8 us -> 92.1 us (1.11)
  local copies, waits for them, and re-layouts: 15.4 us -> 22 us
  other arithmetic: 2.63 us -> 5.71 us
  between operations: 5.36 us -> 2.51 us
  Pallas kernels: 24.6 us -> 26.6 us
  waiting for transfers between devices: 2.81 us -> 4.44 us
  matrix products: 14.6 us -> 13.6 us
    reshape x4 -> x16, local copies, waits for them, and re-layouts: 2.82 us -> 13.9 us  [half(): jnp.dot(corner, edge, preferred_element_type=jnp.float32)]
    dot_general x4 -> x0, matrix products: 5.29 us -> none  [the longest x2 2.65 us: per_device(): new_up = jnp.dot(above_t, upper, precision=lax.Precision.HIGHEST)]
    add x8 -> x0, local copies, waits for them, and re-layouts: 3.95 us -> none  [the longest x4 2.93 us: per_device(): lower + upper_nb]
    dot_general x8, matrix products: 6.5 us -> 10 us  [half(): jnp.dot(corner, edge, preferred_element_type=jnp.float32)]
    add x0 -> x4, other arithmetic: none -> 2.91 us  [the longest x2 2.78 us: per_device(): lower_nb + upper]
    pallas_call x2, Pallas kernels: 13.7 us -> 15.5 us  [polar_factor_t(): pl.pallas_call(polar_kernel, out_shape=(jax.ShapeDtypeStruct(stack.shape,...]
    ppermute x12, waiting for transfers between devices: 2.81 us -> 4.44 us  [shifted(): return lax.ppermute(tree, ('gx', 'gy'), pairs)]
  transfers between devices with their start and end apart: 12 -> 12, of which waited for: 1 -> 2; matrix products, arithmetic and copies ran while one was open for 32% -> 33% of each run, Pallas kernels for 22% -> 14%
where the time goes in v2:
time: 92.1 us; the launch traced here: 91.5 us
  Pallas kernels  26.6 us (29%)
  local copies, waits for them, and re-layouts  22 us (24%)
  starting transfers between devices  16.6 us (18%)
  matrix products  13.6 us (15%)
  other arithmetic  5.71 us (6%)
  waiting for transfers between devices  4.44 us (5%)
  between operations  2.51 us (3%)
    ppermute x12, starting transfers between devices, shifted(): return lax.ppermute(tree, ('gx', 'gy'), pairs)  16.6 us
    pallas_call x2, Pallas kernels, polar_factor_t(): pl.pallas_call(polar_kernel, out_shape=(jax.ShapeDtypeStruct(stack.shape,...  15.5 us
    reshape x16, local copies, waits for them, and re-layouts, half(): jnp.dot(corner, edge, preferred_element_type=jnp.float32)  13.9 us
    pallas_call x2, Pallas kernels, edge_contract(): pl.pallas_call(edge_kernel, out_shape=jax.ShapeDtypeStruct((dd, n, LANES)...  11.1 us
    dot_general x8, matrix products, half(): jnp.dot(corner, edge, preferred_element_type=jnp.float32)  10 us
    ppermute x12, waiting for transfers between devices, shifted(): return lax.ppermute(tree, ('gx', 'gy'), pairs)  4.44 us
    unnamed x27, local copies, waits for them, and re-layouts  3 us
    add x2, other arithmetic, per_device(): lower_nb + upper  2.78 us
  transfers between devices with their start and end apart: 12, of which 2 were waited for; matrix products, arithmetic and copies ran while one was open for 33% of the time, Pallas kernels for 14%

profile of v2, /device:TPU:0, one launch (start us, length us, event | category | flops | bytes accessed | tf_op | source)
XLA Modules:
  0.0 91.5 jit_solution(5578442571738275538)
XLA Ops:
  0.6 3.0 %collective-permute-start.2 = (bf16[96,96]{1,0:T(8,128)(2,1)}, bf16[96,96]{1,0:T(8,128)(2,1)S(1)}, u32[]{:S(2)}, u32[]{:S(2)}) collective-permute-start(bf16[96,96]{1,0:T(8,128)(2,1)} %bitcast.106), channel_id=1, source_target_pairs={{0,1},{1,2},{2,3},{3,4},{4,5},{5,6},{6,7},{7,0},{8,9},{9,10},{10,1... | collective-permute-start | bytes 55304 | tf_op jit(solution)/shard_map/ppermute | solution.py:66
  3.7 1.5 %collective-permute-start.3 = (bf16[96,1536]{1,0:T(8,128)(2,1)}, bf16[96,1536]{1,0:T(8,128)(2,1)}, u32[]{:S(2)}, u32[]{:S(2)}) collective-permute-start(bf16[96,1536]{1,0:T(8,128)(2,1)} %bitcast.101), channel_id=1, source_target_pairs={{0,1},{1,2},{2,3},{3,4},{4,5},{5,6},{6,7},{7,0},{8,9},{9,10},{10,1... | collective-permute-start | bytes 884744 | tf_op jit(solution)/shard_map/ppermute | solution.py:66
  5.2 3.2 %collective-permute-start = (bf16[96,96]{1,0:T(8,128)(2,1)}, bf16[96,96]{1,0:T(8,128)(2,1)S(1)}, u32[]{:S(2)}, u32[]{:S(2)}) collective-permute-start(bf16[96,96]{1,0:T(8,128)(2,1)} %bitcast.107), channel_id=1, source_target_pairs={{0,7},{1,0},{2,1},{3,2},{4,3},{5,4},{6,5},{7,6},{8,15},{9,8},{10,9... | collective-permute-start | bytes 55304 | tf_op jit(solution)/shard_map/ppermute | solution.py:66
  8.4 0.4 collective-permute-start.1
  8.8 1.2 %fusion.76 = f32[96,1536]{1,0:T(8,128)S(1)} fusion(bf16[1,1,96,1536]{3,2,1,0:T(8,128)(2,1)} %param.9, bf16[1,1,96,96]{3,2,1,0:T(8,128)(2,1)} %param.8), kind=kOutput, calls=%fused_computation.126 | convolution fusion | flops 28311552 | bytes 903168 | tf_op jit(solution)/shard_map/dot_general | solution.py:170
  10.0 1.2 %fusion.81 = f32[96,1536]{1,0:T(8,128)S(1)} fusion(bf16[1,1,96,1536]{3,2,1,0:T(8,128)(2,1)} %param.12, bf16[1,1,96,96]{3,2,1,0:T(8,128)(2,1)} %param.11), kind=kOutput, calls=%fused_computation.131 | convolution fusion | flops 28311552 | bytes 903168 | tf_op jit(solution)/shard_map/dot_general | solution.py:170
  11.3 0.3 reshape.124
  11.6 0.3 reshape.121
  12.1 0.3 copy.24
  12.5 0.4 convolution_bitcast_fusion
  12.9 1.2 %fusion.44 = f32[2,256,256]{2,1,0:T(8,128)} fusion(f32[2,16,256]{2,1,0:T(8,128)S(1)} %convolution_bitcast_fusion, s32[256]{0:T(256)S(1)} %get-tuple-element.19, s32[256]{0:T(256)S(1)} %get-tuple-element.23, s32[256]{0:T(256)S(1)} %get-tuple-element.20, s32[256]{0:T(256)S(1)} %get-tuple-element.24, pred[256]{0:T(512)(128)(4,1)S(1)} %get-tuple-element.22, ...), kind=kOutput, calls=%fused_computation.82 | convolution fusion | flops 25231360 | bytes 561664 | tf_op jit(solution)/shard_map/ra,sab,bc->src/dot_general | solution.py:139
  14.1 0.2 convolution_bitcast_fusion.1
  14.3 0.6 compare_reduce_fusion
  15.0 0.9 fusion.2
  15.9 0.3 copy.27
  16.4 0.4 fusion.12
  16.8 0.5 copy-done.5
  17.3 0.4 fusion.t_ref
  17.8 1.1 %copy.18 = f32[1,1536,96]{1,2,0:T(8,128)} copy(f32[1,1536,96]{2,1,0:T(8,128)S(1)} %reshape.124) | data formatting | bytes 1179648 | tf_op jit(solution)/shard_map/reshape | solution.py:170
  18.8 1.1 %copy.15 = f32[1,1536,96]{1,2,0:T(8,128)} copy(f32[1,1536,96]{2,1,0:T(8,128)S(1)} %reshape.121) | data formatting | bytes 1179648 | tf_op jit(solution)/shard_map/reshape | solution.py:170
  19.9 0.3 reshape_squeeze.12.wd_ref
  20.3 2.0 %fusion.97 = f32[96,1536]{1,0:T(8,128)} fusion(bf16[96,96]{1,0:T(8,128)(2,1)S(1)} %collective-permute-done.2, bf16[96,1536]{1,0:T(8,128)(2,1)} %collective-permute-done.3), kind=kOutput, calls=%fused_computation.147 | convolution fusion | flops 28311552 | bytes 903168 | tf_op jit(solution)/shard_map/dot_general | solution.py:170
  22.3 1.3 %reshape.123 = f32[1,1536,96]{2,1,0:T(8,128)S(1)} reshape(f32[96,1536]{1,0:T(8,128)} %fusion.97) | data formatting | bytes 1179648 | tf_op jit(solution)/shard_map/reshape | solution.py:170
  23.6 1.1 %copy.17 = f32[1,1536,96]{1,2,0:T(8,128)} copy(f32[1,1536,96]{2,1,0:T(8,128)S(1)} %reshape.123) | data formatting | bytes 1179648 | tf_op jit(solution)/shard_map/reshape | solution.py:170
  24.7 2.0 %fusion.96 = f32[96,1536]{1,0:T(8,128)} fusion(bf16[96,96]{1,0:T(8,128)(2,1)S(1)} %collective-permute-done, bf16[96,1536]{1,0:T(8,128)(2,1)} %collective-permute-done.1), kind=kOutput, calls=%fused_computation.146 | convolution fusion | flops 28311552 | bytes 903168 | tf_op jit(solution)/shard_map/dot_general | solution.py:170
  26.7 1.3 %reshape.122 = f32[1,1536,96]{2,1,0:T(8,128)S(1)} reshape(f32[96,1536]{1,0:T(8,128)} %fusion.96) | data formatting | bytes 1179648 | tf_op jit(solution)/shard_map/reshape | solution.py:170
  28.0 1.1 %copy.16 = f32[1,1536,96]{1,2,0:T(8,128)} copy(f32[1,1536,96]{2,1,0:T(8,128)S(1)} %reshape.122) | data formatting | bytes 1179648 | tf_op jit(solution)/shard_map/reshape | solution.py:170
  29.1 1.4 %add.108 = f32[1,1536,96]{1,2,0:T(8,128)S(1)} add(f32[1,1536,96]{1,2,0:T(8,128)} %copy.17, f32[1,1536,96]{1,2,0:T(8,128)} %copy.18) | non-fusion elementwise | flops 147456 | bytes 1769472 | tf_op jit(solution)/shard_map/add | solution.py:177
  30.6 0.2 copy-done.3
  30.9 7.7 %shard_map.103 = (bf16[2,96,1536]{2,1,0:T(8,128)(2,1)S(1)}, bf16[2,96,96]{2,1,0:T(8,128)(2,1)S(1)}) custom-call(f32[2,96,1536]{2,1,0:T(8,128)S(1)} %maximum_bitcast_fusion.y_ref, f32[2,1536,96]{2,1,0:T(8,128)S(1)} %pad_maximum_fusion.h_ref), custom_call_target="tpu_custom_call" | custom-call | tf_op jit(solution)/shard_map/pallas_call | solution.py:49
  38.7 2.7 %collective-permute-start.4 = (bf16[96,96]{1,0:T(8,128)(2,1)S(1)}, bf16[96,96]{1,0:T(8,128)(2,1)S(1)}, u32[]{:S(2)}, u32[]{:S(2)}) collective-permute-start(bf16[96,96]{1,0:T(8,128)(2,1)S(1)} %get-tuple-element.18), channel_id=1, source_target_pairs={{0,8},{1,9},{2,10},{3,11},{4,12},{5,13},{6,14},{7,15},{8,16},{9,17... | collective-permute-start | bytes 55304 | tf_op jit(solution)/shard_map/ppermute | solution.py:66
  41.4 3.3 %collective-permute-start.5 = (bf16[96,96]{1,0:T(8,128)(2,1)S(1)}, bf16[96,96]{1,0:T(8,128)(2,1)S(1)}, u32[]{:S(2)}, u32[]{:S(2)}) collective-permute-start(bf16[96,96]{1,0:T(8,128)(2,1)S(1)} %get-tuple-element.17), channel_id=1, source_target_pairs={{0,15},{1,8},{2,9},{3,10},{4,11},{5,12},{6,13},{7,14},{8,23},{9,16... | collective-permute-start | bytes 55304 | tf_op jit(solution)/shard_map/ppermute | solution.py:66
  44.8 0.2 copy.23
  45.2 5.5 %shard_map.105 = f32[16,96,128]{2,1,0:T(8,128)S(1)} custom-call(bf16[1536,96]{1,0:T(8,128)(2,1)S(1)} %reshape_squeeze.12.wd_ref, bf16[96,2048]{1,0:T(8,128)(2,1)S(1)} %bitcast.95, bf16[256,256]{1,0:T(8,128)(2,1)S(1)} %fusion.t_ref, bf16[96,1536]{1,0:T(8,128)(2,1)S(1)} %get-tuple-element.13.qt_ref), custom_call_target="tpu_custom_call" | custom-call | tf_op jit(solution)/shard_map/pallas_call | solution.py:110
  50.7 0.8 multiply_reduce_fusion.1
  52.2 0.2 copy.28
  52.4 1.1 %convert_element_type.42 = bf16[96,1536]{1,0:T(8,128)(2,1)} reshape(bf16[96,16,96]{2,1,0:T(8,128)(2,1)S(1)} %copy.28) | data formatting | bytes 589824 | tf_op jit(solution)/shard_map/convert_element_type | solution.py:187
  53.6 0.2 fusion.74
  53.8 0.3 reshape.128
  54.1 0.2 fusion.79
  54.3 0.3 reshape.125
  54.7 2.0 %fusion.99 = f32[96,1536]{1,0:T(8,128)} fusion(bf16[96,96]{1,0:T(8,128)(2,1)S(1)} %collective-permute-done.6, bf16[96,1536]{1,0:T(8,128)(2,1)} %collective-permute-done.3), kind=kOutput, calls=%fused_computation.149 | convolution fusion | flops 28311552 | bytes 903168 | tf_op jit(solution)/shard_map/dot_general | solution.py:170
  56.7 1.1 %copy.22 = f32[1,1536,96]{1,2,0:T(8,128)} copy(f32[1,1536,96]{2,1,0:T(8,128)S(1)} %reshape.128) | data formatting | bytes 1179648 | tf_op jit(solution)/shard_map/reshape | solution.py:170
  57.8 1.1 %copy.19 = f32[1,1536,96]{1,2,0:T(8,128)} copy(f32[1,1536,96]{2,1,0:T(8,128)S(1)} %reshape.125) | data formatting | bytes 1179648 | tf_op jit(solution)/shard_map/reshape | solution.py:170
  58.9 1.3 %reshape.127 = f32[1,1536,96]{2,1,0:T(8,128)S(1)} reshape(f32[96,1536]{1,0:T(8,128)} %fusion.99) | data formatting | bytes 1179648 | tf_op jit(solution)/shard_map/reshape | solution.py:170
  60.2 1.1 %copy.21 = f32[1,1536,96]{1,2,0:T(8,128)} copy(f32[1,1536,96]{2,1,0:T(8,128)S(1)} %reshape.127) | data formatting | bytes 1179648 | tf_op jit(solution)/shard_map/reshape | solution.py:170
  61.3 1.2 %fusion.98 = f32[96,1536]{1,0:T(8,128)S(1)} fusion(bf16[96,96]{1,0:T(8,128)(2,1)S(1)} %collective-permute-done.5, bf16[96,1536]{1,0:T(8,128)(2,1)} %collective-permute-done.1), kind=kOutput, calls=%fused_computation.148 | convolution fusion | flops 28311552 | bytes 903168 | tf_op jit(solution)/shard_map/dot_general | solution.py:170
  62.5 0.3 reshape.126
  62.7 1.1 %copy.20 = f32[1,1536,96]{1,2,0:T(8,128)} copy(f32[1,1536,96]{2,1,0:T(8,128)S(1)} %reshape.126) | data formatting | bytes 1179648 | tf_op jit(solution)/shard_map/reshape | solution.py:170
  63.8 1.4 %add.110 = f32[1,1536,96]{1,2,0:T(8,128)S(1)} add(f32[1,1536,96]{1,2,0:T(8,128)} %copy.21, f32[1,1536,96]{1,2,0:T(8,128)} %copy.22) | non-fusion elementwise | flops 147456 | bytes 1769472 | tf_op jit(solution)/shard_map/add | solution.py:177
  65.4 7.8 %shard_map.104 = (bf16[2,96,1536]{2,1,0:T(8,128)(2,1)S(1)}, bf16[2,96,96]{2,1,0:T(8,128)(2,1)S(1)}) custom-call(f32[2,96,1536]{2,1,0:T(8,128)S(1)} %maximum_bitcast_fusion.1.y_ref, f32[2,1536,96]{2,1,0:T(8,128)S(1)} %pad_maximum_fusion.1.h_ref), custom_call_target="tpu_custom_call" | custom-call | tf_op jit(solution)/shard_map/pallas_call | solution.py:49
  73.2 0.2 copy.29
  73.7 1.3 %reshape.132.wd_ref = bf16[1536,96]{1,0:T(8,128)(2,1)S(1)} reshape(bf16[96,1536]{1,0:T(8,128)(2,1)} %collective-permute-done.9) | data formatting | bytes 589824 | tf_op jit(solution)/shard_map/reshape | solution.py:106
  75.0 5.7 %shard_map.106 = f32[16,96,128]{2,1,0:T(8,128)S(1)} custom-call(bf16[1536,96]{1,0:T(8,128)(2,1)S(1)} %reshape.132.wd_ref, bf16[96,2048]{1,0:T(8,128)(2,1)S(1)} %bitcast.94, bf16[256,256]{1,0:T(8,128)(2,1)S(1)} %fusion.t_ref, bf16[96,1536]{1,0:T(8,128)(2,1)S(1)} %get-tuple-element.11.qt_ref), custom_call_target="tpu_custom_call" | custom-call | tf_op jit(solution)/shard_map/pallas_call | solution.py:110
  80.6 0.8 multiply_reduce_fusion
  82.2 0.2 copy.30
  82.4 0.4 convert_element_type.45
  82.8 1.8 %collective-permute-start.10 = (bf16[96,1536]{1,0:T(8,128)(2,1)S(1)}, bf16[96,1536]{1,0:T(8,128)(2,1)S(1)}, u32[]{:S(2)}, u32[]{:S(2)}) collective-permute-start(bf16[96,1536]{1,0:T(8,128)(2,1)S(1)} %convert_element_type.45), channel_id=1, source_target_pairs={{0,8},{1,9},{2,10},{3,11},{4,12},{5,13},{6,14},{7,15},{8,16},{9,17... | collective-permute-start | bytes 884744 | tf_op jit(solution)/shard_map/ppermute | solution.py:66
  84.7 0.5 collective-permute-start.11
  85.1 4.2 %collective-permute-done.8 = bf16[96,96]{1,0:T(8,128)(2,1)S(1)} collective-permute-done((bf16[96,96]{1,0:T(8,128)(2,1)S(1)}, bf16[96,96]{1,0:T(8,128)(2,1)S(1)}, u32[]{:S(2)}, u32[]{:S(2)}) %collective-permute-start.8) | collective-permute-done | bytes 18464 | tf_op jit(solution)/shard_map/ppermute | solution.py:66
  89.3 0.3 collective-permute-done.11
  89.5 0.6 copy.43
  90.2 0.7 copy.44
  90.9 0.6 copy.45
  (59 shorter events, 1.8 us)
Async XLA Ops:
  0.6 13.5 %copy-start = (f32[2,2]{1,0:T(2,128)S(1)}, f32[2,2]{1,0:T(2,128)}, u32[]{:S(2)}) copy-start(f32[2,2]{1,0:T(2,128)} %param.14) | copy-start | bytes 52
  0.6 19.6 %collective-permute-start.2 = (bf16[96,96]{1,0:T(8,128)(2,1)}, bf16[96,96]{1,0:T(8,128)(2,1)S(1)}, u32[]{:S(2)}, u32[]{:S(2)}) collective-permute-start(bf16[96,96]{1,0:T(8,128)(2,1)} %bitcast.106), channel_id=1, source_target_pairs={{0,1},{1,2},{2,3},{3,4},{4,5},{5,6},{6,7},{7,0},{8,9},{9,10},{10,1... | collective-permute-start | bytes 55304 | tf_op jit(solution)/shard_map/ppermute | solution.py:66
  3.7 16.6 %collective-permute-start.3 = (bf16[96,1536]{1,0:T(8,128)(2,1)}, bf16[96,1536]{1,0:T(8,128)(2,1)}, u32[]{:S(2)}, u32[]{:S(2)}) collective-permute-start(bf16[96,1536]{1,0:T(8,128)(2,1)} %bitcast.101), channel_id=1, source_target_pairs={{0,1},{1,2},{2,3},{3,4},{4,5},{5,6},{6,7},{7,0},{8,9},{9,10},{10,1... | collective-permute-start | bytes 884744 | tf_op jit(solution)/shard_map/ppermute | solution.py:66
  5.2 19.5 %collective-permute-start = (bf16[96,96]{1,0:T(8,128)(2,1)}, bf16[96,96]{1,0:T(8,128)(2,1)S(1)}, u32[]{:S(2)}, u32[]{:S(2)}) collective-permute-start(bf16[96,96]{1,0:T(8,128)(2,1)} %bitcast.107), channel_id=1, source_target_pairs={{0,7},{1,0},{2,1},{3,2},{4,3},{5,4},{6,5},{7,6},{8,15},{9,8},{10,9... | collective-permute-start | bytes 55304 | tf_op jit(solution)/shard_map/ppermute | solution.py:66
  8.4 16.3 %collective-permute-start.1 = (bf16[96,1536]{1,0:T(8,128)(2,1)}, bf16[96,1536]{1,0:T(8,128)(2,1)}, u32[]{:S(2)}, u32[]{:S(2)}) collective-permute-start(bf16[96,1536]{1,0:T(8,128)(2,1)} %bitcast.100), channel_id=1, source_target_pairs={{0,7},{1,0},{2,1},{3,2},{4,3},{5,4},{6,5},{7,6},{8,15},{9,8},{10,9... | collective-permute-start | bytes 884744 | tf_op jit(solution)/shard_map/ppermute | solution.py:66
  11.2 0.7 copy-start.9
  11.6 2.7 %copy-start.10 = (s32[4]{0:T(128)S(1)}, s32[4]{0:T(128)}, u32[]{:S(2)}) copy-start(s32[4]{0:T(128)} %param.15) | copy-start | bytes 52
  16.3 1.0 %copy-start.5 = (f32[2,256,256]{2,1,0:T(8,128)S(1)}, f32[2,256,256]{2,1,0:T(8,128)}, u32[]{:S(2)}) copy-start(f32[2,256,256]{2,1,0:T(8,128)} %fusion.44) | copy-start | bytes 1572868
  18.8 1.1 %copy-start.8 = (bf16[1,1,96,1536]{3,2,1,0:T(8,128)(2,1)S(1)}, bf16[1,1,96,1536]{3,2,1,0:T(8,128)(2,1)}, u32[]{:S(2)}) copy-start(bf16[1,1,96,1536]{3,2,1,0:T(8,128)(2,1)} %param.10) | copy-start | bytes 884740
  29.1 1.4 %copy-start.1 = (f32[1,1536,96]{1,2,0:T(8,128)S(1)}, f32[1,1536,96]{1,2,0:T(8,128)}, u32[]{:S(2)}) copy-start(f32[1,1536,96]{1,2,0:T(8,128)} %copy.15) | copy-start | bytes 1769476
  29.1 1.6 %copy-start.3 = (f32[1,1536,96]{1,2,0:T(8,128)S(1)}, f32[1,1536,96]{1,2,0:T(8,128)}, u32[]{:S(2)}) copy-start(f32[1,1536,96]{1,2,0:T(8,128)} %copy.16) | copy-start | bytes 1769476
  38.7 16.0 %collective-permute-start.6 = (bf16[96,96]{1,0:T(8,128)(2,1)S(1)}, bf16[96,96]{1,0:T(8,128)(2,1)S(1)}, u32[]{:S(2)}, u32[]{:S(2)}) collective-permute-start(bf16[96,96]{1,0:T(8,128)(2,1)S(1)} %get-tuple-element.18), channel_id=1, source_target_pairs={{0,9},{1,10},{2,11},{3,12},{4,13},{5,14},{6,15},{7,8},{8,17},{9,18... | collective-permute-start | bytes 55304 | tf_op jit(solution)/shard_map/ppermute | solution.py:66
  38.7 15.3 %collective-permute-start.4 = (bf16[96,96]{1,0:T(8,128)(2,1)S(1)}, bf16[96,96]{1,0:T(8,128)(2,1)S(1)}, u32[]{:S(2)}, u32[]{:S(2)}) collective-permute-start(bf16[96,96]{1,0:T(8,128)(2,1)S(1)} %get-tuple-element.18), channel_id=1, source_target_pairs={{0,8},{1,9},{2,10},{3,11},{4,12},{5,13},{6,14},{7,15},{8,16},{9,17... | collective-permute-start | bytes 55304 | tf_op jit(solution)/shard_map/ppermute | solution.py:66
  41.4 12.2 %collective-permute-start.7 = (bf16[96,96]{1,0:T(8,128)(2,1)S(1)}, bf16[96,96]{1,0:T(8,128)(2,1)S(1)}, u32[]{:S(2)}, u32[]{:S(2)}) collective-permute-start(bf16[96,96]{1,0:T(8,128)(2,1)S(1)} %get-tuple-element.17), channel_id=1, source_target_pairs={{0,8},{1,9},{2,10},{3,11},{4,12},{5,13},{6,14},{7,15},{8,16},{9,17... | collective-permute-start | bytes 55304 | tf_op jit(solution)/shard_map/ppermute | solution.py:66
  41.4 19.9 %collective-permute-start.5 = (bf16[96,96]{1,0:T(8,128)(2,1)S(1)}, bf16[96,96]{1,0:T(8,128)(2,1)S(1)}, u32[]{:S(2)}, u32[]{:S(2)}) collective-permute-start(bf16[96,96]{1,0:T(8,128)(2,1)S(1)} %get-tuple-element.17), channel_id=1, source_target_pairs={{0,15},{1,8},{2,9},{3,10},{4,11},{5,12},{6,13},{7,14},{8,23},{9,16... | collective-permute-start | bytes 55304 | tf_op jit(solution)/shard_map/ppermute | solution.py:66
  50.7 2.9 %copy-start.6 = (bf16[1,1,96,1536]{3,2,1,0:T(8,128)(2,1)S(1)}, bf16[1,1,96,1536]{3,2,1,0:T(8,128)(2,1)}, u32[]{:S(2)}) copy-start(bf16[1,1,96,1536]{3,2,1,0:T(8,128)(2,1)} %param.9) | copy-start | bytes 884740
  52.4 1.6 %copy-start.7 = (bf16[1,1,96,1536]{3,2,1,0:T(8,128)(2,1)S(1)}, bf16[1,1,96,1536]{3,2,1,0:T(8,128)(2,1)}, u32[]{:S(2)}) copy-start(bf16[1,1,96,1536]{3,2,1,0:T(8,128)(2,1)} %param.12) | copy-start | bytes 884740
  53.5 20.1 %collective-permute-start.9 = (bf16[96,1536]{1,0:T(8,128)(2,1)}, bf16[96,1536]{1,0:T(8,128)(2,1)}, u32[]{:S(2)}, u32[]{:S(2)}) collective-permute-start(bf16[96,1536]{1,0:T(8,128)(2,1)} %convert_element_type.42), channel_id=1, source_target_pairs={{0,8},{1,9},{2,10},{3,11},{4,12},{5,13},{6,14},{7,15},{8,16},{9,17... | collective-permute-start | bytes 884744 | tf_op jit(solution)/shard_map/ppermute | solution.py:66
  62.7 2.5 %copy-start.2 = (f32[1,1536,96]{1,2,0:T(8,128)S(1)}, f32[1,1536,96]{1,2,0:T(8,128)}, u32[]{:S(2)}) copy-start(f32[1,1536,96]{1,2,0:T(8,128)} %copy.19) | copy-start | bytes 1769476
  63.8 1.4 %copy-start.4 = (f32[1,1536,96]{1,2,0:T(8,128)S(1)}, f32[1,1536,96]{1,2,0:T(8,128)}, u32[]{:S(2)}) copy-start(f32[1,1536,96]{1,2,0:T(8,128)} %copy.20) | copy-start | bytes 1769476
  82.8 6.7 %collective-permute-start.10 = (bf16[96,1536]{1,0:T(8,128)(2,1)S(1)}, bf16[96,1536]{1,0:T(8,128)(2,1)S(1)}, u32[]{:S(2)}, u32[]{:S(2)}) collective-permute-start(bf16[96,1536]{1,0:T(8,128)(2,1)S(1)} %convert_element_type.45), channel_id=1, source_target_pairs={{0,8},{1,9},{2,10},{3,11},{4,12},{5,13},{6,14},{7,15},{8,16},{9,17... | collective-permute-start | bytes 884744 | tf_op jit(solution)/shard_map/ppermute | solution.py:66
  84.6 4.7 %collective-permute-start.8 = (bf16[96,96]{1,0:T(8,128)(2,1)S(1)}, bf16[96,96]{1,0:T(8,128)(2,1)S(1)}, u32[]{:S(2)}, u32[]{:S(2)}) collective-permute-start(bf16[96,96]{1,0:T(8,128)(2,1)S(1)} %get-tuple-element.16), channel_id=1, source_target_pairs={{0,8},{1,9},{2,10},{3,11},{4,12},{5,13},{6,14},{7,15},{8,16},{9,17... | collective-permute-start | bytes 55304 | tf_op jit(solution)/shard_map/ppermute | solution.py:66
  84.7 4.9 %collective-permute-start.11 = (bf16[96,96]{1,0:T(8,128)(2,1)S(1)}, bf16[96,96]{1,0:T(8,128)(2,1)S(1)}, u32[]{:S(2)}, u32[]{:S(2)}) collective-permute-start(bf16[96,96]{1,0:T(8,128)(2,1)S(1)} %get-tuple-element.15), channel_id=1, source_target_pairs={{0,8},{1,9},{2,10},{3,11},{4,12},{5,13},{6,14},{7,15},{8,16},{9,17... | collective-permute-start | bytes 55304 | tf_op jit(solution)/shard_map/ppermute | solution.py:66

commit v3 on v1

--- a/solution.py
+++ b/solution.py
@@ -159,21 +159,20 @@
     up_corner_nb, north_nb = shifted((corner_up, north_edge), 0, -1)
     low_corner_nb, south_nb = shifted((corner_low, south_edge), 0, 1)
     n = env_width
+    edges = jnp.stack([south_edge, north_nb, south_nb, north_edge])
+    hi = lax.Precision.HIGHEST
     for step in range(STEPS):
-        def half(corner, edge):
-            return jnp.dot(corner, edge, preferred_element_type=jnp.float32).reshape(n * double_bond, n)
-
-        upper = half(corner_up, north_edge)
-        lower = half(corner_low, south_edge)
-        upper_nb = half(up_corner_nb, north_nb)
-        lower_nb = half(low_corner_nb, south_nb)
-        projs = polar_factor_t(jnp.swapaxes(jnp.stack([lower + upper_nb, lower_nb + upper]), 1, 2))
+        corners_in = jnp.stack([corner_low, up_corner_nb, low_corner_nb, corner_up])
+        halves = jnp.einsum("bwa,bak->bwk", corners_in, edges, preferred_element_type=jnp.float32)
+        halves = halves.reshape(4, n * double_bond, n)
+        mats = halves[0::2] + halves[1::2]
+        projs = polar_factor_t(jnp.swapaxes(mats, 1, 2))
         below_t = projs[0]
         above_t = projs[1]
-        new_up = jnp.dot(above_t, upper, precision=lax.Precision.HIGHEST)
-        new_low = jnp.dot(below_t, lower, precision=lax.Precision.HIGHEST)
-        new_up = unit_scaled(new_up).astype(jnp.bfloat16)
-        new_low = unit_scaled(new_low).astype(jnp.bfloat16)
+        corners = jnp.einsum("bir,brj->bij", projs, halves[0::3], precision=hi)
+        corners = jax.vmap(unit_scaled)(corners).astype(jnp.bfloat16)
+        new_low = corners[0]
+        new_up = corners[1]
         if step + 1 < STEPS:
             up_corner_nb = shifted(new_up, 1, -1)
             low_corner_nb = shifted(new_low, 1, 1)

time: 82.8 us -> 97.3 us (1.18)
  local copies, waits for them, and re-layouts: 15.4 us -> 26.4 us
  waiting for transfers between devices: 2.81 us -> 8.38 us
  matrix products: 14.6 us -> 9.14 us
  other arithmetic: 2.63 us -> 6.52 us
  between operations: 5.36 us -> 2.55 us
  starting transfers between devices: 17 us -> 19.3 us
    unnamed x27 -> x43, local copies, waits for them, and re-layouts: 3.5 us -> 10.2 us
    slice x0 -> x4, local copies, waits for them, and re-layouts: none -> 5.78 us  [the longest x2 5.33 us: per_device(): mats = halves[0::2] + halves[1::2]]
    ppermute x12, waiting for transfers between devices: 2.81 us -> 8.38 us  [shifted(): return lax.ppermute(tree, ('gx', 'gy'), pairs)]
    dot_general x12 -> x4, matrix products: 11.8 us -> 6.36 us  [the longest x2 3.45 us: per_device(): jnp.einsum('bwa,bak->bwk', corners_in, edges, preferred_element_type=jnp....]
    add x8 -> x0, local copies, waits for them, and re-layouts: 3.95 us -> none  [the longest x4 2.93 us: per_device(): lower + upper_nb]
    transpose x2, other arithmetic: 0.16 us -> 3.12 us  [per_device(): projs = polar_factor_t(jnp.swapaxes(mats, 1, 2))]
    reshape x4 -> x2, local copies, waits for them, and re-layouts: 2.82 us -> 5.12 us  [per_device(): halves = halves.reshape(4, n * double_bond, n)]
    ppermute x12, starting transfers between devices: 17 us -> 19.3 us  [shifted(): return lax.ppermute(tree, ('gx', 'gy'), pairs)]
  transfers between devices with their start and end apart: 12 -> 12, of which waited for: 1 -> 4; matrix products, arithmetic and copies ran while one was open for 32% -> 23% of each run, Pallas kernels for 22% -> 13%
where the time goes in v3:
time: 97.3 us; the launch traced here: 96.9 us
  local copies, waits for them, and re-layouts  26.4 us (27%)
  Pallas kernels  24.6 us (25%)
  starting transfers between devices  19.3 us (20%)
  matrix products  9.14 us (9%)
  waiting for transfers between devices  8.38 us (9%)
  other arithmetic  6.52 us (7%)
  between operations  2.55 us (3%)
    ppermute x12, starting transfers between devices, shifted(): return lax.ppermute(tree, ('gx', 'gy'), pairs)  19.3 us
    pallas_call x2, Pallas kernels, polar_factor_t(): pl.pallas_call(polar_kernel, out_shape=jax.ShapeDtypeStruct(stack.shape,...  13.7 us
    pallas_call x2, Pallas kernels, edge_contract(): pl.pallas_call(edge_kernel, out_shape=jax.ShapeDtypeStruct((dd, n, LANES)...  10.9 us
    unnamed x43, local copies, waits for them, and re-layouts  10.2 us
    ppermute x12, waiting for transfers between devices, shifted(): return lax.ppermute(tree, ('gx', 'gy'), pairs)  8.38 us
    slice x2, local copies, waits for them, and re-layouts, per_device(): mats = halves[0::2] + halves[1::2]  5.33 us
    reshape x2, local copies, waits for them, and re-layouts, per_device(): halves = halves.reshape(4, n * double_bond, n)  5.12 us
    dot_general x2, matrix products, per_device(): jnp.einsum('bwa,bak->bwk', corners_in, edges, preferred_element_type=jnp....  3.45 us
  transfers between devices with their start and end apart: 12, of which 4 were waited for; matrix products, arithmetic and copies ran while one was open for 23% of the time, Pallas kernels for 13%

profile of v3, /device:TPU:0, one launch (start us, length us, event | category | flops | bytes accessed | tf_op | source)
XLA Modules:
  0.0 96.9 jit_solution(11100136481983798780)
XLA Ops:
  0.6 3.0 %collective-permute-start.1 = (bf16[96,96]{1,0:T(8,128)(2,1)}, bf16[96,96]{1,0:T(8,128)(2,1)S(1)}, u32[]{:S(2)}, u32[]{:S(2)}) collective-permute-start(bf16[96,96]{1,0:T(8,128)(2,1)} %bitcast.108), channel_id=1, source_target_pairs={{0,1},{1,2},{2,3},{3,4},{4,5},{5,6},{6,7},{7,0},{8,9},{9,10},{10,1... | collective-permute-start | bytes 55304 | tf_op jit(solution)/shard_map/ppermute | solution.py:60
  3.7 3.1 %collective-permute-start = (bf16[96,96]{1,0:T(8,128)(2,1)}, bf16[96,96]{1,0:T(8,128)(2,1)S(1)}, u32[]{:S(2)}, u32[]{:S(2)}) collective-permute-start(bf16[96,96]{1,0:T(8,128)(2,1)} %bitcast.106), channel_id=1, source_target_pairs={{0,7},{1,0},{2,1},{3,2},{4,3},{5,4},{6,5},{7,6},{8,15},{9,8},{10,9... | collective-permute-start | bytes 55304 | tf_op jit(solution)/shard_map/ppermute | solution.py:60
  6.8 4.7 %collective-permute-start.2 = (bf16[96,1536]{1,0:T(8,128)(2,1)}, bf16[96,1536]{1,0:T(8,128)(2,1)S(1)}, u32[]{:S(2)}, u32[]{:S(2)}) collective-permute-start(bf16[96,1536]{1,0:T(8,128)(2,1)} %bitcast.96), channel_id=1, source_target_pairs={{0,7},{1,0},{2,1},{3,2},{4,3},{5,4},{6,5},{7,6},{8,15},{9,8},{10,9... | collective-permute-start | bytes 884744 | tf_op jit(solution)/shard_map/ppermute | solution.py:60
  11.6 0.2 convolution_bitcast_fusion.1
  11.8 0.8 reshape_squeeze.7
  12.6 1.3 %compare_reduce_fusion = pred[]{:T(512)} fusion(s32[4]{0:T(128)} %param.15, s32[]{:T(128)S(6)} %add.95), kind=kLoop, calls=%fused_computation.136 | loop fusion | flops 7 | bytes 21 | tf_op jit(solution)/shard_map/reduce_or | solution.py:151
  13.9 0.9 fusion.6
  14.8 0.3 copy.23
  15.1 0.1 reshape.57
  15.2 0.3 copy.20
  15.5 0.1 reshape.56
  15.6 0.4 convolution_bitcast_fusion
  16.0 0.4 fusion.64
  16.5 0.4 fusion.18
  16.9 0.4 fusion.4.t_ref
  17.4 0.3 reshape_squeeze.6.wd_ref
  17.7 2.2 %collective-permute-done.3 = bf16[96,1536]{1,0:T(8,128)(2,1)S(1)} collective-permute-done((bf16[96,1536]{1,0:T(8,128)(2,1)}, bf16[96,1536]{1,0:T(8,128)(2,1)S(1)}, u32[]{:S(2)}, u32[]{:S(2)}) %collective-permute-start.3) | collective-permute-done | bytes 294944 | tf_op jit(solution)/shard_map/ppermute | solution.py:60
  20.0 1.8 %collective-permute-done.2 = bf16[96,1536]{1,0:T(8,128)(2,1)S(1)} collective-permute-done((bf16[96,1536]{1,0:T(8,128)(2,1)}, bf16[96,1536]{1,0:T(8,128)(2,1)S(1)}, u32[]{:S(2)}, u32[]{:S(2)}) %collective-permute-start.2) | collective-permute-done | bytes 294944 | tf_op jit(solution)/shard_map/ppermute | solution.py:60
  21.8 0.7 copy-done.12
  22.5 1.5 %fusion.10 = f32[4,96,1536]{2,1,0:T(8,128)S(1)} fusion(bf16[1,96,1536]{2,1,0:T(8,128)(2,1)S(1)} %bitcast.97, bf16[1,96,1536]{2,1,0:T(8,128)(2,1)} %bitcast.102, bf16[1,96,1536]{2,1,0:T(8,128)(2,1)} %bitcast.104, bf16[1,96,1536]{2,1,0:T(8,128)(2,1)S(1)} %bitcast.100, bf16[1,96,96]{2,1,0:T(8,128)(2,1)S(1)} %bitcast.107, bf16[1,96,96]{2,1,0:T(8,128)(2,1)S(1)} %bitcast.110, ...), kind=kOutput, calls=%fused_computation.31 | convolution fusion | flops 115126272 | bytes 3612672 | tf_op jit(solution)/shard_map/bwa,bak->bwk/dot_general | solution.py:166
  24.1 2.2 %reshape.53 = f32[4,1536,96]{2,1,0:T(8,128)} reshape(f32[4,96,1536]{2,1,0:T(8,128)S(1)} %fusion.10) | data formatting | bytes 4718592 | tf_op jit(solution)/shard_map/reshape | solution.py:167
  26.3 3.2 %fusion.109 = (f32[2,1536,96]{2,1,0:T(8,128)}, f32[2,1536,96]{2,1,0:T(8,128)S(1)}) fusion(f32[4,1536,96]{2,1,0:T(8,128)} %reshape.53), kind=kLoop, calls=%fused_computation.164 | loop fusion | bytes 4718592 | tf_op jit(solution)/shard_map/slice | solution.py:168
  29.6 1.9 %copy.29 = f32[2,1536,96]{1,2,0:T(8,128)S(1)} copy(f32[2,1536,96]{2,1,0:T(8,128)} %get-tuple-element.5) | data formatting | bytes 2359296
  31.4 1.5 %copy.28 = f32[2,1536,96]{1,2,0:T(8,128)} copy(f32[2,1536,96]{2,1,0:T(8,128)S(1)} %get-tuple-element.6) | data formatting | bytes 2359296
  32.9 1.6 %add_bitcast_fusion.1.y_ref = f32[2,96,1536]{2,1,0:T(8,128)S(1)} fusion(f32[2,1536,96]{1,2,0:T(8,128)} %copy.28, f32[2,1536,96]{1,2,0:T(8,128)S(1)} %copy.29), kind=kLoop, calls=%fused_computation.8 | loop fusion | flops 294912 | bytes 3538944 | tf_op jit(solution)/shard_map/transpose | solution.py:169
  34.5 6.9 %shard_map.103 = f32[2,96,1536]{2,1,0:T(8,128)S(1)} custom-call(f32[2,96,1536]{2,1,0:T(8,128)S(1)} %add_bitcast_fusion.1.y_ref), custom_call_target="tpu_custom_call" | custom-call | tf_op jit(solution)/shard_map/pallas_call | solution.py:46
  41.4 1.4 %multiply_reduce_fusion.3 = (f32[2]{0:T(128)S(1)}, f32[2,96,96]{2,1,0:T(8,128)S(1)}) fusion(f32[2,96,1536]{2,1,0:T(8,128)S(1)} %shard_map.103, f32[4,1536,96]{2,1,0:T(8,128)S(1)} %copy-done.3), kind=kOutput, calls=%fused_computation.63 | convolution fusion | flops 339775488 | bytes 2826248 | tf_op jit(solution)/shard_map/bir,brj->bij/dot_general | solution.py:172
  42.9 0.1 divide_convert_fusion.3
  43.1 1.7 %collective-permute-start.4 = (bf16[96,96]{1,0:T(8,128)(2,1)S(1)}, bf16[96,96]{1,0:T(8,128)(2,1)S(1)}, u32[]{:S(2)}, u32[]{:S(2)}) collective-permute-start(bf16[96,96]{1,0:T(8,128)(2,1)S(1)} %get-tuple-element.13), channel_id=1, source_target_pairs={{0,8},{1,9},{2,10},{3,11},{4,12},{5,13},{6,14},{7,15},{8,16},{9,17... | collective-permute-start | bytes 55304 | tf_op jit(solution)/shard_map/ppermute | solution.py:60
  44.8 4.4 %collective-permute-start.5 = (bf16[96,96]{1,0:T(8,128)(2,1)S(1)}, bf16[96,96]{1,0:T(8,128)(2,1)S(1)}, u32[]{:S(2)}, u32[]{:S(2)}) collective-permute-start(bf16[96,96]{1,0:T(8,128)(2,1)S(1)} %get-tuple-element.14), channel_id=1, source_target_pairs={{0,15},{1,8},{2,9},{3,10},{4,11},{5,12},{6,13},{7,14},{8,23},{9,16... | collective-permute-start | bytes 55304 | tf_op jit(solution)/shard_map/ppermute | solution.py:60
  49.2 0.2 copy.19
  49.4 0.1 pad.7
  49.5 0.1 copy.41
  49.6 5.5 %shard_map.105 = f32[16,96,128]{2,1,0:T(8,128)S(1)} custom-call(bf16[1536,96]{1,0:T(8,128)(2,1)S(1)} %reshape_squeeze.6.wd_ref, bf16[96,2048]{1,0:T(8,128)(2,1)S(1)} %bitcast.87, bf16[256,256]{1,0:T(8,128)(2,1)S(1)} %fusion.4.t_ref, bf16[96,1536]{1,0:T(8,128)(2,1)S(1)} %get-tuple-element.9.qt_ref), custom_call_target="tpu_custom_call" | custom-call | tf_op jit(solution)/shard_map/pallas_call | solution.py:104
  55.1 0.8 multiply_reduce_fusion.1
  56.6 0.1 fusion.7
  56.7 0.2 copy.24
  56.8 1.1 %convert_element_type.68 = bf16[96,1536]{1,0:T(8,128)(2,1)} reshape(bf16[96,16,96]{2,1,0:T(8,128)(2,1)S(1)} %copy.24) | data formatting | bytes 589824 | tf_op jit(solution)/shard_map/convert_element_type | solution.py:180
  58.0 1.9 %fusion.9 = f32[4,96,1536]{2,1,0:T(8,128)} fusion(bf16[1,96,1536]{2,1,0:T(8,128)(2,1)S(1)} %bitcast.98, bf16[1,96,1536]{2,1,0:T(8,128)(2,1)S(1)} %bitcast.103, bf16[1,96,1536]{2,1,0:T(8,128)(2,1)S(1)} %bitcast.105, bf16[1,96,1536]{2,1,0:T(8,128)(2,1)S(1)} %bitcast.101, bf16[1,96,96]{2,1,0:T(8,128)(2,1)S(1)} %bitcast.114, ...), kind=kOutput, calls=%fused_computation.30 | convolution fusion | flops 115126272 | bytes 3612672 | tf_op jit(solution)/shard_map/bwa,bak->bwk/dot_general | solution.py:166
  60.0 2.9 %reshape.54 = f32[4,1536,96]{2,1,0:T(8,128)S(1)} reshape(f32[4,96,1536]{2,1,0:T(8,128)} %fusion.9) | data formatting | bytes 4718592 | tf_op jit(solution)/shard_map/reshape | solution.py:167
  62.9 2.1 %fusion.108 = (f32[2,1536,96]{2,1,0:T(8,128)}, f32[2,1536,96]{2,1,0:T(8,128)}) fusion(f32[4,1536,96]{2,1,0:T(8,128)S(1)} %reshape.54), kind=kLoop, calls=%fused_computation.163 | loop fusion | bytes 4718592 | tf_op jit(solution)/shard_map/slice | solution.py:168
  64.9 0.5 copy-done.1
  65.4 2.0 %copy.32 = f32[2,1536,96]{1,2,0:T(8,128)S(1)} copy(f32[2,1536,96]{2,1,0:T(8,128)} %get-tuple-element.3) | data formatting | bytes 2359296
  67.4 1.5 %copy.31 = f32[2,1536,96]{1,2,0:T(8,128)} copy(f32[2,1536,96]{2,1,0:T(8,128)S(1)} %copy-done.4) | data formatting | bytes 2359296
  68.9 1.5 %add_bitcast_fusion.y_ref = f32[2,96,1536]{2,1,0:T(8,128)S(1)} fusion(f32[2,1536,96]{1,2,0:T(8,128)} %copy.31, f32[2,1536,96]{1,2,0:T(8,128)S(1)} %copy.32), kind=kLoop, calls=%fused_computation.7 | loop fusion | flops 294912 | bytes 3538944 | tf_op jit(solution)/shard_map/transpose | solution.py:169
  70.4 6.9 %shard_map.104 = f32[2,96,1536]{2,1,0:T(8,128)S(1)} custom-call(f32[2,96,1536]{2,1,0:T(8,128)S(1)} %add_bitcast_fusion.y_ref), custom_call_target="tpu_custom_call" | custom-call | tf_op jit(solution)/shard_map/pallas_call | solution.py:46
  77.4 1.5 %multiply_reduce_fusion.2 = (f32[2]{0:T(128)S(1)}, f32[2,96,96]{2,1,0:T(8,128)S(1)}) fusion(f32[2,96,1536]{2,1,0:T(8,128)S(1)} %shard_map.104, f32[4,1536,96]{2,1,0:T(8,128)S(1)} %copy-done.2), kind=kOutput, calls=%fused_computation.61 | convolution fusion | flops 339775488 | bytes 2826248 | tf_op jit(solution)/shard_map/bir,brj->bij/dot_general | solution.py:172
  78.9 0.2 copy.25
  79.1 0.1 pad.8
  79.2 0.1 copy.40
  79.3 1.3 %reshape.58.wd_ref = bf16[1536,96]{1,0:T(8,128)(2,1)S(1)} reshape(bf16[96,1536]{1,0:T(8,128)(2,1)} %collective-permute-done.9) | data formatting | bytes 589824 | tf_op jit(solution)/shard_map/reshape | solution.py:100
  80.6 5.5 %shard_map.106 = f32[16,96,128]{2,1,0:T(8,128)S(1)} custom-call(bf16[1536,96]{1,0:T(8,128)(2,1)S(1)} %reshape.58.wd_ref, bf16[96,2048]{1,0:T(8,128)(2,1)S(1)} %bitcast.86, bf16[256,256]{1,0:T(8,128)(2,1)S(1)} %fusion.4.t_ref, bf16[96,1536]{1,0:T(8,128)(2,1)S(1)} %get-tuple-element.7.qt_ref), custom_call_target="tpu_custom_call" | custom-call | tf_op jit(solution)/shard_map/pallas_call | solution.py:104
  86.1 0.8 multiply_reduce_fusion
  87.7 0.2 copy.26
  87.9 0.4 convert_element_type.73
  88.3 1.6 %collective-permute-start.10 = (bf16[96,1536]{1,0:T(8,128)(2,1)S(1)}, bf16[96,1536]{1,0:T(8,128)(2,1)S(1)}, u32[]{:S(2)}, u32[]{:S(2)}) collective-permute-start(bf16[96,1536]{1,0:T(8,128)(2,1)S(1)} %convert_element_type.73), channel_id=1, source_target_pairs={{0,8},{1,9},{2,10},{3,11},{4,12},{5,13},{6,14},{7,15},{8,16},{9,17... | collective-permute-start | bytes 884744 | tf_op jit(solution)/shard_map/ppermute | solution.py:60
  89.9 0.1 divide_convert_fusion.2
  90.0 0.1 collective-permute-start.11
  90.1 0.6 collective-permute-start.8
  90.7 4.0 %collective-permute-done.11 = bf16[96,96]{1,0:T(8,128)(2,1)S(1)} collective-permute-done((bf16[96,96]{1,0:T(8,128)(2,1)S(1)}, bf16[96,96]{1,0:T(8,128)(2,1)S(1)}, u32[]{:S(2)}, u32[]{:S(2)}) %collective-permute-start.11) | collective-permute-done | bytes 18464 | tf_op jit(solution)/shard_map/ppermute | solution.py:60
  94.7 0.3 collective-permute-done.8
  95.0 0.6 copy.45
  95.6 0.7 copy.46
  96.3 0.6 copy.47
  (59 shorter events, 0.5 us)
Async XLA Ops:
  0.6 11.0 %copy-start = (f32[2,2]{1,0:T(2,128)S(1)}, f32[2,2]{1,0:T(2,128)}, u32[]{:S(2)}) copy-start(f32[2,2]{1,0:T(2,128)} %param.14) | copy-start | bytes 52
  0.6 17.1 %collective-permute-start.1 = (bf16[96,96]{1,0:T(8,128)(2,1)}, bf16[96,96]{1,0:T(8,128)(2,1)S(1)}, u32[]{:S(2)}, u32[]{:S(2)}) collective-permute-start(bf16[96,96]{1,0:T(8,128)(2,1)} %bitcast.108), channel_id=1, source_target_pairs={{0,1},{1,2},{2,3},{3,4},{4,5},{5,6},{6,7},{7,0},{8,9},{9,10},{10,1... | collective-permute-start | bytes 55304 | tf_op jit(solution)/shard_map/ppermute | solution.py:60
  3.7 14.0 %collective-permute-start = (bf16[96,96]{1,0:T(8,128)(2,1)}, bf16[96,96]{1,0:T(8,128)(2,1)S(1)}, u32[]{:S(2)}, u32[]{:S(2)}) collective-permute-start(bf16[96,96]{1,0:T(8,128)(2,1)} %bitcast.106), channel_id=1, source_target_pairs={{0,7},{1,0},{2,1},{3,2},{4,3},{5,4},{6,5},{7,6},{8,15},{9,8},{10,9... | collective-permute-start | bytes 55304 | tf_op jit(solution)/shard_map/ppermute | solution.py:60
  6.8 13.2 %collective-permute-start.3 = (bf16[96,1536]{1,0:T(8,128)(2,1)}, bf16[96,1536]{1,0:T(8,128)(2,1)S(1)}, u32[]{:S(2)}, u32[]{:S(2)}) collective-permute-start(bf16[96,1536]{1,0:T(8,128)(2,1)} %bitcast.99), channel_id=1, source_target_pairs={{0,1},{1,2},{2,3},{3,4},{4,5},{5,6},{6,7},{7,0},{8,9},{9,10},{10,1... | collective-permute-start | bytes 884744 | tf_op jit(solution)/shard_map/ppermute | solution.py:60
  6.8 15.0 %collective-permute-start.2 = (bf16[96,1536]{1,0:T(8,128)(2,1)}, bf16[96,1536]{1,0:T(8,128)(2,1)S(1)}, u32[]{:S(2)}, u32[]{:S(2)}) collective-permute-start(bf16[96,1536]{1,0:T(8,128)(2,1)} %bitcast.96), channel_id=1, source_target_pairs={{0,7},{1,0},{2,1},{3,2},{4,3},{5,4},{6,5},{7,6},{8,15},{9,8},{10,9... | collective-permute-start | bytes 884744 | tf_op jit(solution)/shard_map/ppermute | solution.py:60
  16.0 1.3 %copy-start.5 = (bf16[1,1,96,1536]{3,2,1,0:T(8,128)(2,1)S(1)}, bf16[1,1,96,1536]{3,2,1,0:T(8,128)(2,1)}, u32[]{:S(2)}) copy-start(bf16[1,1,96,1536]{3,2,1,0:T(8,128)(2,1)} %param.10) | copy-start | bytes 884740
  16.5 6.0 %copy-start.6 = (bf16[1,1,96,1536]{3,2,1,0:T(8,128)(2,1)S(1)}, bf16[1,1,96,1536]{3,2,1,0:T(8,128)(2,1)}, u32[]{:S(2)}) copy-start(bf16[1,1,96,1536]{3,2,1,0:T(8,128)(2,1)} %param.9) | copy-start | bytes 884740
  16.5 6.0 %copy-start.8 = (bf16[1,1,96,1536]{3,2,1,0:T(8,128)(2,1)S(1)}, bf16[1,1,96,1536]{3,2,1,0:T(8,128)(2,1)}, u32[]{:S(2)}) copy-start(bf16[1,1,96,1536]{3,2,1,0:T(8,128)(2,1)} %param.12) | copy-start | bytes 884740
  16.5 6.0 %copy-start.14 = (bf16[1,1,96,96]{3,2,1,0:T(8,128)(2,1)S(1)}, bf16[1,1,96,96]{3,2,1,0:T(8,128)(2,1)}, u32[]{:S(2)}) copy-start(bf16[1,1,96,96]{3,2,1,0:T(8,128)(2,1)} %param.8) | copy-start | bytes 55300
  16.5 6.0 %copy-start.15 = (bf16[1,1,96,96]{3,2,1,0:T(8,128)(2,1)S(1)}, bf16[1,1,96,96]{3,2,1,0:T(8,128)(2,1)}, u32[]{:S(2)}) copy-start(bf16[1,1,96,96]{3,2,1,0:T(8,128)(2,1)} %param.11) | copy-start | bytes 55300
  17.7 4.1 %copy-start.16 = (bf16[96,96]{1,0:T(8,128)(2,1)}, bf16[96,96]{1,0:T(8,128)(2,1)S(1)}, u32[]{:S(2)}) copy-start(bf16[96,96]{1,0:T(8,128)(2,1)S(1)} %collective-permute-done) | copy-start | bytes 55300
  20.0 1.8 %copy-start.10 = (bf16[96,1536]{1,0:T(8,128)(2,1)}, bf16[96,1536]{1,0:T(8,128)(2,1)S(1)}, u32[]{:S(2)}) copy-start(bf16[96,1536]{1,0:T(8,128)(2,1)S(1)} %collective-permute-done.3) | copy-start | bytes 884740
  21.8 0.7 copy-start.12
  32.9 8.5 %copy-start.3 = (f32[4,1536,96]{2,1,0:T(8,128)S(1)}, f32[4,1536,96]{2,1,0:T(8,128)}, u32[]{:S(2)}) copy-start(f32[4,1536,96]{2,1,0:T(8,128)} %reshape.53) | copy-start | bytes 7077892
  43.0 14.9 %collective-permute-start.6 = (bf16[96,96]{1,0:T(8,128)(2,1)S(1)}, bf16[96,96]{1,0:T(8,128)(2,1)S(1)}, u32[]{:S(2)}, u32[]{:S(2)}) collective-permute-start(bf16[96,96]{1,0:T(8,128)(2,1)S(1)} %get-tuple-element.13), channel_id=1, source_target_pairs={{0,9},{1,10},{2,11},{3,12},{4,13},{5,14},{6,15},{7,8},{8,17},{9,18... | collective-permute-start | bytes 55304 | tf_op jit(solution)/shard_map/ppermute | solution.py:60
  43.1 14.9 %collective-permute-start.4 = (bf16[96,96]{1,0:T(8,128)(2,1)S(1)}, bf16[96,96]{1,0:T(8,128)(2,1)S(1)}, u32[]{:S(2)}, u32[]{:S(2)}) collective-permute-start(bf16[96,96]{1,0:T(8,128)(2,1)S(1)} %get-tuple-element.13), channel_id=1, source_target_pairs={{0,8},{1,9},{2,10},{3,11},{4,12},{5,13},{6,14},{7,15},{8,16},{9,17... | collective-permute-start | bytes 55304 | tf_op jit(solution)/shard_map/ppermute | solution.py:60
  44.8 13.2 %collective-permute-start.7 = (bf16[96,96]{1,0:T(8,128)(2,1)S(1)}, bf16[96,96]{1,0:T(8,128)(2,1)S(1)}, u32[]{:S(2)}, u32[]{:S(2)}) collective-permute-start(bf16[96,96]{1,0:T(8,128)(2,1)S(1)} %get-tuple-element.14), channel_id=1, source_target_pairs={{0,8},{1,9},{2,10},{3,11},{4,12},{5,13},{6,14},{7,15},{8,16},{9,17... | collective-permute-start | bytes 55304 | tf_op jit(solution)/shard_map/ppermute | solution.py:60
  44.8 13.2 %collective-permute-start.5 = (bf16[96,96]{1,0:T(8,128)(2,1)S(1)}, bf16[96,96]{1,0:T(8,128)(2,1)S(1)}, u32[]{:S(2)}, u32[]{:S(2)}) collective-permute-start(bf16[96,96]{1,0:T(8,128)(2,1)S(1)} %get-tuple-element.14), channel_id=1, source_target_pairs={{0,15},{1,8},{2,9},{3,10},{4,11},{5,12},{6,13},{7,14},{8,23},{9,16... | collective-permute-start | bytes 55304 | tf_op jit(solution)/shard_map/ppermute | solution.py:60
  56.6 1.4 %copy-start.7 = (bf16[1,1,96,1536]{3,2,1,0:T(8,128)(2,1)S(1)}, bf16[1,1,96,1536]{3,2,1,0:T(8,128)(2,1)}, u32[]{:S(2)}) copy-start(bf16[1,1,96,1536]{3,2,1,0:T(8,128)(2,1)} %param.9) | copy-start | bytes 884740
  56.6 1.4 %copy-start.9 = (bf16[1,1,96,1536]{3,2,1,0:T(8,128)(2,1)S(1)}, bf16[1,1,96,1536]{3,2,1,0:T(8,128)(2,1)}, u32[]{:S(2)}) copy-start(bf16[1,1,96,1536]{3,2,1,0:T(8,128)(2,1)} %param.12) | copy-start | bytes 884740
  56.6 1.4 %copy-start.11 = (bf16[96,1536]{1,0:T(8,128)(2,1)S(1)}, bf16[96,1536]{1,0:T(8,128)(2,1)}, u32[]{:S(2)}) copy-start(bf16[96,1536]{1,0:T(8,128)(2,1)} %copy-done.10) | copy-start | bytes 884740
  56.6 1.4 %copy-start.13 = (bf16[96,1536]{1,0:T(8,128)(2,1)S(1)}, bf16[96,1536]{1,0:T(8,128)(2,1)}, u32[]{:S(2)}) copy-start(bf16[96,1536]{1,0:T(8,128)(2,1)} %copy-done.12) | copy-start | bytes 884740
  58.0 21.4 %collective-permute-start.9 = (bf16[96,1536]{1,0:T(8,128)(2,1)}, bf16[96,1536]{1,0:T(8,128)(2,1)}, u32[]{:S(2)}, u32[]{:S(2)}) collective-permute-start(bf16[96,1536]{1,0:T(8,128)(2,1)} %convert_element_type.68), channel_id=1, source_target_pairs={{0,8},{1,9},{2,10},{3,11},{4,12},{5,13},{6,14},{7,15},{8,16},{9,17... | collective-permute-start | bytes 884744 | tf_op jit(solution)/shard_map/ppermute | solution.py:60
  62.8 2.6 %copy-start.1 = (f32[4,1536,96]{2,1,0:T(8,128)}, f32[4,1536,96]{2,1,0:T(8,128)S(1)}, u32[]{:S(2)}) copy-start(f32[4,1536,96]{2,1,0:T(8,128)S(1)} %reshape.54) | copy-start | bytes 7077892
  65.4 2.0 %copy-start.4 = (f32[2,1536,96]{2,1,0:T(8,128)S(1)}, f32[2,1536,96]{2,1,0:T(8,128)}, u32[]{:S(2)}) copy-start(f32[2,1536,96]{2,1,0:T(8,128)} %get-tuple-element.4) | copy-start | bytes 3538948
  70.4 7.0 %copy-start.2 = (f32[4,1536,96]{2,1,0:T(8,128)S(1)}, f32[4,1536,96]{2,1,0:T(8,128)}, u32[]{:S(2)}) copy-start(f32[4,1536,96]{2,1,0:T(8,128)} %copy-done.1) | copy-start | bytes 7077892
  88.3 6.7 %collective-permute-start.10 = (bf16[96,1536]{1,0:T(8,128)(2,1)S(1)}, bf16[96,1536]{1,0:T(8,128)(2,1)S(1)}, u32[]{:S(2)}, u32[]{:S(2)}) collective-permute-start(bf16[96,1536]{1,0:T(8,128)(2,1)S(1)} %convert_element_type.73), channel_id=1, source_target_pairs={{0,8},{1,9},{2,10},{3,11},{4,12},{5,13},{6,14},{7,15},{8,16},{9,17... | collective-permute-start | bytes 884744 | tf_op jit(solution)/shard_map/ppermute | solution.py:60
  90.0 4.7 %collective-permute-start.11 = (bf16[96,96]{1,0:T(8,128)(2,1)S(1)}, bf16[96,96]{1,0:T(8,128)(2,1)S(1)}, u32[]{:S(2)}, u32[]{:S(2)}) collective-permute-start(bf16[96,96]{1,0:T(8,128)(2,1)S(1)} %get-tuple-element.11), channel_id=1, source_target_pairs={{0,8},{1,9},{2,10},{3,11},{4,12},{5,13},{6,14},{7,15},{8,16},{9,17... | collective-permute-start | bytes 55304 | tf_op jit(solution)/shard_map/ppermute | solution.py:60
  90.1 4.9 %collective-permute-start.8 = (bf16[96,96]{1,0:T(8,128)(2,1)S(1)}, bf16[96,96]{1,0:T(8,128)(2,1)S(1)}, u32[]{:S(2)}, u32[]{:S(2)}) collective-permute-start(bf16[96,96]{1,0:T(8,128)(2,1)S(1)} %get-tuple-element.12), channel_id=1, source_target_pairs={{0,8},{1,9},{2,10},{3,11},{4,12},{5,13},{6,14},{7,15},{8,16},{9,17... | collective-permute-start | bytes 55304 | tf_op jit(solution)/shard_map/ppermute | solution.py:60

commit v4 on v1

--- a/solution.py
+++ b/solution.py
@@ -66,7 +66,7 @@
 
 def edge_kernel(wd_ref, pm_ref, t_ref, qt_ref, o_ref, f_ref, g_ref):
     n = qt_ref.shape[0]
-    dd = o_ref.shape[0]
+    dd = math.isqrt(t_ref.shape[0])
     group = 4
     wd = wd_ref[...]
     for d0 in range(0, dd, group):
@@ -88,10 +88,17 @@
 
     lax.fori_loop(0, n // per, mid_body, 0)
     qt = qt_ref[...]
+    parts = []
+    total = jnp.zeros((1, 1), jnp.float32)
     for r0 in range(0, dd, group):
         part = jnp.dot(qt, g_ref[:, r0 * LANES:(r0 + group) * LANES], preferred_element_type=jnp.float32)
+        parts.append(part)
+        total = total + jnp.sum(part * part, keepdims=True)
+    scale = lax.rsqrt(total / (n * dd * n) + 1e-06)
+    for r0, part in zip(range(0, dd, group), parts):
         for k in range(group):
-            o_ref[r0 + k] = part[:, k * LANES:(k + 1) * LANES]
+            r = r0 + k
+            o_ref[:, r * n:(r + 1) * n] = (part[:, k * LANES:k * LANES + n] * scale).astype(o_ref.dtype)
 
 
 def edge_contract(west, low_t, up_t, site):
@@ -103,14 +110,14 @@
     qt = up_t
     out = pl.pallas_call(
         edge_kernel,
-        out_shape=jax.ShapeDtypeStruct((dd, n, LANES), jnp.float32),
+        out_shape=jax.ShapeDtypeStruct((n, dd * n), jnp.bfloat16),
         scratch_shapes=[
             pltpu.VMEM((n, dd, dd, LANES), jnp.bfloat16),
             pltpu.VMEM((n * dd, dd * LANES), jnp.bfloat16),
         ],
         compiler_params=pltpu.CompilerParams(vmem_limit_bytes=48 * 1024 * 1024),
     )(wd, pm, site, qt)
-    return jnp.transpose(out[:, :, :n], (1, 0, 2)).reshape(n, dd * n)
+    return out
 
 
 def one_hot(rows, cols, row_key, col_key):
@@ -170,15 +177,14 @@
         projs = polar_factor_t(jnp.swapaxes(jnp.stack([lower + upper_nb, lower_nb + upper]), 1, 2))
         below_t = projs[0]
         above_t = projs[1]
-        new_up = jnp.dot(above_t, upper, precision=lax.Precision.HIGHEST)
-        new_low = jnp.dot(below_t, lower, precision=lax.Precision.HIGHEST)
+        new_up = jnp.dot(above_t, upper, precision=lax.Precision.HIGH)
+        new_low = jnp.dot(below_t, lower, precision=lax.Precision.HIGH)
         new_up = unit_scaled(new_up).astype(jnp.bfloat16)
         new_low = unit_scaled(new_low).astype(jnp.bfloat16)
         if step + 1 < STEPS:
             up_corner_nb = shifted(new_up, 1, -1)
             low_corner_nb = shifted(new_low, 1, 1)
         edge_new = edge_contract(west_edge, below_t.astype(jnp.bfloat16), above_t.astype(jnp.bfloat16), site)
-        edge_new = unit_scaled(edge_new).astype(jnp.bfloat16)
         corner_up, west_edge, corner_low = shifted((new_up, edge_new, new_low), 1, 0)
     return (corner_up[None, None], west_edge[None, None], corner_low[None, None])
 

time: 82.8 us -> 83.3 us (level)
  between operations: 5.36 us -> 3.91 us
  local copies, waits for them, and re-layouts: 15.4 us -> 16.4 us
    add x4, local copies, waits for them, and re-layouts: 1.01 us -> 2.91 us  [per_device(): lower_nb + upper]
    add x4, local copies, waits for them, and re-layouts: 2.93 us -> 4.82 us  [per_device(): lower + upper_nb]
    convert_element_type x4 -> x0, local copies, waits for them, and re-layouts: 1.84 us -> none  [per_device(): edge_new = unit_scaled(edge_new).astype(jnp.bfloat16)]
    dot_general x8, matrix products: 6.5 us -> 8.15 us  [half(): jnp.dot(corner, edge, preferred_element_type=jnp.float32)]
    reduce_sum x2 -> x0, other arithmetic: 1.62 us -> none  [unit_scaled(): return tensor / jnp.sqrt(jnp.mean(tensor * tensor) + 1e-06)]
    transpose x2, other arithmetic: 0.16 us -> 1.4 us  [per_device(): jnp.swapaxes(jnp.stack([lower + upper_nb, lower_nb + upper]), 1, 2)]
    dot_general x4, matrix products: 5.29 us -> 4.21 us  [the longest x2 2.1 us: per_device(): new_up = jnp.dot(above_t, upper, precision=lax.Precision.HIGH)]
    reshape x4, local copies, waits for them, and re-layouts: 2.82 us -> 1.93 us  [half(): jnp.dot(corner, edge, preferred_element_type=jnp.float32)]
  transfers between devices with their start and end apart: 12 -> 12, of which waited for: 1 -> 1; matrix products, arithmetic and copies ran while one was open for 32% -> 33% of each run, Pallas kernels for 22% -> 22%
where the time goes in v4:
time: 83.3 us; the launch traced here: 82.8 us
  Pallas kernels  25.4 us (30%)
  starting transfers between devices  16.9 us (20%)
  local copies, waits for them, and re-layouts  16.4 us (20%)
  matrix products  15.1 us (18%)
  between operations  3.91 us (5%)
  waiting for transfers between devices  3.03 us (4%)
  other arithmetic  2.11 us (3%)
    ppermute x12, starting transfers between devices, shifted(): return lax.ppermute(tree, ('gx', 'gy'), pairs)  16.9 us
    pallas_call x2, Pallas kernels, polar_factor_t(): pl.pallas_call(polar_kernel, out_shape=jax.ShapeDtypeStruct(stack.shape,...  13.7 us
    pallas_call x2, Pallas kernels, edge_contract(): pl.pallas_call(edge_kernel, out_shape=jax.ShapeDtypeStruct((n, dd * n), j...  11.7 us
    dot_general x8, matrix products, half(): jnp.dot(corner, edge, preferred_element_type=jnp.float32)  8.15 us
    add x4, local copies, waits for them, and re-layouts, per_device(): lower + upper_nb  4.82 us
    unnamed x25, local copies, waits for them, and re-layouts  3.43 us
    ppermute x12, waiting for transfers between devices, shifted(): return lax.ppermute(tree, ('gx', 'gy'), pairs)  3.03 us
    add x4, local copies, waits for them, and re-layouts, per_device(): lower_nb + upper  2.91 us
  transfers between devices with their start and end apart: 12, of which 1 were waited for; matrix products, arithmetic and copies ran while one was open for 33% of the time, Pallas kernels for 22%

profile of v4, /device:TPU:0, one launch (start us, length us, event | category | flops | bytes accessed | tf_op | source)
XLA Modules:
  0.0 82.8 jit_solution(11498210713182228503)
XLA Ops:
  0.7 6.1 %collective-permute-start.1 = (bf16[96,1536]{1,0:T(8,128)(2,1)}, bf16[96,1536]{1,0:T(8,128)(2,1)S(1)}, u32[]{:S(2)}, u32[]{:S(2)}) collective-permute-start(bf16[96,1536]{1,0:T(8,128)(2,1)} %bitcast.113), channel_id=1, source_target_pairs={{0,7},{1,0},{2,1},{3,2},{4,3},{5,4},{6,5},{7,6},{8,15},{9,8},{10,9... | collective-permute-start | bytes 884744 | tf_op jit(solution)/shard_map/ppermute | solution.py:60
  6.7 0.5 collective-permute-start
  7.2 1.5 %collective-permute-start.3 = (bf16[96,1536]{1,0:T(8,128)(2,1)}, bf16[96,1536]{1,0:T(8,128)(2,1)}, u32[]{:S(2)}, u32[]{:S(2)}) collective-permute-start(bf16[96,1536]{1,0:T(8,128)(2,1)} %bitcast.112), channel_id=1, source_target_pairs={{0,1},{1,2},{2,3},{3,4},{4,5},{5,6},{6,7},{7,0},{8,9},{9,10},{10,1... | collective-permute-start | bytes 884744 | tf_op jit(solution)/shard_map/ppermute | solution.py:60
  8.8 1.2 %fusion.89 = f32[96,1536]{1,0:T(8,128)S(1)} fusion(bf16[1,1,96,1536]{3,2,1,0:T(8,128)(2,1)} %param.12, bf16[1,1,96,96]{3,2,1,0:T(8,128)(2,1)} %param.11), kind=kOutput, calls=%fused_computation.143 | convolution fusion | flops 28311552 | bytes 903168 | tf_op jit(solution)/shard_map/dot_general | solution.py:171
  10.0 1.2 %fusion.84 = f32[96,1536]{1,0:T(8,128)S(1)} fusion(bf16[1,1,96,1536]{3,2,1,0:T(8,128)(2,1)} %param.9, bf16[1,1,96,96]{3,2,1,0:T(8,128)(2,1)} %param.8), kind=kOutput, calls=%fused_computation.138 | convolution fusion | flops 28311552 | bytes 903168 | tf_op jit(solution)/shard_map/dot_general | solution.py:171
  11.3 0.1 reshape_squeeze.7
  11.5 0.3 copy.18
  11.8 0.1 reshape.119
  11.9 0.4 convolution_bitcast_fusion
  12.3 0.4 fusion.52
  12.7 0.2 convolution_bitcast_fusion.1
  12.9 0.6 compare_reduce_fusion
  13.6 0.9 %fusion.2 = bf16[2,4,4,4,4]{3,0,1,2,4:T(2,128)(2,1)S(1)} fusion(f32[2,2,1,1,1]{1,0,4,3,2:T(2,128)S(1)} %convolution_bitcast_fusion.1, pred[]{:T(512)} %compare_reduce_fusion, bf16[2,4,4,4,4]{4,3,2,1,0:T(4,128)(2,1)S(1)} %reshape_squeeze.7), kind=kOutput, calls=%fused_computation.10 | convolution fusion | flops 13824 | bytes 2065 | tf_op jit(solution)/shard_map/st,tabcd->sabcd/dot_general | solution.py:154
  14.5 0.3 copy.21
  14.8 0.1 reshape.120
  14.9 0.4 fusion.20
  15.3 0.4 fusion.t_ref
  15.7 0.3 reshape.115
  16.0 1.2 %reshape.116 = f32[1536,96]{1,0:T(8,128)} reshape(f32[96,1536]{1,0:T(8,128)S(1)} %fusion.84) | data formatting | bytes 1179648 | tf_op jit(solution)/shard_map/reshape | solution.py:171
  17.2 0.3 reshape_squeeze.6.wd_ref
  17.5 0.7 copy-done.5
  18.2 1.1 %convolution_add_fusion.3 = f32[96,1536]{1,0:T(8,128)} fusion(f32[96,1536]{1,0:T(8,128)S(1)} %fusion.89, bf16[96,96]{1,0:T(8,128)(2,1)S(1)} %collective-permute-done, bf16[96,1536]{1,0:T(8,128)(2,1)S(1)} %collective-permute-done.1), kind=kOutput, calls=%fused_computation.3 | convolution fusion | flops 28459008 | bytes 1492992 | tf_op jit(solution)/shard_map/dot_general | solution.py:171
  19.3 1.3 %add.126 = f32[1,1536,96]{2,1,0:T(8,128)S(1)} reshape(f32[96,1536]{1,0:T(8,128)} %convolution_add_fusion.3) | data formatting | bytes 1179648 | tf_op jit(solution)/shard_map/add | solution.py:177
  20.6 1.1 %copy.13 = f32[1,1536,96]{1,2,0:T(8,128)} copy(f32[1,1536,96]{2,1,0:T(8,128)S(1)} %add.126) | data formatting | bytes 1179648 | tf_op jit(solution)/shard_map/add | solution.py:177
  21.7 1.2 %convolution_add_fusion.2 = f32[96,1536]{1,0:T(8,128)S(1)} fusion(f32[96,1536]{1,0:T(8,128)S(1)} %fusion.84, bf16[96,96]{1,0:T(8,128)(2,1)S(1)} %collective-permute-done.2, bf16[96,1536]{1,0:T(8,128)(2,1)} %collective-permute-done.3), kind=kOutput, calls=%fused_computation.2 | convolution fusion | flops 28459008 | bytes 1492992 | tf_op jit(solution)/shard_map/dot_general | solution.py:171
  22.9 0.3 add.128
  23.2 0.3 copy.14
  23.4 0.5 copy-done.2
  24.1 6.8 %shard_map.103 = f32[2,96,1536]{2,1,0:T(8,128)S(1)} custom-call(f32[2,96,1536]{2,1,0:T(8,128)S(1)} %maximum_bitcast_fusion.y_ref), custom_call_target="tpu_custom_call" | custom-call | tf_op jit(solution)/shard_map/pallas_call | solution.py:46
  30.9 1.1 %multiply_reduce_fusion.2 = (f32[]{:T(128)}, f32[96,96]{1,0:T(8,128)S(1)}) fusion(f32[1536,96]{1,0:T(8,128)S(1)} %copy-done.1, f32[2,96,1536]{2,1,0:T(8,128)S(1)} %shard_map.103), kind=kOutput, calls=%fused_computation.72 | convolution fusion | flops 84953088 | bytes 1413124 | tf_op jit(solution)/shard_map/dot_general | solution.py:180
  32.7 3.0 %collective-permute-start.5 = (bf16[96,96]{1,0:T(8,128)(2,1)S(1)}, bf16[96,96]{1,0:T(8,128)(2,1)S(1)}, u32[]{:S(2)}, u32[]{:S(2)}) collective-permute-start(bf16[96,96]{1,0:T(8,128)(2,1)S(1)} %divide_convert_fusion.2), channel_id=1, source_target_pairs={{0,15},{1,8},{2,9},{3,10},{4,11},{5,12},{6,13},{7,14},{8,23},{9,16... | collective-permute-start | bytes 55304 | tf_op jit(solution)/shard_map/ppermute | solution.py:60
  35.7 2.7 %collective-permute-start.7 = (bf16[96,96]{1,0:T(8,128)(2,1)S(1)}, bf16[96,96]{1,0:T(8,128)(2,1)S(1)}, u32[]{:S(2)}, u32[]{:S(2)}) collective-permute-start(bf16[96,96]{1,0:T(8,128)(2,1)S(1)} %divide_convert_fusion.2), channel_id=1, source_target_pairs={{0,8},{1,9},{2,10},{3,11},{4,12},{5,13},{6,14},{7,15},{8,16},{9,17... | collective-permute-start | bytes 55304 | tf_op jit(solution)/shard_map/ppermute | solution.py:60
  38.5 1.1 %multiply_reduce_fusion.3 = (f32[]{:T(128)}, f32[96,96]{1,0:T(8,128)S(1)}) fusion(f32[1536,96]{1,0:T(8,128)S(1)} %reshape.115, f32[2,96,1536]{2,1,0:T(8,128)S(1)} %shard_map.103), kind=kOutput, calls=%fused_computation.74 | convolution fusion | flops 84953088 | bytes 1413124 | tf_op jit(solution)/shard_map/dot_general | solution.py:181
  40.3 0.2 collective-permute-start.6
  40.6 0.2 copy.17
  40.9 0.1 copy.31
  41.1 5.8 %shard_map.105 = bf16[96,1536]{1,0:T(8,128)(2,1)S(1)} custom-call(bf16[1536,96]{1,0:T(8,128)(2,1)S(1)} %reshape_squeeze.6.wd_ref, bf16[96,2048]{1,0:T(8,128)(2,1)S(1)} %bitcast.107, bf16[256,256]{1,0:T(8,128)(2,1)S(1)} %fusion.t_ref, bf16[96,1536]{1,0:T(8,128)(2,1)S(1)} %get-tuple-element.5.qt_ref), custom_call_target="tpu_custom_call" | custom-call | tf_op jit(solution)/shard_map/pallas_call | solution.py:111
  46.9 0.5 collective-permute-start.9
  47.4 0.2 fusion.87
  47.6 1.1 %convolution_add_fusion.1 = f32[96,1536]{1,0:T(8,128)} fusion(f32[96,1536]{1,0:T(8,128)S(1)} %fusion.87, bf16[96,96]{1,0:T(8,128)(2,1)S(1)} %collective-permute-done.5, bf16[96,1536]{1,0:T(8,128)(2,1)S(1)} %copy-done.6), kind=kOutput, calls=%fused_computation.1 | convolution fusion | flops 28459008 | bytes 1492992 | tf_op jit(solution)/shard_map/dot_general | solution.py:171
  48.7 0.2 fusion.82
  48.9 0.3 reshape.123
  49.2 1.3 %add.132 = f32[1,1536,96]{2,1,0:T(8,128)S(1)} reshape(f32[96,1536]{1,0:T(8,128)} %convolution_add_fusion.1) | data formatting | bytes 1179648 | tf_op jit(solution)/shard_map/add | solution.py:177
  50.5 1.1 %copy.15 = f32[1,1536,96]{1,2,0:T(8,128)} copy(f32[1,1536,96]{2,1,0:T(8,128)S(1)} %add.132) | data formatting | bytes 1179648 | tf_op jit(solution)/shard_map/add | solution.py:177
  51.6 0.3 reshape.117
  51.8 2.0 %convolution_add_fusion = f32[96,1536]{1,0:T(8,128)} fusion(f32[96,1536]{1,0:T(8,128)S(1)} %fusion.82, bf16[96,96]{1,0:T(8,128)(2,1)S(1)} %collective-permute-done.6, bf16[96,1536]{1,0:T(8,128)(2,1)} %collective-permute-done.3), kind=kOutput, calls=%fused_computation | convolution fusion | flops 28459008 | bytes 1492992 | tf_op jit(solution)/shard_map/dot_general | solution.py:171
  53.9 1.3 %add.134 = f32[1,1536,96]{2,1,0:T(8,128)S(1)} reshape(f32[96,1536]{1,0:T(8,128)} %convolution_add_fusion) | data formatting | bytes 1179648 | tf_op jit(solution)/shard_map/add | solution.py:177
  55.2 1.1 %copy.16 = f32[1,1536,96]{1,2,0:T(8,128)} copy(f32[1,1536,96]{2,1,0:T(8,128)S(1)} %add.134) | data formatting | bytes 1179648 | tf_op jit(solution)/shard_map/add | solution.py:177
  56.3 1.3 %maximum_bitcast_fusion.1.y_ref = f32[2,96,1536]{2,1,0:T(8,128)S(1)} fusion(f32[1,1536,96]{1,2,0:T(8,128)} %copy.16, f32[1,1536,96]{1,2,0:T(8,128)} %copy.15), kind=kLoop, calls=%fused_computation.7 | loop fusion | flops 294912 | bytes 2359296 | tf_op jit(solution)/shard_map/transpose | solution.py:177
  57.6 6.9 %shard_map.104 = f32[2,96,1536]{2,1,0:T(8,128)S(1)} custom-call(f32[2,96,1536]{2,1,0:T(8,128)S(1)} %maximum_bitcast_fusion.1.y_ref), custom_call_target="tpu_custom_call" | custom-call | tf_op jit(solution)/shard_map/pallas_call | solution.py:46
  64.5 1.1 %multiply_reduce_fusion = (f32[]{:T(128)}, f32[96,96]{1,0:T(8,128)S(1)}) fusion(f32[1536,96]{1,0:T(8,128)S(1)} %reshape.123, f32[2,96,1536]{2,1,0:T(8,128)S(1)} %shard_map.104), kind=kOutput, calls=%fused_computation.68 | convolution fusion | flops 84953088 | bytes 1413124 | tf_op jit(solution)/shard_map/dot_general | solution.py:181
  66.2 0.5 collective-permute-start.11
  66.8 0.2 copy.22
  67.0 0.1 pad.8
  67.1 0.1 copy.30
  67.2 1.3 %reshape.121.wd_ref = bf16[1536,96]{1,0:T(8,128)(2,1)S(1)} reshape(bf16[96,1536]{1,0:T(8,128)(2,1)} %collective-permute-done.9) | data formatting | bytes 589824 | tf_op jit(solution)/shard_map/reshape | solution.py:107
  68.5 5.9 %shard_map.106 = bf16[96,1536]{1,0:T(8,128)(2,1)S(1)} custom-call(bf16[1536,96]{1,0:T(8,128)(2,1)S(1)} %reshape.121.wd_ref, bf16[96,2048]{1,0:T(8,128)(2,1)S(1)} %bitcast.106, bf16[256,256]{1,0:T(8,128)(2,1)S(1)} %fusion.t_ref, bf16[96,1536]{1,0:T(8,128)(2,1)S(1)} %get-tuple-element.3.qt_ref), custom_call_target="tpu_custom_call" | custom-call | tf_op jit(solution)/shard_map/pallas_call | solution.py:111
  74.4 1.4 %collective-permute-start.10 = (bf16[96,1536]{1,0:T(8,128)(2,1)S(1)}, bf16[96,1536]{1,0:T(8,128)(2,1)S(1)}, u32[]{:S(2)}, u32[]{:S(2)}) collective-permute-start(bf16[96,1536]{1,0:T(8,128)(2,1)S(1)} %shard_map.106), channel_id=1, source_target_pairs={{0,8},{1,9},{2,10},{3,11},{4,12},{5,13},{6,14},{7,15},{8,16},{9,17... | collective-permute-start | bytes 884744 | tf_op jit(solution)/shard_map/ppermute | solution.py:60
  75.8 1.1 %multiply_reduce_fusion.1 = (f32[]{:T(128)}, f32[96,96]{1,0:T(8,128)S(1)}) fusion(f32[1536,96]{1,0:T(8,128)S(1)} %reshape.117, f32[2,96,1536]{2,1,0:T(8,128)S(1)} %shard_map.104), kind=kOutput, calls=%fused_computation.70 | convolution fusion | flops 84953088 | bytes 1413124 | tf_op jit(solution)/shard_map/dot_general | solution.py:180
  77.6 0.3 collective-permute-start.8
  77.9 3.0 %collective-permute-done.8 = bf16[96,96]{1,0:T(8,128)(2,1)S(1)} collective-permute-done((bf16[96,96]{1,0:T(8,128)(2,1)S(1)}, bf16[96,96]{1,0:T(8,128)(2,1)S(1)}, u32[]{:S(2)}, u32[]{:S(2)}) %collective-permute-start.8) | collective-permute-done | bytes 18464 | tf_op jit(solution)/shard_map/ppermute | solution.py:60
  80.9 0.6 copy.35
  81.5 0.7 copy.36
  82.2 0.6 copy.37
  (45 shorter events, 0.5 us)
Async XLA Ops:
  0.6 12.1 %copy-start = (f32[2,2]{1,0:T(2,128)S(1)}, f32[2,2]{1,0:T(2,128)}, u32[]{:S(2)}) copy-start(f32[2,2]{1,0:T(2,128)} %param.14) | copy-start | bytes 52
  0.6 10.7 %copy-start.8 = (bf16[1,1,2,256]{3,2,1,0:T(2,128)(2,1)S(1)}, bf16[1,1,2,256]{3,2,1,0:T(2,128)(2,1)}, u32[]{:S(2)}) copy-start(bf16[1,1,2,256]{3,2,1,0:T(2,128)(2,1)} %param.13) | copy-start | bytes 3076
  0.7 16.9 %collective-permute-start.1 = (bf16[96,1536]{1,0:T(8,128)(2,1)}, bf16[96,1536]{1,0:T(8,128)(2,1)S(1)}, u32[]{:S(2)}, u32[]{:S(2)}) collective-permute-start(bf16[96,1536]{1,0:T(8,128)(2,1)} %bitcast.113), channel_id=1, source_target_pairs={{0,7},{1,0},{2,1},{3,2},{4,3},{5,4},{6,5},{7,6},{8,15},{9,8},{10,9... | collective-permute-start | bytes 884744 | tf_op jit(solution)/shard_map/ppermute | solution.py:60
  6.7 10.8 %collective-permute-start = (bf16[96,96]{1,0:T(8,128)(2,1)}, bf16[96,96]{1,0:T(8,128)(2,1)S(1)}, u32[]{:S(2)}, u32[]{:S(2)}) collective-permute-start(bf16[96,96]{1,0:T(8,128)(2,1)} %bitcast.118), channel_id=1, source_target_pairs={{0,7},{1,0},{2,1},{3,2},{4,3},{5,4},{6,5},{7,6},{8,15},{9,8},{10,9... | collective-permute-start | bytes 55304 | tf_op jit(solution)/shard_map/ppermute | solution.py:60
  7.2 14.5 %collective-permute-start.3 = (bf16[96,1536]{1,0:T(8,128)(2,1)}, bf16[96,1536]{1,0:T(8,128)(2,1)}, u32[]{:S(2)}, u32[]{:S(2)}) collective-permute-start(bf16[96,1536]{1,0:T(8,128)(2,1)} %bitcast.112), channel_id=1, source_target_pairs={{0,1},{1,2},{2,3},{3,4},{4,5},{5,6},{6,7},{7,0},{8,9},{9,10},{10,1... | collective-permute-start | bytes 884744 | tf_op jit(solution)/shard_map/ppermute | solution.py:60
  8.8 12.9 %collective-permute-start.2 = (bf16[96,96]{1,0:T(8,128)(2,1)}, bf16[96,96]{1,0:T(8,128)(2,1)S(1)}, u32[]{:S(2)}, u32[]{:S(2)}) collective-permute-start(bf16[96,96]{1,0:T(8,128)(2,1)} %bitcast.119), channel_id=1, source_target_pairs={{0,1},{1,2},{2,3},{3,4},{4,5},{5,6},{6,7},{7,0},{8,9},{9,10},{10,1... | collective-permute-start | bytes 55304 | tf_op jit(solution)/shard_map/ppermute | solution.py:60
  10.0 2.9 %copy-start.9 = (s32[4]{0:T(128)S(1)}, s32[4]{0:T(128)}, u32[]{:S(2)}) copy-start(s32[4]{0:T(128)} %param.15) | copy-start | bytes 52
  15.7 1.4 %copy-start.7 = (bf16[1,1,96,1536]{3,2,1,0:T(8,128)(2,1)S(1)}, bf16[1,1,96,1536]{3,2,1,0:T(8,128)(2,1)}, u32[]{:S(2)}) copy-start(bf16[1,1,96,1536]{3,2,1,0:T(8,128)(2,1)} %param.10) | copy-start | bytes 884740
  17.5 0.7 copy-start.5
  22.9 1.1 %copy-start.2 = (f32[1,1536,96]{1,2,0:T(8,128)S(1)}, f32[1,1536,96]{1,2,0:T(8,128)}, u32[]{:S(2)}) copy-start(f32[1,1536,96]{1,2,0:T(8,128)} %copy.13) | copy-start | bytes 1769476
  24.1 6.9 %copy-start.1 = (f32[1536,96]{1,0:T(8,128)S(1)}, f32[1536,96]{1,0:T(8,128)}, u32[]{:S(2)}) copy-start(f32[1536,96]{1,0:T(8,128)} %reshape.116) | copy-start | bytes 1769476
  32.7 14.9 %collective-permute-start.5 = (bf16[96,96]{1,0:T(8,128)(2,1)S(1)}, bf16[96,96]{1,0:T(8,128)(2,1)S(1)}, u32[]{:S(2)}, u32[]{:S(2)}) collective-permute-start(bf16[96,96]{1,0:T(8,128)(2,1)S(1)} %divide_convert_fusion.2), channel_id=1, source_target_pairs={{0,15},{1,8},{2,9},{3,10},{4,11},{5,12},{6,13},{7,14},{8,23},{9,16... | collective-permute-start | bytes 55304 | tf_op jit(solution)/shard_map/ppermute | solution.py:60
  35.7 12.9 %collective-permute-start.7 = (bf16[96,96]{1,0:T(8,128)(2,1)S(1)}, bf16[96,96]{1,0:T(8,128)(2,1)S(1)}, u32[]{:S(2)}, u32[]{:S(2)}) collective-permute-start(bf16[96,96]{1,0:T(8,128)(2,1)S(1)} %divide_convert_fusion.2), channel_id=1, source_target_pairs={{0,8},{1,9},{2,10},{3,11},{4,12},{5,13},{6,14},{7,15},{8,16},{9,17... | collective-permute-start | bytes 55304 | tf_op jit(solution)/shard_map/ppermute | solution.py:60
  40.2 7.2 %collective-permute-start.4 = (bf16[96,96]{1,0:T(8,128)(2,1)S(1)}, bf16[96,96]{1,0:T(8,128)(2,1)S(1)}, u32[]{:S(2)}, u32[]{:S(2)}) collective-permute-start(bf16[96,96]{1,0:T(8,128)(2,1)S(1)} %divide_convert_fusion.3), channel_id=1, source_target_pairs={{0,8},{1,9},{2,10},{3,11},{4,12},{5,13},{6,14},{7,15},{8,16},{9,17... | collective-permute-start | bytes 55304 | tf_op jit(solution)/shard_map/ppermute | solution.py:60
  40.3 11.6 %collective-permute-start.6 = (bf16[96,96]{1,0:T(8,128)(2,1)S(1)}, bf16[96,96]{1,0:T(8,128)(2,1)S(1)}, u32[]{:S(2)}, u32[]{:S(2)}) collective-permute-start(bf16[96,96]{1,0:T(8,128)(2,1)S(1)} %divide_convert_fusion.3), channel_id=1, source_target_pairs={{0,9},{1,10},{2,11},{3,12},{4,13},{5,14},{6,15},{7,8},{8,17},{9,18... | collective-permute-start | bytes 55304 | tf_op jit(solution)/shard_map/ppermute | solution.py:60
  40.9 6.5 %copy-start.3 = (bf16[1,1,96,1536]{3,2,1,0:T(8,128)(2,1)S(1)}, bf16[1,1,96,1536]{3,2,1,0:T(8,128)(2,1)}, u32[]{:S(2)}) copy-start(bf16[1,1,96,1536]{3,2,1,0:T(8,128)(2,1)} %param.12) | copy-start | bytes 884740
  41.0 6.6 %copy-start.6 = (bf16[96,1536]{1,0:T(8,128)(2,1)S(1)}, bf16[96,1536]{1,0:T(8,128)(2,1)}, u32[]{:S(2)}) copy-start(bf16[96,1536]{1,0:T(8,128)(2,1)} %copy-done.5) | copy-start | bytes 884740
  46.9 1.8 %copy-start.4 = (bf16[1,1,96,1536]{3,2,1,0:T(8,128)(2,1)S(1)}, bf16[1,1,96,1536]{3,2,1,0:T(8,128)(2,1)}, u32[]{:S(2)}) copy-start(bf16[1,1,96,1536]{3,2,1,0:T(8,128)(2,1)} %param.9) | copy-start | bytes 884740
  46.9 20.3 %collective-permute-start.9 = (bf16[96,1536]{1,0:T(8,128)(2,1)S(1)}, bf16[96,1536]{1,0:T(8,128)(2,1)}, u32[]{:S(2)}, u32[]{:S(2)}) collective-permute-start(bf16[96,1536]{1,0:T(8,128)(2,1)S(1)} %shard_map.105), channel_id=1, source_target_pairs={{0,8},{1,9},{2,10},{3,11},{4,12},{5,13},{6,14},{7,15},{8,16},{9,17... | collective-permute-start | bytes 884744 | tf_op jit(solution)/shard_map/ppermute | solution.py:60
  66.2 11.6 %collective-permute-start.11 = (bf16[96,96]{1,0:T(8,128)(2,1)S(1)}, bf16[96,96]{1,0:T(8,128)(2,1)S(1)}, u32[]{:S(2)}, u32[]{:S(2)}) collective-permute-start(bf16[96,96]{1,0:T(8,128)(2,1)S(1)} %divide_convert_fusion), channel_id=1, source_target_pairs={{0,8},{1,9},{2,10},{3,11},{4,12},{5,13},{6,14},{7,15},{8,16},{9,17... | collective-permute-start | bytes 55304 | tf_op jit(solution)/shard_map/ppermute | solution.py:60
  74.4 6.5 %collective-permute-start.10 = (bf16[96,1536]{1,0:T(8,128)(2,1)S(1)}, bf16[96,1536]{1,0:T(8,128)(2,1)S(1)}, u32[]{:S(2)}, u32[]{:S(2)}) collective-permute-start(bf16[96,1536]{1,0:T(8,128)(2,1)S(1)} %shard_map.106), channel_id=1, source_target_pairs={{0,8},{1,9},{2,10},{3,11},{4,12},{5,13},{6,14},{7,15},{8,16},{9,17... | collective-permute-start | bytes 884744 | tf_op jit(solution)/shard_map/ppermute | solution.py:60
  77.6 3.3 %collective-permute-start.8 = (bf16[96,96]{1,0:T(8,128)(2,1)S(1)}, bf16[96,96]{1,0:T(8,128)(2,1)S(1)}, u32[]{:S(2)}, u32[]{:S(2)}) collective-permute-start(bf16[96,96]{1,0:T(8,128)(2,1)S(1)} %divide_convert_fusion.1), channel_id=1, source_target_pairs={{0,8},{1,9},{2,10},{3,11},{4,12},{5,13},{6,14},{7,15},{8,16},{9,17... | collective-permute-start | bytes 55304 | tf_op jit(solution)/shard_map/ppermute | solution.py:60

commit v5 on v4

--- a/solution.py
+++ b/solution.py
@@ -166,14 +166,24 @@
     up_corner_nb, north_nb = shifted((corner_up, north_edge), 0, -1)
     low_corner_nb, south_nb = shifted((corner_low, south_edge), 0, 1)
     n = env_width
+    offsets = [0] * (STEPS - 1) + [1]
+    here = (north_edge, south_edge, north_nb, south_nb, site)
+    left_north, left_south, left_site = shifted((north_edge, south_edge, site), 1, 0)
+    left = (left_north, left_south, shifted(north_edge, 1, -1), shifted(south_edge, 1, 1), left_site)
+    if offsets[0]:
+        corner_up, west_edge, corner_low = shifted((corner_up, west_edge, corner_low), 1, 0)
+        up_corner_nb = shifted(c_upper[0, 0], 1, -1)
+        low_corner_nb = shifted(c_lower[0, 0], 1, 1)
     for step in range(STEPS):
+        north_e, south_e, north_n, south_n, site_now = left if offsets[step] else here
+
         def half(corner, edge):
             return jnp.dot(corner, edge, preferred_element_type=jnp.float32).reshape(n * double_bond, n)
 
-        upper = half(corner_up, north_edge)
-        lower = half(corner_low, south_edge)
-        upper_nb = half(up_corner_nb, north_nb)
-        lower_nb = half(low_corner_nb, south_nb)
+        upper = half(corner_up, north_e)
+        lower = half(corner_low, south_e)
+        upper_nb = half(up_corner_nb, north_n)
+        lower_nb = half(low_corner_nb, south_n)
         projs = polar_factor_t(jnp.swapaxes(jnp.stack([lower + upper_nb, lower_nb + upper]), 1, 2))
         below_t = projs[0]
         above_t = projs[1]
@@ -182,10 +192,14 @@
         new_up = unit_scaled(new_up).astype(jnp.bfloat16)
         new_low = unit_scaled(new_low).astype(jnp.bfloat16)
         if step + 1 < STEPS:
-            up_corner_nb = shifted(new_up, 1, -1)
-            low_corner_nb = shifted(new_low, 1, 1)
-        edge_new = edge_contract(west_edge, below_t.astype(jnp.bfloat16), above_t.astype(jnp.bfloat16), site)
-        corner_up, west_edge, corner_low = shifted((new_up, edge_new, new_low), 1, 0)
+            dx = 1 + offsets[step + 1] - offsets[step]
+            up_corner_nb = shifted(new_up, dx, -1)
+            low_corner_nb = shifted(new_low, dx, 1)
+        edge_new = edge_contract(west_edge, below_t.astype(jnp.bfloat16), above_t.astype(jnp.bfloat16), site_now)
+        if step + 1 < STEPS:
+            corner_up, west_edge, corner_low = shifted((new_up, edge_new, new_low), dx, 0)
+        else:
+            corner_up, west_edge, corner_low = new_up, edge_new, new_low
     return (corner_up[None, None], west_edge[None, None], corner_low[None, None])
 
 

time: 83.3 us -> 106 us (1.27)
  waiting for transfers between devices: 3.03 us -> 13.8 us
  local copies, waits for them, and re-layouts: 16.4 us -> 20.4 us
  matrix products: 15.1 us -> 18.9 us
  starting transfers between devices: 16.9 us -> 19.3 us
    ppermute x12 -> x14, waiting for transfers between devices: 3.03 us -> 13.8 us  [shifted(): return lax.ppermute(tree, ('gx', 'gy'), pairs)]
    dot_general x8, matrix products: 8.15 us -> 12 us  [half(): jnp.dot(corner, edge, preferred_element_type=jnp.float32)]
    add x4, local copies, waits for them, and re-layouts: 2.91 us -> 6.18 us  [per_device(): lower_nb + upper]
    ppermute x12 -> x14, starting transfers between devices: 16.9 us -> 19.3 us  [shifted(): return lax.ppermute(tree, ('gx', 'gy'), pairs)]
    unnamed x25 -> x18, local copies, waits for them, and re-layouts: 3.43 us -> 2.01 us
    add x4, local copies, waits for them, and re-layouts: 4.82 us -> 6.04 us  [per_device(): lower + upper_nb]
  transfers between devices with their start and end apart: 12 -> 14, of which waited for: 1 -> 2; matrix products, arithmetic and copies ran while one was open for 33% -> 38% of each run, Pallas kernels for 22% -> 19%
where the time goes in v5:
time: 106 us; the launch traced here: 105 us
  Pallas kernels  26.1 us (25%)
  local copies, waits for them, and re-layouts  20.4 us (19%)
  starting transfers between devices  19.3 us (18%)
  matrix products  18.9 us (18%)
  waiting for transfers between devices  13.8 us (13%)
  between operations  3.81 us (4%)
  other arithmetic  2.54 us (2%)
    ppermute x14, starting transfers between devices, shifted(): return lax.ppermute(tree, ('gx', 'gy'), pairs)  19.3 us
    ppermute x14, waiting for transfers between devices, shifted(): return lax.ppermute(tree, ('gx', 'gy'), pairs)  13.8 us
    pallas_call x2, Pallas kernels, polar_factor_t(): pl.pallas_call(polar_kernel, out_shape=jax.ShapeDtypeStruct(stack.shape,...  13.7 us
    pallas_call x2, Pallas kernels, edge_contract(): pl.pallas_call(edge_kernel, out_shape=jax.ShapeDtypeStruct((n, dd * n), j...  12.4 us
    dot_general x8, matrix products, half(): jnp.dot(corner, edge, preferred_element_type=jnp.float32)  12 us
    add x4, local copies, waits for them, and re-layouts, per_device(): lower_nb + upper  6.18 us
    add x4, local copies, waits for them, and re-layouts, per_device(): lower + upper_nb  6.04 us
    reshape x4, local copies, waits for them, and re-layouts, half(): jnp.dot(corner, edge, preferred_element_type=jnp.float32)  2.83 us
  transfers between devices with their start and end apart: 14, of which 2 were waited for; matrix products, arithmetic and copies ran while one was open for 38% of the time, Pallas kernels for 19%

profile of v5, /device:TPU:0, one launch (start us, length us, event | category | flops | bytes accessed | tf_op | source)
XLA Modules:
  0.0 104.8 jit_solution(3728293636744254682)
XLA Ops:
  0.7 6.1 %collective-permute-start.1 = (bf16[96,1536]{1,0:T(8,128)(2,1)}, bf16[96,1536]{1,0:T(8,128)(2,1)}, u32[]{:S(2)}, u32[]{:S(2)}) collective-permute-start(bf16[96,1536]{1,0:T(8,128)(2,1)} %bitcast.5), channel_id=1, source_target_pairs={{0,7},{1,0},{2,1},{3,2},{4,3},{5,4},{6,5},{7,6},{8,15},{9,8},{10,9... | collective-permute-start | bytes 884744 | tf_op jit(solution)/shard_map/ppermute | solution.py:60
  6.7 0.8 collective-permute-start.9
  7.6 0.6 collective-permute-start.2
  8.2 1.2 %fusion.87 = f32[96,1536]{1,0:T(8,128)S(1)} fusion(bf16[1,1,96,1536]{3,2,1,0:T(8,128)(2,1)} %param.12, bf16[1,1,96,96]{3,2,1,0:T(8,128)(2,1)} %param.11), kind=kOutput, calls=%fused_computation.141 | convolution fusion | flops 28311552 | bytes 903168 | tf_op jit(solution)/shard_map/dot_general | solution.py:181
  9.5 1.2 %fusion.84 = f32[96,1536]{1,0:T(8,128)S(1)} fusion(bf16[1,1,96,1536]{3,2,1,0:T(8,128)(2,1)} %param.9, bf16[1,1,96,96]{3,2,1,0:T(8,128)(2,1)} %param.8), kind=kOutput, calls=%fused_computation.138 | convolution fusion | flops 28311552 | bytes 903168 | tf_op jit(solution)/shard_map/dot_general | solution.py:181
  10.7 0.1 reshape_squeeze.7
  10.8 0.3 copy.18
  11.1 0.1 reshape.119
  11.2 0.4 convolution_bitcast_fusion
  11.6 0.4 fusion.54
  12.1 0.2 convolution_bitcast_fusion.1
  12.3 0.6 compare_reduce_fusion
  12.9 0.9 fusion.2
  13.8 0.3 copy.21
  14.1 0.1 reshape.120
  14.2 0.4 fusion.20
  14.6 0.4 fusion.t_ref
  15.1 1.2 %reshape.116 = f32[1536,96]{1,0:T(8,128)} reshape(f32[96,1536]{1,0:T(8,128)S(1)} %fusion.84) | data formatting | bytes 1179648 | tf_op jit(solution)/shard_map/reshape | solution.py:181
  16.3 0.3 reshape.115
  16.5 0.3 reshape_squeeze.6.wd_ref
  16.8 9.1 %collective-permute-done.2 = bf16[96,96]{1,0:T(8,128)(2,1)S(1)} collective-permute-done((bf16[96,96]{1,0:T(8,128)(2,1)}, bf16[96,96]{1,0:T(8,128)(2,1)S(1)}, u32[]{:S(2)}, u32[]{:S(2)}) %collective-permute-start.2) | collective-permute-done | bytes 18464 | tf_op jit(solution)/shard_map/ppermute | solution.py:60
  25.9 0.4 collective-permute-start.5
  26.4 0.7 copy-done.4
  27.1 4.2 %collective-permute-start = (bf16[96,96]{1,0:T(8,128)(2,1)S(1)}, bf16[96,96]{1,0:T(8,128)(2,1)S(1)}, u32[]{:S(2)}, u32[]{:S(2)}) collective-permute-start(bf16[96,96]{1,0:T(8,128)(2,1)S(1)} %bitcast.115), channel_id=1, source_target_pairs={{0,7},{1,0},{2,1},{3,2},{4,3},{5,4},{6,5},{7,6},{8,15},{9,8},{10,9... | collective-permute-start | bytes 55304 | tf_op jit(solution)/shard_map/ppermute | solution.py:60
  31.2 1.2 %convolution_add_fusion.2 = f32[96,1536]{1,0:T(8,128)S(1)} fusion(f32[96,1536]{1,0:T(8,128)S(1)} %fusion.84, bf16[96,96]{1,0:T(8,128)(2,1)S(1)} %collective-permute-done.2, bf16[96,1536]{1,0:T(8,128)(2,1)} %copy-done.4), kind=kOutput, calls=%fused_computation.2 | convolution fusion | flops 28459008 | bytes 1492992 | tf_op jit(solution)/shard_map/dot_general | solution.py:181
  32.4 1.2 %add.128 = f32[1,1536,96]{2,1,0:T(8,128)} reshape(f32[96,1536]{1,0:T(8,128)S(1)} %convolution_add_fusion.2) | data formatting | bytes 1179648 | tf_op jit(solution)/shard_map/add | solution.py:187
  33.6 1.4 %copy.14 = f32[1,1536,96]{1,2,0:T(8,128)S(1)} copy(f32[1,1536,96]{2,1,0:T(8,128)} %add.128) | data formatting | bytes 1179648 | tf_op jit(solution)/shard_map/add | solution.py:187
  35.0 2.5 %collective-permute-start.7 = (bf16[96,1536]{1,0:T(8,128)(2,1)}, bf16[96,1536]{1,0:T(8,128)(2,1)}, u32[]{:S(2)}, u32[]{:S(2)}) collective-permute-start(bf16[96,1536]{1,0:T(8,128)(2,1)} %bitcast.5), channel_id=1, source_target_pairs={{0,15},{1,8},{2,9},{3,10},{4,11},{5,12},{6,13},{7,14},{8,23},{9,16... | collective-permute-start | bytes 884744 | tf_op jit(solution)/shard_map/ppermute | solution.py:60
  37.5 2.0 %convolution_add_fusion.3 = f32[96,1536]{1,0:T(8,128)} fusion(f32[96,1536]{1,0:T(8,128)S(1)} %fusion.87, bf16[96,96]{1,0:T(8,128)(2,1)S(1)} %collective-permute-done, bf16[96,1536]{1,0:T(8,128)(2,1)} %collective-permute-done.1), kind=kOutput, calls=%fused_computation.3 | convolution fusion | flops 28459008 | bytes 1492992 | tf_op jit(solution)/shard_map/dot_general | solution.py:181
  39.5 1.3 %add.126 = f32[1,1536,96]{2,1,0:T(8,128)S(1)} reshape(f32[96,1536]{1,0:T(8,128)} %convolution_add_fusion.3) | data formatting | bytes 1179648 | tf_op jit(solution)/shard_map/add | solution.py:187
  40.8 1.1 %copy.13 = f32[1,1536,96]{1,2,0:T(8,128)} copy(f32[1,1536,96]{2,1,0:T(8,128)S(1)} %add.126) | data formatting | bytes 1179648 | tf_op jit(solution)/shard_map/add | solution.py:187
  41.9 1.1 %maximum_bitcast_fusion.y_ref = f32[2,96,1536]{2,1,0:T(8,128)S(1)} fusion(f32[1,1536,96]{1,2,0:T(8,128)S(1)} %copy.14, f32[1,1536,96]{1,2,0:T(8,128)} %copy.13), kind=kLoop, calls=%fused_computation.6 | loop fusion | flops 294912 | bytes 2359296 | tf_op jit(solution)/shard_map/transpose | solution.py:187
  43.1 6.8 %shard_map.103 = f32[2,96,1536]{2,1,0:T(8,128)S(1)} custom-call(f32[2,96,1536]{2,1,0:T(8,128)S(1)} %maximum_bitcast_fusion.y_ref), custom_call_target="tpu_custom_call" | custom-call | tf_op jit(solution)/shard_map/pallas_call | solution.py:46
  50.0 1.1 %copy-done.1 = f32[1536,96]{1,0:T(8,128)S(1)} copy-done((f32[1536,96]{1,0:T(8,128)S(1)}, f32[1536,96]{1,0:T(8,128)}, u32[]{:S(2)}) %copy-start.1) | copy-done | bytes 589848
  51.0 1.0 multiply_reduce_fusion.2
  52.8 1.5 %collective-permute-start.10 = (bf16[96,96]{1,0:T(8,128)(2,1)S(1)}, bf16[96,96]{1,0:T(8,128)(2,1)S(1)}, u32[]{:S(2)}, u32[]{:S(2)}) collective-permute-start(bf16[96,96]{1,0:T(8,128)(2,1)S(1)} %divide_convert_fusion.2), channel_id=1, source_target_pairs={{0,16},{1,17},{2,18},{3,19},{4,20},{5,21},{6,22},{7,23},{8,24},{9,... | collective-permute-start | bytes 55304 | tf_op jit(solution)/shard_map/ppermute | solution.py:60
  54.3 1.0 multiply_reduce_fusion.3
  56.0 0.2 copy.17
  56.4 0.1 copy.31
  56.5 5.8 %shard_map.105 = bf16[96,1536]{1,0:T(8,128)(2,1)S(1)} custom-call(bf16[1536,96]{1,0:T(8,128)(2,1)S(1)} %reshape_squeeze.6.wd_ref, bf16[96,2048]{1,0:T(8,128)(2,1)S(1)} %bitcast.107, bf16[256,256]{1,0:T(8,128)(2,1)S(1)} %fusion.t_ref, bf16[96,1536]{1,0:T(8,128)(2,1)S(1)} %get-tuple-element.5.qt_ref), custom_call_target="tpu_custom_call" | custom-call | tf_op jit(solution)/shard_map/pallas_call | solution.py:111
  62.3 0.2 collective-permute-start.13
  62.5 0.3 collective-permute-start.8
  62.9 1.2 %fusion.103 = f32[96,1536]{1,0:T(8,128)S(1)} fusion(bf16[96,96]{1,0:T(8,128)(2,1)S(1)} %collective-permute-done.10, bf16[96,1536]{1,0:T(8,128)(2,1)} %collective-permute-done.11), kind=kOutput, calls=%fused_computation.157 | convolution fusion | flops 28311552 | bytes 903168 | tf_op jit(solution)/shard_map/dot_general | solution.py:181
  64.1 1.2 %collective-permute-start.4 = (bf16[96,96]{1,0:T(8,128)(2,1)S(1)}, bf16[96,96]{1,0:T(8,128)(2,1)S(1)}, u32[]{:S(2)}, u32[]{:S(2)}) collective-permute-start(bf16[96,96]{1,0:T(8,128)(2,1)S(1)} %divide_convert_fusion.3), channel_id=1, source_target_pairs={{0,16},{1,17},{2,18},{3,19},{4,20},{5,21},{6,22},{7,23},{8,24},{9,... | collective-permute-start | bytes 55304 | tf_op jit(solution)/shard_map/ppermute | solution.py:60
  65.2 4.7 %collective-permute-done.8 = bf16[96,96]{1,0:T(8,128)(2,1)S(1)} collective-permute-done((bf16[96,96]{1,0:T(8,128)(2,1)S(1)}, bf16[96,96]{1,0:T(8,128)(2,1)S(1)}, u32[]{:S(2)}, u32[]{:S(2)}) %collective-permute-start.8) | collective-permute-done | bytes 18464 | tf_op jit(solution)/shard_map/ppermute | solution.py:60
  70.0 0.9 collective-permute-start.6
  70.9 2.0 %convolution_add_fusion = f32[96,1536]{1,0:T(8,128)} fusion(f32[96,1536]{1,0:T(8,128)S(1)} %fusion.103, bf16[96,96]{1,0:T(8,128)(2,1)S(1)} %collective-permute-done.8, bf16[96,1536]{1,0:T(8,128)(2,1)} %collective-permute-done.9), kind=kOutput, calls=%fused_computation | convolution fusion | flops 28459008 | bytes 1492992 | tf_op jit(solution)/shard_map/dot_general | solution.py:181
  72.9 0.6 collective-permute-start.12
  73.5 1.2 %fusion.102 = f32[96,1536]{1,0:T(8,128)S(1)} fusion(bf16[96,96]{1,0:T(8,128)(2,1)S(1)} %collective-permute-done.4, bf16[96,1536]{1,0:T(8,128)(2,1)} %collective-permute-done.5), kind=kOutput, calls=%fused_computation.156 | convolution fusion | flops 28311552 | bytes 903168 | tf_op jit(solution)/shard_map/dot_general | solution.py:181
  74.7 0.3 reshape.117
  74.9 2.2 %add.134 = f32[1,1536,96]{2,1,0:T(8,128)} reshape(f32[96,1536]{1,0:T(8,128)} %convolution_add_fusion) | data formatting | bytes 1179648 | tf_op jit(solution)/shard_map/add | solution.py:187
  77.1 1.4 %copy.16 = f32[1,1536,96]{1,2,0:T(8,128)S(1)} copy(f32[1,1536,96]{2,1,0:T(8,128)} %add.134) | data formatting | bytes 1179648 | tf_op jit(solution)/shard_map/add | solution.py:187
  78.5 1.2 %reshape.123 = f32[1536,96]{1,0:T(8,128)} reshape(f32[96,1536]{1,0:T(8,128)S(1)} %fusion.102) | data formatting | bytes 1179648 | tf_op jit(solution)/shard_map/reshape | solution.py:181
  79.7 2.0 %convolution_add_fusion.1 = f32[96,1536]{1,0:T(8,128)} fusion(f32[96,1536]{1,0:T(8,128)S(1)} %fusion.102, bf16[96,96]{1,0:T(8,128)(2,1)S(1)} %collective-permute-done.6, bf16[96,1536]{1,0:T(8,128)(2,1)} %collective-permute-done.7), kind=kOutput, calls=%fused_computation.1 | convolution fusion | flops 28459008 | bytes 1492992 | tf_op jit(solution)/shard_map/dot_general | solution.py:181
  81.7 2.2 %add.132 = f32[1,1536,96]{2,1,0:T(8,128)} reshape(f32[96,1536]{1,0:T(8,128)} %convolution_add_fusion.1) | data formatting | bytes 1179648 | tf_op jit(solution)/shard_map/add | solution.py:187
  84.0 1.4 %copy.15 = f32[1,1536,96]{1,2,0:T(8,128)S(1)} copy(f32[1,1536,96]{2,1,0:T(8,128)} %add.132) | data formatting | bytes 1179648 | tf_op jit(solution)/shard_map/add | solution.py:187
  85.5 6.8 %shard_map.104 = f32[2,96,1536]{2,1,0:T(8,128)S(1)} custom-call(f32[2,96,1536]{2,1,0:T(8,128)S(1)} %maximum_bitcast_fusion.1.y_ref), custom_call_target="tpu_custom_call" | custom-call | tf_op jit(solution)/shard_map/pallas_call | solution.py:46
  92.4 1.1 %multiply_reduce_fusion.1 = (f32[]{:T(128)}, f32[96,96]{1,0:T(8,128)S(1)}) fusion(f32[1536,96]{1,0:T(8,128)S(1)} %reshape.117, f32[2,96,1536]{2,1,0:T(8,128)S(1)} %shard_map.104), kind=kOutput, calls=%fused_computation.70 | convolution fusion | flops 84953088 | bytes 1413124 | tf_op jit(solution)/shard_map/dot_general | solution.py:190
  93.4 1.0 multiply_reduce_fusion
  95.9 0.2 copy.22
  96.2 0.1 copy.30
  96.3 0.6 fusion.44
  96.9 1.3 %reshape.121.wd_ref = bf16[1536,96]{1,0:T(8,128)(2,1)S(1)} reshape(bf16[96,1536]{1,0:T(8,128)(2,1)} %collective-permute-done.12) | data formatting | bytes 589824 | tf_op jit(solution)/shard_map/reshape | solution.py:107
  98.2 6.6 %shard_map.106 = bf16[96,1536]{1,0:T(8,128)(2,1)} custom-call(bf16[1536,96]{1,0:T(8,128)(2,1)S(1)} %reshape.121.wd_ref, bf16[96,2048]{1,0:T(8,128)(2,1)S(1)} %bitcast.106, bf16[256,256]{1,0:T(8,128)(2,1)S(1)} %collective-permute-done.13.t_ref, bf16[96,1536]{1,0:T(8,128)(2,1)S(1)} %get-tuple-element.3.qt_ref), custom_call_target="tpu_custom_call" | custom-call | tf_op jit(solution)/shard_map/pallas_call | solution.py:111
  (41 shorter events, 0.5 us)
Async XLA Ops:
  0.6 11.4 %copy-start = (f32[2,2]{1,0:T(2,128)S(1)}, f32[2,2]{1,0:T(2,128)}, u32[]{:S(2)}) copy-start(f32[2,2]{1,0:T(2,128)} %param.14) | copy-start | bytes 52
  0.6 10.0 %copy-start.6 = (bf16[1,1,2,256]{3,2,1,0:T(2,128)(2,1)S(1)}, bf16[1,1,2,256]{3,2,1,0:T(2,128)(2,1)}, u32[]{:S(2)}) copy-start(bf16[1,1,2,256]{3,2,1,0:T(2,128)(2,1)} %param.13) | copy-start | bytes 3076
  0.7 36.8 %collective-permute-start.1 = (bf16[96,1536]{1,0:T(8,128)(2,1)}, bf16[96,1536]{1,0:T(8,128)(2,1)}, u32[]{:S(2)}, u32[]{:S(2)}) collective-permute-start(bf16[96,1536]{1,0:T(8,128)(2,1)} %bitcast.5), channel_id=1, source_target_pairs={{0,7},{1,0},{2,1},{3,2},{4,3},{5,4},{6,5},{7,6},{8,15},{9,8},{10,9... | collective-permute-start | bytes 884744 | tf_op jit(solution)/shard_map/ppermute | solution.py:60
  6.7 55.6 %collective-permute-start.11 = (bf16[96,1536]{1,0:T(8,128)(2,1)}, bf16[96,1536]{1,0:T(8,128)(2,1)}, u32[]{:S(2)}, u32[]{:S(2)}) collective-permute-start(bf16[96,1536]{1,0:T(8,128)(2,1)} %bitcast.5), channel_id=1, source_target_pairs={{0,8},{1,9},{2,10},{3,11},{4,12},{5,13},{6,14},{7,15},{8,16},{9,17... | collective-permute-start | bytes 884744 | tf_op jit(solution)/shard_map/ppermute | solution.py:60
  6.7 19.6 %collective-permute-start.3 = (bf16[96,1536]{1,0:T(8,128)(2,1)}, bf16[96,1536]{1,0:T(8,128)(2,1)S(1)}, u32[]{:S(2)}, u32[]{:S(2)}) collective-permute-start(bf16[96,1536]{1,0:T(8,128)(2,1)} %bitcast.3), channel_id=1, source_target_pairs={{0,1},{1,2},{2,3},{3,4},{4,5},{5,6},{6,7},{7,0},{8,9},{9,10},{10,1... | collective-permute-start | bytes 884744 | tf_op jit(solution)/shard_map/ppermute | solution.py:60
  6.7 57.3 %collective-permute-start.9 = (bf16[96,1536]{1,0:T(8,128)(2,1)}, bf16[96,1536]{1,0:T(8,128)(2,1)}, u32[]{:S(2)}, u32[]{:S(2)}) collective-permute-start(bf16[96,1536]{1,0:T(8,128)(2,1)} %bitcast.3), channel_id=1, source_target_pairs={{0,9},{1,10},{2,11},{3,12},{4,13},{5,14},{6,15},{7,8},{8,17},{9,18... | collective-permute-start | bytes 884744 | tf_op jit(solution)/shard_map/ppermute | solution.py:60
  7.6 18.4 %collective-permute-start.2 = (bf16[96,96]{1,0:T(8,128)(2,1)}, bf16[96,96]{1,0:T(8,128)(2,1)S(1)}, u32[]{:S(2)}, u32[]{:S(2)}) collective-permute-start(bf16[96,96]{1,0:T(8,128)(2,1)} %bitcast.114), channel_id=1, source_target_pairs={{0,1},{1,2},{2,3},{3,4},{4,5},{5,6},{6,7},{7,0},{8,9},{9,10},{10,1... | collective-permute-start | bytes 55304 | tf_op jit(solution)/shard_map/ppermute | solution.py:60
  9.5 2.8 %copy-start.7 = (s32[4]{0:T(128)S(1)}, s32[4]{0:T(128)}, u32[]{:S(2)}) copy-start(s32[4]{0:T(128)} %param.15) | copy-start | bytes 52
  15.1 1.4 %copy-start.3 = (bf16[1,1,96,1536]{3,2,1,0:T(8,128)(2,1)S(1)}, bf16[1,1,96,1536]{3,2,1,0:T(8,128)(2,1)}, u32[]{:S(2)}) copy-start(bf16[1,1,96,1536]{3,2,1,0:T(8,128)(2,1)} %param.10) | copy-start | bytes 884740
  16.2 10.8 %copy-start.5 = (bf16[1,1,96,96]{3,2,1,0:T(8,128)(2,1)S(1)}, bf16[1,1,96,96]{3,2,1,0:T(8,128)(2,1)}, u32[]{:S(2)}) copy-start(bf16[1,1,96,96]{3,2,1,0:T(8,128)(2,1)} %param.8) | copy-start | bytes 55300
  25.9 46.9 %collective-permute-start.5 = (bf16[96,1536]{1,0:T(8,128)(2,1)}, bf16[96,1536]{1,0:T(8,128)(2,1)}, u32[]{:S(2)}, u32[]{:S(2)}) collective-permute-start(bf16[96,1536]{1,0:T(8,128)(2,1)} %bitcast.3), channel_id=1, source_target_pairs={{0,8},{1,9},{2,10},{3,11},{4,12},{5,13},{6,14},{7,15},{8,16},{9,17... | collective-permute-start | bytes 884744 | tf_op jit(solution)/shard_map/ppermute | solution.py:60
  26.4 0.7 copy-start.4
  27.1 7.9 %collective-permute-start = (bf16[96,96]{1,0:T(8,128)(2,1)S(1)}, bf16[96,96]{1,0:T(8,128)(2,1)S(1)}, u32[]{:S(2)}, u32[]{:S(2)}) collective-permute-start(bf16[96,96]{1,0:T(8,128)(2,1)S(1)} %bitcast.115), channel_id=1, source_target_pairs={{0,7},{1,0},{2,1},{3,2},{4,3},{5,4},{6,5},{7,6},{8,15},{9,8},{10,9... | collective-permute-start | bytes 55304 | tf_op jit(solution)/shard_map/ppermute | solution.py:60
  35.0 44.7 %collective-permute-start.7 = (bf16[96,1536]{1,0:T(8,128)(2,1)}, bf16[96,1536]{1,0:T(8,128)(2,1)}, u32[]{:S(2)}, u32[]{:S(2)}) collective-permute-start(bf16[96,1536]{1,0:T(8,128)(2,1)} %bitcast.5), channel_id=1, source_target_pairs={{0,15},{1,8},{2,9},{3,10},{4,11},{5,12},{6,13},{7,14},{8,23},{9,16... | collective-permute-start | bytes 884744 | tf_op jit(solution)/shard_map/ppermute | solution.py:60
  49.9 1.1 %copy-start.1 = (f32[1536,96]{1,0:T(8,128)S(1)}, f32[1536,96]{1,0:T(8,128)}, u32[]{:S(2)}) copy-start(f32[1536,96]{1,0:T(8,128)} %reshape.116) | copy-start | bytes 1769476
  52.8 9.7 %collective-permute-start.10 = (bf16[96,96]{1,0:T(8,128)(2,1)S(1)}, bf16[96,96]{1,0:T(8,128)(2,1)S(1)}, u32[]{:S(2)}, u32[]{:S(2)}) collective-permute-start(bf16[96,96]{1,0:T(8,128)(2,1)S(1)} %divide_convert_fusion.2), channel_id=1, source_target_pairs={{0,16},{1,17},{2,18},{3,19},{4,20},{5,21},{6,22},{7,23},{8,24},{9,... | collective-permute-start | bytes 55304 | tf_op jit(solution)/shard_map/ppermute | solution.py:60
  62.3 35.9 %collective-permute-start.13 = (bf16[256,256]{1,0:T(8,128)(2,1)S(1)}, bf16[256,256]{1,0:T(8,128)(2,1)S(1)}, u32[]{:S(2)}, u32[]{:S(2)}) collective-permute-start(bf16[256,256]{1,0:T(8,128)(2,1)S(1)} %fusion.t_ref), channel_id=1, source_target_pairs={{0,8},{1,9},{2,10},{3,11},{4,12},{5,13},{6,14},{7,15},{8,16},{9,17... | collective-permute-start | bytes 393224 | tf_op jit(solution)/shard_map/ppermute | solution.py:60
  62.5 7.4 %collective-permute-start.8 = (bf16[96,96]{1,0:T(8,128)(2,1)S(1)}, bf16[96,96]{1,0:T(8,128)(2,1)S(1)}, u32[]{:S(2)}, u32[]{:S(2)}) collective-permute-start(bf16[96,96]{1,0:T(8,128)(2,1)S(1)} %divide_convert_fusion.3), channel_id=1, source_target_pairs={{0,17},{1,18},{2,19},{3,20},{4,21},{5,22},{6,23},{7,16},{8,25},{9,... | collective-permute-start | bytes 55304 | tf_op jit(solution)/shard_map/ppermute | solution.py:60
  64.1 9.4 %collective-permute-start.4 = (bf16[96,96]{1,0:T(8,128)(2,1)S(1)}, bf16[96,96]{1,0:T(8,128)(2,1)S(1)}, u32[]{:S(2)}, u32[]{:S(2)}) collective-permute-start(bf16[96,96]{1,0:T(8,128)(2,1)S(1)} %divide_convert_fusion.3), channel_id=1, source_target_pairs={{0,16},{1,17},{2,18},{3,19},{4,20},{5,21},{6,22},{7,23},{8,24},{9,... | collective-permute-start | bytes 55304 | tf_op jit(solution)/shard_map/ppermute | solution.py:60
  70.0 9.7 %collective-permute-start.6 = (bf16[96,96]{1,0:T(8,128)(2,1)S(1)}, bf16[96,96]{1,0:T(8,128)(2,1)S(1)}, u32[]{:S(2)}, u32[]{:S(2)}) collective-permute-start(bf16[96,96]{1,0:T(8,128)(2,1)S(1)} %divide_convert_fusion.2), channel_id=1, source_target_pairs={{0,23},{1,16},{2,17},{3,18},{4,19},{5,20},{6,21},{7,22},{8,31},{9,... | collective-permute-start | bytes 55304 | tf_op jit(solution)/shard_map/ppermute | solution.py:60
  72.9 24.1 %collective-permute-start.12 = (bf16[96,1536]{1,0:T(8,128)(2,1)S(1)}, bf16[96,1536]{1,0:T(8,128)(2,1)}, u32[]{:S(2)}, u32[]{:S(2)}) collective-permute-start(bf16[96,1536]{1,0:T(8,128)(2,1)S(1)} %shard_map.105), channel_id=1, source_target_pairs={{0,16},{1,17},{2,18},{3,19},{4,20},{5,21},{6,22},{7,23},{8,24},{9,... | collective-permute-start | bytes 884744 | tf_op jit(solution)/shard_map/ppermute | solution.py:60
  92.3 1.1 %copy-start.2 = (f32[1536,96]{1,0:T(8,128)S(1)}, f32[1536,96]{1,0:T(8,128)}, u32[]{:S(2)}) copy-start(f32[1536,96]{1,0:T(8,128)} %reshape.123) | copy-start | bytes 1769476

commit v6 on v1

--- a/solution.py
+++ b/solution.py
@@ -27,6 +27,13 @@
     bh, bl = split_bf16(b)
     out = lambda p, q: lax.dot_general(p, q, (dims, ((), ())), preferred_element_type=jnp.float32)
     return out(ah, bh) + (out(ah, bl) + out(al, bh))
+
+
+def gram3(y):
+    yh, yl = split_bf16(y)
+    out = lambda p, q: lax.dot_general(p, q, (((1,), (1,)), ((), ())), preferred_element_type=jnp.float32)
+    cross = out(yh, yl)
+    return out(yh, yh) + (cross + cross.T)
 
 
 def polar_kernel(y_ref, o_ref):
@@ -36,7 +43,7 @@
         y = y_ref[b]
         ys.append(y / jnp.sqrt(jnp.sum(y * y) + 1e-06))
     for sweep in range(NS_ITERS):
-        grams = [dot3(y, y, ((1,), (1,))) for y in ys]
+        grams = [gram3(y) for y in ys]
         ys = [1.5 * y - 0.5 * dot3(g, y, ((1,), (0,))) for g, y in zip(grams, ys)]
     for b in range(count):
         o_ref[b] = ys[b]
@@ -75,7 +82,7 @@
         for k in range(group):
             f_ref[:, d0 + k] = part[:, k * LANES:(k + 1) * LANES].reshape(n, dd, LANES)
     t = t_ref[...]
-    per = math.gcd(n, 24)
+    per = math.gcd(n, 48)
 
     def mid_body(h, carry):
         x = jnp.concatenate([f_ref[h * per + k].reshape(dd * dd, LANES) for k in range(per)], axis=1)

time: 82.8 us -> 78.9 us (0.953)
  Pallas kernels: 24.6 us -> 20.7 us
    pallas_call x2, Pallas kernels: 13.7 us -> 10.5 us  [polar_factor_t(): pl.pallas_call(polar_kernel, out_shape=jax.ShapeDtypeStruct(stack.shape,...]
  transfers between devices with their start and end apart: 12 -> 12, of which waited for: 1 -> 1; matrix products, arithmetic and copies ran while one was open for 32% -> 33% of each run, Pallas kernels for 22% -> 20%
where the time goes in v6:
time: 78.9 us; the launch traced here: 78.4 us
  Pallas kernels  20.7 us (26%)
  starting transfers between devices  16.9 us (21%)
  local copies, waits for them, and re-layouts  15.4 us (20%)
  matrix products  14.6 us (19%)
  between operations  5.36 us (7%)
  waiting for transfers between devices  2.81 us (4%)
  other arithmetic  2.63 us (3%)
    ppermute x12, starting transfers between devices, shifted(): return lax.ppermute(tree, ('gx', 'gy'), pairs)  16.9 us
    pallas_call x2, Pallas kernels, polar_factor_t(): pl.pallas_call(polar_kernel, out_shape=jax.ShapeDtypeStruct(stack.shape,...  10.5 us
    pallas_call x2, Pallas kernels, edge_contract(): pl.pallas_call(edge_kernel, out_shape=jax.ShapeDtypeStruct((dd, n, LANES)...  10.2 us
    dot_general x8, matrix products, half(): jnp.dot(corner, edge, preferred_element_type=jnp.float32)  6.5 us
    unnamed x27, local copies, waits for them, and re-layouts  3.52 us
    add x4, local copies, waits for them, and re-layouts, per_device(): lower + upper_nb  2.93 us
    reshape x4, local copies, waits for them, and re-layouts, half(): jnp.dot(corner, edge, preferred_element_type=jnp.float32)  2.82 us
    ppermute x12, waiting for transfers between devices, shifted(): return lax.ppermute(tree, ('gx', 'gy'), pairs)  2.81 us
  transfers between devices with their start and end apart: 12, of which 1 were waited for; matrix products, arithmetic and copies ran while one was open for 33% of the time, Pallas kernels for 20%

profile of v6, /device:TPU:0, one launch (start us, length us, event | category | flops | bytes accessed | tf_op | source)
XLA Modules:
  0.0 78.4 jit_solution(8193615779655813628)
XLA Ops:
  0.7 6.1 %collective-permute-start.1 = (bf16[96,1536]{1,0:T(8,128)(2,1)}, bf16[96,1536]{1,0:T(8,128)(2,1)S(1)}, u32[]{:S(2)}, u32[]{:S(2)}) collective-permute-start(bf16[96,1536]{1,0:T(8,128)(2,1)} %bitcast.117), channel_id=1, source_target_pairs={{0,7},{1,0},{2,1},{3,2},{4,3},{5,4},{6,5},{7,6},{8,15},{9,8},{10,9... | collective-permute-start | bytes 884744 | tf_op jit(solution)/shard_map/ppermute | solution.py:67
  6.7 0.5 collective-permute-start
  7.2 1.5 %collective-permute-start.3 = (bf16[96,1536]{1,0:T(8,128)(2,1)}, bf16[96,1536]{1,0:T(8,128)(2,1)}, u32[]{:S(2)}, u32[]{:S(2)}) collective-permute-start(bf16[96,1536]{1,0:T(8,128)(2,1)} %bitcast.116), channel_id=1, source_target_pairs={{0,1},{1,2},{2,3},{3,4},{4,5},{5,6},{6,7},{7,0},{8,9},{9,10},{10,1... | collective-permute-start | bytes 884744 | tf_op jit(solution)/shard_map/ppermute | solution.py:67
  8.8 1.2 %fusion.91 = f32[96,1536]{1,0:T(8,128)S(1)} fusion(bf16[1,1,96,1536]{3,2,1,0:T(8,128)(2,1)} %param.12, bf16[1,1,96,96]{3,2,1,0:T(8,128)(2,1)} %param.11), kind=kOutput, calls=%fused_computation.149 | convolution fusion | flops 28311552 | bytes 903168 | tf_op jit(solution)/shard_map/dot_general | solution.py:171
  10.0 1.2 %fusion.86 = f32[96,1536]{1,0:T(8,128)S(1)} fusion(bf16[1,1,96,1536]{3,2,1,0:T(8,128)(2,1)} %param.9, bf16[1,1,96,96]{3,2,1,0:T(8,128)(2,1)} %param.8), kind=kOutput, calls=%fused_computation.144 | convolution fusion | flops 28311552 | bytes 903168 | tf_op jit(solution)/shard_map/dot_general | solution.py:171
  11.3 0.1 reshape_squeeze.7
  11.5 0.3 copy.18
  11.9 0.4 convolution_bitcast_fusion
  12.3 0.4 fusion.54
  12.7 0.2 convolution_bitcast_fusion.1
  12.9 0.6 compare_reduce_fusion
  13.6 0.9 %fusion.2 = bf16[2,4,4,4,4]{3,0,1,2,4:T(2,128)(2,1)S(1)} fusion(f32[2,2,1,1,1]{1,0,4,3,2:T(2,128)S(1)} %convolution_bitcast_fusion.1, pred[]{:T(512)} %compare_reduce_fusion, bf16[2,4,4,4,4]{4,3,2,1,0:T(4,128)(2,1)S(1)} %reshape_squeeze.7), kind=kOutput, calls=%fused_computation.10 | convolution fusion | flops 13824 | bytes 2065 | tf_op jit(solution)/shard_map/st,tabcd->sabcd/dot_general | solution.py:154
  14.5 0.3 copy.21
  14.9 0.4 fusion.22
  15.3 0.4 fusion.t_ref
  15.7 0.3 reshape.123
  16.0 1.2 %reshape.124 = f32[1536,96]{1,0:T(8,128)} reshape(f32[96,1536]{1,0:T(8,128)S(1)} %fusion.86) | data formatting | bytes 1179648 | tf_op jit(solution)/shard_map/reshape | solution.py:171
  17.2 0.3 reshape_squeeze.6.wd_ref
  17.5 0.7 copy-done.6
  18.2 1.1 %convolution_add_fusion.3 = f32[96,1536]{1,0:T(8,128)} fusion(f32[96,1536]{1,0:T(8,128)S(1)} %fusion.91, bf16[96,96]{1,0:T(8,128)(2,1)S(1)} %collective-permute-done, bf16[96,1536]{1,0:T(8,128)(2,1)S(1)} %collective-permute-done.1), kind=kOutput, calls=%fused_computation.3 | convolution fusion | flops 28459008 | bytes 1492992 | tf_op jit(solution)/shard_map/dot_general | solution.py:171
  19.3 1.3 %add.132 = f32[1,1536,96]{2,1,0:T(8,128)S(1)} reshape(f32[96,1536]{1,0:T(8,128)} %convolution_add_fusion.3) | data formatting | bytes 1179648 | tf_op jit(solution)/shard_map/add | solution.py:177
  20.6 1.1 %copy.13 = f32[1,1536,96]{1,2,0:T(8,128)} copy(f32[1,1536,96]{2,1,0:T(8,128)S(1)} %add.132) | data formatting | bytes 1179648 | tf_op jit(solution)/shard_map/add | solution.py:177
  21.7 1.2 %convolution_add_fusion.2 = f32[96,1536]{1,0:T(8,128)S(1)} fusion(f32[96,1536]{1,0:T(8,128)S(1)} %fusion.86, bf16[96,96]{1,0:T(8,128)(2,1)S(1)} %collective-permute-done.2, bf16[96,1536]{1,0:T(8,128)(2,1)} %collective-permute-done.3), kind=kOutput, calls=%fused_computation.2 | convolution fusion | flops 28459008 | bytes 1492992 | tf_op jit(solution)/shard_map/dot_general | solution.py:171
  22.9 0.3 add.134
  23.2 0.3 copy.14
  23.5 0.5 copy-done.3
  24.1 5.3 %shard_map.103 = f32[2,96,1536]{2,1,0:T(8,128)S(1)} custom-call(f32[2,96,1536]{2,1,0:T(8,128)S(1)} %maximum_bitcast_fusion.y_ref), custom_call_target="tpu_custom_call" | custom-call | tf_op jit(solution)/shard_map/pallas_call | solution.py:53
  29.4 1.3 %multiply_reduce_fusion.4 = (f32[]{:T(128)}, f32[96,96]{1,0:T(8,128)S(1)}) fusion(f32[1536,96]{1,0:T(8,128)S(1)} %copy-done.2, f32[2,96,1536]{2,1,0:T(8,128)S(1)} %shard_map.103), kind=kOutput, calls=%fused_computation.78 | convolution fusion | flops 169887744 | bytes 1413124 | tf_op jit(solution)/shard_map/dot_general | solution.py:180
  31.4 3.0 %collective-permute-start.5 = (bf16[96,96]{1,0:T(8,128)(2,1)S(1)}, bf16[96,96]{1,0:T(8,128)(2,1)S(1)}, u32[]{:S(2)}, u32[]{:S(2)}) collective-permute-start(bf16[96,96]{1,0:T(8,128)(2,1)S(1)} %divide_convert_fusion.4), channel_id=1, source_target_pairs={{0,15},{1,8},{2,9},{3,10},{4,11},{5,12},{6,13},{7,14},{8,23},{9,16... | collective-permute-start | bytes 55304 | tf_op jit(solution)/shard_map/ppermute | solution.py:67
  34.4 2.7 %collective-permute-start.7 = (bf16[96,96]{1,0:T(8,128)(2,1)S(1)}, bf16[96,96]{1,0:T(8,128)(2,1)S(1)}, u32[]{:S(2)}, u32[]{:S(2)}) collective-permute-start(bf16[96,96]{1,0:T(8,128)(2,1)S(1)} %divide_convert_fusion.4), channel_id=1, source_target_pairs={{0,8},{1,9},{2,10},{3,11},{4,12},{5,13},{6,14},{7,15},{8,16},{9,17... | collective-permute-start | bytes 55304 | tf_op jit(solution)/shard_map/ppermute | solution.py:67
  37.2 1.3 %multiply_reduce_fusion.5 = (f32[]{:T(128)}, f32[96,96]{1,0:T(8,128)S(1)}) fusion(f32[1536,96]{1,0:T(8,128)S(1)} %reshape.123, f32[2,96,1536]{2,1,0:T(8,128)S(1)} %shard_map.103), kind=kOutput, calls=%fused_computation.80 | convolution fusion | flops 169887744 | bytes 1413124 | tf_op jit(solution)/shard_map/dot_general | solution.py:181
  39.3 0.2 collective-permute-start.6
  39.6 0.2 copy.17
  40.0 5.1 %shard_map.105 = f32[16,96,128]{2,1,0:T(8,128)S(1)} custom-call(bf16[1536,96]{1,0:T(8,128)(2,1)S(1)} %reshape_squeeze.6.wd_ref, bf16[96,2048]{1,0:T(8,128)(2,1)S(1)} %bitcast.111, bf16[256,256]{1,0:T(8,128)(2,1)S(1)} %fusion.t_ref, bf16[96,1536]{1,0:T(8,128)(2,1)S(1)} %get-tuple-element.5.qt_ref), custom_call_target="tpu_custom_call" | custom-call | tf_op jit(solution)/shard_map/pallas_call | solution.py:111
  45.1 0.8 %multiply_reduce_fusion.1 = f32[]{:T(128)} fusion(f32[16,96,128]{2,1,0:T(8,128)S(1)} %shard_map.105), kind=kLoop, calls=%fused_computation.16 | loop fusion | flops 294911 | bytes 589828 | tf_op jit(solution)/shard_map/reduce_sum | solution.py:71
  46.7 0.2 copy.22
  46.9 1.1 %convert_element_type.80 = bf16[96,1536]{1,0:T(8,128)(2,1)} reshape(bf16[96,16,96]{2,1,0:T(8,128)(2,1)S(1)} %copy.22) | data formatting | bytes 589824 | tf_op jit(solution)/shard_map/convert_element_type | solution.py:188
  48.0 0.4 collective-permute-start.9
  48.4 0.2 fusion.89
  48.6 0.2 convolution_add_fusion.1
  49.0 0.2 fusion.84
  49.2 0.3 reshape.131
  49.4 0.3 add.138
  49.7 0.3 copy.15
  50.0 1.2 %reshape.125 = f32[1536,96]{1,0:T(8,128)} reshape(f32[96,1536]{1,0:T(8,128)S(1)} %fusion.84) | data formatting | bytes 1179648 | tf_op jit(solution)/shard_map/reshape | solution.py:171
  51.1 1.2 %convolution_add_fusion = f32[96,1536]{1,0:T(8,128)S(1)} fusion(f32[96,1536]{1,0:T(8,128)S(1)} %fusion.84, bf16[96,96]{1,0:T(8,128)(2,1)S(1)} %collective-permute-done.6, bf16[96,1536]{1,0:T(8,128)(2,1)} %collective-permute-done.3), kind=kOutput, calls=%fused_computation | convolution fusion | flops 28459008 | bytes 1492992 | tf_op jit(solution)/shard_map/dot_general | solution.py:171
  52.3 0.3 add.140
  52.6 0.3 copy.16
  52.9 5.3 %shard_map.104 = f32[2,96,1536]{2,1,0:T(8,128)S(1)} custom-call(f32[2,96,1536]{2,1,0:T(8,128)S(1)} %maximum_bitcast_fusion.1.y_ref), custom_call_target="tpu_custom_call" | custom-call | tf_op jit(solution)/shard_map/pallas_call | solution.py:53
  58.2 1.3 %multiply_reduce_fusion.2 = (f32[]{:T(128)}, f32[96,96]{1,0:T(8,128)S(1)}) fusion(f32[1536,96]{1,0:T(8,128)S(1)} %reshape.131, f32[2,96,1536]{2,1,0:T(8,128)S(1)} %shard_map.104), kind=kOutput, calls=%fused_computation.74 | convolution fusion | flops 169887744 | bytes 1413124 | tf_op jit(solution)/shard_map/dot_general | solution.py:181
  60.2 0.7 collective-permute-start.11
  60.9 0.2 copy.23
  61.4 1.3 %reshape.129.wd_ref = bf16[1536,96]{1,0:T(8,128)(2,1)S(1)} reshape(bf16[96,1536]{1,0:T(8,128)(2,1)} %collective-permute-done.9) | data formatting | bytes 589824 | tf_op jit(solution)/shard_map/reshape | solution.py:107
  62.7 5.1 %shard_map.106 = f32[16,96,128]{2,1,0:T(8,128)S(1)} custom-call(bf16[1536,96]{1,0:T(8,128)(2,1)S(1)} %reshape.129.wd_ref, bf16[96,2048]{1,0:T(8,128)(2,1)S(1)} %bitcast.110, bf16[256,256]{1,0:T(8,128)(2,1)S(1)} %fusion.t_ref, bf16[96,1536]{1,0:T(8,128)(2,1)S(1)} %get-tuple-element.3.qt_ref), custom_call_target="tpu_custom_call" | custom-call | tf_op jit(solution)/shard_map/pallas_call | solution.py:111
  67.8 0.8 %multiply_reduce_fusion = f32[]{:T(128)} fusion(f32[16,96,128]{2,1,0:T(8,128)S(1)} %shard_map.106), kind=kLoop, calls=%fused_computation.14 | loop fusion | flops 294911 | bytes 589828 | tf_op jit(solution)/shard_map/reduce_sum | solution.py:71
  69.4 0.2 copy.24
  69.5 0.4 convert_element_type.86
  69.9 1.2 %collective-permute-start.10 = (bf16[96,1536]{1,0:T(8,128)(2,1)S(1)}, bf16[96,1536]{1,0:T(8,128)(2,1)S(1)}, u32[]{:S(2)}, u32[]{:S(2)}) collective-permute-start(bf16[96,1536]{1,0:T(8,128)(2,1)S(1)} %convert_element_type.86), channel_id=1, source_target_pairs={{0,8},{1,9},{2,10},{3,11},{4,12},{5,13},{6,14},{7,15},{8,16},{9,17... | collective-permute-start | bytes 884744 | tf_op jit(solution)/shard_map/ppermute | solution.py:67
  71.1 1.3 %multiply_reduce_fusion.3 = (f32[]{:T(128)}, f32[96,96]{1,0:T(8,128)S(1)}) fusion(f32[1536,96]{1,0:T(8,128)S(1)} %copy-done.1, f32[2,96,1536]{2,1,0:T(8,128)S(1)} %shard_map.104), kind=kOutput, calls=%fused_computation.76 | convolution fusion | flops 169887744 | bytes 1413124 | tf_op jit(solution)/shard_map/dot_general | solution.py:180
  73.2 0.5 collective-permute-start.8
  73.7 2.8 %collective-permute-done.8 = bf16[96,96]{1,0:T(8,128)(2,1)S(1)} collective-permute-done((bf16[96,96]{1,0:T(8,128)(2,1)S(1)}, bf16[96,96]{1,0:T(8,128)(2,1)S(1)}, u32[]{:S(2)}, u32[]{:S(2)}) %collective-permute-start.8) | collective-permute-done | bytes 18464 | tf_op jit(solution)/shard_map/ppermute | solution.py:67
  76.5 0.6 copy.37
  77.1 0.7 copy.38
  77.8 0.6 copy.39
  (55 shorter events, 1.3 us)
Async XLA Ops:
  0.6 12.1 %copy-start = (f32[2,2]{1,0:T(2,128)S(1)}, f32[2,2]{1,0:T(2,128)}, u32[]{:S(2)}) copy-start(f32[2,2]{1,0:T(2,128)} %param.14) | copy-start | bytes 52
  0.6 10.7 %copy-start.9 = (bf16[1,1,2,256]{3,2,1,0:T(2,128)(2,1)S(1)}, bf16[1,1,2,256]{3,2,1,0:T(2,128)(2,1)}, u32[]{:S(2)}) copy-start(bf16[1,1,2,256]{3,2,1,0:T(2,128)(2,1)} %param.13) | copy-start | bytes 3076
  0.7 16.8 %collective-permute-start.1 = (bf16[96,1536]{1,0:T(8,128)(2,1)}, bf16[96,1536]{1,0:T(8,128)(2,1)S(1)}, u32[]{:S(2)}, u32[]{:S(2)}) collective-permute-start(bf16[96,1536]{1,0:T(8,128)(2,1)} %bitcast.117), channel_id=1, source_target_pairs={{0,7},{1,0},{2,1},{3,2},{4,3},{5,4},{6,5},{7,6},{8,15},{9,8},{10,9... | collective-permute-start | bytes 884744 | tf_op jit(solution)/shard_map/ppermute | solution.py:67
  6.7 10.7 %collective-permute-start = (bf16[96,96]{1,0:T(8,128)(2,1)}, bf16[96,96]{1,0:T(8,128)(2,1)S(1)}, u32[]{:S(2)}, u32[]{:S(2)}) collective-permute-start(bf16[96,96]{1,0:T(8,128)(2,1)} %bitcast.122), channel_id=1, source_target_pairs={{0,7},{1,0},{2,1},{3,2},{4,3},{5,4},{6,5},{7,6},{8,15},{9,8},{10,9... | collective-permute-start | bytes 55304 | tf_op jit(solution)/shard_map/ppermute | solution.py:67
  7.2 14.5 %collective-permute-start.3 = (bf16[96,1536]{1,0:T(8,128)(2,1)}, bf16[96,1536]{1,0:T(8,128)(2,1)}, u32[]{:S(2)}, u32[]{:S(2)}) collective-permute-start(bf16[96,1536]{1,0:T(8,128)(2,1)} %bitcast.116), channel_id=1, source_target_pairs={{0,1},{1,2},{2,3},{3,4},{4,5},{5,6},{6,7},{7,0},{8,9},{9,10},{10,1... | collective-permute-start | bytes 884744 | tf_op jit(solution)/shard_map/ppermute | solution.py:67
  8.8 13.0 %collective-permute-start.2 = (bf16[96,96]{1,0:T(8,128)(2,1)}, bf16[96,96]{1,0:T(8,128)(2,1)S(1)}, u32[]{:S(2)}, u32[]{:S(2)}) collective-permute-start(bf16[96,96]{1,0:T(8,128)(2,1)} %bitcast.123), channel_id=1, source_target_pairs={{0,1},{1,2},{2,3},{3,4},{4,5},{5,6},{6,7},{7,0},{8,9},{9,10},{10,1... | collective-permute-start | bytes 55304 | tf_op jit(solution)/shard_map/ppermute | solution.py:67
  10.0 2.9 %copy-start.10 = (s32[4]{0:T(128)S(1)}, s32[4]{0:T(128)}, u32[]{:S(2)}) copy-start(s32[4]{0:T(128)} %param.15) | copy-start | bytes 52
  15.7 1.4 %copy-start.8 = (bf16[1,1,96,1536]{3,2,1,0:T(8,128)(2,1)S(1)}, bf16[1,1,96,1536]{3,2,1,0:T(8,128)(2,1)}, u32[]{:S(2)}) copy-start(bf16[1,1,96,1536]{3,2,1,0:T(8,128)(2,1)} %param.10) | copy-start | bytes 884740
  17.5 0.7 copy-start.6
  22.9 1.1 %copy-start.3 = (f32[1,1536,96]{1,2,0:T(8,128)S(1)}, f32[1,1536,96]{1,2,0:T(8,128)}, u32[]{:S(2)}) copy-start(f32[1,1536,96]{1,2,0:T(8,128)} %copy.13) | copy-start | bytes 1769476
  24.1 5.3 %copy-start.2 = (f32[1536,96]{1,0:T(8,128)S(1)}, f32[1536,96]{1,0:T(8,128)}, u32[]{:S(2)}) copy-start(f32[1536,96]{1,0:T(8,128)} %reshape.124) | copy-start | bytes 1769476
  31.4 17.2 %collective-permute-start.5 = (bf16[96,96]{1,0:T(8,128)(2,1)S(1)}, bf16[96,96]{1,0:T(8,128)(2,1)S(1)}, u32[]{:S(2)}, u32[]{:S(2)}) collective-permute-start(bf16[96,96]{1,0:T(8,128)(2,1)S(1)} %divide_convert_fusion.4), channel_id=1, source_target_pairs={{0,15},{1,8},{2,9},{3,10},{4,11},{5,12},{6,13},{7,14},{8,23},{9,16... | collective-permute-start | bytes 55304 | tf_op jit(solution)/shard_map/ppermute | solution.py:67
  34.4 14.4 %collective-permute-start.7 = (bf16[96,96]{1,0:T(8,128)(2,1)S(1)}, bf16[96,96]{1,0:T(8,128)(2,1)S(1)}, u32[]{:S(2)}, u32[]{:S(2)}) collective-permute-start(bf16[96,96]{1,0:T(8,128)(2,1)S(1)} %divide_convert_fusion.4), channel_id=1, source_target_pairs={{0,8},{1,9},{2,10},{3,11},{4,12},{5,13},{6,14},{7,15},{8,16},{9,17... | collective-permute-start | bytes 55304 | tf_op jit(solution)/shard_map/ppermute | solution.py:67
  39.2 9.2 %collective-permute-start.4 = (bf16[96,96]{1,0:T(8,128)(2,1)S(1)}, bf16[96,96]{1,0:T(8,128)(2,1)S(1)}, u32[]{:S(2)}, u32[]{:S(2)}) collective-permute-start(bf16[96,96]{1,0:T(8,128)(2,1)S(1)} %divide_convert_fusion.5), channel_id=1, source_target_pairs={{0,8},{1,9},{2,10},{3,11},{4,12},{5,13},{6,14},{7,15},{8,16},{9,17... | collective-permute-start | bytes 55304 | tf_op jit(solution)/shard_map/ppermute | solution.py:67
  39.3 11.9 %collective-permute-start.6 = (bf16[96,96]{1,0:T(8,128)(2,1)S(1)}, bf16[96,96]{1,0:T(8,128)(2,1)S(1)}, u32[]{:S(2)}, u32[]{:S(2)}) collective-permute-start(bf16[96,96]{1,0:T(8,128)(2,1)S(1)} %divide_convert_fusion.5), channel_id=1, source_target_pairs={{0,9},{1,10},{2,11},{3,12},{4,13},{5,14},{6,15},{7,8},{8,17},{9,18... | collective-permute-start | bytes 55304 | tf_op jit(solution)/shard_map/ppermute | solution.py:67
  46.6 1.8 %copy-start.4 = (bf16[1,1,96,1536]{3,2,1,0:T(8,128)(2,1)S(1)}, bf16[1,1,96,1536]{3,2,1,0:T(8,128)(2,1)}, u32[]{:S(2)}) copy-start(bf16[1,1,96,1536]{3,2,1,0:T(8,128)(2,1)} %param.12) | copy-start | bytes 884740
  46.7 1.9 %copy-start.7 = (bf16[96,1536]{1,0:T(8,128)(2,1)S(1)}, bf16[96,1536]{1,0:T(8,128)(2,1)}, u32[]{:S(2)}) copy-start(bf16[96,1536]{1,0:T(8,128)(2,1)} %copy-done.6) | copy-start | bytes 884740
  48.0 1.0 %copy-start.5 = (bf16[1,1,96,1536]{3,2,1,0:T(8,128)(2,1)S(1)}, bf16[1,1,96,1536]{3,2,1,0:T(8,128)(2,1)}, u32[]{:S(2)}) copy-start(bf16[1,1,96,1536]{3,2,1,0:T(8,128)(2,1)} %param.9) | copy-start | bytes 884740
  48.0 13.4 %collective-permute-start.9 = (bf16[96,1536]{1,0:T(8,128)(2,1)}, bf16[96,1536]{1,0:T(8,128)(2,1)}, u32[]{:S(2)}, u32[]{:S(2)}) collective-permute-start(bf16[96,1536]{1,0:T(8,128)(2,1)} %convert_element_type.80), channel_id=1, source_target_pairs={{0,8},{1,9},{2,10},{3,11},{4,12},{5,13},{6,14},{7,15},{8,16},{9,17... | collective-permute-start | bytes 884744 | tf_op jit(solution)/shard_map/ppermute | solution.py:67
  60.2 13.5 %collective-permute-start.11 = (bf16[96,96]{1,0:T(8,128)(2,1)S(1)}, bf16[96,96]{1,0:T(8,128)(2,1)S(1)}, u32[]{:S(2)}, u32[]{:S(2)}) collective-permute-start(bf16[96,96]{1,0:T(8,128)(2,1)S(1)} %divide_convert_fusion.2), channel_id=1, source_target_pairs={{0,8},{1,9},{2,10},{3,11},{4,12},{5,13},{6,14},{7,15},{8,16},{9,17... | collective-permute-start | bytes 55304 | tf_op jit(solution)/shard_map/ppermute | solution.py:67
  69.3 1.9 %copy-start.1 = (f32[1536,96]{1,0:T(8,128)S(1)}, f32[1536,96]{1,0:T(8,128)}, u32[]{:S(2)}) copy-start(f32[1536,96]{1,0:T(8,128)} %reshape.125) | copy-start | bytes 1769476
  69.9 6.5 %collective-permute-start.10 = (bf16[96,1536]{1,0:T(8,128)(2,1)S(1)}, bf16[96,1536]{1,0:T(8,128)(2,1)S(1)}, u32[]{:S(2)}, u32[]{:S(2)}) collective-permute-start(bf16[96,1536]{1,0:T(8,128)(2,1)S(1)} %convert_element_type.86), channel_id=1, source_target_pairs={{0,8},{1,9},{2,10},{3,11},{4,12},{5,13},{6,14},{7,15},{8,16},{9,17... | collective-permute-start | bytes 884744 | tf_op jit(solution)/shard_map/ppermute | solution.py:67
  73.2 3.3 %collective-permute-start.8 = (bf16[96,96]{1,0:T(8,128)(2,1)S(1)}, bf16[96,96]{1,0:T(8,128)(2,1)S(1)}, u32[]{:S(2)}, u32[]{:S(2)}) collective-permute-start(bf16[96,96]{1,0:T(8,128)(2,1)S(1)} %divide_convert_fusion.3), channel_id=1, source_target_pairs={{0,8},{1,9},{2,10},{3,11},{4,12},{5,13},{6,14},{7,15},{8,16},{9,17... | collective-permute-start | bytes 55304 | tf_op jit(solution)/shard_map/ppermute | solution.py:67

commit v7 on v1

--- a/solution.py
+++ b/solution.py
@@ -27,6 +27,18 @@
     bh, bl = split_bf16(b)
     out = lambda p, q: lax.dot_general(p, q, (dims, ((), ())), preferred_element_type=jnp.float32)
     return out(ah, bh) + (out(ah, bl) + out(al, bh))
+
+
+def ns_step(y):
+    out = lambda p, q, dims: lax.dot_general(p, q, (dims, ((), ())), preferred_element_type=jnp.float32)
+    yh, yl = split_bf16(y)
+    cross = out(yh, yl, ((1,), (1,)))
+    gram = out(yh, yh, ((1,), (1,))) + (cross + cross.T)
+    eye = (lax.broadcasted_iota(jnp.int32, gram.shape, 0) == lax.broadcasted_iota(jnp.int32, gram.shape, 1))
+    step = jnp.where(eye, 1.5, 0.0) - 0.5 * gram
+    sh, sl = split_bf16(step)
+    dims = ((1,), (0,))
+    return out(sh, yh, dims) + (out(sh, yl, dims) + out(sl, yh, dims))
 
 
 def polar_kernel(y_ref, o_ref):
@@ -36,8 +48,7 @@
         y = y_ref[b]
         ys.append(y / jnp.sqrt(jnp.sum(y * y) + 1e-06))
     for sweep in range(NS_ITERS):
-        grams = [dot3(y, y, ((1,), (1,))) for y in ys]
-        ys = [1.5 * y - 0.5 * dot3(g, y, ((1,), (0,))) for g, y in zip(grams, ys)]
+        ys = [ns_step(y) for y in ys]
     for b in range(count):
         o_ref[b] = ys[b]
 
@@ -75,7 +86,7 @@
         for k in range(group):
             f_ref[:, d0 + k] = part[:, k * LANES:(k + 1) * LANES].reshape(n, dd, LANES)
     t = t_ref[...]
-    per = math.gcd(n, 24)
+    per = math.gcd(n, 48)
 
     def mid_body(h, carry):
         x = jnp.concatenate([f_ref[h * per + k].reshape(dd * dd, LANES) for k in range(per)], axis=1)

time: 82.8 us -> 83.1 us (level)
    pallas_call x2, Pallas kernels: 13.7 us -> 14.8 us  [polar_factor_t(): pl.pallas_call(polar_kernel, out_shape=jax.ShapeDtypeStruct(stack.shape,...]
  transfers between devices with their start and end apart: 12 -> 12, of which waited for: 1 -> 1; matrix products, arithmetic and copies ran while one was open for 32% -> 32% of each run, Pallas kernels for 22% -> 21%
where the time goes in v7:
time: 83.1 us; the launch traced here: 82.7 us
  Pallas kernels  24.9 us (30%)
  starting transfers between devices  17 us (20%)
  local copies, waits for them, and re-layouts  15.4 us (19%)
  matrix products  14.6 us (18%)
  between operations  5.36 us (6%)
  waiting for transfers between devices  2.81 us (3%)
  other arithmetic  2.63 us (3%)
    ppermute x12, starting transfers between devices, shifted(): return lax.ppermute(tree, ('gx', 'gy'), pairs)  17 us
    pallas_call x2, Pallas kernels, polar_factor_t(): pl.pallas_call(polar_kernel, out_shape=jax.ShapeDtypeStruct(stack.shape,...  14.8 us
    pallas_call x2, Pallas kernels, edge_contract(): pl.pallas_call(edge_kernel, out_shape=jax.ShapeDtypeStruct((dd, n, LANES)...  10.2 us
    dot_general x8, matrix products, half(): jnp.dot(corner, edge, preferred_element_type=jnp.float32)  6.5 us
    unnamed x27, local copies, waits for them, and re-layouts  3.51 us
    add x4, local copies, waits for them, and re-layouts, per_device(): lower + upper_nb  2.93 us
    reshape x4, local copies, waits for them, and re-layouts, half(): jnp.dot(corner, edge, preferred_element_type=jnp.float32)  2.82 us
    ppermute x12, waiting for transfers between devices, shifted(): return lax.ppermute(tree, ('gx', 'gy'), pairs)  2.81 us
  transfers between devices with their start and end apart: 12, of which 1 were waited for; matrix products, arithmetic and copies ran while one was open for 32% of the time, Pallas kernels for 21%

profile of v7, /device:TPU:0, one launch (start us, length us, event | category | flops | bytes accessed | tf_op | source)
XLA Modules:
  0.0 82.7 jit_solution(3577787329354482124)
XLA Ops:
  0.7 6.1 %collective-permute-start.1 = (bf16[96,1536]{1,0:T(8,128)(2,1)}, bf16[96,1536]{1,0:T(8,128)(2,1)S(1)}, u32[]{:S(2)}, u32[]{:S(2)}) collective-permute-start(bf16[96,1536]{1,0:T(8,128)(2,1)} %bitcast.117), channel_id=1, source_target_pairs={{0,7},{1,0},{2,1},{3,2},{4,3},{5,4},{6,5},{7,6},{8,15},{9,8},{10,9... | collective-permute-start | bytes 884744 | tf_op jit(solution)/shard_map/ppermute | solution.py:71
  6.7 0.5 collective-permute-start
  7.2 1.5 %collective-permute-start.3 = (bf16[96,1536]{1,0:T(8,128)(2,1)}, bf16[96,1536]{1,0:T(8,128)(2,1)}, u32[]{:S(2)}, u32[]{:S(2)}) collective-permute-start(bf16[96,1536]{1,0:T(8,128)(2,1)} %bitcast.116), channel_id=1, source_target_pairs={{0,1},{1,2},{2,3},{3,4},{4,5},{5,6},{6,7},{7,0},{8,9},{9,10},{10,1... | collective-permute-start | bytes 884744 | tf_op jit(solution)/shard_map/ppermute | solution.py:71
  8.8 1.2 %fusion.91 = f32[96,1536]{1,0:T(8,128)S(1)} fusion(bf16[1,1,96,1536]{3,2,1,0:T(8,128)(2,1)} %param.12, bf16[1,1,96,96]{3,2,1,0:T(8,128)(2,1)} %param.11), kind=kOutput, calls=%fused_computation.149 | convolution fusion | flops 28311552 | bytes 903168 | tf_op jit(solution)/shard_map/dot_general | solution.py:175
  10.0 1.2 %fusion.86 = f32[96,1536]{1,0:T(8,128)S(1)} fusion(bf16[1,1,96,1536]{3,2,1,0:T(8,128)(2,1)} %param.9, bf16[1,1,96,96]{3,2,1,0:T(8,128)(2,1)} %param.8), kind=kOutput, calls=%fused_computation.144 | convolution fusion | flops 28311552 | bytes 903168 | tf_op jit(solution)/shard_map/dot_general | solution.py:175
  11.3 0.1 reshape_squeeze.7
  11.5 0.3 copy.18
  11.9 0.4 convolution_bitcast_fusion
  12.3 0.4 fusion.54
  12.7 0.2 convolution_bitcast_fusion.1
  12.9 0.6 compare_reduce_fusion
  13.6 0.9 %fusion.2 = bf16[2,4,4,4,4]{3,0,1,2,4:T(2,128)(2,1)S(1)} fusion(f32[2,2,1,1,1]{1,0,4,3,2:T(2,128)S(1)} %convolution_bitcast_fusion.1, pred[]{:T(512)} %compare_reduce_fusion, bf16[2,4,4,4,4]{4,3,2,1,0:T(4,128)(2,1)S(1)} %reshape_squeeze.7), kind=kOutput, calls=%fused_computation.10 | convolution fusion | flops 13824 | bytes 2065 | tf_op jit(solution)/shard_map/st,tabcd->sabcd/dot_general | solution.py:158
  14.5 0.3 copy.21
  14.9 0.4 fusion.22
  15.3 0.4 fusion.t_ref
  15.7 0.3 reshape.123
  16.0 1.2 %reshape.124 = f32[1536,96]{1,0:T(8,128)} reshape(f32[96,1536]{1,0:T(8,128)S(1)} %fusion.86) | data formatting | bytes 1179648 | tf_op jit(solution)/shard_map/reshape | solution.py:175
  17.2 0.3 reshape_squeeze.6.wd_ref
  17.5 0.7 copy-done.6
  18.2 1.1 %convolution_add_fusion.3 = f32[96,1536]{1,0:T(8,128)} fusion(f32[96,1536]{1,0:T(8,128)S(1)} %fusion.91, bf16[96,96]{1,0:T(8,128)(2,1)S(1)} %collective-permute-done, bf16[96,1536]{1,0:T(8,128)(2,1)S(1)} %collective-permute-done.1), kind=kOutput, calls=%fused_computation.3 | convolution fusion | flops 28459008 | bytes 1492992 | tf_op jit(solution)/shard_map/dot_general | solution.py:175
  19.3 1.3 %add.132 = f32[1,1536,96]{2,1,0:T(8,128)S(1)} reshape(f32[96,1536]{1,0:T(8,128)} %convolution_add_fusion.3) | data formatting | bytes 1179648 | tf_op jit(solution)/shard_map/add | solution.py:181
  20.6 1.1 %copy.13 = f32[1,1536,96]{1,2,0:T(8,128)} copy(f32[1,1536,96]{2,1,0:T(8,128)S(1)} %add.132) | data formatting | bytes 1179648 | tf_op jit(solution)/shard_map/add | solution.py:181
  21.7 1.2 %convolution_add_fusion.2 = f32[96,1536]{1,0:T(8,128)S(1)} fusion(f32[96,1536]{1,0:T(8,128)S(1)} %fusion.86, bf16[96,96]{1,0:T(8,128)(2,1)S(1)} %collective-permute-done.2, bf16[96,1536]{1,0:T(8,128)(2,1)} %collective-permute-done.3), kind=kOutput, calls=%fused_computation.2 | convolution fusion | flops 28459008 | bytes 1492992 | tf_op jit(solution)/shard_map/dot_general | solution.py:175
  22.9 0.3 add.134
  23.2 0.3 copy.14
  23.5 0.5 copy-done.3
  24.1 7.4 %shard_map.103 = f32[2,96,1536]{2,1,0:T(8,128)S(1)} custom-call(f32[2,96,1536]{2,1,0:T(8,128)S(1)} %maximum_bitcast_fusion.y_ref), custom_call_target="tpu_custom_call" | custom-call | tf_op jit(solution)/shard_map/pallas_call | solution.py:57
  31.5 1.3 %multiply_reduce_fusion.4 = (f32[]{:T(128)}, f32[96,96]{1,0:T(8,128)S(1)}) fusion(f32[1536,96]{1,0:T(8,128)S(1)} %copy-done.2, f32[2,96,1536]{2,1,0:T(8,128)S(1)} %shard_map.103), kind=kOutput, calls=%fused_computation.78 | convolution fusion | flops 169887744 | bytes 1413124 | tf_op jit(solution)/shard_map/dot_general | solution.py:184
  33.5 3.0 %collective-permute-start.5 = (bf16[96,96]{1,0:T(8,128)(2,1)S(1)}, bf16[96,96]{1,0:T(8,128)(2,1)S(1)}, u32[]{:S(2)}, u32[]{:S(2)}) collective-permute-start(bf16[96,96]{1,0:T(8,128)(2,1)S(1)} %divide_convert_fusion.4), channel_id=1, source_target_pairs={{0,15},{1,8},{2,9},{3,10},{4,11},{5,12},{6,13},{7,14},{8,23},{9,16... | collective-permute-start | bytes 55304 | tf_op jit(solution)/shard_map/ppermute | solution.py:71
  36.5 2.7 %collective-permute-start.7 = (bf16[96,96]{1,0:T(8,128)(2,1)S(1)}, bf16[96,96]{1,0:T(8,128)(2,1)S(1)}, u32[]{:S(2)}, u32[]{:S(2)}) collective-permute-start(bf16[96,96]{1,0:T(8,128)(2,1)S(1)} %divide_convert_fusion.4), channel_id=1, source_target_pairs={{0,8},{1,9},{2,10},{3,11},{4,12},{5,13},{6,14},{7,15},{8,16},{9,17... | collective-permute-start | bytes 55304 | tf_op jit(solution)/shard_map/ppermute | solution.py:71
  39.3 1.3 %multiply_reduce_fusion.5 = (f32[]{:T(128)}, f32[96,96]{1,0:T(8,128)S(1)}) fusion(f32[1536,96]{1,0:T(8,128)S(1)} %reshape.123, f32[2,96,1536]{2,1,0:T(8,128)S(1)} %shard_map.103), kind=kOutput, calls=%fused_computation.80 | convolution fusion | flops 169887744 | bytes 1413124 | tf_op jit(solution)/shard_map/dot_general | solution.py:185
  41.4 0.2 collective-permute-start.6
  41.7 0.2 copy.17
  42.1 5.1 %shard_map.105 = f32[16,96,128]{2,1,0:T(8,128)S(1)} custom-call(bf16[1536,96]{1,0:T(8,128)(2,1)S(1)} %reshape_squeeze.6.wd_ref, bf16[96,2048]{1,0:T(8,128)(2,1)S(1)} %bitcast.111, bf16[256,256]{1,0:T(8,128)(2,1)S(1)} %fusion.t_ref, bf16[96,1536]{1,0:T(8,128)(2,1)S(1)} %get-tuple-element.5.qt_ref), custom_call_target="tpu_custom_call" | custom-call | tf_op jit(solution)/shard_map/pallas_call | solution.py:115
  47.2 0.8 multiply_reduce_fusion.1
  48.8 0.2 copy.22
  49.0 1.1 %convert_element_type.80 = bf16[96,1536]{1,0:T(8,128)(2,1)} reshape(bf16[96,16,96]{2,1,0:T(8,128)(2,1)S(1)} %copy.22) | data formatting | bytes 589824 | tf_op jit(solution)/shard_map/convert_element_type | solution.py:192
  50.1 0.4 collective-permute-start.9
  50.5 0.2 fusion.89
  50.8 0.2 convolution_add_fusion.1
  51.1 0.2 fusion.84
  51.3 0.3 reshape.131
  51.5 0.3 add.138
  51.8 0.3 copy.15
  52.1 1.2 %reshape.125 = f32[1536,96]{1,0:T(8,128)} reshape(f32[96,1536]{1,0:T(8,128)S(1)} %fusion.84) | data formatting | bytes 1179648 | tf_op jit(solution)/shard_map/reshape | solution.py:175
  53.2 1.2 %convolution_add_fusion = f32[96,1536]{1,0:T(8,128)S(1)} fusion(f32[96,1536]{1,0:T(8,128)S(1)} %fusion.84, bf16[96,96]{1,0:T(8,128)(2,1)S(1)} %collective-permute-done.6, bf16[96,1536]{1,0:T(8,128)(2,1)} %collective-permute-done.3), kind=kOutput, calls=%fused_computation | convolution fusion | flops 28459008 | bytes 1492992 | tf_op jit(solution)/shard_map/dot_general | solution.py:175
  54.4 0.3 add.140
  54.7 0.3 copy.16
  55.0 7.4 %shard_map.104 = f32[2,96,1536]{2,1,0:T(8,128)S(1)} custom-call(f32[2,96,1536]{2,1,0:T(8,128)S(1)} %maximum_bitcast_fusion.1.y_ref), custom_call_target="tpu_custom_call" | custom-call | tf_op jit(solution)/shard_map/pallas_call | solution.py:57
  62.4 1.3 %multiply_reduce_fusion.2 = (f32[]{:T(128)}, f32[96,96]{1,0:T(8,128)S(1)}) fusion(f32[1536,96]{1,0:T(8,128)S(1)} %reshape.131, f32[2,96,1536]{2,1,0:T(8,128)S(1)} %shard_map.104), kind=kOutput, calls=%fused_computation.74 | convolution fusion | flops 169887744 | bytes 1413124 | tf_op jit(solution)/shard_map/dot_general | solution.py:185
  64.5 0.7 collective-permute-start.11
  65.2 0.2 copy.23
  65.6 1.3 %reshape.129.wd_ref = bf16[1536,96]{1,0:T(8,128)(2,1)S(1)} reshape(bf16[96,1536]{1,0:T(8,128)(2,1)} %collective-permute-done.9) | data formatting | bytes 589824 | tf_op jit(solution)/shard_map/reshape | solution.py:111
  66.9 5.1 %shard_map.106 = f32[16,96,128]{2,1,0:T(8,128)S(1)} custom-call(bf16[1536,96]{1,0:T(8,128)(2,1)S(1)} %reshape.129.wd_ref, bf16[96,2048]{1,0:T(8,128)(2,1)S(1)} %bitcast.110, bf16[256,256]{1,0:T(8,128)(2,1)S(1)} %fusion.t_ref, bf16[96,1536]{1,0:T(8,128)(2,1)S(1)} %get-tuple-element.3.qt_ref), custom_call_target="tpu_custom_call" | custom-call | tf_op jit(solution)/shard_map/pallas_call | solution.py:115
  72.0 0.8 multiply_reduce_fusion
  73.6 0.2 copy.24
  73.8 0.4 convert_element_type.86
  74.2 1.2 %collective-permute-start.10 = (bf16[96,1536]{1,0:T(8,128)(2,1)S(1)}, bf16[96,1536]{1,0:T(8,128)(2,1)S(1)}, u32[]{:S(2)}, u32[]{:S(2)}) collective-permute-start(bf16[96,1536]{1,0:T(8,128)(2,1)S(1)} %convert_element_type.86), channel_id=1, source_target_pairs={{0,8},{1,9},{2,10},{3,11},{4,12},{5,13},{6,14},{7,15},{8,16},{9,17... | collective-permute-start | bytes 884744 | tf_op jit(solution)/shard_map/ppermute | solution.py:71
  75.4 1.3 %multiply_reduce_fusion.3 = (f32[]{:T(128)}, f32[96,96]{1,0:T(8,128)S(1)}) fusion(f32[1536,96]{1,0:T(8,128)S(1)} %copy-done.1, f32[2,96,1536]{2,1,0:T(8,128)S(1)} %shard_map.104), kind=kOutput, calls=%fused_computation.76 | convolution fusion | flops 169887744 | bytes 1413124 | tf_op jit(solution)/shard_map/dot_general | solution.py:184
  77.4 0.5 collective-permute-start.8
  77.9 2.8 %collective-permute-done.8 = bf16[96,96]{1,0:T(8,128)(2,1)S(1)} collective-permute-done((bf16[96,96]{1,0:T(8,128)(2,1)S(1)}, bf16[96,96]{1,0:T(8,128)(2,1)S(1)}, u32[]{:S(2)}, u32[]{:S(2)}) %collective-permute-start.8) | collective-permute-done | bytes 18464 | tf_op jit(solution)/shard_map/ppermute | solution.py:71
  80.7 0.6 copy.37
  81.3 0.7 copy.38
  82.1 0.6 copy.39
  (55 shorter events, 1.3 us)
Async XLA Ops:
  0.6 12.1 %copy-start = (f32[2,2]{1,0:T(2,128)S(1)}, f32[2,2]{1,0:T(2,128)}, u32[]{:S(2)}) copy-start(f32[2,2]{1,0:T(2,128)} %param.14) | copy-start | bytes 52
  0.6 10.7 %copy-start.9 = (bf16[1,1,2,256]{3,2,1,0:T(2,128)(2,1)S(1)}, bf16[1,1,2,256]{3,2,1,0:T(2,128)(2,1)}, u32[]{:S(2)}) copy-start(bf16[1,1,2,256]{3,2,1,0:T(2,128)(2,1)} %param.13) | copy-start | bytes 3076
  0.7 16.8 %collective-permute-start.1 = (bf16[96,1536]{1,0:T(8,128)(2,1)}, bf16[96,1536]{1,0:T(8,128)(2,1)S(1)}, u32[]{:S(2)}, u32[]{:S(2)}) collective-permute-start(bf16[96,1536]{1,0:T(8,128)(2,1)} %bitcast.117), channel_id=1, source_target_pairs={{0,7},{1,0},{2,1},{3,2},{4,3},{5,4},{6,5},{7,6},{8,15},{9,8},{10,9... | collective-permute-start | bytes 884744 | tf_op jit(solution)/shard_map/ppermute | solution.py:71
  6.7 10.7 %collective-permute-start = (bf16[96,96]{1,0:T(8,128)(2,1)}, bf16[96,96]{1,0:T(8,128)(2,1)S(1)}, u32[]{:S(2)}, u32[]{:S(2)}) collective-permute-start(bf16[96,96]{1,0:T(8,128)(2,1)} %bitcast.122), channel_id=1, source_target_pairs={{0,7},{1,0},{2,1},{3,2},{4,3},{5,4},{6,5},{7,6},{8,15},{9,8},{10,9... | collective-permute-start | bytes 55304 | tf_op jit(solution)/shard_map/ppermute | solution.py:71
  7.2 14.5 %collective-permute-start.3 = (bf16[96,1536]{1,0:T(8,128)(2,1)}, bf16[96,1536]{1,0:T(8,128)(2,1)}, u32[]{:S(2)}, u32[]{:S(2)}) collective-permute-start(bf16[96,1536]{1,0:T(8,128)(2,1)} %bitcast.116), channel_id=1, source_target_pairs={{0,1},{1,2},{2,3},{3,4},{4,5},{5,6},{6,7},{7,0},{8,9},{9,10},{10,1... | collective-permute-start | bytes 884744 | tf_op jit(solution)/shard_map/ppermute | solution.py:71
  8.8 13.0 %collective-permute-start.2 = (bf16[96,96]{1,0:T(8,128)(2,1)}, bf16[96,96]{1,0:T(8,128)(2,1)S(1)}, u32[]{:S(2)}, u32[]{:S(2)}) collective-permute-start(bf16[96,96]{1,0:T(8,128)(2,1)} %bitcast.123), channel_id=1, source_target_pairs={{0,1},{1,2},{2,3},{3,4},{4,5},{5,6},{6,7},{7,0},{8,9},{9,10},{10,1... | collective-permute-start | bytes 55304 | tf_op jit(solution)/shard_map/ppermute | solution.py:71
  10.0 2.9 %copy-start.10 = (s32[4]{0:T(128)S(1)}, s32[4]{0:T(128)}, u32[]{:S(2)}) copy-start(s32[4]{0:T(128)} %param.15) | copy-start | bytes 52
  15.7 1.4 %copy-start.8 = (bf16[1,1,96,1536]{3,2,1,0:T(8,128)(2,1)S(1)}, bf16[1,1,96,1536]{3,2,1,0:T(8,128)(2,1)}, u32[]{:S(2)}) copy-start(bf16[1,1,96,1536]{3,2,1,0:T(8,128)(2,1)} %param.10) | copy-start | bytes 884740
  17.5 0.7 copy-start.6
  22.9 1.1 %copy-start.3 = (f32[1,1536,96]{1,2,0:T(8,128)S(1)}, f32[1,1536,96]{1,2,0:T(8,128)}, u32[]{:S(2)}) copy-start(f32[1,1536,96]{1,2,0:T(8,128)} %copy.13) | copy-start | bytes 1769476
  24.1 7.4 %copy-start.2 = (f32[1536,96]{1,0:T(8,128)S(1)}, f32[1536,96]{1,0:T(8,128)}, u32[]{:S(2)}) copy-start(f32[1536,96]{1,0:T(8,128)} %reshape.124) | copy-start | bytes 1769476
  33.5 17.2 %collective-permute-start.5 = (bf16[96,96]{1,0:T(8,128)(2,1)S(1)}, bf16[96,96]{1,0:T(8,128)(2,1)S(1)}, u32[]{:S(2)}, u32[]{:S(2)}) collective-permute-start(bf16[96,96]{1,0:T(8,128)(2,1)S(1)} %divide_convert_fusion.4), channel_id=1, source_target_pairs={{0,15},{1,8},{2,9},{3,10},{4,11},{5,12},{6,13},{7,14},{8,23},{9,16... | collective-permute-start | bytes 55304 | tf_op jit(solution)/shard_map/ppermute | solution.py:71
  36.5 14.4 %collective-permute-start.7 = (bf16[96,96]{1,0:T(8,128)(2,1)S(1)}, bf16[96,96]{1,0:T(8,128)(2,1)S(1)}, u32[]{:S(2)}, u32[]{:S(2)}) collective-permute-start(bf16[96,96]{1,0:T(8,128)(2,1)S(1)} %divide_convert_fusion.4), channel_id=1, source_target_pairs={{0,8},{1,9},{2,10},{3,11},{4,12},{5,13},{6,14},{7,15},{8,16},{9,17... | collective-permute-start | bytes 55304 | tf_op jit(solution)/shard_map/ppermute | solution.py:71
  41.3 9.2 %collective-permute-start.4 = (bf16[96,96]{1,0:T(8,128)(2,1)S(1)}, bf16[96,96]{1,0:T(8,128)(2,1)S(1)}, u32[]{:S(2)}, u32[]{:S(2)}) collective-permute-start(bf16[96,96]{1,0:T(8,128)(2,1)S(1)} %divide_convert_fusion.5), channel_id=1, source_target_pairs={{0,8},{1,9},{2,10},{3,11},{4,12},{5,13},{6,14},{7,15},{8,16},{9,17... | collective-permute-start | bytes 55304 | tf_op jit(solution)/shard_map/ppermute | solution.py:71
  41.4 11.9 %collective-permute-start.6 = (bf16[96,96]{1,0:T(8,128)(2,1)S(1)}, bf16[96,96]{1,0:T(8,128)(2,1)S(1)}, u32[]{:S(2)}, u32[]{:S(2)}) collective-permute-start(bf16[96,96]{1,0:T(8,128)(2,1)S(1)} %divide_convert_fusion.5), channel_id=1, source_target_pairs={{0,9},{1,10},{2,11},{3,12},{4,13},{5,14},{6,15},{7,8},{8,17},{9,18... | collective-permute-start | bytes 55304 | tf_op jit(solution)/shard_map/ppermute | solution.py:71
  48.7 1.8 %copy-start.4 = (bf16[1,1,96,1536]{3,2,1,0:T(8,128)(2,1)S(1)}, bf16[1,1,96,1536]{3,2,1,0:T(8,128)(2,1)}, u32[]{:S(2)}) copy-start(bf16[1,1,96,1536]{3,2,1,0:T(8,128)(2,1)} %param.12) | copy-start | bytes 884740
  48.8 1.9 %copy-start.7 = (bf16[96,1536]{1,0:T(8,128)(2,1)S(1)}, bf16[96,1536]{1,0:T(8,128)(2,1)}, u32[]{:S(2)}) copy-start(bf16[96,1536]{1,0:T(8,128)(2,1)} %copy-done.6) | copy-start | bytes 884740
  50.1 1.0 %copy-start.5 = (bf16[1,1,96,1536]{3,2,1,0:T(8,128)(2,1)S(1)}, bf16[1,1,96,1536]{3,2,1,0:T(8,128)(2,1)}, u32[]{:S(2)}) copy-start(bf16[1,1,96,1536]{3,2,1,0:T(8,128)(2,1)} %param.9) | copy-start | bytes 884740
  50.1 15.5 %collective-permute-start.9 = (bf16[96,1536]{1,0:T(8,128)(2,1)}, bf16[96,1536]{1,0:T(8,128)(2,1)}, u32[]{:S(2)}, u32[]{:S(2)}) collective-permute-start(bf16[96,1536]{1,0:T(8,128)(2,1)} %convert_element_type.80), channel_id=1, source_target_pairs={{0,8},{1,9},{2,10},{3,11},{4,12},{5,13},{6,14},{7,15},{8,16},{9,17... | collective-permute-start | bytes 884744 | tf_op jit(solution)/shard_map/ppermute | solution.py:71
  64.5 13.5 %collective-permute-start.11 = (bf16[96,96]{1,0:T(8,128)(2,1)S(1)}, bf16[96,96]{1,0:T(8,128)(2,1)S(1)}, u32[]{:S(2)}, u32[]{:S(2)}) collective-permute-start(bf16[96,96]{1,0:T(8,128)(2,1)S(1)} %divide_convert_fusion.2), channel_id=1, source_target_pairs={{0,8},{1,9},{2,10},{3,11},{4,12},{5,13},{6,14},{7,15},{8,16},{9,17... | collective-permute-start | bytes 55304 | tf_op jit(solution)/shard_map/ppermute | solution.py:71
  73.5 1.9 %copy-start.1 = (f32[1536,96]{1,0:T(8,128)S(1)}, f32[1536,96]{1,0:T(8,128)}, u32[]{:S(2)}) copy-start(f32[1536,96]{1,0:T(8,128)} %reshape.125) | copy-start | bytes 1769476
  74.2 6.5 %collective-permute-start.10 = (bf16[96,1536]{1,0:T(8,128)(2,1)S(1)}, bf16[96,1536]{1,0:T(8,128)(2,1)S(1)}, u32[]{:S(2)}, u32[]{:S(2)}) collective-permute-start(bf16[96,1536]{1,0:T(8,128)(2,1)S(1)} %convert_element_type.86), channel_id=1, source_target_pairs={{0,8},{1,9},{2,10},{3,11},{4,12},{5,13},{6,14},{7,15},{8,16},{9,17... | collective-permute-start | bytes 884744 | tf_op jit(solution)/shard_map/ppermute | solution.py:71
  77.4 3.3 %collective-permute-start.8 = (bf16[96,96]{1,0:T(8,128)(2,1)S(1)}, bf16[96,96]{1,0:T(8,128)(2,1)S(1)}, u32[]{:S(2)}, u32[]{:S(2)}) collective-permute-start(bf16[96,96]{1,0:T(8,128)(2,1)S(1)} %divide_convert_fusion.3), channel_id=1, source_target_pairs={{0,8},{1,9},{2,10},{3,11},{4,12},{5,13},{6,14},{7,15},{8,16},{9,17... | collective-permute-start | bytes 55304 | tf_op jit(solution)/shard_map/ppermute | solution.py:71

commit v8 on v6

--- a/solution.py
+++ b/solution.py
@@ -36,7 +36,7 @@
     return out(yh, yh) + (cross + cross.T)
 
 
-def polar_kernel(y_ref, o_ref):
+def polar_kernel(y_ref, o_ref, h_ref):
     count = y_ref.shape[0]
     ys = []
     for b in range(count):
@@ -47,12 +47,16 @@
         ys = [1.5 * y - 0.5 * dot3(g, y, ((1,), (0,))) for g, y in zip(grams, ys)]
     for b in range(count):
         o_ref[b] = ys[b]
+        h_ref[b] = ys[b].astype(h_ref.dtype)
 
 
 def polar_factor_t(stack):
     return pl.pallas_call(
         polar_kernel,
-        out_shape=jax.ShapeDtypeStruct(stack.shape, jnp.float32),
+        out_shape=(
+            jax.ShapeDtypeStruct(stack.shape, jnp.float32),
+            jax.ShapeDtypeStruct(stack.shape, jnp.bfloat16),
+        ),
         compiler_params=pltpu.CompilerParams(vmem_limit_bytes=32 * 1024 * 1024),
     )(stack)
 
@@ -174,7 +178,7 @@
         lower = half(corner_low, south_edge)
         upper_nb = half(up_corner_nb, north_nb)
         lower_nb = half(low_corner_nb, south_nb)
-        projs = polar_factor_t(jnp.swapaxes(jnp.stack([lower + upper_nb, lower_nb + upper]), 1, 2))
+        projs, projs16 = polar_factor_t(jnp.swapaxes(jnp.stack([lower + upper_nb, lower_nb + upper]), 1, 2))
         below_t = projs[0]
         above_t = projs[1]
         new_up = jnp.dot(above_t, upper, precision=lax.Precision.HIGHEST)
@@ -184,7 +188,7 @@
         if step + 1 < STEPS:
             up_corner_nb = shifted(new_up, 1, -1)
             low_corner_nb = shifted(new_low, 1, 1)
-        edge_new = edge_contract(west_edge, below_t.astype(jnp.bfloat16), above_t.astype(jnp.bfloat16), site)
+        edge_new = edge_contract(west_edge, projs16[0], projs16[1], site)
         edge_new = unit_scaled(edge_new).astype(jnp.bfloat16)
         corner_up, west_edge, corner_low = shifted((new_up, edge_new, new_low), 1, 0)
     return (corner_up[None, None], west_edge[None, None], corner_low[None, None])

time: 78.9 us -> 75.2 us (0.953)
  matrix products: 14.6 us -> 11.8 us
  local copies, waits for them, and re-layouts: 15.4 us -> 14.4 us
    dot_general x8, matrix products: 6.5 us -> 3.72 us  [half(): jnp.dot(corner, edge, preferred_element_type=jnp.float32)]
    reshape x4, local copies, waits for them, and re-layouts: 2.82 us -> 4.75 us  [half(): jnp.dot(corner, edge, preferred_element_type=jnp.float32)]
    add x4, local copies, waits for them, and re-layouts: 2.93 us -> 1.01 us  [per_device(): lower + upper_nb]
    unnamed x27 -> x29, local copies, waits for them, and re-layouts: 3.52 us -> 2.5 us
  transfers between devices with their start and end apart: 12 -> 12, of which waited for: 1 -> 1; matrix products, arithmetic and copies ran while one was open for 33% -> 32% of each run, Pallas kernels for 20% -> 21%
where the time goes in v8:
time: 75.2 us; the launch traced here: 75 us
  Pallas kernels  20.7 us (28%)
  starting transfers between devices  17.3 us (23%)
  local copies, waits for them, and re-layouts  14.4 us (19%)
  matrix products  11.8 us (16%)
  between operations  5.39 us (7%)
  waiting for transfers between devices  2.81 us (4%)
  other arithmetic  2.63 us (3%)
    ppermute x12, starting transfers between devices, shifted(): return lax.ppermute(tree, ('gx', 'gy'), pairs)  17.3 us
    pallas_call x2, Pallas kernels, polar_factor_t(): pl.pallas_call(polar_kernel, out_shape=(jax.ShapeDtypeStruct(stack.shape,...  10.5 us
    pallas_call x2, Pallas kernels, edge_contract(): pl.pallas_call(edge_kernel, out_shape=jax.ShapeDtypeStruct((dd, n, LANES)...  10.2 us
    reshape x4, local copies, waits for them, and re-layouts, half(): jnp.dot(corner, edge, preferred_element_type=jnp.float32)  4.75 us
    dot_general x8, matrix products, half(): jnp.dot(corner, edge, preferred_element_type=jnp.float32)  3.72 us
    ppermute x12, waiting for transfers between devices, shifted(): return lax.ppermute(tree, ('gx', 'gy'), pairs)  2.81 us
    dot_general x2, matrix products, per_device(): new_up = jnp.dot(above_t, upper, precision=lax.Precision.HIGHEST)  2.65 us
    dot_general x2, matrix products, per_device(): new_low = jnp.dot(below_t, lower, precision=lax.Precision.HIGHEST)  2.65 us
  transfers between devices with their start and end apart: 12, of which 1 were waited for; matrix products, arithmetic and copies ran while one was open for 32% of the time, Pallas kernels for 21%

profile of v8, /device:TPU:0, one launch (start us, length us, event | category | flops | bytes accessed | tf_op | source)
XLA Modules:
  0.0 75.0 jit_solution(10887040701708959314)
XLA Ops:
  0.7 6.1 %collective-permute-start.1 = (bf16[96,1536]{1,0:T(8,128)(2,1)}, bf16[96,1536]{1,0:T(8,128)(2,1)S(1)}, u32[]{:S(2)}, u32[]{:S(2)}) collective-permute-start(bf16[96,1536]{1,0:T(8,128)(2,1)} %bitcast.117), channel_id=1, source_target_pairs={{0,7},{1,0},{2,1},{3,2},{4,3},{5,4},{6,5},{7,6},{8,15},{9,8},{10,9... | collective-permute-start | bytes 884744 | tf_op jit(solution)/shard_map/ppermute | solution.py:71
  6.7 0.5 collective-permute-start
  7.2 1.5 %collective-permute-start.3 = (bf16[96,1536]{1,0:T(8,128)(2,1)}, bf16[96,1536]{1,0:T(8,128)(2,1)S(1)}, u32[]{:S(2)}, u32[]{:S(2)}) collective-permute-start(bf16[96,1536]{1,0:T(8,128)(2,1)} %bitcast.116), channel_id=1, source_target_pairs={{0,1},{1,2},{2,3},{3,4},{4,5},{5,6},{6,7},{7,0},{8,9},{9,10},{10,1... | collective-permute-start | bytes 884744 | tf_op jit(solution)/shard_map/ppermute | solution.py:71
  8.8 1.2 %fusion.93 = f32[96,1536]{1,0:T(8,128)S(1)} fusion(bf16[1,1,96,1536]{3,2,1,0:T(8,128)(2,1)} %param.12, bf16[1,1,96,96]{3,2,1,0:T(8,128)(2,1)} %param.11), kind=kOutput, calls=%fused_computation.149 | convolution fusion | flops 28311552 | bytes 903168 | tf_op jit(solution)/shard_map/dot_general | solution.py:175
  10.0 1.2 %fusion.88 = f32[96,1536]{1,0:T(8,128)S(1)} fusion(bf16[1,1,96,1536]{3,2,1,0:T(8,128)(2,1)} %param.9, bf16[1,1,96,96]{3,2,1,0:T(8,128)(2,1)} %param.8), kind=kOutput, calls=%fused_computation.144 | convolution fusion | flops 28311552 | bytes 903168 | tf_op jit(solution)/shard_map/dot_general | solution.py:175
  11.3 0.1 reshape_squeeze.14
  11.5 0.3 copy.18
  11.9 0.4 convolution_bitcast_fusion
  12.3 0.4 fusion.56
  12.7 0.2 convolution_bitcast_fusion.1
  12.9 0.6 compare_reduce_fusion
  13.6 0.9 %fusion.2 = bf16[2,4,4,4,4]{3,0,1,2,4:T(2,128)(2,1)S(1)} fusion(f32[2,2,1,1,1]{1,0,4,3,2:T(2,128)S(1)} %convolution_bitcast_fusion.1, pred[]{:T(512)} %compare_reduce_fusion, bf16[2,4,4,4,4]{4,3,2,1,0:T(4,128)(2,1)S(1)} %reshape_squeeze.14), kind=kOutput, calls=%fused_computation.10 | convolution fusion | flops 13824 | bytes 2065 | tf_op jit(solution)/shard_map/st,tabcd->sabcd/dot_general | solution.py:158
  14.5 0.3 copy.21
  14.9 0.4 fusion.24
  15.3 0.4 fusion.t_ref
  15.7 1.2 %reshape.117 = f32[1536,96]{1,0:T(8,128)} reshape(f32[96,1536]{1,0:T(8,128)S(1)} %fusion.93) | data formatting | bytes 1179648 | tf_op jit(solution)/shard_map/reshape | solution.py:175
  16.9 1.2 %reshape.118 = f32[1536,96]{1,0:T(8,128)} reshape(f32[96,1536]{1,0:T(8,128)S(1)} %fusion.88) | data formatting | bytes 1179648 | tf_op jit(solution)/shard_map/reshape | solution.py:175
  18.1 0.3 reshape_squeeze.12.wd_ref
  18.5 0.2 convolution_add_fusion.3
  18.7 0.3 add.132
  19.0 0.2 copy-done.7
  19.2 0.3 copy.13
  19.5 0.2 convolution_add_fusion.2
  19.7 0.3 add.134
  19.9 0.3 copy.14
  20.3 5.3 %shard_map.103 = (f32[2,96,1536]{2,1,0:T(8,128)S(1)}, bf16[2,96,1536]{2,1,0:T(8,128)(2,1)S(1)}) custom-call(f32[2,96,1536]{2,1,0:T(8,128)S(1)} %maximum_bitcast_fusion.y_ref), custom_call_target="tpu_custom_call" | custom-call | tf_op jit(solution)/shard_map/pallas_call | solution.py:54
  25.6 1.3 %multiply_reduce_fusion.4 = (f32[]{:T(128)}, f32[96,96]{1,0:T(8,128)S(1)}) fusion(f32[1536,96]{1,0:T(8,128)S(1)} %copy-done.3, f32[2,96,1536]{2,1,0:T(8,128)S(1)} %get-tuple-element.7), kind=kOutput, calls=%fused_computation.78 | convolution fusion | flops 169887744 | bytes 1413124 | tf_op jit(solution)/shard_map/dot_general | solution.py:184
  27.6 3.3 %collective-permute-start.5 = (bf16[96,96]{1,0:T(8,128)(2,1)S(1)}, bf16[96,96]{1,0:T(8,128)(2,1)S(1)}, u32[]{:S(2)}, u32[]{:S(2)}) collective-permute-start(bf16[96,96]{1,0:T(8,128)(2,1)S(1)} %divide_convert_fusion.4), channel_id=1, source_target_pairs={{0,15},{1,8},{2,9},{3,10},{4,11},{5,12},{6,13},{7,14},{8,23},{9,16... | collective-permute-start | bytes 55304 | tf_op jit(solution)/shard_map/ppermute | solution.py:71
  30.9 2.8 %collective-permute-start.7 = (bf16[96,96]{1,0:T(8,128)(2,1)S(1)}, bf16[96,96]{1,0:T(8,128)(2,1)S(1)}, u32[]{:S(2)}, u32[]{:S(2)}) collective-permute-start(bf16[96,96]{1,0:T(8,128)(2,1)S(1)} %divide_convert_fusion.4), channel_id=1, source_target_pairs={{0,8},{1,9},{2,10},{3,11},{4,12},{5,13},{6,14},{7,15},{8,16},{9,17... | collective-permute-start | bytes 55304 | tf_op jit(solution)/shard_map/ppermute | solution.py:71
  33.7 1.3 %multiply_reduce_fusion.5 = (f32[]{:T(128)}, f32[96,96]{1,0:T(8,128)S(1)}) fusion(f32[1536,96]{1,0:T(8,128)S(1)} %copy-done.2, f32[2,96,1536]{2,1,0:T(8,128)S(1)} %get-tuple-element.7), kind=kOutput, calls=%fused_computation.80 | convolution fusion | flops 169887744 | bytes 1413124 | tf_op jit(solution)/shard_map/dot_general | solution.py:185
  35.8 0.2 collective-permute-start.6
  36.1 0.2 copy.17
  36.5 5.1 %shard_map.105 = f32[16,96,128]{2,1,0:T(8,128)S(1)} custom-call(bf16[1536,96]{1,0:T(8,128)(2,1)S(1)} %reshape_squeeze.12.wd_ref, bf16[96,2048]{1,0:T(8,128)(2,1)S(1)} %bitcast.111, bf16[256,256]{1,0:T(8,128)(2,1)S(1)} %fusion.t_ref, bf16[96,1536]{1,0:T(8,128)(2,1)S(1)} %get-tuple-element.13.qt_ref), custom_call_target="tpu_custom_call" | custom-call | tf_op jit(solution)/shard_map/pallas_call | solution.py:115
  41.6 0.8 %multiply_reduce_fusion.1 = f32[]{:T(128)} fusion(f32[16,96,128]{2,1,0:T(8,128)S(1)} %shard_map.105), kind=kLoop, calls=%fused_computation.16 | loop fusion | flops 294911 | bytes 589828 | tf_op jit(solution)/shard_map/reduce_sum | solution.py:75
  43.2 0.2 copy.22
  43.4 1.1 %convert_element_type.57 = bf16[96,1536]{1,0:T(8,128)(2,1)} reshape(bf16[96,16,96]{2,1,0:T(8,128)(2,1)S(1)} %copy.22) | data formatting | bytes 589824 | tf_op jit(solution)/shard_map/convert_element_type | solution.py:192
  44.5 0.4 collective-permute-start.9
  44.9 0.2 fusion.91
  45.2 0.2 convolution_add_fusion.1
  45.5 0.2 fusion.86
  45.7 1.2 %reshape.125 = f32[1536,96]{1,0:T(8,128)} reshape(f32[96,1536]{1,0:T(8,128)S(1)} %fusion.91) | data formatting | bytes 1179648 | tf_op jit(solution)/shard_map/reshape | solution.py:175
  46.9 0.3 add.138
  47.2 0.3 copy.15
  47.4 1.2 %reshape.119 = f32[1536,96]{1,0:T(8,128)} reshape(f32[96,1536]{1,0:T(8,128)S(1)} %fusion.86) | data formatting | bytes 1179648 | tf_op jit(solution)/shard_map/reshape | solution.py:175
  48.6 0.2 convolution_add_fusion
  48.8 0.3 add.140
  49.1 0.3 copy.16
  49.5 5.3 %shard_map.104 = (f32[2,96,1536]{2,1,0:T(8,128)S(1)}, bf16[2,96,1536]{2,1,0:T(8,128)(2,1)S(1)}) custom-call(f32[2,96,1536]{2,1,0:T(8,128)S(1)} %maximum_bitcast_fusion.1.y_ref), custom_call_target="tpu_custom_call" | custom-call | tf_op jit(solution)/shard_map/pallas_call | solution.py:54
  54.7 1.3 %multiply_reduce_fusion.2 = (f32[]{:T(128)}, f32[96,96]{1,0:T(8,128)S(1)}) fusion(f32[1536,96]{1,0:T(8,128)S(1)} %copy-done.4, f32[2,96,1536]{2,1,0:T(8,128)S(1)} %get-tuple-element.8), kind=kOutput, calls=%fused_computation.74 | convolution fusion | flops 169887744 | bytes 1413124 | tf_op jit(solution)/shard_map/dot_general | solution.py:185
  56.8 0.7 collective-permute-start.11
  57.5 0.2 copy.23
  57.8 0.1 copy.32
  57.9 1.3 %reshape.123.wd_ref = bf16[1536,96]{1,0:T(8,128)(2,1)S(1)} reshape(bf16[96,1536]{1,0:T(8,128)(2,1)} %collective-permute-done.9) | data formatting | bytes 589824 | tf_op jit(solution)/shard_map/reshape | solution.py:111
  59.2 5.1 %shard_map.106 = f32[16,96,128]{2,1,0:T(8,128)S(1)} custom-call(bf16[1536,96]{1,0:T(8,128)(2,1)S(1)} %reshape.123.wd_ref, bf16[96,2048]{1,0:T(8,128)(2,1)S(1)} %bitcast.110, bf16[256,256]{1,0:T(8,128)(2,1)S(1)} %fusion.t_ref, bf16[96,1536]{1,0:T(8,128)(2,1)S(1)} %get-tuple-element.11.qt_ref), custom_call_target="tpu_custom_call" | custom-call | tf_op jit(solution)/shard_map/pallas_call | solution.py:115
  64.3 0.8 %multiply_reduce_fusion = f32[]{:T(128)} fusion(f32[16,96,128]{2,1,0:T(8,128)S(1)} %shard_map.106), kind=kLoop, calls=%fused_computation.14 | loop fusion | flops 294911 | bytes 589828 | tf_op jit(solution)/shard_map/reduce_sum | solution.py:75
  65.9 0.2 copy.24
  66.1 0.4 convert_element_type.60
  66.5 1.2 %collective-permute-start.10 = (bf16[96,1536]{1,0:T(8,128)(2,1)S(1)}, bf16[96,1536]{1,0:T(8,128)(2,1)S(1)}, u32[]{:S(2)}, u32[]{:S(2)}) collective-permute-start(bf16[96,1536]{1,0:T(8,128)(2,1)S(1)} %convert_element_type.60), channel_id=1, source_target_pairs={{0,8},{1,9},{2,10},{3,11},{4,12},{5,13},{6,14},{7,15},{8,16},{9,17... | collective-permute-start | bytes 884744 | tf_op jit(solution)/shard_map/ppermute | solution.py:71
  67.7 1.3 %multiply_reduce_fusion.3 = (f32[]{:T(128)}, f32[96,96]{1,0:T(8,128)S(1)}) fusion(f32[1536,96]{1,0:T(8,128)S(1)} %copy-done.1, f32[2,96,1536]{2,1,0:T(8,128)S(1)} %get-tuple-element.8), kind=kOutput, calls=%fused_computation.76 | convolution fusion | flops 169887744 | bytes 1413124 | tf_op jit(solution)/shard_map/dot_general | solution.py:184
  69.7 0.5 collective-permute-start.8
  70.2 2.8 %collective-permute-done.8 = bf16[96,96]{1,0:T(8,128)(2,1)S(1)} collective-permute-done((bf16[96,96]{1,0:T(8,128)(2,1)S(1)}, bf16[96,96]{1,0:T(8,128)(2,1)S(1)}, u32[]{:S(2)}, u32[]{:S(2)}) %collective-permute-start.8) | collective-permute-done | bytes 18464 | tf_op jit(solution)/shard_map/ppermute | solution.py:71
  73.0 0.6 copy.37
  73.6 0.7 copy.38
  74.3 0.6 copy.39
  (57 shorter events, 1.2 us)
Async XLA Ops:
  0.6 12.1 %copy-start = (f32[2,2]{1,0:T(2,128)S(1)}, f32[2,2]{1,0:T(2,128)}, u32[]{:S(2)}) copy-start(f32[2,2]{1,0:T(2,128)} %param.14) | copy-start | bytes 52
  0.6 10.7 %copy-start.10 = (bf16[1,1,2,256]{3,2,1,0:T(2,128)(2,1)S(1)}, bf16[1,1,2,256]{3,2,1,0:T(2,128)(2,1)}, u32[]{:S(2)}) copy-start(bf16[1,1,2,256]{3,2,1,0:T(2,128)(2,1)} %param.13) | copy-start | bytes 3076
  0.7 17.8 %collective-permute-start.1 = (bf16[96,1536]{1,0:T(8,128)(2,1)}, bf16[96,1536]{1,0:T(8,128)(2,1)S(1)}, u32[]{:S(2)}, u32[]{:S(2)}) collective-permute-start(bf16[96,1536]{1,0:T(8,128)(2,1)} %bitcast.117), channel_id=1, source_target_pairs={{0,7},{1,0},{2,1},{3,2},{4,3},{5,4},{6,5},{7,6},{8,15},{9,8},{10,9... | collective-permute-start | bytes 884744 | tf_op jit(solution)/shard_map/ppermute | solution.py:71
  6.7 11.7 %collective-permute-start = (bf16[96,96]{1,0:T(8,128)(2,1)}, bf16[96,96]{1,0:T(8,128)(2,1)S(1)}, u32[]{:S(2)}, u32[]{:S(2)}) collective-permute-start(bf16[96,96]{1,0:T(8,128)(2,1)} %bitcast.122), channel_id=1, source_target_pairs={{0,7},{1,0},{2,1},{3,2},{4,3},{5,4},{6,5},{7,6},{8,15},{9,8},{10,9... | collective-permute-start | bytes 55304 | tf_op jit(solution)/shard_map/ppermute | solution.py:71
  7.2 12.2 %collective-permute-start.3 = (bf16[96,1536]{1,0:T(8,128)(2,1)}, bf16[96,1536]{1,0:T(8,128)(2,1)S(1)}, u32[]{:S(2)}, u32[]{:S(2)}) collective-permute-start(bf16[96,1536]{1,0:T(8,128)(2,1)} %bitcast.116), channel_id=1, source_target_pairs={{0,1},{1,2},{2,3},{3,4},{4,5},{5,6},{6,7},{7,0},{8,9},{9,10},{10,1... | collective-permute-start | bytes 884744 | tf_op jit(solution)/shard_map/ppermute | solution.py:71
  8.8 10.7 %collective-permute-start.2 = (bf16[96,96]{1,0:T(8,128)(2,1)}, bf16[96,96]{1,0:T(8,128)(2,1)S(1)}, u32[]{:S(2)}, u32[]{:S(2)}) collective-permute-start(bf16[96,96]{1,0:T(8,128)(2,1)} %bitcast.123), channel_id=1, source_target_pairs={{0,1},{1,2},{2,3},{3,4},{4,5},{5,6},{6,7},{7,0},{8,9},{9,10},{10,1... | collective-permute-start | bytes 55304 | tf_op jit(solution)/shard_map/ppermute | solution.py:71
  10.0 2.9 %copy-start.11 = (s32[4]{0:T(128)S(1)}, s32[4]{0:T(128)}, u32[]{:S(2)}) copy-start(s32[4]{0:T(128)} %param.15) | copy-start | bytes 52
  15.7 2.4 %copy-start.9 = (bf16[1,1,96,1536]{3,2,1,0:T(8,128)(2,1)S(1)}, bf16[1,1,96,1536]{3,2,1,0:T(8,128)(2,1)}, u32[]{:S(2)}) copy-start(bf16[1,1,96,1536]{3,2,1,0:T(8,128)(2,1)} %param.10) | copy-start | bytes 884740
  18.5 0.7 copy-start.7
  20.2 5.4 %copy-start.3 = (f32[1536,96]{1,0:T(8,128)S(1)}, f32[1536,96]{1,0:T(8,128)}, u32[]{:S(2)}) copy-start(f32[1536,96]{1,0:T(8,128)} %reshape.118) | copy-start | bytes 1769476
  20.3 13.4 %copy-start.2 = (f32[1536,96]{1,0:T(8,128)S(1)}, f32[1536,96]{1,0:T(8,128)}, u32[]{:S(2)}) copy-start(f32[1536,96]{1,0:T(8,128)} %reshape.117) | copy-start | bytes 1769476
  27.6 17.5 %collective-permute-start.5 = (bf16[96,96]{1,0:T(8,128)(2,1)S(1)}, bf16[96,96]{1,0:T(8,128)(2,1)S(1)}, u32[]{:S(2)}, u32[]{:S(2)}) collective-permute-start(bf16[96,96]{1,0:T(8,128)(2,1)S(1)} %divide_convert_fusion.4), channel_id=1, source_target_pairs={{0,15},{1,8},{2,9},{3,10},{4,11},{5,12},{6,13},{7,14},{8,23},{9,16... | collective-permute-start | bytes 55304 | tf_op jit(solution)/shard_map/ppermute | solution.py:71
  30.9 14.5 %collective-permute-start.7 = (bf16[96,96]{1,0:T(8,128)(2,1)S(1)}, bf16[96,96]{1,0:T(8,128)(2,1)S(1)}, u32[]{:S(2)}, u32[]{:S(2)}) collective-permute-start(bf16[96,96]{1,0:T(8,128)(2,1)S(1)} %divide_convert_fusion.4), channel_id=1, source_target_pairs={{0,8},{1,9},{2,10},{3,11},{4,12},{5,13},{6,14},{7,15},{8,16},{9,17... | collective-permute-start | bytes 55304 | tf_op jit(solution)/shard_map/ppermute | solution.py:71
  35.7 9.2 %collective-permute-start.4 = (bf16[96,96]{1,0:T(8,128)(2,1)S(1)}, bf16[96,96]{1,0:T(8,128)(2,1)S(1)}, u32[]{:S(2)}, u32[]{:S(2)}) collective-permute-start(bf16[96,96]{1,0:T(8,128)(2,1)S(1)} %divide_convert_fusion.5), channel_id=1, source_target_pairs={{0,8},{1,9},{2,10},{3,11},{4,12},{5,13},{6,14},{7,15},{8,16},{9,17... | collective-permute-start | bytes 55304 | tf_op jit(solution)/shard_map/ppermute | solution.py:71
  35.8 12.8 %collective-permute-start.6 = (bf16[96,96]{1,0:T(8,128)(2,1)S(1)}, bf16[96,96]{1,0:T(8,128)(2,1)S(1)}, u32[]{:S(2)}, u32[]{:S(2)}) collective-permute-start(bf16[96,96]{1,0:T(8,128)(2,1)S(1)} %divide_convert_fusion.5), channel_id=1, source_target_pairs={{0,9},{1,10},{2,11},{3,12},{4,13},{5,14},{6,15},{7,8},{8,17},{9,18... | collective-permute-start | bytes 55304 | tf_op jit(solution)/shard_map/ppermute | solution.py:71
  43.1 1.8 %copy-start.5 = (bf16[1,1,96,1536]{3,2,1,0:T(8,128)(2,1)S(1)}, bf16[1,1,96,1536]{3,2,1,0:T(8,128)(2,1)}, u32[]{:S(2)}) copy-start(bf16[1,1,96,1536]{3,2,1,0:T(8,128)(2,1)} %param.12) | copy-start | bytes 884740
  43.2 1.9 %copy-start.8 = (bf16[96,1536]{1,0:T(8,128)(2,1)S(1)}, bf16[96,1536]{1,0:T(8,128)(2,1)}, u32[]{:S(2)}) copy-start(bf16[96,1536]{1,0:T(8,128)(2,1)} %copy-done.7) | copy-start | bytes 884740
  44.5 1.0 %copy-start.6 = (bf16[1,1,96,1536]{3,2,1,0:T(8,128)(2,1)S(1)}, bf16[1,1,96,1536]{3,2,1,0:T(8,128)(2,1)}, u32[]{:S(2)}) copy-start(bf16[1,1,96,1536]{3,2,1,0:T(8,128)(2,1)} %param.9) | copy-start | bytes 884740
  44.5 13.4 %collective-permute-start.9 = (bf16[96,1536]{1,0:T(8,128)(2,1)}, bf16[96,1536]{1,0:T(8,128)(2,1)}, u32[]{:S(2)}, u32[]{:S(2)}) collective-permute-start(bf16[96,1536]{1,0:T(8,128)(2,1)} %convert_element_type.57), channel_id=1, source_target_pairs={{0,8},{1,9},{2,10},{3,11},{4,12},{5,13},{6,14},{7,15},{8,16},{9,17... | collective-permute-start | bytes 884744 | tf_op jit(solution)/shard_map/ppermute | solution.py:71
  49.4 5.3 %copy-start.4 = (f32[1536,96]{1,0:T(8,128)S(1)}, f32[1536,96]{1,0:T(8,128)}, u32[]{:S(2)}) copy-start(f32[1536,96]{1,0:T(8,128)} %reshape.125) | copy-start | bytes 1769476
  56.8 13.5 %collective-permute-start.11 = (bf16[96,96]{1,0:T(8,128)(2,1)S(1)}, bf16[96,96]{1,0:T(8,128)(2,1)S(1)}, u32[]{:S(2)}, u32[]{:S(2)}) collective-permute-start(bf16[96,96]{1,0:T(8,128)(2,1)S(1)} %divide_convert_fusion.2), channel_id=1, source_target_pairs={{0,8},{1,9},{2,10},{3,11},{4,12},{5,13},{6,14},{7,15},{8,16},{9,17... | collective-permute-start | bytes 55304 | tf_op jit(solution)/shard_map/ppermute | solution.py:71
  65.8 1.9 %copy-start.1 = (f32[1536,96]{1,0:T(8,128)S(1)}, f32[1536,96]{1,0:T(8,128)}, u32[]{:S(2)}) copy-start(f32[1536,96]{1,0:T(8,128)} %reshape.119) | copy-start | bytes 1769476
  66.5 6.5 %collective-permute-start.10 = (bf16[96,1536]{1,0:T(8,128)(2,1)S(1)}, bf16[96,1536]{1,0:T(8,128)(2,1)S(1)}, u32[]{:S(2)}, u32[]{:S(2)}) collective-permute-start(bf16[96,1536]{1,0:T(8,128)(2,1)S(1)} %convert_element_type.60), channel_id=1, source_target_pairs={{0,8},{1,9},{2,10},{3,11},{4,12},{5,13},{6,14},{7,15},{8,16},{9,17... | collective-permute-start | bytes 884744 | tf_op jit(solution)/shard_map/ppermute | solution.py:71
  69.7 3.3 %collective-permute-start.8 = (bf16[96,96]{1,0:T(8,128)(2,1)S(1)}, bf16[96,96]{1,0:T(8,128)(2,1)S(1)}, u32[]{:S(2)}, u32[]{:S(2)}) collective-permute-start(bf16[96,96]{1,0:T(8,128)(2,1)S(1)} %divide_convert_fusion.3), channel_id=1, source_target_pairs={{0,8},{1,9},{2,10},{3,11},{4,12},{5,13},{6,14},{7,15},{8,16},{9,17... | collective-permute-start | bytes 55304 | tf_op jit(solution)/shard_map/ppermute | solution.py:71

commit v9 on v8

--- a/solution.py
+++ b/solution.py
@@ -181,8 +181,8 @@
         projs, projs16 = polar_factor_t(jnp.swapaxes(jnp.stack([lower + upper_nb, lower_nb + upper]), 1, 2))
         below_t = projs[0]
         above_t = projs[1]
-        new_up = jnp.dot(above_t, upper, precision=lax.Precision.HIGHEST)
-        new_low = jnp.dot(below_t, lower, precision=lax.Precision.HIGHEST)
+        new_up = jnp.dot(above_t, upper, precision=lax.Precision.HIGH)
+        new_low = jnp.dot(below_t, lower, precision=lax.Precision.HIGH)
         new_up = unit_scaled(new_up).astype(jnp.bfloat16)
         new_low = unit_scaled(new_low).astype(jnp.bfloat16)
         if step + 1 < STEPS:

time: 75.2 us -> 74.3 us (0.988)
  matrix products: 11.8 us -> 10.7 us
    dot_general x4, matrix products: 5.3 us -> 4.17 us  [the longest x2 2.09 us: per_device(): new_low = jnp.dot(below_t, lower, precision=lax.Precision.HIGH)]
where the time goes in v9:
time: 74.3 us; the launch traced here: 74 us
  Pallas kernels  20.7 us (28%)
  starting transfers between devices  17.2 us (23%)
  local copies, waits for them, and re-layouts  14.4 us (19%)
  matrix products  10.7 us (14%)
  between operations  5.39 us (7%)
  waiting for transfers between devices  3.01 us (4%)
  other arithmetic  2.63 us (4%)
    ppermute x12, starting transfers between devices, shifted(): return lax.ppermute(tree, ('gx', 'gy'), pairs)  17.2 us
    pallas_call x2, Pallas kernels, polar_factor_t(): pl.pallas_call(polar_kernel, out_shape=(jax.ShapeDtypeStruct(stack.shape,...  10.5 us
    pallas_call x2, Pallas kernels, edge_contract(): pl.pallas_call(edge_kernel, out_shape=jax.ShapeDtypeStruct((dd, n, LANES)...  10.2 us
    reshape x4, local copies, waits for them, and re-layouts, half(): jnp.dot(corner, edge, preferred_element_type=jnp.float32)  4.75 us
    dot_general x8, matrix products, half(): jnp.dot(corner, edge, preferred_element_type=jnp.float32)  3.72 us
    ppermute x12, waiting for transfers between devices, shifted(): return lax.ppermute(tree, ('gx', 'gy'), pairs)  3.01 us
    unnamed x29, local copies, waits for them, and re-layouts  2.51 us
    dot_general x2, matrix products, per_device(): new_low = jnp.dot(below_t, lower, precision=lax.Precision.HIGH)  2.09 us
  transfers between devices with their start and end apart: 12, of which 1 were waited for; matrix products, arithmetic and copies ran while one was open for 32% of the time, Pallas kernels for 21%

profile of v9, /device:TPU:0, one launch (start us, length us, event | category | flops | bytes accessed | tf_op | source)
XLA Modules:
  0.0 74.0 jit_solution(4637533522349446995)
XLA Ops:
  0.7 6.1 %collective-permute-start.1 = (bf16[96,1536]{1,0:T(8,128)(2,1)}, bf16[96,1536]{1,0:T(8,128)(2,1)S(1)}, u32[]{:S(2)}, u32[]{:S(2)}) collective-permute-start(bf16[96,1536]{1,0:T(8,128)(2,1)} %bitcast.117), channel_id=1, source_target_pairs={{0,7},{1,0},{2,1},{3,2},{4,3},{5,4},{6,5},{7,6},{8,15},{9,8},{10,9... | collective-permute-start | bytes 884744 | tf_op jit(solution)/shard_map/ppermute | solution.py:71
  6.7 0.5 collective-permute-start
  7.2 1.5 %collective-permute-start.3 = (bf16[96,1536]{1,0:T(8,128)(2,1)}, bf16[96,1536]{1,0:T(8,128)(2,1)S(1)}, u32[]{:S(2)}, u32[]{:S(2)}) collective-permute-start(bf16[96,1536]{1,0:T(8,128)(2,1)} %bitcast.116), channel_id=1, source_target_pairs={{0,1},{1,2},{2,3},{3,4},{4,5},{5,6},{6,7},{7,0},{8,9},{9,10},{10,1... | collective-permute-start | bytes 884744 | tf_op jit(solution)/shard_map/ppermute | solution.py:71
  8.8 1.2 %fusion.93 = f32[96,1536]{1,0:T(8,128)S(1)} fusion(bf16[1,1,96,1536]{3,2,1,0:T(8,128)(2,1)} %param.12, bf16[1,1,96,96]{3,2,1,0:T(8,128)(2,1)} %param.11), kind=kOutput, calls=%fused_computation.149 | convolution fusion | flops 28311552 | bytes 903168 | tf_op jit(solution)/shard_map/dot_general | solution.py:175
  10.0 1.2 %fusion.88 = f32[96,1536]{1,0:T(8,128)S(1)} fusion(bf16[1,1,96,1536]{3,2,1,0:T(8,128)(2,1)} %param.9, bf16[1,1,96,96]{3,2,1,0:T(8,128)(2,1)} %param.8), kind=kOutput, calls=%fused_computation.144 | convolution fusion | flops 28311552 | bytes 903168 | tf_op jit(solution)/shard_map/dot_general | solution.py:175
  11.3 0.1 reshape_squeeze.14
  11.5 0.3 copy.18
  11.9 0.4 convolution_bitcast_fusion
  12.3 0.4 fusion.56
  12.7 0.2 convolution_bitcast_fusion.1
  12.9 0.6 compare_reduce_fusion
  13.6 0.9 %fusion.2 = bf16[2,4,4,4,4]{3,0,1,2,4:T(2,128)(2,1)S(1)} fusion(f32[2,2,1,1,1]{1,0,4,3,2:T(2,128)S(1)} %convolution_bitcast_fusion.1, pred[]{:T(512)} %compare_reduce_fusion, bf16[2,4,4,4,4]{4,3,2,1,0:T(4,128)(2,1)S(1)} %reshape_squeeze.14), kind=kOutput, calls=%fused_computation.10 | convolution fusion | flops 13824 | bytes 2065 | tf_op jit(solution)/shard_map/st,tabcd->sabcd/dot_general | solution.py:158
  14.5 0.3 copy.21
  14.9 0.4 fusion.24
  15.3 0.4 fusion.t_ref
  15.7 1.2 %reshape.117 = f32[1536,96]{1,0:T(8,128)} reshape(f32[96,1536]{1,0:T(8,128)S(1)} %fusion.93) | data formatting | bytes 1179648 | tf_op jit(solution)/shard_map/reshape | solution.py:175
  16.9 1.2 %reshape.118 = f32[1536,96]{1,0:T(8,128)} reshape(f32[96,1536]{1,0:T(8,128)S(1)} %fusion.88) | data formatting | bytes 1179648 | tf_op jit(solution)/shard_map/reshape | solution.py:175
  18.1 0.3 reshape_squeeze.12.wd_ref
  18.5 0.2 convolution_add_fusion.3
  18.7 0.3 add.132
  19.0 0.2 copy-done.7
  19.2 0.3 copy.13
  19.5 0.2 convolution_add_fusion.2
  19.7 0.3 add.134
  19.9 0.3 copy.14
  20.3 5.3 %shard_map.103 = (f32[2,96,1536]{2,1,0:T(8,128)S(1)}, bf16[2,96,1536]{2,1,0:T(8,128)(2,1)S(1)}) custom-call(f32[2,96,1536]{2,1,0:T(8,128)S(1)} %maximum_bitcast_fusion.y_ref), custom_call_target="tpu_custom_call" | custom-call | tf_op jit(solution)/shard_map/pallas_call | solution.py:54
  25.6 1.0 %multiply_reduce_fusion.4 = (f32[]{:T(128)}, f32[96,96]{1,0:T(8,128)S(1)}) fusion(f32[1536,96]{1,0:T(8,128)S(1)} %copy-done.3, f32[2,96,1536]{2,1,0:T(8,128)S(1)} %get-tuple-element.7), kind=kOutput, calls=%fused_computation.78 | convolution fusion | flops 84953088 | bytes 1413124 | tf_op jit(solution)/shard_map/dot_general | solution.py:184
  27.3 3.3 %collective-permute-start.5 = (bf16[96,96]{1,0:T(8,128)(2,1)S(1)}, bf16[96,96]{1,0:T(8,128)(2,1)S(1)}, u32[]{:S(2)}, u32[]{:S(2)}) collective-permute-start(bf16[96,96]{1,0:T(8,128)(2,1)S(1)} %divide_convert_fusion.4), channel_id=1, source_target_pairs={{0,15},{1,8},{2,9},{3,10},{4,11},{5,12},{6,13},{7,14},{8,23},{9,16... | collective-permute-start | bytes 55304 | tf_op jit(solution)/shard_map/ppermute | solution.py:71
  30.6 2.8 %collective-permute-start.7 = (bf16[96,96]{1,0:T(8,128)(2,1)S(1)}, bf16[96,96]{1,0:T(8,128)(2,1)S(1)}, u32[]{:S(2)}, u32[]{:S(2)}) collective-permute-start(bf16[96,96]{1,0:T(8,128)(2,1)S(1)} %divide_convert_fusion.4), channel_id=1, source_target_pairs={{0,8},{1,9},{2,10},{3,11},{4,12},{5,13},{6,14},{7,15},{8,16},{9,17... | collective-permute-start | bytes 55304 | tf_op jit(solution)/shard_map/ppermute | solution.py:71
  33.4 1.0 %multiply_reduce_fusion.5 = (f32[]{:T(128)}, f32[96,96]{1,0:T(8,128)S(1)}) fusion(f32[1536,96]{1,0:T(8,128)S(1)} %copy-done.2, f32[2,96,1536]{2,1,0:T(8,128)S(1)} %get-tuple-element.7), kind=kOutput, calls=%fused_computation.80 | convolution fusion | flops 84953088 | bytes 1413124 | tf_op jit(solution)/shard_map/dot_general | solution.py:185
  35.2 0.2 collective-permute-start.6
  35.5 0.2 copy.17
  35.8 0.1 copy.33
  36.0 5.1 %shard_map.105 = f32[16,96,128]{2,1,0:T(8,128)S(1)} custom-call(bf16[1536,96]{1,0:T(8,128)(2,1)S(1)} %reshape_squeeze.12.wd_ref, bf16[96,2048]{1,0:T(8,128)(2,1)S(1)} %bitcast.111, bf16[256,256]{1,0:T(8,128)(2,1)S(1)} %fusion.t_ref, bf16[96,1536]{1,0:T(8,128)(2,1)S(1)} %get-tuple-element.13.qt_ref), custom_call_target="tpu_custom_call" | custom-call | tf_op jit(solution)/shard_map/pallas_call | solution.py:115
  41.0 0.8 %multiply_reduce_fusion.1 = f32[]{:T(128)} fusion(f32[16,96,128]{2,1,0:T(8,128)S(1)} %shard_map.105), kind=kLoop, calls=%fused_computation.16 | loop fusion | flops 294911 | bytes 589828 | tf_op jit(solution)/shard_map/reduce_sum | solution.py:75
  42.7 0.2 copy.22
  42.8 1.1 %convert_element_type.57 = bf16[96,1536]{1,0:T(8,128)(2,1)} reshape(bf16[96,16,96]{2,1,0:T(8,128)(2,1)S(1)} %copy.22) | data formatting | bytes 589824 | tf_op jit(solution)/shard_map/convert_element_type | solution.py:192
  43.9 0.4 collective-permute-start.9
  44.3 0.2 fusion.91
  44.6 0.2 convolution_add_fusion.1
  44.9 0.2 fusion.86
  45.1 1.2 %reshape.125 = f32[1536,96]{1,0:T(8,128)} reshape(f32[96,1536]{1,0:T(8,128)S(1)} %fusion.91) | data formatting | bytes 1179648 | tf_op jit(solution)/shard_map/reshape | solution.py:175
  46.3 0.3 add.138
  46.6 0.3 copy.15
  46.8 1.2 %reshape.119 = f32[1536,96]{1,0:T(8,128)} reshape(f32[96,1536]{1,0:T(8,128)S(1)} %fusion.86) | data formatting | bytes 1179648 | tf_op jit(solution)/shard_map/reshape | solution.py:175
  48.0 0.2 convolution_add_fusion
  48.3 0.3 add.140
  48.5 0.3 copy.16
  48.9 5.3 %shard_map.104 = (f32[2,96,1536]{2,1,0:T(8,128)S(1)}, bf16[2,96,1536]{2,1,0:T(8,128)(2,1)S(1)}) custom-call(f32[2,96,1536]{2,1,0:T(8,128)S(1)} %maximum_bitcast_fusion.1.y_ref), custom_call_target="tpu_custom_call" | custom-call | tf_op jit(solution)/shard_map/pallas_call | solution.py:54
  54.2 1.0 %multiply_reduce_fusion.2 = (f32[]{:T(128)}, f32[96,96]{1,0:T(8,128)S(1)}) fusion(f32[1536,96]{1,0:T(8,128)S(1)} %copy-done.4, f32[2,96,1536]{2,1,0:T(8,128)S(1)} %get-tuple-element.8), kind=kOutput, calls=%fused_computation.74 | convolution fusion | flops 84953088 | bytes 1413124 | tf_op jit(solution)/shard_map/dot_general | solution.py:185
  55.9 0.7 collective-permute-start.11
  56.6 0.2 copy.23
  57.1 1.3 %reshape.123.wd_ref = bf16[1536,96]{1,0:T(8,128)(2,1)S(1)} reshape(bf16[96,1536]{1,0:T(8,128)(2,1)} %collective-permute-done.9) | data formatting | bytes 589824 | tf_op jit(solution)/shard_map/reshape | solution.py:111
  58.4 5.1 %shard_map.106 = f32[16,96,128]{2,1,0:T(8,128)S(1)} custom-call(bf16[1536,96]{1,0:T(8,128)(2,1)S(1)} %reshape.123.wd_ref, bf16[96,2048]{1,0:T(8,128)(2,1)S(1)} %bitcast.110, bf16[256,256]{1,0:T(8,128)(2,1)S(1)} %fusion.t_ref, bf16[96,1536]{1,0:T(8,128)(2,1)S(1)} %get-tuple-element.11.qt_ref), custom_call_target="tpu_custom_call" | custom-call | tf_op jit(solution)/shard_map/pallas_call | solution.py:115
  63.5 0.8 %multiply_reduce_fusion = f32[]{:T(128)} fusion(f32[16,96,128]{2,1,0:T(8,128)S(1)} %shard_map.106), kind=kLoop, calls=%fused_computation.14 | loop fusion | flops 294911 | bytes 589828 | tf_op jit(solution)/shard_map/reduce_sum | solution.py:75
  65.1 0.2 copy.24
  65.2 0.4 convert_element_type.60
  65.6 1.2 %collective-permute-start.10 = (bf16[96,1536]{1,0:T(8,128)(2,1)S(1)}, bf16[96,1536]{1,0:T(8,128)(2,1)S(1)}, u32[]{:S(2)}, u32[]{:S(2)}) collective-permute-start(bf16[96,1536]{1,0:T(8,128)(2,1)S(1)} %convert_element_type.60), channel_id=1, source_target_pairs={{0,8},{1,9},{2,10},{3,11},{4,12},{5,13},{6,14},{7,15},{8,16},{9,17... | collective-permute-start | bytes 884744 | tf_op jit(solution)/shard_map/ppermute | solution.py:71
  66.8 1.0 %multiply_reduce_fusion.3 = (f32[]{:T(128)}, f32[96,96]{1,0:T(8,128)S(1)}) fusion(f32[1536,96]{1,0:T(8,128)S(1)} %copy-done.1, f32[2,96,1536]{2,1,0:T(8,128)S(1)} %get-tuple-element.8), kind=kOutput, calls=%fused_computation.76 | convolution fusion | flops 84953088 | bytes 1413124 | tf_op jit(solution)/shard_map/dot_general | solution.py:184
  68.6 0.5 collective-permute-start.8
  69.1 3.0 %collective-permute-done.8 = bf16[96,96]{1,0:T(8,128)(2,1)S(1)} collective-permute-done((bf16[96,96]{1,0:T(8,128)(2,1)S(1)}, bf16[96,96]{1,0:T(8,128)(2,1)S(1)}, u32[]{:S(2)}, u32[]{:S(2)}) %collective-permute-start.8) | collective-permute-done | bytes 18464 | tf_op jit(solution)/shard_map/ppermute | solution.py:71
  72.1 0.6 copy.37
  72.7 0.7 copy.38
  73.4 0.6 copy.39
  (57 shorter events, 1.2 us)
Async XLA Ops:
  0.6 12.1 %copy-start = (f32[2,2]{1,0:T(2,128)S(1)}, f32[2,2]{1,0:T(2,128)}, u32[]{:S(2)}) copy-start(f32[2,2]{1,0:T(2,128)} %param.14) | copy-start | bytes 52
  0.6 10.7 %copy-start.10 = (bf16[1,1,2,256]{3,2,1,0:T(2,128)(2,1)S(1)}, bf16[1,1,2,256]{3,2,1,0:T(2,128)(2,1)}, u32[]{:S(2)}) copy-start(bf16[1,1,2,256]{3,2,1,0:T(2,128)(2,1)} %param.13) | copy-start | bytes 3076
  0.7 17.8 %collective-permute-start.1 = (bf16[96,1536]{1,0:T(8,128)(2,1)}, bf16[96,1536]{1,0:T(8,128)(2,1)S(1)}, u32[]{:S(2)}, u32[]{:S(2)}) collective-permute-start(bf16[96,1536]{1,0:T(8,128)(2,1)} %bitcast.117), channel_id=1, source_target_pairs={{0,7},{1,0},{2,1},{3,2},{4,3},{5,4},{6,5},{7,6},{8,15},{9,8},{10,9... | collective-permute-start | bytes 884744 | tf_op jit(solution)/shard_map/ppermute | solution.py:71
  6.7 11.7 %collective-permute-start = (bf16[96,96]{1,0:T(8,128)(2,1)}, bf16[96,96]{1,0:T(8,128)(2,1)S(1)}, u32[]{:S(2)}, u32[]{:S(2)}) collective-permute-start(bf16[96,96]{1,0:T(8,128)(2,1)} %bitcast.122), channel_id=1, source_target_pairs={{0,7},{1,0},{2,1},{3,2},{4,3},{5,4},{6,5},{7,6},{8,15},{9,8},{10,9... | collective-permute-start | bytes 55304 | tf_op jit(solution)/shard_map/ppermute | solution.py:71
  7.2 12.2 %collective-permute-start.3 = (bf16[96,1536]{1,0:T(8,128)(2,1)}, bf16[96,1536]{1,0:T(8,128)(2,1)S(1)}, u32[]{:S(2)}, u32[]{:S(2)}) collective-permute-start(bf16[96,1536]{1,0:T(8,128)(2,1)} %bitcast.116), channel_id=1, source_target_pairs={{0,1},{1,2},{2,3},{3,4},{4,5},{5,6},{6,7},{7,0},{8,9},{9,10},{10,1... | collective-permute-start | bytes 884744 | tf_op jit(solution)/shard_map/ppermute | solution.py:71
  8.8 10.7 %collective-permute-start.2 = (bf16[96,96]{1,0:T(8,128)(2,1)}, bf16[96,96]{1,0:T(8,128)(2,1)S(1)}, u32[]{:S(2)}, u32[]{:S(2)}) collective-permute-start(bf16[96,96]{1,0:T(8,128)(2,1)} %bitcast.123), channel_id=1, source_target_pairs={{0,1},{1,2},{2,3},{3,4},{4,5},{5,6},{6,7},{7,0},{8,9},{9,10},{10,1... | collective-permute-start | bytes 55304 | tf_op jit(solution)/shard_map/ppermute | solution.py:71
  10.0 2.9 %copy-start.11 = (s32[4]{0:T(128)S(1)}, s32[4]{0:T(128)}, u32[]{:S(2)}) copy-start(s32[4]{0:T(128)} %param.15) | copy-start | bytes 52
  15.7 2.4 %copy-start.9 = (bf16[1,1,96,1536]{3,2,1,0:T(8,128)(2,1)S(1)}, bf16[1,1,96,1536]{3,2,1,0:T(8,128)(2,1)}, u32[]{:S(2)}) copy-start(bf16[1,1,96,1536]{3,2,1,0:T(8,128)(2,1)} %param.10) | copy-start | bytes 884740
  18.5 0.7 copy-start.7
  20.2 5.4 %copy-start.3 = (f32[1536,96]{1,0:T(8,128)S(1)}, f32[1536,96]{1,0:T(8,128)}, u32[]{:S(2)}) copy-start(f32[1536,96]{1,0:T(8,128)} %reshape.118) | copy-start | bytes 1769476
  20.3 13.1 %copy-start.2 = (f32[1536,96]{1,0:T(8,128)S(1)}, f32[1536,96]{1,0:T(8,128)}, u32[]{:S(2)}) copy-start(f32[1536,96]{1,0:T(8,128)} %reshape.117) | copy-start | bytes 1769476
  27.3 17.2 %collective-permute-start.5 = (bf16[96,96]{1,0:T(8,128)(2,1)S(1)}, bf16[96,96]{1,0:T(8,128)(2,1)S(1)}, u32[]{:S(2)}, u32[]{:S(2)}) collective-permute-start(bf16[96,96]{1,0:T(8,128)(2,1)S(1)} %divide_convert_fusion.4), channel_id=1, source_target_pairs={{0,15},{1,8},{2,9},{3,10},{4,11},{5,12},{6,13},{7,14},{8,23},{9,16... | collective-permute-start | bytes 55304 | tf_op jit(solution)/shard_map/ppermute | solution.py:71
  30.6 14.2 %collective-permute-start.7 = (bf16[96,96]{1,0:T(8,128)(2,1)S(1)}, bf16[96,96]{1,0:T(8,128)(2,1)S(1)}, u32[]{:S(2)}, u32[]{:S(2)}) collective-permute-start(bf16[96,96]{1,0:T(8,128)(2,1)S(1)} %divide_convert_fusion.4), channel_id=1, source_target_pairs={{0,8},{1,9},{2,10},{3,11},{4,12},{5,13},{6,14},{7,15},{8,16},{9,17... | collective-permute-start | bytes 55304 | tf_op jit(solution)/shard_map/ppermute | solution.py:71
  35.2 9.2 %collective-permute-start.4 = (bf16[96,96]{1,0:T(8,128)(2,1)S(1)}, bf16[96,96]{1,0:T(8,128)(2,1)S(1)}, u32[]{:S(2)}, u32[]{:S(2)}) collective-permute-start(bf16[96,96]{1,0:T(8,128)(2,1)S(1)} %divide_convert_fusion.5), channel_id=1, source_target_pairs={{0,8},{1,9},{2,10},{3,11},{4,12},{5,13},{6,14},{7,15},{8,16},{9,17... | collective-permute-start | bytes 55304 | tf_op jit(solution)/shard_map/ppermute | solution.py:71
  35.2 12.8 %collective-permute-start.6 = (bf16[96,96]{1,0:T(8,128)(2,1)S(1)}, bf16[96,96]{1,0:T(8,128)(2,1)S(1)}, u32[]{:S(2)}, u32[]{:S(2)}) collective-permute-start(bf16[96,96]{1,0:T(8,128)(2,1)S(1)} %divide_convert_fusion.5), channel_id=1, source_target_pairs={{0,9},{1,10},{2,11},{3,12},{4,13},{5,14},{6,15},{7,8},{8,17},{9,18... | collective-permute-start | bytes 55304 | tf_op jit(solution)/shard_map/ppermute | solution.py:71
  42.6 1.8 %copy-start.5 = (bf16[1,1,96,1536]{3,2,1,0:T(8,128)(2,1)S(1)}, bf16[1,1,96,1536]{3,2,1,0:T(8,128)(2,1)}, u32[]{:S(2)}) copy-start(bf16[1,1,96,1536]{3,2,1,0:T(8,128)(2,1)} %param.12) | copy-start | bytes 884740
  42.6 1.9 %copy-start.8 = (bf16[96,1536]{1,0:T(8,128)(2,1)S(1)}, bf16[96,1536]{1,0:T(8,128)(2,1)}, u32[]{:S(2)}) copy-start(bf16[96,1536]{1,0:T(8,128)(2,1)} %copy-done.7) | copy-start | bytes 884740
  43.9 1.0 %copy-start.6 = (bf16[1,1,96,1536]{3,2,1,0:T(8,128)(2,1)S(1)}, bf16[1,1,96,1536]{3,2,1,0:T(8,128)(2,1)}, u32[]{:S(2)}) copy-start(bf16[1,1,96,1536]{3,2,1,0:T(8,128)(2,1)} %param.9) | copy-start | bytes 884740
  43.9 13.1 %collective-permute-start.9 = (bf16[96,1536]{1,0:T(8,128)(2,1)}, bf16[96,1536]{1,0:T(8,128)(2,1)}, u32[]{:S(2)}, u32[]{:S(2)}) collective-permute-start(bf16[96,1536]{1,0:T(8,128)(2,1)} %convert_element_type.57), channel_id=1, source_target_pairs={{0,8},{1,9},{2,10},{3,11},{4,12},{5,13},{6,14},{7,15},{8,16},{9,17... | collective-permute-start | bytes 884744 | tf_op jit(solution)/shard_map/ppermute | solution.py:71
  48.9 5.3 %copy-start.4 = (f32[1536,96]{1,0:T(8,128)S(1)}, f32[1536,96]{1,0:T(8,128)}, u32[]{:S(2)}) copy-start(f32[1536,96]{1,0:T(8,128)} %reshape.125) | copy-start | bytes 1769476
  55.9 13.2 %collective-permute-start.11 = (bf16[96,96]{1,0:T(8,128)(2,1)S(1)}, bf16[96,96]{1,0:T(8,128)(2,1)S(1)}, u32[]{:S(2)}, u32[]{:S(2)}) collective-permute-start(bf16[96,96]{1,0:T(8,128)(2,1)S(1)} %divide_convert_fusion.2), channel_id=1, source_target_pairs={{0,8},{1,9},{2,10},{3,11},{4,12},{5,13},{6,14},{7,15},{8,16},{9,17... | collective-permute-start | bytes 55304 | tf_op jit(solution)/shard_map/ppermute | solution.py:71
  65.0 1.9 %copy-start.1 = (f32[1536,96]{1,0:T(8,128)S(1)}, f32[1536,96]{1,0:T(8,128)}, u32[]{:S(2)}) copy-start(f32[1536,96]{1,0:T(8,128)} %reshape.119) | copy-start | bytes 1769476
  65.6 6.5 %collective-permute-start.10 = (bf16[96,1536]{1,0:T(8,128)(2,1)S(1)}, bf16[96,1536]{1,0:T(8,128)(2,1)S(1)}, u32[]{:S(2)}, u32[]{:S(2)}) collective-permute-start(bf16[96,1536]{1,0:T(8,128)(2,1)S(1)} %convert_element_type.60), channel_id=1, source_target_pairs={{0,8},{1,9},{2,10},{3,11},{4,12},{5,13},{6,14},{7,15},{8,16},{9,17... | collective-permute-start | bytes 884744 | tf_op jit(solution)/shard_map/ppermute | solution.py:71
  68.6 3.5 %collective-permute-start.8 = (bf16[96,96]{1,0:T(8,128)(2,1)S(1)}, bf16[96,96]{1,0:T(8,128)(2,1)S(1)}, u32[]{:S(2)}, u32[]{:S(2)}) collective-permute-start(bf16[96,96]{1,0:T(8,128)(2,1)S(1)} %divide_convert_fusion.3), channel_id=1, source_target_pairs={{0,8},{1,9},{2,10},{3,11},{4,12},{5,13},{6,14},{7,15},{8,16},{9,17... | collective-permute-start | bytes 55304 | tf_op jit(solution)/shard_map/ppermute | solution.py:71

commit v10 on v9

--- a/solution.py
+++ b/solution.py
@@ -86,7 +86,7 @@
         for k in range(group):
             f_ref[:, d0 + k] = part[:, k * LANES:(k + 1) * LANES].reshape(n, dd, LANES)
     t = t_ref[...]
-    per = math.gcd(n, 48)
+    per = n
 
     def mid_body(h, carry):
         x = jnp.concatenate([f_ref[h * per + k].reshape(dd * dd, LANES) for k in range(per)], axis=1)

time: 74.3 us -> 73.2 us (0.985)
  Pallas kernels: 20.7 us -> 19.6 us
    pallas_call x2, Pallas kernels: 10.2 us -> 9.05 us  [edge_contract(): pl.pallas_call(edge_kernel, out_shape=jax.ShapeDtypeStruct((dd, n, LANES)...]
  transfers between devices with their start and end apart: 12 -> 12, of which waited for: 1 -> 1; matrix products, arithmetic and copies ran while one was open for 32% -> 32% of each run, Pallas kernels for 21% -> 20%
where the time goes in v10:
time: 73.2 us; the launch traced here: 72.9 us
  Pallas kernels  19.6 us (27%)
  starting transfers between devices  17.3 us (24%)
  local copies, waits for them, and re-layouts  14.4 us (20%)
  matrix products  10.7 us (15%)
  between operations  5.39 us (7%)
  waiting for transfers between devices  3.01 us (4%)
  other arithmetic  2.62 us (4%)
    ppermute x12, starting transfers between devices, shifted(): return lax.ppermute(tree, ('gx', 'gy'), pairs)  17.3 us
    pallas_call x2, Pallas kernels, polar_factor_t(): pl.pallas_call(polar_kernel, out_shape=(jax.ShapeDtypeStruct(stack.shape,...  10.5 us
    pallas_call x2, Pallas kernels, edge_contract(): pl.pallas_call(edge_kernel, out_shape=jax.ShapeDtypeStruct((dd, n, LANES)...  9.05 us
    reshape x4, local copies, waits for them, and re-layouts, half(): jnp.dot(corner, edge, preferred_element_type=jnp.float32)  4.75 us
    dot_general x8, matrix products, half(): jnp.dot(corner, edge, preferred_element_type=jnp.float32)  3.72 us
    ppermute x12, waiting for transfers between devices, shifted(): return lax.ppermute(tree, ('gx', 'gy'), pairs)  3.01 us
    unnamed x29, local copies, waits for them, and re-layouts  2.5 us
    dot_general x2, matrix products, per_device(): new_low = jnp.dot(below_t, lower, precision=lax.Precision.HIGH)  2.09 us
  transfers between devices with their start and end apart: 12, of which 1 were waited for; matrix products, arithmetic and copies ran while one was open for 32% of the time, Pallas kernels for 20%

profile of v10, /device:TPU:0, one launch (start us, length us, event | category | flops | bytes accessed | tf_op | source)
XLA Modules:
  0.0 72.9 jit_solution(1840987289208688168)
XLA Ops:
  0.7 6.1 %collective-permute-start.1 = (bf16[96,1536]{1,0:T(8,128)(2,1)}, bf16[96,1536]{1,0:T(8,128)(2,1)S(1)}, u32[]{:S(2)}, u32[]{:S(2)}) collective-permute-start(bf16[96,1536]{1,0:T(8,128)(2,1)} %bitcast.117), channel_id=1, source_target_pairs={{0,7},{1,0},{2,1},{3,2},{4,3},{5,4},{6,5},{7,6},{8,15},{9,8},{10,9... | collective-permute-start | bytes 884744 | tf_op jit(solution)/shard_map/ppermute | solution.py:71
  6.7 0.5 collective-permute-start
  7.2 1.5 %collective-permute-start.3 = (bf16[96,1536]{1,0:T(8,128)(2,1)}, bf16[96,1536]{1,0:T(8,128)(2,1)S(1)}, u32[]{:S(2)}, u32[]{:S(2)}) collective-permute-start(bf16[96,1536]{1,0:T(8,128)(2,1)} %bitcast.116), channel_id=1, source_target_pairs={{0,1},{1,2},{2,3},{3,4},{4,5},{5,6},{6,7},{7,0},{8,9},{9,10},{10,1... | collective-permute-start | bytes 884744 | tf_op jit(solution)/shard_map/ppermute | solution.py:71
  8.8 1.2 %fusion.93 = f32[96,1536]{1,0:T(8,128)S(1)} fusion(bf16[1,1,96,1536]{3,2,1,0:T(8,128)(2,1)} %param.12, bf16[1,1,96,96]{3,2,1,0:T(8,128)(2,1)} %param.11), kind=kOutput, calls=%fused_computation.149 | convolution fusion | flops 28311552 | bytes 903168 | tf_op jit(solution)/shard_map/dot_general | solution.py:175
  10.0 1.2 %fusion.88 = f32[96,1536]{1,0:T(8,128)S(1)} fusion(bf16[1,1,96,1536]{3,2,1,0:T(8,128)(2,1)} %param.9, bf16[1,1,96,96]{3,2,1,0:T(8,128)(2,1)} %param.8), kind=kOutput, calls=%fused_computation.144 | convolution fusion | flops 28311552 | bytes 903168 | tf_op jit(solution)/shard_map/dot_general | solution.py:175
  11.3 0.1 reshape_squeeze.14
  11.5 0.3 copy.18
  11.9 0.4 convolution_bitcast_fusion
  12.3 0.4 fusion.56
  12.7 0.2 convolution_bitcast_fusion.1
  12.9 0.6 compare_reduce_fusion
  13.6 0.9 %fusion.2 = bf16[2,4,4,4,4]{3,0,1,2,4:T(2,128)(2,1)S(1)} fusion(f32[2,2,1,1,1]{1,0,4,3,2:T(2,128)S(1)} %convolution_bitcast_fusion.1, pred[]{:T(512)} %compare_reduce_fusion, bf16[2,4,4,4,4]{4,3,2,1,0:T(4,128)(2,1)S(1)} %reshape_squeeze.14), kind=kOutput, calls=%fused_computation.10 | convolution fusion | flops 13824 | bytes 2065 | tf_op jit(solution)/shard_map/st,tabcd->sabcd/dot_general | solution.py:158
  14.5 0.3 copy.21
  14.9 0.4 fusion.24
  15.3 0.4 fusion.t_ref
  15.7 1.2 %reshape.117 = f32[1536,96]{1,0:T(8,128)} reshape(f32[96,1536]{1,0:T(8,128)S(1)} %fusion.93) | data formatting | bytes 1179648 | tf_op jit(solution)/shard_map/reshape | solution.py:175
  16.9 1.2 %reshape.118 = f32[1536,96]{1,0:T(8,128)} reshape(f32[96,1536]{1,0:T(8,128)S(1)} %fusion.88) | data formatting | bytes 1179648 | tf_op jit(solution)/shard_map/reshape | solution.py:175
  18.1 0.3 reshape_squeeze.12.wd_ref
  18.5 0.2 convolution_add_fusion.3
  18.7 0.3 add.132
  19.0 0.2 copy-done.7
  19.2 0.3 copy.13
  19.5 0.2 convolution_add_fusion.2
  19.7 0.3 add.134
  19.9 0.3 copy.14
  20.3 5.3 %shard_map.103 = (f32[2,96,1536]{2,1,0:T(8,128)S(1)}, bf16[2,96,1536]{2,1,0:T(8,128)(2,1)S(1)}) custom-call(f32[2,96,1536]{2,1,0:T(8,128)S(1)} %maximum_bitcast_fusion.y_ref), custom_call_target="tpu_custom_call" | custom-call | tf_op jit(solution)/shard_map/pallas_call | solution.py:54
  25.6 1.0 %multiply_reduce_fusion.4 = (f32[]{:T(128)}, f32[96,96]{1,0:T(8,128)S(1)}) fusion(f32[1536,96]{1,0:T(8,128)S(1)} %copy-done.3, f32[2,96,1536]{2,1,0:T(8,128)S(1)} %get-tuple-element.7), kind=kOutput, calls=%fused_computation.78 | convolution fusion | flops 84953088 | bytes 1413124 | tf_op jit(solution)/shard_map/dot_general | solution.py:184
  27.3 3.3 %collective-permute-start.5 = (bf16[96,96]{1,0:T(8,128)(2,1)S(1)}, bf16[96,96]{1,0:T(8,128)(2,1)S(1)}, u32[]{:S(2)}, u32[]{:S(2)}) collective-permute-start(bf16[96,96]{1,0:T(8,128)(2,1)S(1)} %divide_convert_fusion.4), channel_id=1, source_target_pairs={{0,15},{1,8},{2,9},{3,10},{4,11},{5,12},{6,13},{7,14},{8,23},{9,16... | collective-permute-start | bytes 55304 | tf_op jit(solution)/shard_map/ppermute | solution.py:71
  30.6 2.8 %collective-permute-start.7 = (bf16[96,96]{1,0:T(8,128)(2,1)S(1)}, bf16[96,96]{1,0:T(8,128)(2,1)S(1)}, u32[]{:S(2)}, u32[]{:S(2)}) collective-permute-start(bf16[96,96]{1,0:T(8,128)(2,1)S(1)} %divide_convert_fusion.4), channel_id=1, source_target_pairs={{0,8},{1,9},{2,10},{3,11},{4,12},{5,13},{6,14},{7,15},{8,16},{9,17... | collective-permute-start | bytes 55304 | tf_op jit(solution)/shard_map/ppermute | solution.py:71
  33.4 1.0 %multiply_reduce_fusion.5 = (f32[]{:T(128)}, f32[96,96]{1,0:T(8,128)S(1)}) fusion(f32[1536,96]{1,0:T(8,128)S(1)} %copy-done.2, f32[2,96,1536]{2,1,0:T(8,128)S(1)} %get-tuple-element.7), kind=kOutput, calls=%fused_computation.80 | convolution fusion | flops 84953088 | bytes 1413124 | tf_op jit(solution)/shard_map/dot_general | solution.py:185
  35.2 0.2 collective-permute-start.6
  35.5 0.2 copy.17
  35.8 0.1 copy.33
  36.0 4.5 %shard_map.105 = f32[16,96,128]{2,1,0:T(8,128)S(1)} custom-call(bf16[1536,96]{1,0:T(8,128)(2,1)S(1)} %reshape_squeeze.12.wd_ref, bf16[96,2048]{1,0:T(8,128)(2,1)S(1)} %bitcast.111, bf16[256,256]{1,0:T(8,128)(2,1)S(1)} %fusion.t_ref, bf16[96,1536]{1,0:T(8,128)(2,1)S(1)} %get-tuple-element.13.qt_ref), custom_call_target="tpu_custom_call" | custom-call | tf_op jit(solution)/shard_map/pallas_call | solution.py:115
  40.5 0.8 %multiply_reduce_fusion.1 = f32[]{:T(128)} fusion(f32[16,96,128]{2,1,0:T(8,128)S(1)} %shard_map.105), kind=kLoop, calls=%fused_computation.16 | loop fusion | flops 294911 | bytes 589828 | tf_op jit(solution)/shard_map/reduce_sum | solution.py:75
  42.1 0.2 copy.22
  42.3 1.1 %convert_element_type.57 = bf16[96,1536]{1,0:T(8,128)(2,1)} reshape(bf16[96,16,96]{2,1,0:T(8,128)(2,1)S(1)} %copy.22) | data formatting | bytes 589824 | tf_op jit(solution)/shard_map/convert_element_type | solution.py:192
  43.4 0.4 collective-permute-start.9
  43.8 0.2 fusion.91
  44.0 0.2 convolution_add_fusion.1
  44.3 0.2 fusion.86
  44.6 1.2 %reshape.125 = f32[1536,96]{1,0:T(8,128)} reshape(f32[96,1536]{1,0:T(8,128)S(1)} %fusion.91) | data formatting | bytes 1179648 | tf_op jit(solution)/shard_map/reshape | solution.py:175
  45.8 0.3 add.138
  46.0 0.3 copy.15
  46.3 1.2 %reshape.119 = f32[1536,96]{1,0:T(8,128)} reshape(f32[96,1536]{1,0:T(8,128)S(1)} %fusion.86) | data formatting | bytes 1179648 | tf_op jit(solution)/shard_map/reshape | solution.py:175
  47.5 0.2 convolution_add_fusion
  47.7 0.3 add.140
  47.9 0.3 copy.16
  48.3 5.3 %shard_map.104 = (f32[2,96,1536]{2,1,0:T(8,128)S(1)}, bf16[2,96,1536]{2,1,0:T(8,128)(2,1)S(1)}) custom-call(f32[2,96,1536]{2,1,0:T(8,128)S(1)} %maximum_bitcast_fusion.1.y_ref), custom_call_target="tpu_custom_call" | custom-call | tf_op jit(solution)/shard_map/pallas_call | solution.py:54
  53.6 1.0 %multiply_reduce_fusion.2 = (f32[]{:T(128)}, f32[96,96]{1,0:T(8,128)S(1)}) fusion(f32[1536,96]{1,0:T(8,128)S(1)} %copy-done.4, f32[2,96,1536]{2,1,0:T(8,128)S(1)} %get-tuple-element.8), kind=kOutput, calls=%fused_computation.74 | convolution fusion | flops 84953088 | bytes 1413124 | tf_op jit(solution)/shard_map/dot_general | solution.py:185
  55.3 0.7 collective-permute-start.11
  56.1 0.2 copy.23
  56.5 1.3 %reshape.123.wd_ref = bf16[1536,96]{1,0:T(8,128)(2,1)S(1)} reshape(bf16[96,1536]{1,0:T(8,128)(2,1)} %collective-permute-done.9) | data formatting | bytes 589824 | tf_op jit(solution)/shard_map/reshape | solution.py:111
  57.8 4.5 %shard_map.106 = f32[16,96,128]{2,1,0:T(8,128)S(1)} custom-call(bf16[1536,96]{1,0:T(8,128)(2,1)S(1)} %reshape.123.wd_ref, bf16[96,2048]{1,0:T(8,128)(2,1)S(1)} %bitcast.110, bf16[256,256]{1,0:T(8,128)(2,1)S(1)} %fusion.t_ref, bf16[96,1536]{1,0:T(8,128)(2,1)S(1)} %get-tuple-element.11.qt_ref), custom_call_target="tpu_custom_call" | custom-call | tf_op jit(solution)/shard_map/pallas_call | solution.py:115
  62.4 0.8 %multiply_reduce_fusion = f32[]{:T(128)} fusion(f32[16,96,128]{2,1,0:T(8,128)S(1)} %shard_map.106), kind=kLoop, calls=%fused_computation.14 | loop fusion | flops 294911 | bytes 589828 | tf_op jit(solution)/shard_map/reduce_sum | solution.py:75
  64.0 0.2 copy.24
  64.1 0.4 convert_element_type.60
  64.5 1.2 %collective-permute-start.10 = (bf16[96,1536]{1,0:T(8,128)(2,1)S(1)}, bf16[96,1536]{1,0:T(8,128)(2,1)S(1)}, u32[]{:S(2)}, u32[]{:S(2)}) collective-permute-start(bf16[96,1536]{1,0:T(8,128)(2,1)S(1)} %convert_element_type.60), channel_id=1, source_target_pairs={{0,8},{1,9},{2,10},{3,11},{4,12},{5,13},{6,14},{7,15},{8,16},{9,17... | collective-permute-start | bytes 884744 | tf_op jit(solution)/shard_map/ppermute | solution.py:71
  65.7 1.0 %multiply_reduce_fusion.3 = (f32[]{:T(128)}, f32[96,96]{1,0:T(8,128)S(1)}) fusion(f32[1536,96]{1,0:T(8,128)S(1)} %copy-done.1, f32[2,96,1536]{2,1,0:T(8,128)S(1)} %get-tuple-element.8), kind=kOutput, calls=%fused_computation.76 | convolution fusion | flops 84953088 | bytes 1413124 | tf_op jit(solution)/shard_map/dot_general | solution.py:184
  67.5 0.5 collective-permute-start.8
  68.0 3.0 %collective-permute-done.8 = bf16[96,96]{1,0:T(8,128)(2,1)S(1)} collective-permute-done((bf16[96,96]{1,0:T(8,128)(2,1)S(1)}, bf16[96,96]{1,0:T(8,128)(2,1)S(1)}, u32[]{:S(2)}, u32[]{:S(2)}) %collective-permute-start.8) | collective-permute-done | bytes 18464 | tf_op jit(solution)/shard_map/ppermute | solution.py:71
  71.0 0.6 copy.37
  71.6 0.7 copy.38
  72.3 0.6 copy.39
  (57 shorter events, 1.2 us)
Async XLA Ops:
  0.6 12.1 %copy-start = (f32[2,2]{1,0:T(2,128)S(1)}, f32[2,2]{1,0:T(2,128)}, u32[]{:S(2)}) copy-start(f32[2,2]{1,0:T(2,128)} %param.14) | copy-start | bytes 52
  0.6 10.7 %copy-start.10 = (bf16[1,1,2,256]{3,2,1,0:T(2,128)(2,1)S(1)}, bf16[1,1,2,256]{3,2,1,0:T(2,128)(2,1)}, u32[]{:S(2)}) copy-start(bf16[1,1,2,256]{3,2,1,0:T(2,128)(2,1)} %param.13) | copy-start | bytes 3076
  0.7 17.8 %collective-permute-start.1 = (bf16[96,1536]{1,0:T(8,128)(2,1)}, bf16[96,1536]{1,0:T(8,128)(2,1)S(1)}, u32[]{:S(2)}, u32[]{:S(2)}) collective-permute-start(bf16[96,1536]{1,0:T(8,128)(2,1)} %bitcast.117), channel_id=1, source_target_pairs={{0,7},{1,0},{2,1},{3,2},{4,3},{5,4},{6,5},{7,6},{8,15},{9,8},{10,9... | collective-permute-start | bytes 884744 | tf_op jit(solution)/shard_map/ppermute | solution.py:71
  6.7 11.7 %collective-permute-start = (bf16[96,96]{1,0:T(8,128)(2,1)}, bf16[96,96]{1,0:T(8,128)(2,1)S(1)}, u32[]{:S(2)}, u32[]{:S(2)}) collective-permute-start(bf16[96,96]{1,0:T(8,128)(2,1)} %bitcast.122), channel_id=1, source_target_pairs={{0,7},{1,0},{2,1},{3,2},{4,3},{5,4},{6,5},{7,6},{8,15},{9,8},{10,9... | collective-permute-start | bytes 55304 | tf_op jit(solution)/shard_map/ppermute | solution.py:71
  7.2 12.2 %collective-permute-start.3 = (bf16[96,1536]{1,0:T(8,128)(2,1)}, bf16[96,1536]{1,0:T(8,128)(2,1)S(1)}, u32[]{:S(2)}, u32[]{:S(2)}) collective-permute-start(bf16[96,1536]{1,0:T(8,128)(2,1)} %bitcast.116), channel_id=1, source_target_pairs={{0,1},{1,2},{2,3},{3,4},{4,5},{5,6},{6,7},{7,0},{8,9},{9,10},{10,1... | collective-permute-start | bytes 884744 | tf_op jit(solution)/shard_map/ppermute | solution.py:71
  8.8 10.7 %collective-permute-start.2 = (bf16[96,96]{1,0:T(8,128)(2,1)}, bf16[96,96]{1,0:T(8,128)(2,1)S(1)}, u32[]{:S(2)}, u32[]{:S(2)}) collective-permute-start(bf16[96,96]{1,0:T(8,128)(2,1)} %bitcast.123), channel_id=1, source_target_pairs={{0,1},{1,2},{2,3},{3,4},{4,5},{5,6},{6,7},{7,0},{8,9},{9,10},{10,1... | collective-permute-start | bytes 55304 | tf_op jit(solution)/shard_map/ppermute | solution.py:71
  10.0 2.9 %copy-start.11 = (s32[4]{0:T(128)S(1)}, s32[4]{0:T(128)}, u32[]{:S(2)}) copy-start(s32[4]{0:T(128)} %param.15) | copy-start | bytes 52
  15.7 2.4 %copy-start.9 = (bf16[1,1,96,1536]{3,2,1,0:T(8,128)(2,1)S(1)}, bf16[1,1,96,1536]{3,2,1,0:T(8,128)(2,1)}, u32[]{:S(2)}) copy-start(bf16[1,1,96,1536]{3,2,1,0:T(8,128)(2,1)} %param.10) | copy-start | bytes 884740
  18.5 0.7 copy-start.7
  20.2 5.4 %copy-start.3 = (f32[1536,96]{1,0:T(8,128)S(1)}, f32[1536,96]{1,0:T(8,128)}, u32[]{:S(2)}) copy-start(f32[1536,96]{1,0:T(8,128)} %reshape.118) | copy-start | bytes 1769476
  20.3 13.1 %copy-start.2 = (f32[1536,96]{1,0:T(8,128)S(1)}, f32[1536,96]{1,0:T(8,128)}, u32[]{:S(2)}) copy-start(f32[1536,96]{1,0:T(8,128)} %reshape.117) | copy-start | bytes 1769476
  27.3 16.7 %collective-permute-start.5 = (bf16[96,96]{1,0:T(8,128)(2,1)S(1)}, bf16[96,96]{1,0:T(8,128)(2,1)S(1)}, u32[]{:S(2)}, u32[]{:S(2)}) collective-permute-start(bf16[96,96]{1,0:T(8,128)(2,1)S(1)} %divide_convert_fusion.4), channel_id=1, source_target_pairs={{0,15},{1,8},{2,9},{3,10},{4,11},{5,12},{6,13},{7,14},{8,23},{9,16... | collective-permute-start | bytes 55304 | tf_op jit(solution)/shard_map/ppermute | solution.py:71
  30.6 13.6 %collective-permute-start.7 = (bf16[96,96]{1,0:T(8,128)(2,1)S(1)}, bf16[96,96]{1,0:T(8,128)(2,1)S(1)}, u32[]{:S(2)}, u32[]{:S(2)}) collective-permute-start(bf16[96,96]{1,0:T(8,128)(2,1)S(1)} %divide_convert_fusion.4), channel_id=1, source_target_pairs={{0,8},{1,9},{2,10},{3,11},{4,12},{5,13},{6,14},{7,15},{8,16},{9,17... | collective-permute-start | bytes 55304 | tf_op jit(solution)/shard_map/ppermute | solution.py:71
  35.2 8.6 %collective-permute-start.4 = (bf16[96,96]{1,0:T(8,128)(2,1)S(1)}, bf16[96,96]{1,0:T(8,128)(2,1)S(1)}, u32[]{:S(2)}, u32[]{:S(2)}) collective-permute-start(bf16[96,96]{1,0:T(8,128)(2,1)S(1)} %divide_convert_fusion.5), channel_id=1, source_target_pairs={{0,8},{1,9},{2,10},{3,11},{4,12},{5,13},{6,14},{7,15},{8,16},{9,17... | collective-permute-start | bytes 55304 | tf_op jit(solution)/shard_map/ppermute | solution.py:71
  35.2 12.2 %collective-permute-start.6 = (bf16[96,96]{1,0:T(8,128)(2,1)S(1)}, bf16[96,96]{1,0:T(8,128)(2,1)S(1)}, u32[]{:S(2)}, u32[]{:S(2)}) collective-permute-start(bf16[96,96]{1,0:T(8,128)(2,1)S(1)} %divide_convert_fusion.5), channel_id=1, source_target_pairs={{0,9},{1,10},{2,11},{3,12},{4,13},{5,14},{6,15},{7,8},{8,17},{9,18... | collective-permute-start | bytes 55304 | tf_op jit(solution)/shard_map/ppermute | solution.py:71
  42.0 1.8 %copy-start.5 = (bf16[1,1,96,1536]{3,2,1,0:T(8,128)(2,1)S(1)}, bf16[1,1,96,1536]{3,2,1,0:T(8,128)(2,1)}, u32[]{:S(2)}) copy-start(bf16[1,1,96,1536]{3,2,1,0:T(8,128)(2,1)} %param.12) | copy-start | bytes 884740
  42.1 1.9 %copy-start.8 = (bf16[96,1536]{1,0:T(8,128)(2,1)S(1)}, bf16[96,1536]{1,0:T(8,128)(2,1)}, u32[]{:S(2)}) copy-start(bf16[96,1536]{1,0:T(8,128)(2,1)} %copy-done.7) | copy-start | bytes 884740
  43.4 1.0 %copy-start.6 = (bf16[1,1,96,1536]{3,2,1,0:T(8,128)(2,1)S(1)}, bf16[1,1,96,1536]{3,2,1,0:T(8,128)(2,1)}, u32[]{:S(2)}) copy-start(bf16[1,1,96,1536]{3,2,1,0:T(8,128)(2,1)} %param.9) | copy-start | bytes 884740
  43.4 13.2 %collective-permute-start.9 = (bf16[96,1536]{1,0:T(8,128)(2,1)}, bf16[96,1536]{1,0:T(8,128)(2,1)}, u32[]{:S(2)}, u32[]{:S(2)}) collective-permute-start(bf16[96,1536]{1,0:T(8,128)(2,1)} %convert_element_type.57), channel_id=1, source_target_pairs={{0,8},{1,9},{2,10},{3,11},{4,12},{5,13},{6,14},{7,15},{8,16},{9,17... | collective-permute-start | bytes 884744 | tf_op jit(solution)/shard_map/ppermute | solution.py:71
  48.3 5.3 %copy-start.4 = (f32[1536,96]{1,0:T(8,128)S(1)}, f32[1536,96]{1,0:T(8,128)}, u32[]{:S(2)}) copy-start(f32[1536,96]{1,0:T(8,128)} %reshape.125) | copy-start | bytes 1769476
  55.3 12.7 %collective-permute-start.11 = (bf16[96,96]{1,0:T(8,128)(2,1)S(1)}, bf16[96,96]{1,0:T(8,128)(2,1)S(1)}, u32[]{:S(2)}, u32[]{:S(2)}) collective-permute-start(bf16[96,96]{1,0:T(8,128)(2,1)S(1)} %divide_convert_fusion.2), channel_id=1, source_target_pairs={{0,8},{1,9},{2,10},{3,11},{4,12},{5,13},{6,14},{7,15},{8,16},{9,17... | collective-permute-start | bytes 55304 | tf_op jit(solution)/shard_map/ppermute | solution.py:71
  63.9 1.9 %copy-start.1 = (f32[1536,96]{1,0:T(8,128)S(1)}, f32[1536,96]{1,0:T(8,128)}, u32[]{:S(2)}) copy-start(f32[1536,96]{1,0:T(8,128)} %reshape.119) | copy-start | bytes 1769476
  64.5 6.5 %collective-permute-start.10 = (bf16[96,1536]{1,0:T(8,128)(2,1)S(1)}, bf16[96,1536]{1,0:T(8,128)(2,1)S(1)}, u32[]{:S(2)}, u32[]{:S(2)}) collective-permute-start(bf16[96,1536]{1,0:T(8,128)(2,1)S(1)} %convert_element_type.60), channel_id=1, source_target_pairs={{0,8},{1,9},{2,10},{3,11},{4,12},{5,13},{6,14},{7,15},{8,16},{9,17... | collective-permute-start | bytes 884744 | tf_op jit(solution)/shard_map/ppermute | solution.py:71
  67.5 3.5 %collective-permute-start.8 = (bf16[96,96]{1,0:T(8,128)(2,1)S(1)}, bf16[96,96]{1,0:T(8,128)(2,1)S(1)}, u32[]{:S(2)}, u32[]{:S(2)}) collective-permute-start(bf16[96,96]{1,0:T(8,128)(2,1)S(1)} %divide_convert_fusion.3), channel_id=1, source_target_pairs={{0,8},{1,9},{2,10},{3,11},{4,12},{5,13},{6,14},{7,15},{8,16},{9,17... | collective-permute-start | bytes 55304 | tf_op jit(solution)/shard_map/ppermute | solution.py:71

commit v11 on v10

--- a/solution.py
+++ b/solution.py
@@ -34,6 +34,16 @@
     out = lambda p, q: lax.dot_general(p, q, (((1,), (1,)), ((), ())), preferred_element_type=jnp.float32)
     cross = out(yh, yl)
     return out(yh, yh) + (cross + cross.T)
+
+
+def ns_step(y):
+    out = lambda p, q, dims: lax.dot_general(p, q, (dims, ((), ())), preferred_element_type=jnp.float32)
+    yh, yl = split_bf16(y)
+    cross = out(yh, yl, ((1,), (1,)))
+    gram = out(yh, yh, ((1,), (1,))) + (cross + cross.T)
+    gh, gl = split_bf16(gram)
+    dims = ((1,), (0,))
+    return 1.5 * y - 0.5 * (out(gh, yh, dims) + (out(gh, yl, dims) + out(gl, yh, dims)))
 
 
 def polar_kernel(y_ref, o_ref, h_ref):
@@ -43,8 +53,7 @@
         y = y_ref[b]
         ys.append(y / jnp.sqrt(jnp.sum(y * y) + 1e-06))
     for sweep in range(NS_ITERS):
-        grams = [gram3(y) for y in ys]
-        ys = [1.5 * y - 0.5 * dot3(g, y, ((1,), (0,))) for g, y in zip(grams, ys)]
+        ys = [ns_step(y) for y in ys]
     for b in range(count):
         o_ref[b] = ys[b]
         h_ref[b] = ys[b].astype(h_ref.dtype)

time: 73.2 us -> 77.5 us (1.059)
  Pallas kernels: 19.6 us -> 23.8 us
    pallas_call x2, Pallas kernels: 10.5 us -> 14.8 us  [polar_factor_t(): pl.pallas_call(polar_kernel, out_shape=(jax.ShapeDtypeStruct(stack.shape,...]
  transfers between devices with their start and end apart: 12 -> 12, of which waited for: 1 -> 1; matrix products, arithmetic and copies ran while one was open for 32% -> 30% of each run, Pallas kernels for 20% -> 21%
where the time goes in v11:
time: 77.5 us; the launch traced here: 77.2 us
  Pallas kernels  23.8 us (31%)
  starting transfers between devices  17.3 us (22%)
  local copies, waits for them, and re-layouts  14.4 us (19%)
  matrix products  10.7 us (14%)
  between operations  5.39 us (7%)
  waiting for transfers between devices  3.03 us (4%)
  other arithmetic  2.62 us (3%)
    ppermute x12, starting transfers between devices, shifted(): return lax.ppermute(tree, ('gx', 'gy'), pairs)  17.3 us
    pallas_call x2, Pallas kernels, polar_factor_t(): pl.pallas_call(polar_kernel, out_shape=(jax.ShapeDtypeStruct(stack.shape,...  14.8 us
    pallas_call x2, Pallas kernels, edge_contract(): pl.pallas_call(edge_kernel, out_shape=jax.ShapeDtypeStruct((dd, n, LANES)...  9.05 us
    reshape x4, local copies, waits for them, and re-layouts, half(): jnp.dot(corner, edge, preferred_element_type=jnp.float32)  4.75 us
    dot_general x8, matrix products, half(): jnp.dot(corner, edge, preferred_element_type=jnp.float32)  3.73 us
    ppermute x12, waiting for transfers between devices, shifted(): return lax.ppermute(tree, ('gx', 'gy'), pairs)  3.03 us
    unnamed x29, local copies, waits for them, and re-layouts  2.5 us
    dot_general x2, matrix products, per_device(): new_low = jnp.dot(below_t, lower, precision=lax.Precision.HIGH)  2.09 us
  transfers between devices with their start and end apart: 12, of which 1 were waited for; matrix products, arithmetic and copies ran while one was open for 30% of the time, Pallas kernels for 21%

profile of v11, /device:TPU:0, one launch (start us, length us, event | category | flops | bytes accessed | tf_op | source)
XLA Modules:
  0.0 77.2 jit_solution(3534506752678183862)
XLA Ops:
  0.7 6.1 %collective-permute-start.1 = (bf16[96,1536]{1,0:T(8,128)(2,1)}, bf16[96,1536]{1,0:T(8,128)(2,1)S(1)}, u32[]{:S(2)}, u32[]{:S(2)}) collective-permute-start(bf16[96,1536]{1,0:T(8,128)(2,1)} %bitcast.117), channel_id=1, source_target_pairs={{0,7},{1,0},{2,1},{3,2},{4,3},{5,4},{6,5},{7,6},{8,15},{9,8},{10,9... | collective-permute-start | bytes 884744 | tf_op jit(solution)/shard_map/ppermute | solution.py:80
  6.7 0.5 collective-permute-start
  7.2 1.5 %collective-permute-start.3 = (bf16[96,1536]{1,0:T(8,128)(2,1)}, bf16[96,1536]{1,0:T(8,128)(2,1)S(1)}, u32[]{:S(2)}, u32[]{:S(2)}) collective-permute-start(bf16[96,1536]{1,0:T(8,128)(2,1)} %bitcast.116), channel_id=1, source_target_pairs={{0,1},{1,2},{2,3},{3,4},{4,5},{5,6},{6,7},{7,0},{8,9},{9,10},{10,1... | collective-permute-start | bytes 884744 | tf_op jit(solution)/shard_map/ppermute | solution.py:80
  8.8 1.2 %fusion.93 = f32[96,1536]{1,0:T(8,128)S(1)} fusion(bf16[1,1,96,1536]{3,2,1,0:T(8,128)(2,1)} %param.12, bf16[1,1,96,96]{3,2,1,0:T(8,128)(2,1)} %param.11), kind=kOutput, calls=%fused_computation.149 | convolution fusion | flops 28311552 | bytes 903168 | tf_op jit(solution)/shard_map/dot_general | solution.py:184
  10.0 1.2 %fusion.88 = f32[96,1536]{1,0:T(8,128)S(1)} fusion(bf16[1,1,96,1536]{3,2,1,0:T(8,128)(2,1)} %param.9, bf16[1,1,96,96]{3,2,1,0:T(8,128)(2,1)} %param.8), kind=kOutput, calls=%fused_computation.144 | convolution fusion | flops 28311552 | bytes 903168 | tf_op jit(solution)/shard_map/dot_general | solution.py:184
  11.3 0.1 reshape_squeeze.14
  11.5 0.3 copy.18
  11.9 0.4 convolution_bitcast_fusion
  12.3 0.4 fusion.56
  12.7 0.2 convolution_bitcast_fusion.1
  12.9 0.6 compare_reduce_fusion
  13.6 0.9 %fusion.2 = bf16[2,4,4,4,4]{3,0,1,2,4:T(2,128)(2,1)S(1)} fusion(f32[2,2,1,1,1]{1,0,4,3,2:T(2,128)S(1)} %convolution_bitcast_fusion.1, pred[]{:T(512)} %compare_reduce_fusion, bf16[2,4,4,4,4]{4,3,2,1,0:T(4,128)(2,1)S(1)} %reshape_squeeze.14), kind=kOutput, calls=%fused_computation.10 | convolution fusion | flops 13824 | bytes 2065 | tf_op jit(solution)/shard_map/st,tabcd->sabcd/dot_general | solution.py:167
  14.5 0.3 copy.21
  14.9 0.4 fusion.24
  15.3 0.4 fusion.t_ref
  15.7 1.2 %reshape.117 = f32[1536,96]{1,0:T(8,128)} reshape(f32[96,1536]{1,0:T(8,128)S(1)} %fusion.93) | data formatting | bytes 1179648 | tf_op jit(solution)/shard_map/reshape | solution.py:184
  16.9 1.2 %reshape.118 = f32[1536,96]{1,0:T(8,128)} reshape(f32[96,1536]{1,0:T(8,128)S(1)} %fusion.88) | data formatting | bytes 1179648 | tf_op jit(solution)/shard_map/reshape | solution.py:184
  18.1 0.3 reshape_squeeze.12.wd_ref
  18.5 0.2 convolution_add_fusion.3
  18.7 0.3 add.132
  19.0 0.2 copy-done.7
  19.2 0.3 copy.13
  19.5 0.2 convolution_add_fusion.2
  19.7 0.3 add.134
  19.9 0.3 copy.14
  20.3 7.4 %shard_map.103 = (f32[2,96,1536]{2,1,0:T(8,128)S(1)}, bf16[2,96,1536]{2,1,0:T(8,128)(2,1)S(1)}) custom-call(f32[2,96,1536]{2,1,0:T(8,128)S(1)} %maximum_bitcast_fusion.y_ref), custom_call_target="tpu_custom_call" | custom-call | tf_op jit(solution)/shard_map/pallas_call | solution.py:63
  27.7 1.0 %multiply_reduce_fusion.4 = (f32[]{:T(128)}, f32[96,96]{1,0:T(8,128)S(1)}) fusion(f32[1536,96]{1,0:T(8,128)S(1)} %copy-done.3, f32[2,96,1536]{2,1,0:T(8,128)S(1)} %get-tuple-element.7), kind=kOutput, calls=%fused_computation.78 | convolution fusion | flops 84953088 | bytes 1413124 | tf_op jit(solution)/shard_map/dot_general | solution.py:193
  29.5 3.3 %collective-permute-start.5 = (bf16[96,96]{1,0:T(8,128)(2,1)S(1)}, bf16[96,96]{1,0:T(8,128)(2,1)S(1)}, u32[]{:S(2)}, u32[]{:S(2)}) collective-permute-start(bf16[96,96]{1,0:T(8,128)(2,1)S(1)} %divide_convert_fusion.4), channel_id=1, source_target_pairs={{0,15},{1,8},{2,9},{3,10},{4,11},{5,12},{6,13},{7,14},{8,23},{9,16... | collective-permute-start | bytes 55304 | tf_op jit(solution)/shard_map/ppermute | solution.py:80
  32.8 2.8 %collective-permute-start.7 = (bf16[96,96]{1,0:T(8,128)(2,1)S(1)}, bf16[96,96]{1,0:T(8,128)(2,1)S(1)}, u32[]{:S(2)}, u32[]{:S(2)}) collective-permute-start(bf16[96,96]{1,0:T(8,128)(2,1)S(1)} %divide_convert_fusion.4), channel_id=1, source_target_pairs={{0,8},{1,9},{2,10},{3,11},{4,12},{5,13},{6,14},{7,15},{8,16},{9,17... | collective-permute-start | bytes 55304 | tf_op jit(solution)/shard_map/ppermute | solution.py:80
  35.5 1.0 %multiply_reduce_fusion.5 = (f32[]{:T(128)}, f32[96,96]{1,0:T(8,128)S(1)}) fusion(f32[1536,96]{1,0:T(8,128)S(1)} %copy-done.2, f32[2,96,1536]{2,1,0:T(8,128)S(1)} %get-tuple-element.7), kind=kOutput, calls=%fused_computation.80 | convolution fusion | flops 84953088 | bytes 1413124 | tf_op jit(solution)/shard_map/dot_general | solution.py:194
  37.4 0.2 collective-permute-start.6
  37.7 0.2 copy.17
  38.0 0.1 copy.33
  38.1 4.5 %shard_map.105 = f32[16,96,128]{2,1,0:T(8,128)S(1)} custom-call(bf16[1536,96]{1,0:T(8,128)(2,1)S(1)} %reshape_squeeze.12.wd_ref, bf16[96,2048]{1,0:T(8,128)(2,1)S(1)} %bitcast.111, bf16[256,256]{1,0:T(8,128)(2,1)S(1)} %fusion.t_ref, bf16[96,1536]{1,0:T(8,128)(2,1)S(1)} %get-tuple-element.13.qt_ref), custom_call_target="tpu_custom_call" | custom-call | tf_op jit(solution)/shard_map/pallas_call | solution.py:124
  42.6 0.8 %multiply_reduce_fusion.1 = f32[]{:T(128)} fusion(f32[16,96,128]{2,1,0:T(8,128)S(1)} %shard_map.105), kind=kLoop, calls=%fused_computation.16 | loop fusion | flops 294911 | bytes 589828 | tf_op jit(solution)/shard_map/reduce_sum | solution.py:84
  44.2 0.2 copy.22
  44.4 1.1 %convert_element_type.57 = bf16[96,1536]{1,0:T(8,128)(2,1)} reshape(bf16[96,16,96]{2,1,0:T(8,128)(2,1)S(1)} %copy.22) | data formatting | bytes 589824 | tf_op jit(solution)/shard_map/convert_element_type | solution.py:201
  45.5 0.4 collective-permute-start.9
  45.9 0.2 fusion.91
  46.2 0.2 convolution_add_fusion.1
  46.5 0.2 fusion.86
  46.7 1.2 %reshape.125 = f32[1536,96]{1,0:T(8,128)} reshape(f32[96,1536]{1,0:T(8,128)S(1)} %fusion.91) | data formatting | bytes 1179648 | tf_op jit(solution)/shard_map/reshape | solution.py:184
  47.9 0.3 add.138
  48.2 0.3 copy.15
  48.4 1.2 %reshape.119 = f32[1536,96]{1,0:T(8,128)} reshape(f32[96,1536]{1,0:T(8,128)S(1)} %fusion.86) | data formatting | bytes 1179648 | tf_op jit(solution)/shard_map/reshape | solution.py:184
  49.6 0.2 convolution_add_fusion
  49.8 0.3 add.140
  50.1 0.3 copy.16
  50.4 7.4 %shard_map.104 = (f32[2,96,1536]{2,1,0:T(8,128)S(1)}, bf16[2,96,1536]{2,1,0:T(8,128)(2,1)S(1)}) custom-call(f32[2,96,1536]{2,1,0:T(8,128)S(1)} %maximum_bitcast_fusion.1.y_ref), custom_call_target="tpu_custom_call" | custom-call | tf_op jit(solution)/shard_map/pallas_call | solution.py:63
  57.9 1.0 %multiply_reduce_fusion.2 = (f32[]{:T(128)}, f32[96,96]{1,0:T(8,128)S(1)}) fusion(f32[1536,96]{1,0:T(8,128)S(1)} %copy-done.4, f32[2,96,1536]{2,1,0:T(8,128)S(1)} %get-tuple-element.8), kind=kOutput, calls=%fused_computation.74 | convolution fusion | flops 84953088 | bytes 1413124 | tf_op jit(solution)/shard_map/dot_general | solution.py:194
  59.6 0.7 collective-permute-start.11
  60.4 0.2 copy.23
  60.8 1.3 %reshape.123.wd_ref = bf16[1536,96]{1,0:T(8,128)(2,1)S(1)} reshape(bf16[96,1536]{1,0:T(8,128)(2,1)} %collective-permute-done.9) | data formatting | bytes 589824 | tf_op jit(solution)/shard_map/reshape | solution.py:120
  62.1 4.5 %shard_map.106 = f32[16,96,128]{2,1,0:T(8,128)S(1)} custom-call(bf16[1536,96]{1,0:T(8,128)(2,1)S(1)} %reshape.123.wd_ref, bf16[96,2048]{1,0:T(8,128)(2,1)S(1)} %bitcast.110, bf16[256,256]{1,0:T(8,128)(2,1)S(1)} %fusion.t_ref, bf16[96,1536]{1,0:T(8,128)(2,1)S(1)} %get-tuple-element.11.qt_ref), custom_call_target="tpu_custom_call" | custom-call | tf_op jit(solution)/shard_map/pallas_call | solution.py:124
  66.6 0.8 %multiply_reduce_fusion = f32[]{:T(128)} fusion(f32[16,96,128]{2,1,0:T(8,128)S(1)} %shard_map.106), kind=kLoop, calls=%fused_computation.14 | loop fusion | flops 294911 | bytes 589828 | tf_op jit(solution)/shard_map/reduce_sum | solution.py:84
  68.2 0.2 copy.24
  68.4 0.4 convert_element_type.60
  68.8 1.2 %collective-permute-start.10 = (bf16[96,1536]{1,0:T(8,128)(2,1)S(1)}, bf16[96,1536]{1,0:T(8,128)(2,1)S(1)}, u32[]{:S(2)}, u32[]{:S(2)}) collective-permute-start(bf16[96,1536]{1,0:T(8,128)(2,1)S(1)} %convert_element_type.60), channel_id=1, source_target_pairs={{0,8},{1,9},{2,10},{3,11},{4,12},{5,13},{6,14},{7,15},{8,16},{9,17... | collective-permute-start | bytes 884744 | tf_op jit(solution)/shard_map/ppermute | solution.py:80
  70.0 1.0 %multiply_reduce_fusion.3 = (f32[]{:T(128)}, f32[96,96]{1,0:T(8,128)S(1)}) fusion(f32[1536,96]{1,0:T(8,128)S(1)} %copy-done.1, f32[2,96,1536]{2,1,0:T(8,128)S(1)} %get-tuple-element.8), kind=kOutput, calls=%fused_computation.76 | convolution fusion | flops 84953088 | bytes 1413124 | tf_op jit(solution)/shard_map/dot_general | solution.py:193
  71.8 0.5 collective-permute-start.8
  72.3 3.0 %collective-permute-done.8 = bf16[96,96]{1,0:T(8,128)(2,1)S(1)} collective-permute-done((bf16[96,96]{1,0:T(8,128)(2,1)S(1)}, bf16[96,96]{1,0:T(8,128)(2,1)S(1)}, u32[]{:S(2)}, u32[]{:S(2)}) %collective-permute-start.8) | collective-permute-done | bytes 18464 | tf_op jit(solution)/shard_map/ppermute | solution.py:80
  75.3 0.6 copy.37
  75.9 0.7 copy.38
  76.6 0.6 copy.39
  (57 shorter events, 1.2 us)
Async XLA Ops:
  0.6 12.1 %copy-start = (f32[2,2]{1,0:T(2,128)S(1)}, f32[2,2]{1,0:T(2,128)}, u32[]{:S(2)}) copy-start(f32[2,2]{1,0:T(2,128)} %param.14) | copy-start | bytes 52
  0.6 10.7 %copy-start.10 = (bf16[1,1,2,256]{3,2,1,0:T(2,128)(2,1)S(1)}, bf16[1,1,2,256]{3,2,1,0:T(2,128)(2,1)}, u32[]{:S(2)}) copy-start(bf16[1,1,2,256]{3,2,1,0:T(2,128)(2,1)} %param.13) | copy-start | bytes 3076
  0.7 17.8 %collective-permute-start.1 = (bf16[96,1536]{1,0:T(8,128)(2,1)}, bf16[96,1536]{1,0:T(8,128)(2,1)S(1)}, u32[]{:S(2)}, u32[]{:S(2)}) collective-permute-start(bf16[96,1536]{1,0:T(8,128)(2,1)} %bitcast.117), channel_id=1, source_target_pairs={{0,7},{1,0},{2,1},{3,2},{4,3},{5,4},{6,5},{7,6},{8,15},{9,8},{10,9... | collective-permute-start | bytes 884744 | tf_op jit(solution)/shard_map/ppermute | solution.py:80
  6.7 11.7 %collective-permute-start = (bf16[96,96]{1,0:T(8,128)(2,1)}, bf16[96,96]{1,0:T(8,128)(2,1)S(1)}, u32[]{:S(2)}, u32[]{:S(2)}) collective-permute-start(bf16[96,96]{1,0:T(8,128)(2,1)} %bitcast.122), channel_id=1, source_target_pairs={{0,7},{1,0},{2,1},{3,2},{4,3},{5,4},{6,5},{7,6},{8,15},{9,8},{10,9... | collective-permute-start | bytes 55304 | tf_op jit(solution)/shard_map/ppermute | solution.py:80
  7.2 12.2 %collective-permute-start.3 = (bf16[96,1536]{1,0:T(8,128)(2,1)}, bf16[96,1536]{1,0:T(8,128)(2,1)S(1)}, u32[]{:S(2)}, u32[]{:S(2)}) collective-permute-start(bf16[96,1536]{1,0:T(8,128)(2,1)} %bitcast.116), channel_id=1, source_target_pairs={{0,1},{1,2},{2,3},{3,4},{4,5},{5,6},{6,7},{7,0},{8,9},{9,10},{10,1... | collective-permute-start | bytes 884744 | tf_op jit(solution)/shard_map/ppermute | solution.py:80
  8.8 10.7 %collective-permute-start.2 = (bf16[96,96]{1,0:T(8,128)(2,1)}, bf16[96,96]{1,0:T(8,128)(2,1)S(1)}, u32[]{:S(2)}, u32[]{:S(2)}) collective-permute-start(bf16[96,96]{1,0:T(8,128)(2,1)} %bitcast.123), channel_id=1, source_target_pairs={{0,1},{1,2},{2,3},{3,4},{4,5},{5,6},{6,7},{7,0},{8,9},{9,10},{10,1... | collective-permute-start | bytes 55304 | tf_op jit(solution)/shard_map/ppermute | solution.py:80
  10.0 2.9 %copy-start.11 = (s32[4]{0:T(128)S(1)}, s32[4]{0:T(128)}, u32[]{:S(2)}) copy-start(s32[4]{0:T(128)} %param.15) | copy-start | bytes 52
  15.7 2.4 %copy-start.9 = (bf16[1,1,96,1536]{3,2,1,0:T(8,128)(2,1)S(1)}, bf16[1,1,96,1536]{3,2,1,0:T(8,128)(2,1)}, u32[]{:S(2)}) copy-start(bf16[1,1,96,1536]{3,2,1,0:T(8,128)(2,1)} %param.10) | copy-start | bytes 884740
  18.5 0.7 copy-start.7
  20.2 7.5 %copy-start.3 = (f32[1536,96]{1,0:T(8,128)S(1)}, f32[1536,96]{1,0:T(8,128)}, u32[]{:S(2)}) copy-start(f32[1536,96]{1,0:T(8,128)} %reshape.118) | copy-start | bytes 1769476
  20.3 15.2 %copy-start.2 = (f32[1536,96]{1,0:T(8,128)S(1)}, f32[1536,96]{1,0:T(8,128)}, u32[]{:S(2)}) copy-start(f32[1536,96]{1,0:T(8,128)} %reshape.117) | copy-start | bytes 1769476
  29.5 16.7 %collective-permute-start.5 = (bf16[96,96]{1,0:T(8,128)(2,1)S(1)}, bf16[96,96]{1,0:T(8,128)(2,1)S(1)}, u32[]{:S(2)}, u32[]{:S(2)}) collective-permute-start(bf16[96,96]{1,0:T(8,128)(2,1)S(1)} %divide_convert_fusion.4), channel_id=1, source_target_pairs={{0,15},{1,8},{2,9},{3,10},{4,11},{5,12},{6,13},{7,14},{8,23},{9,16... | collective-permute-start | bytes 55304 | tf_op jit(solution)/shard_map/ppermute | solution.py:80
  32.8 13.6 %collective-permute-start.7 = (bf16[96,96]{1,0:T(8,128)(2,1)S(1)}, bf16[96,96]{1,0:T(8,128)(2,1)S(1)}, u32[]{:S(2)}, u32[]{:S(2)}) collective-permute-start(bf16[96,96]{1,0:T(8,128)(2,1)S(1)} %divide_convert_fusion.4), channel_id=1, source_target_pairs={{0,8},{1,9},{2,10},{3,11},{4,12},{5,13},{6,14},{7,15},{8,16},{9,17... | collective-permute-start | bytes 55304 | tf_op jit(solution)/shard_map/ppermute | solution.py:80
  37.3 8.6 %collective-permute-start.4 = (bf16[96,96]{1,0:T(8,128)(2,1)S(1)}, bf16[96,96]{1,0:T(8,128)(2,1)S(1)}, u32[]{:S(2)}, u32[]{:S(2)}) collective-permute-start(bf16[96,96]{1,0:T(8,128)(2,1)S(1)} %divide_convert_fusion.5), channel_id=1, source_target_pairs={{0,8},{1,9},{2,10},{3,11},{4,12},{5,13},{6,14},{7,15},{8,16},{9,17... | collective-permute-start | bytes 55304 | tf_op jit(solution)/shard_map/ppermute | solution.py:80
  37.4 12.2 %collective-permute-start.6 = (bf16[96,96]{1,0:T(8,128)(2,1)S(1)}, bf16[96,96]{1,0:T(8,128)(2,1)S(1)}, u32[]{:S(2)}, u32[]{:S(2)}) collective-permute-start(bf16[96,96]{1,0:T(8,128)(2,1)S(1)} %divide_convert_fusion.5), channel_id=1, source_target_pairs={{0,9},{1,10},{2,11},{3,12},{4,13},{5,14},{6,15},{7,8},{8,17},{9,18... | collective-permute-start | bytes 55304 | tf_op jit(solution)/shard_map/ppermute | solution.py:80
  44.1 1.8 %copy-start.5 = (bf16[1,1,96,1536]{3,2,1,0:T(8,128)(2,1)S(1)}, bf16[1,1,96,1536]{3,2,1,0:T(8,128)(2,1)}, u32[]{:S(2)}) copy-start(bf16[1,1,96,1536]{3,2,1,0:T(8,128)(2,1)} %param.12) | copy-start | bytes 884740
  44.2 1.9 %copy-start.8 = (bf16[96,1536]{1,0:T(8,128)(2,1)S(1)}, bf16[96,1536]{1,0:T(8,128)(2,1)}, u32[]{:S(2)}) copy-start(bf16[96,1536]{1,0:T(8,128)(2,1)} %copy-done.7) | copy-start | bytes 884740
  45.5 1.0 %copy-start.6 = (bf16[1,1,96,1536]{3,2,1,0:T(8,128)(2,1)S(1)}, bf16[1,1,96,1536]{3,2,1,0:T(8,128)(2,1)}, u32[]{:S(2)}) copy-start(bf16[1,1,96,1536]{3,2,1,0:T(8,128)(2,1)} %param.9) | copy-start | bytes 884740
  45.5 15.3 %collective-permute-start.9 = (bf16[96,1536]{1,0:T(8,128)(2,1)}, bf16[96,1536]{1,0:T(8,128)(2,1)}, u32[]{:S(2)}, u32[]{:S(2)}) collective-permute-start(bf16[96,1536]{1,0:T(8,128)(2,1)} %convert_element_type.57), channel_id=1, source_target_pairs={{0,8},{1,9},{2,10},{3,11},{4,12},{5,13},{6,14},{7,15},{8,16},{9,17... | collective-permute-start | bytes 884744 | tf_op jit(solution)/shard_map/ppermute | solution.py:80
  50.4 7.4 %copy-start.4 = (f32[1536,96]{1,0:T(8,128)S(1)}, f32[1536,96]{1,0:T(8,128)}, u32[]{:S(2)}) copy-start(f32[1536,96]{1,0:T(8,128)} %reshape.125) | copy-start | bytes 1769476
  59.6 12.7 %collective-permute-start.11 = (bf16[96,96]{1,0:T(8,128)(2,1)S(1)}, bf16[96,96]{1,0:T(8,128)(2,1)S(1)}, u32[]{:S(2)}, u32[]{:S(2)}) collective-permute-start(bf16[96,96]{1,0:T(8,128)(2,1)S(1)} %divide_convert_fusion.2), channel_id=1, source_target_pairs={{0,8},{1,9},{2,10},{3,11},{4,12},{5,13},{6,14},{7,15},{8,16},{9,17... | collective-permute-start | bytes 55304 | tf_op jit(solution)/shard_map/ppermute | solution.py:80
  68.2 1.8 %copy-start.1 = (f32[1536,96]{1,0:T(8,128)S(1)}, f32[1536,96]{1,0:T(8,128)}, u32[]{:S(2)}) copy-start(f32[1536,96]{1,0:T(8,128)} %reshape.119) | copy-start | bytes 1769476
  68.8 6.5 %collective-permute-start.10 = (bf16[96,1536]{1,0:T(8,128)(2,1)S(1)}, bf16[96,1536]{1,0:T(8,128)(2,1)S(1)}, u32[]{:S(2)}, u32[]{:S(2)}) collective-permute-start(bf16[96,1536]{1,0:T(8,128)(2,1)S(1)} %convert_element_type.60), channel_id=1, source_target_pairs={{0,8},{1,9},{2,10},{3,11},{4,12},{5,13},{6,14},{7,15},{8,16},{9,17... | collective-permute-start | bytes 884744 | tf_op jit(solution)/shard_map/ppermute | solution.py:80
  71.8 3.5 %collective-permute-start.8 = (bf16[96,96]{1,0:T(8,128)(2,1)S(1)}, bf16[96,96]{1,0:T(8,128)(2,1)S(1)}, u32[]{:S(2)}, u32[]{:S(2)}) collective-permute-start(bf16[96,96]{1,0:T(8,128)(2,1)S(1)} %divide_convert_fusion.3), channel_id=1, source_target_pairs={{0,8},{1,9},{2,10},{3,11},{4,12},{5,13},{6,14},{7,15},{8,16},{9,17... | collective-permute-start | bytes 55304 | tf_op jit(solution)/shard_map/ppermute | solution.py:80

commit v12 on v10

--- a/solution.py
+++ b/solution.py
@@ -140,9 +140,8 @@
     b_row = one_hot(size, dd, lambda r: ((r // dd) % q) * q + r % q, lambda c: c)
     k_col = one_hot(dd, size, lambda r: r, lambda c: (c // (q * dd)) * q + (c // q) % q)
     b_col = one_hot(dd, size, lambda r: r, lambda c: ((c // dd) % q) * q + c % q)
-    hi = lax.Precision.HIGHEST
-    ket_wide = jnp.einsum("ra,sab,bc->src", k_row, ket_m, k_col, precision=hi)
-    bra_wide = jnp.einsum("ra,sab,bc->src", b_row, bra_m, b_col, precision=hi)
+    ket_wide = jnp.einsum("ra,sab,bc->src", k_row, ket_m, k_col)
+    bra_wide = jnp.einsum("ra,sab,bc->src", b_row, bra_m, b_col)
     return jnp.sum(ket_wide * bra_wide, axis=0).astype(jnp.bfloat16)
 
 

time: 73.2 us -> 73.6 us (level)
  matrix products: 10.7 us -> 11.5 us
    dot_general x2, matrix products: 2.09 us -> 3.22 us  [per_device(): new_low = jnp.dot(below_t, lower, precision=lax.Precision.HIGH)]
    reshape x4, local copies, waits for them, and re-layouts: 4.75 us -> 3.8 us  [half(): jnp.dot(corner, edge, preferred_element_type=jnp.float32)]
    dot_general x4 -> x2, matrix products: 1.68 us -> 1.36 us  [the longest x1 0.68 us: double_layer(): ket_wide = jnp.einsum('ra,sab,bc->src', k_row, ket_m, k_col)]
  transfers between devices with their start and end apart: 12 -> 12, of which waited for: 1 -> 1; matrix products, arithmetic and copies ran while one was open for 32% -> 32% of each run, Pallas kernels for 20% -> 19%
where the time goes in v12:
time: 73.6 us; the launch traced here: 73.3 us
  Pallas kernels  19.5 us (26%)
  starting transfers between devices  17.2 us (23%)
  local copies, waits for them, and re-layouts  14.1 us (19%)
  matrix products  11.5 us (16%)
  between operations  5.37 us (7%)
  waiting for transfers between devices  3.01 us (4%)
  other arithmetic  2.62 us (4%)
    ppermute x12, starting transfers between devices, shifted(): return lax.ppermute(tree, ('gx', 'gy'), pairs)  17.2 us
    pallas_call x2, Pallas kernels, polar_factor_t(): pl.pallas_call(polar_kernel, out_shape=(jax.ShapeDtypeStruct(stack.shape,...  10.5 us
    pallas_call x2, Pallas kernels, edge_contract(): pl.pallas_call(edge_kernel, out_shape=jax.ShapeDtypeStruct((dd, n, LANES)...  9 us
    reshape x4, local copies, waits for them, and re-layouts, half(): jnp.dot(corner, edge, preferred_element_type=jnp.float32)  3.8 us
    dot_general x8, matrix products, half(): jnp.dot(corner, edge, preferred_element_type=jnp.float32)  3.72 us
    dot_general x2, matrix products, per_device(): new_low = jnp.dot(below_t, lower, precision=lax.Precision.HIGH)  3.22 us
    unnamed x29, local copies, waits for them, and re-layouts  3.21 us
    ppermute x12, waiting for transfers between devices, shifted(): return lax.ppermute(tree, ('gx', 'gy'), pairs)  3.01 us
  transfers between devices with their start and end apart: 12, of which 1 were waited for; matrix products, arithmetic and copies ran while one was open for 32% of the time, Pallas kernels for 19%

profile of v12, /device:TPU:0, one launch (start us, length us, event | category | flops | bytes accessed | tf_op | source)
XLA Modules:
  0.0 73.3 jit_solution(7114008025939566020)
XLA Ops:
  0.7 6.1 %collective-permute-start.1 = (bf16[96,1536]{1,0:T(8,128)(2,1)}, bf16[96,1536]{1,0:T(8,128)(2,1)S(1)}, u32[]{:S(2)}, u32[]{:S(2)}) collective-permute-start(bf16[96,1536]{1,0:T(8,128)(2,1)} %bitcast.119), channel_id=1, source_target_pairs={{0,7},{1,0},{2,1},{3,2},{4,3},{5,4},{6,5},{7,6},{8,15},{9,8},{10,9... | collective-permute-start | bytes 884744 | tf_op jit(solution)/shard_map/ppermute | solution.py:71
  6.8 0.5 collective-permute-start
  7.3 1.5 %collective-permute-start.3 = (bf16[96,1536]{1,0:T(8,128)(2,1)}, bf16[96,1536]{1,0:T(8,128)(2,1)S(1)}, u32[]{:S(2)}, u32[]{:S(2)}) collective-permute-start(bf16[96,1536]{1,0:T(8,128)(2,1)} %bitcast.118), channel_id=1, source_target_pairs={{0,1},{1,2},{2,3},{3,4},{4,5},{5,6},{6,7},{7,0},{8,9},{9,10},{10,1... | collective-permute-start | bytes 884744 | tf_op jit(solution)/shard_map/ppermute | solution.py:71
  8.8 1.2 %fusion.124 = f32[96,1536]{1,0:T(8,128)S(1)} fusion(bf16[1,1,96,1536]{3,2,1,0:T(8,128)(2,1)} %param.12, bf16[1,1,96,96]{3,2,1,0:T(8,128)(2,1)} %param.11), kind=kOutput, calls=%fused_computation.153 | convolution fusion | flops 28311552 | bytes 903168 | tf_op jit(solution)/shard_map/dot_general | solution.py:174
  10.0 1.2 %fusion.119 = f32[96,1536]{1,0:T(8,128)S(1)} fusion(bf16[1,1,96,1536]{3,2,1,0:T(8,128)(2,1)} %param.9, bf16[1,1,96,96]{3,2,1,0:T(8,128)(2,1)} %param.8), kind=kOutput, calls=%fused_computation.148 | convolution fusion | flops 28311552 | bytes 903168 | tf_op jit(solution)/shard_map/dot_general | solution.py:174
  11.3 0.1 reshape_squeeze.14
  11.4 0.3 copy.18
  11.8 0.2 convolution_bitcast_fusion.1
  12.0 0.6 compare_reduce_fusion
  12.7 0.9 %fusion.2 = bf16[2,4,4,4,4]{3,0,1,2,4:T(2,128)(2,1)S(1)} fusion(f32[2,2,1,1,1]{1,0,4,3,2:T(2,128)S(1)} %convolution_bitcast_fusion.1, pred[]{:T(512)} %compare_reduce_fusion, bf16[2,4,4,4,4]{4,3,2,1,0:T(4,128)(2,1)S(1)} %reshape_squeeze.14), kind=kOutput, calls=%fused_computation.10 | convolution fusion | flops 13824 | bytes 2065 | tf_op jit(solution)/shard_map/st,tabcd->sabcd/dot_general | solution.py:157
  13.6 0.7 fusion.5
  14.3 0.3 copy.21
  14.7 0.7 fusion.t_ref
  15.4 1.2 %reshape.117 = f32[1536,96]{1,0:T(8,128)} reshape(f32[96,1536]{1,0:T(8,128)S(1)} %fusion.124) | data formatting | bytes 1179648 | tf_op jit(solution)/shard_map/reshape | solution.py:174
  16.6 1.2 %reshape.118 = f32[1536,96]{1,0:T(8,128)} reshape(f32[96,1536]{1,0:T(8,128)S(1)} %fusion.119) | data formatting | bytes 1179648 | tf_op jit(solution)/shard_map/reshape | solution.py:174
  17.8 0.3 reshape_squeeze.12.wd_ref
  18.1 0.7 copy-done.7
  18.8 0.2 convolution_add_fusion.3
  19.1 0.3 add.132
  19.3 0.3 copy.13
  19.6 0.2 convolution_add_fusion.2
  19.8 0.3 add.134
  20.1 0.2 copy-done.5
  20.3 0.3 copy.14
  20.7 5.3 %shard_map.103 = (f32[2,96,1536]{2,1,0:T(8,128)S(1)}, bf16[2,96,1536]{2,1,0:T(8,128)(2,1)S(1)}) custom-call(f32[2,96,1536]{2,1,0:T(8,128)S(1)} %maximum_bitcast_fusion.y_ref), custom_call_target="tpu_custom_call" | custom-call | tf_op jit(solution)/shard_map/pallas_call | solution.py:54
  26.0 1.1 %multiply_reduce_fusion.4 = (f32[]{:T(128)}, f32[96,96]{1,0:T(8,128)S(1)}) fusion(f32[1536,96]{1,0:T(8,128)S(1)} %copy-done.2, f32[2,96,1536]{2,1,0:T(8,128)S(1)} %get-tuple-element.7), kind=kOutput, calls=%fused_computation.83 | convolution fusion | flops 84953088 | bytes 1413124 | tf_op jit(solution)/shard_map/dot_general | solution.py:183
  27.7 3.2 %collective-permute-start.5 = (bf16[96,96]{1,0:T(8,128)(2,1)S(1)}, bf16[96,96]{1,0:T(8,128)(2,1)S(1)}, u32[]{:S(2)}, u32[]{:S(2)}) collective-permute-start(bf16[96,96]{1,0:T(8,128)(2,1)S(1)} %divide_convert_fusion.4), channel_id=1, source_target_pairs={{0,15},{1,8},{2,9},{3,10},{4,11},{5,12},{6,13},{7,14},{8,23},{9,16... | collective-permute-start | bytes 55304 | tf_op jit(solution)/shard_map/ppermute | solution.py:71
  30.9 2.8 %collective-permute-start.7 = (bf16[96,96]{1,0:T(8,128)(2,1)S(1)}, bf16[96,96]{1,0:T(8,128)(2,1)S(1)}, u32[]{:S(2)}, u32[]{:S(2)}) collective-permute-start(bf16[96,96]{1,0:T(8,128)(2,1)S(1)} %divide_convert_fusion.4), channel_id=1, source_target_pairs={{0,8},{1,9},{2,10},{3,11},{4,12},{5,13},{6,14},{7,15},{8,16},{9,17... | collective-permute-start | bytes 55304 | tf_op jit(solution)/shard_map/ppermute | solution.py:71
  33.6 2.2 %multiply_reduce_fusion.5 = (f32[]{:T(128)}, f32[96,96]{1,0:T(8,128)S(1)}) fusion(f32[1536,96]{1,0:T(8,128)} %reshape.117, f32[2,96,1536]{2,1,0:T(8,128)S(1)} %get-tuple-element.7), kind=kOutput, calls=%fused_computation.85 | convolution fusion | flops 84953088 | bytes 1216516 | tf_op jit(solution)/shard_map/dot_general | solution.py:184
  36.6 0.2 collective-permute-start.6
  36.9 0.2 copy.17
  37.2 0.1 copy.33
  37.3 4.5 %shard_map.105 = f32[16,96,128]{2,1,0:T(8,128)S(1)} custom-call(bf16[1536,96]{1,0:T(8,128)(2,1)S(1)} %reshape_squeeze.12.wd_ref, bf16[96,2048]{1,0:T(8,128)(2,1)S(1)} %bitcast.113, bf16[256,256]{1,0:T(8,128)(2,1)S(1)} %fusion.t_ref, bf16[96,1536]{1,0:T(8,128)(2,1)S(1)} %get-tuple-element.13.qt_ref), custom_call_target="tpu_custom_call" | custom-call | tf_op jit(solution)/shard_map/pallas_call | solution.py:115
  41.8 0.8 %multiply_reduce_fusion.1 = f32[]{:T(128)} fusion(f32[16,96,128]{2,1,0:T(8,128)S(1)} %shard_map.105), kind=kLoop, calls=%fused_computation.18 | loop fusion | flops 294911 | bytes 589828 | tf_op jit(solution)/shard_map/reduce_sum | solution.py:75
  43.4 0.2 copy.22
  43.6 1.1 %convert_element_type.57 = bf16[96,1536]{1,0:T(8,128)(2,1)} reshape(bf16[96,16,96]{2,1,0:T(8,128)(2,1)S(1)} %copy.22) | data formatting | bytes 589824 | tf_op jit(solution)/shard_map/convert_element_type | solution.py:191
  44.7 0.4 collective-permute-start.9
  45.1 0.2 fusion.122
  45.3 0.2 convolution_add_fusion.1
  45.7 0.2 fusion.117
  45.9 0.3 reshape.125
  46.2 0.3 add.138
  46.4 0.3 copy.15
  46.7 1.2 %reshape.119 = f32[1536,96]{1,0:T(8,128)} reshape(f32[96,1536]{1,0:T(8,128)S(1)} %fusion.117) | data formatting | bytes 1179648 | tf_op jit(solution)/shard_map/reshape | solution.py:174
  47.9 0.2 convolution_add_fusion
  48.1 0.3 add.140
  48.4 0.3 copy.16
  48.7 5.3 %shard_map.104 = (f32[2,96,1536]{2,1,0:T(8,128)S(1)}, bf16[2,96,1536]{2,1,0:T(8,128)(2,1)S(1)}) custom-call(f32[2,96,1536]{2,1,0:T(8,128)S(1)} %maximum_bitcast_fusion.1.y_ref), custom_call_target="tpu_custom_call" | custom-call | tf_op jit(solution)/shard_map/pallas_call | solution.py:54
  54.0 1.1 %multiply_reduce_fusion.2 = (f32[]{:T(128)}, f32[96,96]{1,0:T(8,128)S(1)}) fusion(f32[1536,96]{1,0:T(8,128)S(1)} %reshape.125, f32[2,96,1536]{2,1,0:T(8,128)S(1)} %get-tuple-element.8), kind=kOutput, calls=%fused_computation.79 | convolution fusion | flops 84953088 | bytes 1413124 | tf_op jit(solution)/shard_map/dot_general | solution.py:184
  55.7 0.7 collective-permute-start.11
  56.5 0.2 copy.23
  56.8 0.1 copy.32
  56.9 1.3 %reshape.123.wd_ref = bf16[1536,96]{1,0:T(8,128)(2,1)S(1)} reshape(bf16[96,1536]{1,0:T(8,128)(2,1)} %collective-permute-done.9) | data formatting | bytes 589824 | tf_op jit(solution)/shard_map/reshape | solution.py:111
  58.2 4.5 %shard_map.106 = f32[16,96,128]{2,1,0:T(8,128)S(1)} custom-call(bf16[1536,96]{1,0:T(8,128)(2,1)S(1)} %reshape.123.wd_ref, bf16[96,2048]{1,0:T(8,128)(2,1)S(1)} %bitcast.112, bf16[256,256]{1,0:T(8,128)(2,1)S(1)} %fusion.t_ref, bf16[96,1536]{1,0:T(8,128)(2,1)S(1)} %get-tuple-element.11.qt_ref), custom_call_target="tpu_custom_call" | custom-call | tf_op jit(solution)/shard_map/pallas_call | solution.py:115
  62.7 0.8 %multiply_reduce_fusion = f32[]{:T(128)} fusion(f32[16,96,128]{2,1,0:T(8,128)S(1)} %shard_map.106), kind=kLoop, calls=%fused_computation.16 | loop fusion | flops 294911 | bytes 589828 | tf_op jit(solution)/shard_map/reduce_sum | solution.py:75
  64.3 0.2 copy.24
  64.5 0.4 convert_element_type.60
  64.9 1.2 %collective-permute-start.10 = (bf16[96,1536]{1,0:T(8,128)(2,1)S(1)}, bf16[96,1536]{1,0:T(8,128)(2,1)S(1)}, u32[]{:S(2)}, u32[]{:S(2)}) collective-permute-start(bf16[96,1536]{1,0:T(8,128)(2,1)S(1)} %convert_element_type.60), channel_id=1, source_target_pairs={{0,8},{1,9},{2,10},{3,11},{4,12},{5,13},{6,14},{7,15},{8,16},{9,17... | collective-permute-start | bytes 884744 | tf_op jit(solution)/shard_map/ppermute | solution.py:71
  66.1 1.1 %multiply_reduce_fusion.3 = (f32[]{:T(128)}, f32[96,96]{1,0:T(8,128)S(1)}) fusion(f32[1536,96]{1,0:T(8,128)S(1)} %copy-done.1, f32[2,96,1536]{2,1,0:T(8,128)S(1)} %get-tuple-element.8), kind=kOutput, calls=%fused_computation.81 | convolution fusion | flops 84953088 | bytes 1413124 | tf_op jit(solution)/shard_map/dot_general | solution.py:183
  67.8 0.5 collective-permute-start.8
  68.4 3.0 %collective-permute-done.8 = bf16[96,96]{1,0:T(8,128)(2,1)S(1)} collective-permute-done((bf16[96,96]{1,0:T(8,128)(2,1)S(1)}, bf16[96,96]{1,0:T(8,128)(2,1)S(1)}, u32[]{:S(2)}, u32[]{:S(2)}) %collective-permute-start.8) | collective-permute-done | bytes 18464 | tf_op jit(solution)/shard_map/ppermute | solution.py:71
  71.4 0.6 copy.37
  72.0 0.7 copy.38
  72.7 0.6 copy.39
  (55 shorter events, 1.1 us)
Async XLA Ops:
  0.6 11.2 %copy-start = (f32[2,2]{1,0:T(2,128)S(1)}, f32[2,2]{1,0:T(2,128)}, u32[]{:S(2)}) copy-start(f32[2,2]{1,0:T(2,128)} %param.14) | copy-start | bytes 52
  0.6 10.6 %copy-start.10 = (bf16[1,1,2,256]{3,2,1,0:T(2,128)(2,1)S(1)}, bf16[1,1,2,256]{3,2,1,0:T(2,128)(2,1)}, u32[]{:S(2)}) copy-start(bf16[1,1,2,256]{3,2,1,0:T(2,128)(2,1)} %param.13) | copy-start | bytes 3076
  0.7 11.4 %copy-start.11 = (s32[4]{0:T(128)S(1)}, s32[4]{0:T(128)}, u32[]{:S(2)}) copy-start(s32[4]{0:T(128)} %param.15) | copy-start | bytes 52
  0.7 17.4 %collective-permute-start.1 = (bf16[96,1536]{1,0:T(8,128)(2,1)}, bf16[96,1536]{1,0:T(8,128)(2,1)S(1)}, u32[]{:S(2)}, u32[]{:S(2)}) collective-permute-start(bf16[96,1536]{1,0:T(8,128)(2,1)} %bitcast.119), channel_id=1, source_target_pairs={{0,7},{1,0},{2,1},{3,2},{4,3},{5,4},{6,5},{7,6},{8,15},{9,8},{10,9... | collective-permute-start | bytes 884744 | tf_op jit(solution)/shard_map/ppermute | solution.py:71
  6.8 11.3 %collective-permute-start = (bf16[96,96]{1,0:T(8,128)(2,1)}, bf16[96,96]{1,0:T(8,128)(2,1)S(1)}, u32[]{:S(2)}, u32[]{:S(2)}) collective-permute-start(bf16[96,96]{1,0:T(8,128)(2,1)} %bitcast.124), channel_id=1, source_target_pairs={{0,7},{1,0},{2,1},{3,2},{4,3},{5,4},{6,5},{7,6},{8,15},{9,8},{10,9... | collective-permute-start | bytes 55304 | tf_op jit(solution)/shard_map/ppermute | solution.py:71
  7.3 12.3 %collective-permute-start.3 = (bf16[96,1536]{1,0:T(8,128)(2,1)}, bf16[96,1536]{1,0:T(8,128)(2,1)S(1)}, u32[]{:S(2)}, u32[]{:S(2)}) collective-permute-start(bf16[96,1536]{1,0:T(8,128)(2,1)} %bitcast.118), channel_id=1, source_target_pairs={{0,1},{1,2},{2,3},{3,4},{4,5},{5,6},{6,7},{7,0},{8,9},{9,10},{10,1... | collective-permute-start | bytes 884744 | tf_op jit(solution)/shard_map/ppermute | solution.py:71
  8.8 10.8 %collective-permute-start.2 = (bf16[96,96]{1,0:T(8,128)(2,1)}, bf16[96,96]{1,0:T(8,128)(2,1)S(1)}, u32[]{:S(2)}, u32[]{:S(2)}) collective-permute-start(bf16[96,96]{1,0:T(8,128)(2,1)} %bitcast.125), channel_id=1, source_target_pairs={{0,1},{1,2},{2,3},{3,4},{4,5},{5,6},{6,7},{7,0},{8,9},{9,10},{10,1... | collective-permute-start | bytes 55304 | tf_op jit(solution)/shard_map/ppermute | solution.py:71
  15.4 2.4 %copy-start.9 = (bf16[1,1,96,1536]{3,2,1,0:T(8,128)(2,1)S(1)}, bf16[1,1,96,1536]{3,2,1,0:T(8,128)(2,1)}, u32[]{:S(2)}) copy-start(bf16[1,1,96,1536]{3,2,1,0:T(8,128)(2,1)} %param.10) | copy-start | bytes 884740
  18.1 0.7 copy-start.7
  19.6 0.7 copy-start.5
  20.7 5.3 %copy-start.2 = (f32[1536,96]{1,0:T(8,128)S(1)}, f32[1536,96]{1,0:T(8,128)}, u32[]{:S(2)}) copy-start(f32[1536,96]{1,0:T(8,128)} %reshape.118) | copy-start | bytes 1769476
  27.7 17.6 %collective-permute-start.5 = (bf16[96,96]{1,0:T(8,128)(2,1)S(1)}, bf16[96,96]{1,0:T(8,128)(2,1)S(1)}, u32[]{:S(2)}, u32[]{:S(2)}) collective-permute-start(bf16[96,96]{1,0:T(8,128)(2,1)S(1)} %divide_convert_fusion.4), channel_id=1, source_target_pairs={{0,15},{1,8},{2,9},{3,10},{4,11},{5,12},{6,13},{7,14},{8,23},{9,16... | collective-permute-start | bytes 55304 | tf_op jit(solution)/shard_map/ppermute | solution.py:71
  30.9 14.7 %collective-permute-start.7 = (bf16[96,96]{1,0:T(8,128)(2,1)S(1)}, bf16[96,96]{1,0:T(8,128)(2,1)S(1)}, u32[]{:S(2)}, u32[]{:S(2)}) collective-permute-start(bf16[96,96]{1,0:T(8,128)(2,1)S(1)} %divide_convert_fusion.4), channel_id=1, source_target_pairs={{0,8},{1,9},{2,10},{3,11},{4,12},{5,13},{6,14},{7,15},{8,16},{9,17... | collective-permute-start | bytes 55304 | tf_op jit(solution)/shard_map/ppermute | solution.py:71
  36.5 8.6 %collective-permute-start.4 = (bf16[96,96]{1,0:T(8,128)(2,1)S(1)}, bf16[96,96]{1,0:T(8,128)(2,1)S(1)}, u32[]{:S(2)}, u32[]{:S(2)}) collective-permute-start(bf16[96,96]{1,0:T(8,128)(2,1)S(1)} %divide_convert_fusion.5), channel_id=1, source_target_pairs={{0,8},{1,9},{2,10},{3,11},{4,12},{5,13},{6,14},{7,15},{8,16},{9,17... | collective-permute-start | bytes 55304 | tf_op jit(solution)/shard_map/ppermute | solution.py:71
  36.6 11.3 %collective-permute-start.6 = (bf16[96,96]{1,0:T(8,128)(2,1)S(1)}, bf16[96,96]{1,0:T(8,128)(2,1)S(1)}, u32[]{:S(2)}, u32[]{:S(2)}) collective-permute-start(bf16[96,96]{1,0:T(8,128)(2,1)S(1)} %divide_convert_fusion.5), channel_id=1, source_target_pairs={{0,9},{1,10},{2,11},{3,12},{4,13},{5,14},{6,15},{7,8},{8,17},{9,18... | collective-permute-start | bytes 55304 | tf_op jit(solution)/shard_map/ppermute | solution.py:71
  43.3 1.8 %copy-start.3 = (bf16[1,1,96,1536]{3,2,1,0:T(8,128)(2,1)S(1)}, bf16[1,1,96,1536]{3,2,1,0:T(8,128)(2,1)}, u32[]{:S(2)}) copy-start(bf16[1,1,96,1536]{3,2,1,0:T(8,128)(2,1)} %param.12) | copy-start | bytes 884740
  43.4 1.9 %copy-start.8 = (bf16[96,1536]{1,0:T(8,128)(2,1)S(1)}, bf16[96,1536]{1,0:T(8,128)(2,1)}, u32[]{:S(2)}) copy-start(bf16[96,1536]{1,0:T(8,128)(2,1)} %copy-done.7) | copy-start | bytes 884740
  44.7 1.0 %copy-start.4 = (bf16[1,1,96,1536]{3,2,1,0:T(8,128)(2,1)S(1)}, bf16[1,1,96,1536]{3,2,1,0:T(8,128)(2,1)}, u32[]{:S(2)}) copy-start(bf16[1,1,96,1536]{3,2,1,0:T(8,128)(2,1)} %param.9) | copy-start | bytes 884740
  44.7 12.2 %collective-permute-start.9 = (bf16[96,1536]{1,0:T(8,128)(2,1)}, bf16[96,1536]{1,0:T(8,128)(2,1)}, u32[]{:S(2)}, u32[]{:S(2)}) collective-permute-start(bf16[96,1536]{1,0:T(8,128)(2,1)} %convert_element_type.57), channel_id=1, source_target_pairs={{0,8},{1,9},{2,10},{3,11},{4,12},{5,13},{6,14},{7,15},{8,16},{9,17... | collective-permute-start | bytes 884744 | tf_op jit(solution)/shard_map/ppermute | solution.py:71
  46.4 1.5 %copy-start.6 = (bf16[96,1536]{1,0:T(8,128)(2,1)S(1)}, bf16[96,1536]{1,0:T(8,128)(2,1)}, u32[]{:S(2)}) copy-start(bf16[96,1536]{1,0:T(8,128)(2,1)} %copy-done.5) | copy-start | bytes 884740
  55.7 12.6 %collective-permute-start.11 = (bf16[96,96]{1,0:T(8,128)(2,1)S(1)}, bf16[96,96]{1,0:T(8,128)(2,1)S(1)}, u32[]{:S(2)}, u32[]{:S(2)}) collective-permute-start(bf16[96,96]{1,0:T(8,128)(2,1)S(1)} %divide_convert_fusion.2), channel_id=1, source_target_pairs={{0,8},{1,9},{2,10},{3,11},{4,12},{5,13},{6,14},{7,15},{8,16},{9,17... | collective-permute-start | bytes 55304 | tf_op jit(solution)/shard_map/ppermute | solution.py:71
  64.2 1.9 %copy-start.1 = (f32[1536,96]{1,0:T(8,128)S(1)}, f32[1536,96]{1,0:T(8,128)}, u32[]{:S(2)}) copy-start(f32[1536,96]{1,0:T(8,128)} %reshape.119) | copy-start | bytes 1769476
  64.9 6.5 %collective-permute-start.10 = (bf16[96,1536]{1,0:T(8,128)(2,1)S(1)}, bf16[96,1536]{1,0:T(8,128)(2,1)S(1)}, u32[]{:S(2)}, u32[]{:S(2)}) collective-permute-start(bf16[96,1536]{1,0:T(8,128)(2,1)S(1)} %convert_element_type.60), channel_id=1, source_target_pairs={{0,8},{1,9},{2,10},{3,11},{4,12},{5,13},{6,14},{7,15},{8,16},{9,17... | collective-permute-start | bytes 884744 | tf_op jit(solution)/shard_map/ppermute | solution.py:71
  67.8 3.5 %collective-permute-start.8 = (bf16[96,96]{1,0:T(8,128)(2,1)S(1)}, bf16[96,96]{1,0:T(8,128)(2,1)S(1)}, u32[]{:S(2)}, u32[]{:S(2)}) collective-permute-start(bf16[96,96]{1,0:T(8,128)(2,1)S(1)} %divide_convert_fusion.3), channel_id=1, source_target_pairs={{0,8},{1,9},{2,10},{3,11},{4,12},{5,13},{6,14},{7,15},{8,16},{9,17... | collective-permute-start | bytes 55304 | tf_op jit(solution)/shard_map/ppermute | solution.py:71

commit v13 on v10

--- a/solution.py
+++ b/solution.py
@@ -41,7 +41,7 @@
     ys = []
     for b in range(count):
         y = y_ref[b]
-        ys.append(y / jnp.sqrt(jnp.sum(y * y) + 1e-06))
+        ys.append(y * lax.rsqrt(jnp.sum(y * y, keepdims=True) + 1e-06))
     for sweep in range(NS_ITERS):
         grams = [gram3(y) for y in ys]
         ys = [1.5 * y - 0.5 * dot3(g, y, ((1,), (0,))) for g, y in zip(grams, ys)]

time: 73.2 us -> 73.1 us (level)
  no operation moved by 1% of the time
where the time goes in v13:
time: 73.1 us; the launch traced here: 72.8 us
  Pallas kernels  19.5 us (27%)
  starting transfers between devices  17.3 us (24%)
  local copies, waits for them, and re-layouts  14.4 us (20%)
  matrix products  10.7 us (15%)
  between operations  5.39 us (7%)
  waiting for transfers between devices  3.02 us (4%)
  other arithmetic  2.62 us (4%)
    ppermute x12, starting transfers between devices, shifted(): return lax.ppermute(tree, ('gx', 'gy'), pairs)  17.3 us
    pallas_call x2, Pallas kernels, polar_factor_t(): pl.pallas_call(polar_kernel, out_shape=(jax.ShapeDtypeStruct(stack.shape,...  10.4 us
    pallas_call x2, Pallas kernels, edge_contract(): pl.pallas_call(edge_kernel, out_shape=jax.ShapeDtypeStruct((dd, n, LANES)...  9.04 us
    reshape x4, local copies, waits for them, and re-layouts, half(): jnp.dot(corner, edge, preferred_element_type=jnp.float32)  4.75 us
    dot_general x8, matrix products, half(): jnp.dot(corner, edge, preferred_element_type=jnp.float32)  3.72 us
    ppermute x12, waiting for transfers between devices, shifted(): return lax.ppermute(tree, ('gx', 'gy'), pairs)  3.02 us
    unnamed x29, local copies, waits for them, and re-layouts  2.5 us
    dot_general x2, matrix products, per_device(): new_low = jnp.dot(below_t, lower, precision=lax.Precision.HIGH)  2.09 us
  transfers between devices with their start and end apart: 12, of which 1 were waited for; matrix products, arithmetic and copies ran while one was open for 32% of the time, Pallas kernels for 20%

profile of v13, /device:TPU:0, one launch (start us, length us, event | category | flops | bytes accessed | tf_op | source)
XLA Modules:
  0.0 72.8 jit_solution(372935099759287865)
XLA Ops:
  0.7 6.1 %collective-permute-start.1 = (bf16[96,1536]{1,0:T(8,128)(2,1)}, bf16[96,1536]{1,0:T(8,128)(2,1)S(1)}, u32[]{:S(2)}, u32[]{:S(2)}) collective-permute-start(bf16[96,1536]{1,0:T(8,128)(2,1)} %bitcast.117), channel_id=1, source_target_pairs={{0,7},{1,0},{2,1},{3,2},{4,3},{5,4},{6,5},{7,6},{8,15},{9,8},{10,9... | collective-permute-start | bytes 884744 | tf_op jit(solution)/shard_map/ppermute | solution.py:71
  6.7 0.5 collective-permute-start
  7.2 1.5 %collective-permute-start.3 = (bf16[96,1536]{1,0:T(8,128)(2,1)}, bf16[96,1536]{1,0:T(8,128)(2,1)S(1)}, u32[]{:S(2)}, u32[]{:S(2)}) collective-permute-start(bf16[96,1536]{1,0:T(8,128)(2,1)} %bitcast.116), channel_id=1, source_target_pairs={{0,1},{1,2},{2,3},{3,4},{4,5},{5,6},{6,7},{7,0},{8,9},{9,10},{10,1... | collective-permute-start | bytes 884744 | tf_op jit(solution)/shard_map/ppermute | solution.py:71
  8.8 1.2 %fusion.93 = f32[96,1536]{1,0:T(8,128)S(1)} fusion(bf16[1,1,96,1536]{3,2,1,0:T(8,128)(2,1)} %param.12, bf16[1,1,96,96]{3,2,1,0:T(8,128)(2,1)} %param.11), kind=kOutput, calls=%fused_computation.149 | convolution fusion | flops 28311552 | bytes 903168 | tf_op jit(solution)/shard_map/dot_general | solution.py:175
  10.0 1.2 %fusion.88 = f32[96,1536]{1,0:T(8,128)S(1)} fusion(bf16[1,1,96,1536]{3,2,1,0:T(8,128)(2,1)} %param.9, bf16[1,1,96,96]{3,2,1,0:T(8,128)(2,1)} %param.8), kind=kOutput, calls=%fused_computation.144 | convolution fusion | flops 28311552 | bytes 903168 | tf_op jit(solution)/shard_map/dot_general | solution.py:175
  11.3 0.1 reshape_squeeze.14
  11.5 0.3 copy.18
  11.9 0.4 convolution_bitcast_fusion
  12.3 0.4 fusion.56
  12.7 0.2 convolution_bitcast_fusion.1
  12.9 0.6 compare_reduce_fusion
  13.6 0.9 %fusion.2 = bf16[2,4,4,4,4]{3,0,1,2,4:T(2,128)(2,1)S(1)} fusion(f32[2,2,1,1,1]{1,0,4,3,2:T(2,128)S(1)} %convolution_bitcast_fusion.1, pred[]{:T(512)} %compare_reduce_fusion, bf16[2,4,4,4,4]{4,3,2,1,0:T(4,128)(2,1)S(1)} %reshape_squeeze.14), kind=kOutput, calls=%fused_computation.10 | convolution fusion | flops 13824 | bytes 2065 | tf_op jit(solution)/shard_map/st,tabcd->sabcd/dot_general | solution.py:158
  14.5 0.3 copy.21
  14.9 0.4 fusion.24
  15.3 0.4 fusion.t_ref
  15.7 1.2 %reshape.117 = f32[1536,96]{1,0:T(8,128)} reshape(f32[96,1536]{1,0:T(8,128)S(1)} %fusion.93) | data formatting | bytes 1179648 | tf_op jit(solution)/shard_map/reshape | solution.py:175
  16.9 1.2 %reshape.118 = f32[1536,96]{1,0:T(8,128)} reshape(f32[96,1536]{1,0:T(8,128)S(1)} %fusion.88) | data formatting | bytes 1179648 | tf_op jit(solution)/shard_map/reshape | solution.py:175
  18.1 0.3 reshape_squeeze.12.wd_ref
  18.5 0.2 convolution_add_fusion.3
  18.7 0.3 add.132
  19.0 0.2 copy-done.7
  19.2 0.3 copy.13
  19.5 0.2 convolution_add_fusion.2
  19.7 0.3 add.134
  19.9 0.3 copy.14
  20.3 5.2 %shard_map.103 = (f32[2,96,1536]{2,1,0:T(8,128)S(1)}, bf16[2,96,1536]{2,1,0:T(8,128)(2,1)S(1)}) custom-call(f32[2,96,1536]{2,1,0:T(8,128)S(1)} %maximum_bitcast_fusion.y_ref), custom_call_target="tpu_custom_call" | custom-call | tf_op jit(solution)/shard_map/pallas_call | solution.py:54
  25.5 1.0 %multiply_reduce_fusion.4 = (f32[]{:T(128)}, f32[96,96]{1,0:T(8,128)S(1)}) fusion(f32[1536,96]{1,0:T(8,128)S(1)} %copy-done.3, f32[2,96,1536]{2,1,0:T(8,128)S(1)} %get-tuple-element.7), kind=kOutput, calls=%fused_computation.78 | convolution fusion | flops 84953088 | bytes 1413124 | tf_op jit(solution)/shard_map/dot_general | solution.py:184
  27.3 3.3 %collective-permute-start.5 = (bf16[96,96]{1,0:T(8,128)(2,1)S(1)}, bf16[96,96]{1,0:T(8,128)(2,1)S(1)}, u32[]{:S(2)}, u32[]{:S(2)}) collective-permute-start(bf16[96,96]{1,0:T(8,128)(2,1)S(1)} %divide_convert_fusion.4), channel_id=1, source_target_pairs={{0,15},{1,8},{2,9},{3,10},{4,11},{5,12},{6,13},{7,14},{8,23},{9,16... | collective-permute-start | bytes 55304 | tf_op jit(solution)/shard_map/ppermute | solution.py:71
  30.6 2.8 %collective-permute-start.7 = (bf16[96,96]{1,0:T(8,128)(2,1)S(1)}, bf16[96,96]{1,0:T(8,128)(2,1)S(1)}, u32[]{:S(2)}, u32[]{:S(2)}) collective-permute-start(bf16[96,96]{1,0:T(8,128)(2,1)S(1)} %divide_convert_fusion.4), channel_id=1, source_target_pairs={{0,8},{1,9},{2,10},{3,11},{4,12},{5,13},{6,14},{7,15},{8,16},{9,17... | collective-permute-start | bytes 55304 | tf_op jit(solution)/shard_map/ppermute | solution.py:71
  33.4 1.0 %multiply_reduce_fusion.5 = (f32[]{:T(128)}, f32[96,96]{1,0:T(8,128)S(1)}) fusion(f32[1536,96]{1,0:T(8,128)S(1)} %copy-done.2, f32[2,96,1536]{2,1,0:T(8,128)S(1)} %get-tuple-element.7), kind=kOutput, calls=%fused_computation.80 | convolution fusion | flops 84953088 | bytes 1413124 | tf_op jit(solution)/shard_map/dot_general | solution.py:185
  35.2 0.2 collective-permute-start.6
  35.5 0.2 copy.17
  35.8 0.1 copy.33
  35.9 4.5 %shard_map.105 = f32[16,96,128]{2,1,0:T(8,128)S(1)} custom-call(bf16[1536,96]{1,0:T(8,128)(2,1)S(1)} %reshape_squeeze.12.wd_ref, bf16[96,2048]{1,0:T(8,128)(2,1)S(1)} %bitcast.111, bf16[256,256]{1,0:T(8,128)(2,1)S(1)} %fusion.t_ref, bf16[96,1536]{1,0:T(8,128)(2,1)S(1)} %get-tuple-element.13.qt_ref), custom_call_target="tpu_custom_call" | custom-call | tf_op jit(solution)/shard_map/pallas_call | solution.py:115
  40.4 0.8 %multiply_reduce_fusion.1 = f32[]{:T(128)} fusion(f32[16,96,128]{2,1,0:T(8,128)S(1)} %shard_map.105), kind=kLoop, calls=%fused_computation.16 | loop fusion | flops 294911 | bytes 589828 | tf_op jit(solution)/shard_map/reduce_sum | solution.py:75
  42.0 0.2 copy.22
  42.2 1.1 %convert_element_type.57 = bf16[96,1536]{1,0:T(8,128)(2,1)} reshape(bf16[96,16,96]{2,1,0:T(8,128)(2,1)S(1)} %copy.22) | data formatting | bytes 589824 | tf_op jit(solution)/shard_map/convert_element_type | solution.py:192
  43.3 0.4 collective-permute-start.9
  43.7 0.2 fusion.91
  44.0 0.2 convolution_add_fusion.1
  44.3 0.2 fusion.86
  44.5 1.2 %reshape.125 = f32[1536,96]{1,0:T(8,128)} reshape(f32[96,1536]{1,0:T(8,128)S(1)} %fusion.91) | data formatting | bytes 1179648 | tf_op jit(solution)/shard_map/reshape | solution.py:175
  45.7 0.3 add.138
  46.0 0.3 copy.15
  46.2 1.2 %reshape.119 = f32[1536,96]{1,0:T(8,128)} reshape(f32[96,1536]{1,0:T(8,128)S(1)} %fusion.86) | data formatting | bytes 1179648 | tf_op jit(solution)/shard_map/reshape | solution.py:175
  47.4 0.2 convolution_add_fusion
  47.6 0.3 add.140
  47.9 0.3 copy.16
  48.3 5.2 %shard_map.104 = (f32[2,96,1536]{2,1,0:T(8,128)S(1)}, bf16[2,96,1536]{2,1,0:T(8,128)(2,1)S(1)}) custom-call(f32[2,96,1536]{2,1,0:T(8,128)S(1)} %maximum_bitcast_fusion.1.y_ref), custom_call_target="tpu_custom_call" | custom-call | tf_op jit(solution)/shard_map/pallas_call | solution.py:54
  53.5 1.0 %multiply_reduce_fusion.2 = (f32[]{:T(128)}, f32[96,96]{1,0:T(8,128)S(1)}) fusion(f32[1536,96]{1,0:T(8,128)S(1)} %copy-done.4, f32[2,96,1536]{2,1,0:T(8,128)S(1)} %get-tuple-element.8), kind=kOutput, calls=%fused_computation.74 | convolution fusion | flops 84953088 | bytes 1413124 | tf_op jit(solution)/shard_map/dot_general | solution.py:185
  55.3 0.7 collective-permute-start.11
  56.0 0.2 copy.23
  56.4 1.3 %reshape.123.wd_ref = bf16[1536,96]{1,0:T(8,128)(2,1)S(1)} reshape(bf16[96,1536]{1,0:T(8,128)(2,1)} %collective-permute-done.9) | data formatting | bytes 589824 | tf_op jit(solution)/shard_map/reshape | solution.py:111
  57.8 4.5 %shard_map.106 = f32[16,96,128]{2,1,0:T(8,128)S(1)} custom-call(bf16[1536,96]{1,0:T(8,128)(2,1)S(1)} %reshape.123.wd_ref, bf16[96,2048]{1,0:T(8,128)(2,1)S(1)} %bitcast.110, bf16[256,256]{1,0:T(8,128)(2,1)S(1)} %fusion.t_ref, bf16[96,1536]{1,0:T(8,128)(2,1)S(1)} %get-tuple-element.11.qt_ref), custom_call_target="tpu_custom_call" | custom-call | tf_op jit(solution)/shard_map/pallas_call | solution.py:115
  62.3 0.8 %multiply_reduce_fusion = f32[]{:T(128)} fusion(f32[16,96,128]{2,1,0:T(8,128)S(1)} %shard_map.106), kind=kLoop, calls=%fused_computation.14 | loop fusion | flops 294911 | bytes 589828 | tf_op jit(solution)/shard_map/reduce_sum | solution.py:75
  63.9 0.2 copy.24
  64.0 0.4 convert_element_type.60
  64.4 1.2 %collective-permute-start.10 = (bf16[96,1536]{1,0:T(8,128)(2,1)S(1)}, bf16[96,1536]{1,0:T(8,128)(2,1)S(1)}, u32[]{:S(2)}, u32[]{:S(2)}) collective-permute-start(bf16[96,1536]{1,0:T(8,128)(2,1)S(1)} %convert_element_type.60), channel_id=1, source_target_pairs={{0,8},{1,9},{2,10},{3,11},{4,12},{5,13},{6,14},{7,15},{8,16},{9,17... | collective-permute-start | bytes 884744 | tf_op jit(solution)/shard_map/ppermute | solution.py:71
  65.6 1.0 %multiply_reduce_fusion.3 = (f32[]{:T(128)}, f32[96,96]{1,0:T(8,128)S(1)}) fusion(f32[1536,96]{1,0:T(8,128)S(1)} %copy-done.1, f32[2,96,1536]{2,1,0:T(8,128)S(1)} %get-tuple-element.8), kind=kOutput, calls=%fused_computation.76 | convolution fusion | flops 84953088 | bytes 1413124 | tf_op jit(solution)/shard_map/dot_general | solution.py:184
  67.4 0.5 collective-permute-start.8
  67.9 3.0 %collective-permute-done.8 = bf16[96,96]{1,0:T(8,128)(2,1)S(1)} collective-permute-done((bf16[96,96]{1,0:T(8,128)(2,1)S(1)}, bf16[96,96]{1,0:T(8,128)(2,1)S(1)}, u32[]{:S(2)}, u32[]{:S(2)}) %collective-permute-start.8) | collective-permute-done | bytes 18464 | tf_op jit(solution)/shard_map/ppermute | solution.py:71
  70.9 0.6 copy.37
  71.5 0.7 copy.38
  72.2 0.6 copy.39
  (57 shorter events, 1.2 us)
Async XLA Ops:
  0.6 12.1 %copy-start = (f32[2,2]{1,0:T(2,128)S(1)}, f32[2,2]{1,0:T(2,128)}, u32[]{:S(2)}) copy-start(f32[2,2]{1,0:T(2,128)} %param.14) | copy-start | bytes 52
  0.6 10.7 %copy-start.10 = (bf16[1,1,2,256]{3,2,1,0:T(2,128)(2,1)S(1)}, bf16[1,1,2,256]{3,2,1,0:T(2,128)(2,1)}, u32[]{:S(2)}) copy-start(bf16[1,1,2,256]{3,2,1,0:T(2,128)(2,1)} %param.13) | copy-start | bytes 3076
  0.7 17.8 %collective-permute-start.1 = (bf16[96,1536]{1,0:T(8,128)(2,1)}, bf16[96,1536]{1,0:T(8,128)(2,1)S(1)}, u32[]{:S(2)}, u32[]{:S(2)}) collective-permute-start(bf16[96,1536]{1,0:T(8,128)(2,1)} %bitcast.117), channel_id=1, source_target_pairs={{0,7},{1,0},{2,1},{3,2},{4,3},{5,4},{6,5},{7,6},{8,15},{9,8},{10,9... | collective-permute-start | bytes 884744 | tf_op jit(solution)/shard_map/ppermute | solution.py:71
  6.7 11.7 %collective-permute-start = (bf16[96,96]{1,0:T(8,128)(2,1)}, bf16[96,96]{1,0:T(8,128)(2,1)S(1)}, u32[]{:S(2)}, u32[]{:S(2)}) collective-permute-start(bf16[96,96]{1,0:T(8,128)(2,1)} %bitcast.122), channel_id=1, source_target_pairs={{0,7},{1,0},{2,1},{3,2},{4,3},{5,4},{6,5},{7,6},{8,15},{9,8},{10,9... | collective-permute-start | bytes 55304 | tf_op jit(solution)/shard_map/ppermute | solution.py:71
  7.2 12.2 %collective-permute-start.3 = (bf16[96,1536]{1,0:T(8,128)(2,1)}, bf16[96,1536]{1,0:T(8,128)(2,1)S(1)}, u32[]{:S(2)}, u32[]{:S(2)}) collective-permute-start(bf16[96,1536]{1,0:T(8,128)(2,1)} %bitcast.116), channel_id=1, source_target_pairs={{0,1},{1,2},{2,3},{3,4},{4,5},{5,6},{6,7},{7,0},{8,9},{9,10},{10,1... | collective-permute-start | bytes 884744 | tf_op jit(solution)/shard_map/ppermute | solution.py:71
  8.8 10.7 %collective-permute-start.2 = (bf16[96,96]{1,0:T(8,128)(2,1)}, bf16[96,96]{1,0:T(8,128)(2,1)S(1)}, u32[]{:S(2)}, u32[]{:S(2)}) collective-permute-start(bf16[96,96]{1,0:T(8,128)(2,1)} %bitcast.123), channel_id=1, source_target_pairs={{0,1},{1,2},{2,3},{3,4},{4,5},{5,6},{6,7},{7,0},{8,9},{9,10},{10,1... | collective-permute-start | bytes 55304 | tf_op jit(solution)/shard_map/ppermute | solution.py:71
  10.0 2.9 %copy-start.11 = (s32[4]{0:T(128)S(1)}, s32[4]{0:T(128)}, u32[]{:S(2)}) copy-start(s32[4]{0:T(128)} %param.15) | copy-start | bytes 52
  15.7 2.4 %copy-start.9 = (bf16[1,1,96,1536]{3,2,1,0:T(8,128)(2,1)S(1)}, bf16[1,1,96,1536]{3,2,1,0:T(8,128)(2,1)}, u32[]{:S(2)}) copy-start(bf16[1,1,96,1536]{3,2,1,0:T(8,128)(2,1)} %param.10) | copy-start | bytes 884740
  18.5 0.7 copy-start.7
  20.2 5.3 %copy-start.3 = (f32[1536,96]{1,0:T(8,128)S(1)}, f32[1536,96]{1,0:T(8,128)}, u32[]{:S(2)}) copy-start(f32[1536,96]{1,0:T(8,128)} %reshape.118) | copy-start | bytes 1769476
  20.3 13.1 %copy-start.2 = (f32[1536,96]{1,0:T(8,128)S(1)}, f32[1536,96]{1,0:T(8,128)}, u32[]{:S(2)}) copy-start(f32[1536,96]{1,0:T(8,128)} %reshape.117) | copy-start | bytes 1769476
  27.3 16.7 %collective-permute-start.5 = (bf16[96,96]{1,0:T(8,128)(2,1)S(1)}, bf16[96,96]{1,0:T(8,128)(2,1)S(1)}, u32[]{:S(2)}, u32[]{:S(2)}) collective-permute-start(bf16[96,96]{1,0:T(8,128)(2,1)S(1)} %divide_convert_fusion.4), channel_id=1, source_target_pairs={{0,15},{1,8},{2,9},{3,10},{4,11},{5,12},{6,13},{7,14},{8,23},{9,16... | collective-permute-start | bytes 55304 | tf_op jit(solution)/shard_map/ppermute | solution.py:71
  30.6 13.6 %collective-permute-start.7 = (bf16[96,96]{1,0:T(8,128)(2,1)S(1)}, bf16[96,96]{1,0:T(8,128)(2,1)S(1)}, u32[]{:S(2)}, u32[]{:S(2)}) collective-permute-start(bf16[96,96]{1,0:T(8,128)(2,1)S(1)} %divide_convert_fusion.4), channel_id=1, source_target_pairs={{0,8},{1,9},{2,10},{3,11},{4,12},{5,13},{6,14},{7,15},{8,16},{9,17... | collective-permute-start | bytes 55304 | tf_op jit(solution)/shard_map/ppermute | solution.py:71
  35.1 8.6 %collective-permute-start.4 = (bf16[96,96]{1,0:T(8,128)(2,1)S(1)}, bf16[96,96]{1,0:T(8,128)(2,1)S(1)}, u32[]{:S(2)}, u32[]{:S(2)}) collective-permute-start(bf16[96,96]{1,0:T(8,128)(2,1)S(1)} %divide_convert_fusion.5), channel_id=1, source_target_pairs={{0,8},{1,9},{2,10},{3,11},{4,12},{5,13},{6,14},{7,15},{8,16},{9,17... | collective-permute-start | bytes 55304 | tf_op jit(solution)/shard_map/ppermute | solution.py:71
  35.2 12.2 %collective-permute-start.6 = (bf16[96,96]{1,0:T(8,128)(2,1)S(1)}, bf16[96,96]{1,0:T(8,128)(2,1)S(1)}, u32[]{:S(2)}, u32[]{:S(2)}) collective-permute-start(bf16[96,96]{1,0:T(8,128)(2,1)S(1)} %divide_convert_fusion.5), channel_id=1, source_target_pairs={{0,9},{1,10},{2,11},{3,12},{4,13},{5,14},{6,15},{7,8},{8,17},{9,18... | collective-permute-start | bytes 55304 | tf_op jit(solution)/shard_map/ppermute | solution.py:71
  41.9 1.8 %copy-start.5 = (bf16[1,1,96,1536]{3,2,1,0:T(8,128)(2,1)S(1)}, bf16[1,1,96,1536]{3,2,1,0:T(8,128)(2,1)}, u32[]{:S(2)}) copy-start(bf16[1,1,96,1536]{3,2,1,0:T(8,128)(2,1)} %param.12) | copy-start | bytes 884740
  42.0 1.9 %copy-start.8 = (bf16[96,1536]{1,0:T(8,128)(2,1)S(1)}, bf16[96,1536]{1,0:T(8,128)(2,1)}, u32[]{:S(2)}) copy-start(bf16[96,1536]{1,0:T(8,128)(2,1)} %copy-done.7) | copy-start | bytes 884740
  43.3 1.0 %copy-start.6 = (bf16[1,1,96,1536]{3,2,1,0:T(8,128)(2,1)S(1)}, bf16[1,1,96,1536]{3,2,1,0:T(8,128)(2,1)}, u32[]{:S(2)}) copy-start(bf16[1,1,96,1536]{3,2,1,0:T(8,128)(2,1)} %param.9) | copy-start | bytes 884740
  43.3 13.1 %collective-permute-start.9 = (bf16[96,1536]{1,0:T(8,128)(2,1)}, bf16[96,1536]{1,0:T(8,128)(2,1)}, u32[]{:S(2)}, u32[]{:S(2)}) collective-permute-start(bf16[96,1536]{1,0:T(8,128)(2,1)} %convert_element_type.57), channel_id=1, source_target_pairs={{0,8},{1,9},{2,10},{3,11},{4,12},{5,13},{6,14},{7,15},{8,16},{9,17... | collective-permute-start | bytes 884744 | tf_op jit(solution)/shard_map/ppermute | solution.py:71
  48.3 5.2 %copy-start.4 = (f32[1536,96]{1,0:T(8,128)S(1)}, f32[1536,96]{1,0:T(8,128)}, u32[]{:S(2)}) copy-start(f32[1536,96]{1,0:T(8,128)} %reshape.125) | copy-start | bytes 1769476
  55.3 12.6 %collective-permute-start.11 = (bf16[96,96]{1,0:T(8,128)(2,1)S(1)}, bf16[96,96]{1,0:T(8,128)(2,1)S(1)}, u32[]{:S(2)}, u32[]{:S(2)}) collective-permute-start(bf16[96,96]{1,0:T(8,128)(2,1)S(1)} %divide_convert_fusion.2), channel_id=1, source_target_pairs={{0,8},{1,9},{2,10},{3,11},{4,12},{5,13},{6,14},{7,15},{8,16},{9,17... | collective-permute-start | bytes 55304 | tf_op jit(solution)/shard_map/ppermute | solution.py:71
  63.8 1.9 %copy-start.1 = (f32[1536,96]{1,0:T(8,128)S(1)}, f32[1536,96]{1,0:T(8,128)}, u32[]{:S(2)}) copy-start(f32[1536,96]{1,0:T(8,128)} %reshape.119) | copy-start | bytes 1769476
  64.4 6.5 %collective-permute-start.10 = (bf16[96,1536]{1,0:T(8,128)(2,1)S(1)}, bf16[96,1536]{1,0:T(8,128)(2,1)S(1)}, u32[]{:S(2)}, u32[]{:S(2)}) collective-permute-start(bf16[96,1536]{1,0:T(8,128)(2,1)S(1)} %convert_element_type.60), channel_id=1, source_target_pairs={{0,8},{1,9},{2,10},{3,11},{4,12},{5,13},{6,14},{7,15},{8,16},{9,17... | collective-permute-start | bytes 884744 | tf_op jit(solution)/shard_map/ppermute | solution.py:71
  67.4 3.5 %collective-permute-start.8 = (bf16[96,96]{1,0:T(8,128)(2,1)S(1)}, bf16[96,96]{1,0:T(8,128)(2,1)S(1)}, u32[]{:S(2)}, u32[]{:S(2)}) collective-permute-start(bf16[96,96]{1,0:T(8,128)(2,1)S(1)} %divide_convert_fusion.3), channel_id=1, source_target_pairs={{0,8},{1,9},{2,10},{3,11},{4,12},{5,13},{6,14},{7,15},{8,16},{9,17... | collective-permute-start | bytes 55304 | tf_op jit(solution)/shard_map/ppermute | solution.py:71
